TPU v7x, 32 devices: a whole 2x2x4 slice. The times are simulated.
32 devices in a mesh: ctx: 8 (over z, x), head: 4 (over y, core).
Axes of the slice: x: 2, y: 2, z: 4, core: 2. Of those that a mesh axis runs over, the one named last changes fastest.
Arguments:
- queries: bfloat16 [4096, 2048], P('ctx', 'head'), may hold values from -50 to 50
- keys: bfloat16 [4096, 2048], P('ctx', 'head'), may hold values from -4 to 4
- values: bfloat16 [4096, 2048], P('ctx', 'head'), may hold values from -6 to 6
- out_weight: bfloat16 [2048, 2048], P('head'), may hold values from -0.125 to 0.125
- d_out: bfloat16 [4096, 2048], P('ctx', 'head'), may hold values from -6 to 6
- window: int32 [32], replicated, may hold values from 0 to 3
- far_select: int32 [32, 5], replicated, may hold values 0 or 1
Outputs:
- output: bfloat16 [4096, 2048], P('ctx', 'head')
- d_queries: bfloat16 [4096, 2048], P('ctx', 'head')
- d_keys: bfloat16 [4096, 2048], P('ctx', 'head')
- d_values: bfloat16 [4096, 2048], P('ctx', 'head')
All inputs are finite; a program needn't handle non-finite values.
Results may differ from a plain program's by a relative error of at most 0.04.
Values may be sent and summed in bfloat16 or wider, within the bound.
No kernel may reach another device: no remote copies, remote signals or barrier semaphores. Data moves between devices by JAX's collectives and lax.ppermute only.
A program may use at most 128 MiB of HBM per device.

v0:
```python
import jax
import jax.numpy as jnp
from jax import lax
from jax.sharding import PartitionSpec as P

HD = 128
BLK = 128
WIN_MAX = 3
LEVELS = 5
NB = 4


neg_large = -1e30


def passed_along(block, axis, distance):
    devices = range(lax.axis_size(axis))
    route = [(i - distance, i) for i in devices if i - distance in devices]
    return lax.ppermute(block, axis, route)


def full_mask(valid, block_width):
    grid_shape = (block_width, valid.shape[1], block_width)
    query_pos = lax.broadcasted_iota(jnp.int32, grid_shape, 0)
    key_pos = lax.broadcasted_iota(jnp.int32, grid_shape, 2)
    candidate = lax.broadcasted_iota(jnp.int32, grid_shape, 1)
    inside = (key_pos <= query_pos) | (candidate > 0)
    return valid[:, None, None, :, None] & inside[None, None]


def scores_of(queries, keys, allowed):
    score_scale = queries.shape[-1] ** (-0.5)
    raw_scores = (
        jnp.einsum("nqhe,nckhe->nhqck", queries, keys, preferred_element_type=jnp.float32)
        * score_scale
    )
    return jnp.where(allowed, raw_scores, neg_large)


def attend(queries, keys, values, allowed):
    scores = scores_of(queries, keys, allowed)
    row_max = jnp.max(scores, axis=(3, 4), keepdims=True)
    row_total = jnp.sum(jnp.exp(scores - row_max), axis=(3, 4), keepdims=True)
    log_total = row_max + jnp.log(row_total)
    weights = jnp.exp(scores - log_total).astype(jnp.bfloat16)
    attended = jnp.einsum("nhqck,nckhe->nqhe", weights, values, preferred_element_type=jnp.float32)
    return (attended.astype(jnp.bfloat16), log_total[:, :, :, 0, 0])


def attend_grads(queries, d_att, log_total, delta, keys, values, allowed):
    score_scale = queries.shape[-1] ** (-0.5)
    scores = scores_of(queries, keys, allowed)
    probabilities = jnp.exp(scores - log_total[:, :, :, None, None])
    weights = probabilities.astype(jnp.bfloat16)
    value_grad = jnp.einsum("nhqck,nqhe->nckhe", weights, d_att, preferred_element_type=jnp.float32)
    d_prob = jnp.einsum("nqhe,nckhe->nhqck", d_att, values, preferred_element_type=jnp.float32)
    d_score = (probabilities * (d_prob - delta[:, :, :, None, None]) * score_scale).astype(
        jnp.bfloat16
    )
    query_grad = jnp.einsum("nhqck,nckhe->nqhe", d_score, keys, preferred_element_type=jnp.float32)
    key_grad = jnp.einsum("nhqck,nqhe->nckhe", d_score, queries, preferred_element_type=jnp.float32)
    return (query_grad, key_grad, value_grad)


def row_delta(d_att, attended):
    summed = jnp.sum(d_att.astype(jnp.float32) * attended.astype(jnp.float32), axis=3)
    return jnp.transpose(summed, (0, 2, 1))


def window_spread(grads, first):
    spread = None
    for offset in range(1, WIN_MAX + 1):
        padded = jnp.pad(
            grads[:, first + offset - 1], ((NB - offset, offset), (0, 0), (0, 0), (0, 0))
        )
        spread = padded if spread is None else spread + padded
    return spread


def local(queries, keys, values, out_weight, d_out, window, far_select):
    tokens_local = queries.shape[0]
    heads_local = queries.shape[1] // HD
    ctx_count = lax.axis_size("ctx")
    ctx_index = lax.axis_index("ctx")
    block_shape = (NB, BLK, heads_local, HD)
    query_blocks = queries.reshape(block_shape)
    key_blocks = keys.reshape(block_shape)
    value_blocks = values.reshape(block_shape)
    local_ids = jnp.arange(NB, dtype=jnp.int32)
    block_ids = ctx_index * NB + local_ids
    own_window = lax.dynamic_slice_in_dim(window, ctx_index * NB, NB, 0)
    own_select = lax.dynamic_slice_in_dim(far_select, ctx_index * NB, NB, 0)
    fetched = []
    for exponent in range(LEVELS):
        if 2**exponent < ctx_count:
            fetched.append(passed_along((key_blocks, value_blocks), "ctx", 2**exponent))
        else:
            fetched.append((jnp.zeros_like(key_blocks), jnp.zeros_like(value_blocks)))

    def stack_side(own_rows, previous, distant):
        extended = jnp.concatenate([previous, own_rows], axis=0)
        pieces = (
            [own_rows]
            + [extended[NB - offset : 2 * NB - offset] for offset in range(1, WIN_MAX + 1)]
            + distant
        )
        return jnp.stack(pieces, axis=1)

    cand_keys = stack_side(key_blocks, fetched[0][0], [pair[0] for pair in fetched])
    cand_values = stack_side(value_blocks, fetched[0][1], [pair[1] for pair in fetched])
    valid_cols = [block_ids >= 0]
    for offset in range(1, WIN_MAX + 1):
        valid_cols.append((offset <= own_window) & (block_ids - offset >= 0))
    for exponent in range(LEVELS):
        valid_cols.append((own_select[:, exponent] == 1) & (block_ids - NB * 2**exponent >= 0))
    allowed = full_mask(jnp.stack(valid_cols, axis=1), BLK)
    attended, log_total = attend(query_blocks, cand_keys, cand_values, allowed)
    attended_flat = attended.reshape(tokens_local, heads_local * HD)
    partial_out = jnp.dot(attended_flat, out_weight, preferred_element_type=jnp.float32)
    output = lax.psum_scatter(
        partial_out.astype(jnp.bfloat16), "head", scatter_dimension=1, tiled=True
    )
    grad_att = lax.dot_general(
        lax.all_gather(d_out, "head", axis=1, tiled=True),
        out_weight,
        (((1,), (1,)), ((), ())),
        preferred_element_type=jnp.float32,
    )
    grad_blocks = grad_att.astype(jnp.bfloat16).reshape(block_shape)
    delta = row_delta(grad_blocks, attended)
    query_grad, key_grad, value_grad = attend_grads(
        query_blocks, grad_blocks, log_total, delta, cand_keys, cand_values, allowed
    )
    key_spread = window_spread(key_grad, 1)
    value_spread = window_spread(value_grad, 1)
    key_total = key_grad[:, 0] + key_spread[NB:]
    value_total = value_grad[:, 0] + value_spread[NB:]
    send_keys = [key_spread[:NB] + key_grad[:, 1 + WIN_MAX]]
    send_values = [value_spread[:NB] + value_grad[:, 1 + WIN_MAX]]
    for exponent in range(1, LEVELS):
        send_keys.append(key_grad[:, 1 + WIN_MAX + exponent])
        send_values.append(value_grad[:, 1 + WIN_MAX + exponent])
    for exponent in range(LEVELS):
        if 2**exponent < ctx_count:
            back_keys, back_values = (
                passed_along(
                    send_keys[exponent].astype(jnp.bfloat16), "ctx", -(2**exponent)
                ).astype(jnp.float32),
                passed_along(
                    send_values[exponent].astype(jnp.bfloat16), "ctx", -(2**exponent)
                ).astype(jnp.float32),
            )
            key_total = key_total + back_keys
            value_total = value_total + back_values
    flat_shape = (tokens_local, heads_local * HD)
    return (
        output,
        query_grad.reshape(flat_shape).astype(jnp.bfloat16),
        key_total.reshape(flat_shape).astype(jnp.bfloat16),
        value_total.reshape(flat_shape).astype(jnp.bfloat16),
    )


def solution(mesh):
    return jax.shard_map(
        local,
        mesh=mesh,
        in_specs=(
            P("ctx", "head"),
            P("ctx", "head"),
            P("ctx", "head"),
            P("head", None),
            P("ctx", "head"),
            P(),
            P(),
        ),
        out_specs=(P("ctx", "head"), P("ctx", "head"), P("ctx", "head"), P("ctx", "head")),
        check_vma=False,
    )
```

profile of v0, /device:TPU:10, one launch (start us, length us, event | category | flops | bytes accessed | tf_op | source)
XLA Modules:
  0.0 251.2 jit_solution(12330333361425862586)
XLA Ops:
  7.2 1.3 reshape.103
  8.6 0.9 copy.87
  9.4 3.5 %collective-permute-start.1 = (bf16[4,128,4,128]{3,1,2,0:T(8,128)(2,1)}, bf16[4,128,4,128]{3,1,2,0:T(8,128)(2,1)}, u32[]{:S(2)}, u32[]{:S(2)}) collective-permute-start(bf16[4,128,4,128]{3,1,2,0:T(8,128)(2,1)} %copy.87), channel_id=1, source_target_pairs={{0,8},{4,12},{8,16},{12,20},{16,24},{20,28},{1,9},{5,13},{9,17},{1... | collective-permute-start | bytes 1572872 | tf_op jit(solution)/shard_map/ppermute | solution.py:19
  12.9 3.1 %collective-permute-start.2 = (bf16[4,128,4,128]{3,1,2,0:T(8,128)(2,1)}, bf16[4,128,4,128]{3,1,2,0:T(8,128)(2,1)}, u32[]{:S(2)}, u32[]{:S(2)}) collective-permute-start(bf16[4,128,4,128]{3,1,2,0:T(8,128)(2,1)} %copy.87), channel_id=1, source_target_pairs={{0,16},{4,20},{8,24},{12,28},{1,17},{5,21},{9,25},{13,29},{2,18},{... | collective-permute-start | bytes 1572872 | tf_op jit(solution)/shard_map/ppermute | solution.py:19
  16.0 1.9 collective-permute-start
  18.0 1.2 reshape.104
  19.1 1.0 copy.99
  20.1 1.9 collective-permute-start.4
  22.0 3.1 %collective-permute-start.3 = (bf16[4,128,4,128]{3,1,2,0:T(8,128)(2,1)}, bf16[4,128,4,128]{3,1,2,0:T(8,128)(2,1)}, u32[]{:S(2)}, u32[]{:S(2)}) collective-permute-start(bf16[4,128,4,128]{3,1,2,0:T(8,128)(2,1)} %copy.99), channel_id=1, source_target_pairs={{0,4},{4,8},{8,12},{12,16},{16,20},{20,24},{24,28},{1,5},{5,9},{9,... | collective-permute-start | bytes 1572872 | tf_op jit(solution)/shard_map/ppermute | solution.py:19
  25.3 2.0 stack_reshape.6
  27.9 2.0 copy_dynamic-update-slice_fusion.1
  30.0 2.0 stack_reshape.7
  32.3 2.0 reshape.105
  34.4 1.3 copy_dynamic-update-slice_fusion
  35.7 0.3 broadcast_and_fusion
  36.0 55.8 %collective-permute-done.3 = bf16[4,128,4,128]{3,1,2,0:T(8,128)(2,1)} collective-permute-done((bf16[4,128,4,128]{3,1,2,0:T(8,128)(2,1)}, bf16[4,128,4,128]{3,1,2,0:T(8,128)(2,1)}, u32[]{:S(2)}, u32[]{:S(2)}) %collective-permute-start.3) | collective-permute-done | bytes 524320 | tf_op jit(solution)/shard_map/ppermute | solution.py:19
  91.9 1.5 collective-permute-start.5
  93.4 1.1 constant_dynamic-update-slice_fusion.3
  94.4 1.2 constant_dynamic-update-slice_fusion.2
  95.7 1.1 constant_dynamic-update-slice_fusion.1
  97.4 1.2 bitcast_dynamic-update-slice_fusion.5
  98.6 1.1 bitcast_dynamic-update-slice_fusion.4
  99.7 1.1 bitcast_dynamic-update-slice_fusion.3
  100.9 0.3 broadcast_dynamic-update-slice_fusion.1
  101.2 1.5 bitcast_dynamic-update-slice_fusion.2
  102.7 1.4 bitcast_dynamic-update-slice_fusion.1
  104.2 0.3 broadcast_dynamic-update-slice_fusion
  104.6 1.8 fusion.1
  106.3 0.4 copy-done.6
  106.7 2.1 exponential_reduce_fusion
  108.8 1.6 copy-done.2
  110.4 3.7 %convolution_convert_fusion.1 = bf16[512,512]{1,0:T(8,128)(2,1)} fusion(bf16[512,2048]{1,0:T(8,128)(2,1)} %all-gather.2.cloned.1.call-done, bf16[512,2048]{1,0:T(8,128)(2,1)S(1)} %copy-done), kind=kOutput, calls=%fused_computation.15 | convolution fusion | flops 1074003968 | bytes 4718592 | tf_op jit(solution)/shard_map/dot_general | solution.py:123
  114.0 1.2 reshape.107
  115.2 1.0 copy.112
  116.3 1.0 copy.144
  117.3 8.8 %multiply_reduce_fusion = (f32[4,128,4]{1,2,0:T(4,128)S(1)}, bf16[4,128,4,128]{1,3,2,0:T(8,128)(2,1)S(1)}) fusion(bf16[4,128,4,128]{1,3,2,0:T(8,128)(2,1)} %copy.112, bf16[4,9,128,4,128]{4,2,1,3,0:T(8,128)(2,1)} %copy-done.12, f32[4,4,9,128,128]{4,3,2,1,0:T(8,128)} %copy-done.2, f32[4,4,128]{2,1,0:T(4,128)S(1)} %bitcast.211, ...), kind=kOutput, calls=%fused_computation.43 | convolution fusion | flops 614725632 | bytes 15810560 | tf_op jit(solution)/shard_map/nhqck,nckhe->nqhe/dot_general | solution.py:46
  126.1 1.1 copy.110
  127.2 3.9 %convolution_convert_fusion = bf16[512,2048]{1,0:T(8,128)(2,1)} fusion(bf16[512,2048]{1,0:T(8,128)(2,1)S(1)} %copy-done, bf16[64,8,4,128]{3,2,1,0:T(4,128)(2,1)} %bitcast.210), kind=kOutput, calls=%fused_computation.8 | convolution fusion | flops 1074790400 | bytes 4718592 | tf_op jit(solution)/shard_map/dot_general | solution.py:119
  131.1 10.4 %fusion.40 = (bf16[4,9,128,4,128]{2,4,1,3,0:T(8,128)(2,1)S(1)}, f32[4,9,128,4,128]{2,4,1,3,0:T(8,128)}) fusion(bf16[4,128,4,128,1]{1,3,4,2,0:T(8,128)(2,1)S(1)} %copy-done.10, f32[4,4,9,128,128]{4,3,2,1,0:T(8,128)} %copy-done.2, f32[4,4,128]{2,1,0:T(4,128)S(1)} %bitcast.212, pred[4,128,9,128]{1,3,2,0:T(8,128)(4,1)S(1)} %broadcast_and_fusion), kind=kOutput, calls=%fused_computation.105 | convolution fusion | flops 615776256 | bytes 24715264 | tf_op jit(solution)/shard_map/nhqck,nqhe->nckhe/dot_general | solution.py:55
  141.5 1.1 slice_bitcast_fusion.11
  142.6 1.9 collective-permute-start.10
  144.6 1.3 collective-permute-start.11
  145.9 2.2 slice_bitcast_fusion.3
  148.0 0.2 pad_add_fusion
  148.2 2.9 %fusion.7 = bf16[4,128,4,128]{1,3,2,0:T(8,128)(2,1)} fusion(f32[4,9,128,4,128]{2,4,1,3,0:T(8,128)} %get-tuple-element.29, f32[8,128,4,128]{1,3,2,0:T(8,128)S(1)} %pad_add_fusion), kind=kLoop, calls=%fused_computation.21 | loop fusion | flops 524288 | bytes 2621440 | tf_op jit(solution)/shard_map/convert_element_type | solution.py:150
  151.2 8.0 %collective-permute-start.9 = (bf16[4,128,4,128]{1,3,2,0:T(8,128)(2,1)}, bf16[4,128,4,128]{1,3,2,0:T(8,128)(2,1)}, u32[]{:S(2)}, u32[]{:S(2)}) collective-permute-start(bf16[4,128,4,128]{1,3,2,0:T(8,128)(2,1)} %fusion.7), channel_id=1, source_target_pairs={{4,0},{8,4},{12,8},{16,12},{20,16},{24,20},{28,24},{5,1},{9,5},{13... | collective-permute-start | bytes 1572872 | tf_op jit(solution)/shard_map/ppermute | solution.py:19
  159.2 8.2 %multiply_convert_fusion = bf16[4,4,128,9,128]{2,4,3,1,0:T(8,128)(2,1)} fusion(f32[4,4,9,128,128]{4,3,2,1,0:T(8,128)S(1)} %bitcast.196, f32[4,4,128]{2,1,0:T(4,128)S(1)} %bitcast.216, f32[4,4,128]{2,1,0:T(4,128)S(1)} %bitcast.213, pred[4,128,9,128]{1,3,2,0:T(8,128)(4,1)S(1)} %broadcast_and_fusion, bf16[4,128,4,128,1]{1,3,4,2,0:T(8,128)(2,1)} %copy.144, ...), kind=kOutput, calls=%fused_computation.1 | convolution fusion | flops 620494848 | bytes 20004864 | tf_op jit(solution)/shard_map/nqhe,nckhe->nhqck/dot_general | solution.py:56
  167.3 3.2 %fusion.39 = (bf16[4,9,128,4,128]{4,2,1,3,0:T(8,128)(2,1)S(1)}, f32[4,9,128,4,128]{4,2,1,3,0:T(8,128)S(1)}) fusion(bf16[4,4,128,9,128]{2,4,3,1,0:T(8,128)(2,1)} %multiply_convert_fusion, bf16[4,128,4,128,1]{3,2,1,0,4:T(4,128)(2,1)S(1)} %bitcast.203), kind=kOutput, calls=%fused_computation.104 | convolution fusion | flops 606339072 | bytes 19398656 | tf_op jit(solution)/shard_map/nhqck,nqhe->nckhe/dot_general | solution.py:61
  170.6 1.1 slice_bitcast_fusion.13
  171.6 2.3 collective-permute-start.7
  174.0 1.6 collective-permute-start.8
  176.0 0.9 fusion.13
  176.9 2.5 collective-permute-start.6
  179.5 1.6 fusion.4
  181.1 0.3 copy.116
  181.4 0.9 copy.197
  182.3 25.8 %collective-permute-done.9 = bf16[4,128,4,128]{1,3,2,0:T(8,128)(2,1)} collective-permute-done((bf16[4,128,4,128]{1,3,2,0:T(8,128)(2,1)}, bf16[4,128,4,128]{1,3,2,0:T(8,128)(2,1)}, u32[]{:S(2)}, u32[]{:S(2)}) %collective-permute-start.9) | collective-permute-done | bytes 524320 | tf_op jit(solution)/shard_map/ppermute | solution.py:19
  208.1 2.5 fusion.11
  210.6 0.3 copy.133
  210.9 0.9 copy.195
  211.8 29.0 %collective-permute-done.6 = bf16[4,128,4,128]{3,1,2,0:T(8,128)(2,1)} collective-permute-done((bf16[4,128,4,128]{3,1,2,0:T(8,128)(2,1)}, bf16[4,128,4,128]{3,1,2,0:T(8,128)(2,1)}, u32[]{:S(2)}, u32[]{:S(2)}) %collective-permute-start.6) | collective-permute-done | bytes 524320 | tf_op jit(solution)/shard_map/ppermute | solution.py:19
  240.7 2.3 fusion.17
  243.0 0.4 copy.124
  243.5 0.9 copy.196
  (88 shorter events, 2.5 us)
Async XLA Ops:
  7.2 103.2 %copy-start = (bf16[512,2048]{1,0:T(8,128)(2,1)S(1)}, bf16[512,2048]{1,0:T(8,128)(2,1)}, u32[]{:S(2)}) copy-start(bf16[512,2048]{1,0:T(8,128)(2,1)} %param.10) | copy-start | bytes 6291460
  7.2 20.0 %copy-start.13 = (s32[32,5]{0,1:T(8,128)S(1)}, s32[32,5]{0,1:T(8,128)}, u32[]{:S(2)}) copy-start(s32[32,5]{0,1:T(8,128)} %param.13) | copy-start | bytes 1924
  7.2 22.7 %copy-start.14 = (s32[32]{0:T(128)S(1)}, s32[32]{0:T(128)}, u32[]{:S(2)}) copy-start(s32[32]{0:T(128)} %param.12) | copy-start | bytes 388
  7.2 103.2 %all-gather.2.cloned.1.call-start = ((), (), s32[]{:S(2)}) async-start(), calls=%async_computation.2 | async-start | bytes 2621440 | tf_op jit(solution)/shard_map/all_gather | solution.py:124
  9.4 89.1 %collective-permute-start.1 = (bf16[4,128,4,128]{3,1,2,0:T(8,128)(2,1)}, bf16[4,128,4,128]{3,1,2,0:T(8,128)(2,1)}, u32[]{:S(2)}, u32[]{:S(2)}) collective-permute-start(bf16[4,128,4,128]{3,1,2,0:T(8,128)(2,1)} %copy.87), channel_id=1, source_target_pairs={{0,8},{4,12},{8,16},{12,20},{16,24},{20,28},{1,9},{5,13},{9,17},{1... | collective-permute-start | bytes 1572872 | tf_op jit(solution)/shard_map/ppermute | solution.py:19
  12.9 86.8 %collective-permute-start.2 = (bf16[4,128,4,128]{3,1,2,0:T(8,128)(2,1)}, bf16[4,128,4,128]{3,1,2,0:T(8,128)(2,1)}, u32[]{:S(2)}, u32[]{:S(2)}) collective-permute-start(bf16[4,128,4,128]{3,1,2,0:T(8,128)(2,1)} %copy.87), channel_id=1, source_target_pairs={{0,16},{4,20},{8,24},{12,28},{1,17},{5,21},{9,25},{13,29},{2,18},{... | collective-permute-start | bytes 1572872 | tf_op jit(solution)/shard_map/ppermute | solution.py:19
  16.0 79.6 %collective-permute-start = (bf16[4,128,4,128]{3,1,2,0:T(8,128)(2,1)}, bf16[4,128,4,128]{3,1,2,0:T(8,128)(2,1)}, u32[]{:S(2)}, u32[]{:S(2)}) collective-permute-start(bf16[4,128,4,128]{3,1,2,0:T(8,128)(2,1)} %copy.87), channel_id=1, source_target_pairs={{0,4},{4,8},{8,12},{12,16},{16,20},{20,24},{24,28},{1,5},{5,9},{9,... | collective-permute-start | bytes 1572872 | tf_op jit(solution)/shard_map/ppermute | solution.py:19
  19.1 15.2 %copy-start.7 = (bf16[4,128,4,128]{3,2,1,0:T(4,128)(2,1)}, bf16[4,128,4,128]{3,2,1,0:T(4,128)(2,1)S(1)}, u32[]{:S(2)}) copy-start(bf16[4,128,4,128]{3,2,1,0:T(4,128)(2,1)S(1)} %reshape.104) | copy-start | bytes 1572868
  20.1 82.6 %collective-permute-start.4 = (bf16[4,128,4,128]{3,1,2,0:T(8,128)(2,1)}, bf16[4,128,4,128]{3,1,2,0:T(8,128)(2,1)}, u32[]{:S(2)}, u32[]{:S(2)}) collective-permute-start(bf16[4,128,4,128]{3,1,2,0:T(8,128)(2,1)} %copy.99), channel_id=1, source_target_pairs={{0,8},{4,12},{8,16},{12,20},{16,24},{20,28},{1,9},{5,13},{9,17},{1... | collective-permute-start | bytes 1572872 | tf_op jit(solution)/shard_map/ppermute | solution.py:19
  22.0 69.8 %collective-permute-start.3 = (bf16[4,128,4,128]{3,1,2,0:T(8,128)(2,1)}, bf16[4,128,4,128]{3,1,2,0:T(8,128)(2,1)}, u32[]{:S(2)}, u32[]{:S(2)}) collective-permute-start(bf16[4,128,4,128]{3,1,2,0:T(8,128)(2,1)} %copy.99), channel_id=1, source_target_pairs={{0,4},{4,8},{8,12},{12,16},{16,20},{20,24},{24,28},{1,5},{5,9},{9,... | collective-permute-start | bytes 1572872 | tf_op jit(solution)/shard_map/ppermute | solution.py:19
  25.2 219.1 %reduce-scatter.2.cloned.1.call-start = ((), (), s32[]{:S(2)}) async-start(), calls=%async_computation.1 | async-start | bytes 2621440 | tf_op jit(solution)/shard_map/reduce_scatter | solution.py:120
  34.4 62.5 %copy-start.11 = (bf16[4,9,128,4,128]{4,2,1,3,0:T(8,128)(2,1)S(1)}, bf16[4,9,128,4,128]{4,2,1,3,0:T(8,128)(2,1)}, u32[]{:S(2)}) copy-start(bf16[4,9,128,4,128]{4,2,1,3,0:T(8,128)(2,1)} %copy_dynamic-update-slice_fusion.1) | copy-start | bytes 14155780
  91.9 12.2 %collective-permute-start.5 = (bf16[4,128,4,128]{3,1,2,0:T(8,128)(2,1)}, bf16[4,128,4,128]{3,1,2,0:T(8,128)(2,1)S(1)}, u32[]{:S(2)}, u32[]{:S(2)}) collective-permute-start(bf16[4,128,4,128]{3,1,2,0:T(8,128)(2,1)} %copy.99), channel_id=1, source_target_pairs={{0,16},{4,20},{8,24},{12,28},{1,17},{5,21},{9,25},{13,29},{2,18},{... | collective-permute-start | bytes 1572872 | tf_op jit(solution)/shard_map/ppermute | solution.py:19
  97.3 7.3 %copy-start.8 = (bf16[4,128,4,128]{3,2,1,0:T(4,128)(2,1)S(1)}, bf16[4,128,4,128]{3,2,1,0:T(4,128)(2,1)}, u32[]{:S(2)}) copy-start(bf16[4,128,4,128]{3,2,1,0:T(4,128)(2,1)} %reshape.105) | copy-start | bytes 1572868
  101.2 3.3 %copy-start.12 = (bf16[4,9,128,4,128]{4,2,1,3,0:T(8,128)(2,1)}, bf16[4,9,128,4,128]{4,2,1,3,0:T(8,128)(2,1)S(1)}, u32[]{:S(2)}) copy-start(bf16[4,9,128,4,128]{4,2,1,3,0:T(8,128)(2,1)S(1)} %broadcast_dynamic-update-slice_fusion.1) | copy-start | bytes 14155780
  104.6 2.2 copy-start.6
  106.7 3.6 %copy-start.2 = (f32[4,4,9,128,128]{4,3,2,1,0:T(8,128)}, f32[4,4,9,128,128]{4,3,2,1,0:T(8,128)S(1)}, u32[]{:S(2)}) copy-start(f32[4,4,9,128,128]{4,3,2,1,0:T(8,128)S(1)} %get-tuple-element.23) | copy-start | bytes 28311556
  127.2 3.9 %copy-start.10 = (bf16[4,128,4,128,1]{1,3,4,2,0:T(8,128)(2,1)S(1)}, bf16[4,128,4,128,1]{1,3,4,2,0:T(8,128)(2,1)}, u32[]{:S(2)}) copy-start(bf16[4,128,4,128,1]{1,3,4,2,0:T(8,128)(2,1)} %copy.144) | copy-start | bytes 1572868
  131.1 28.0 %slice-start = ((s8[9437184]{0:T(1024)(128)(4,1)}), s8[4194304]{0:T(1024)(128)(4,1)S(1)}, s32[]{:S(2)}) async-start(s8[9437184]{0:T(1024)(128)(4,1)} %bitcast.195), calls=%async_computation.3 | async-start | bytes 8388608
  131.1 28.0 %slice-start.1 = ((s8[9437184]{0:T(1024)(128)(4,1)}), s8[4194304]{0:T(1024)(128)(4,1)S(1)}, s32[]{:S(2)}) async-start(s8[9437184]{0:T(1024)(128)(4,1)} %bitcast.195), calls=%async_computation.4 | async-start | bytes 8388608
  142.6 34.3 %collective-permute-start.10 = (bf16[4,128,4,128]{1,3,2,0:T(8,128)(2,1)}, bf16[4,128,4,128]{1,3,2,0:T(8,128)(2,1)}, u32[]{:S(2)}, u32[]{:S(2)}) collective-permute-start(bf16[4,128,4,128]{1,3,2,0:T(8,128)(2,1)} %get-tuple-element.10), channel_id=1, source_target_pairs={{8,0},{12,4},{16,8},{20,12},{24,16},{28,20},{9,1},{13,5},{17,9},{2... | collective-permute-start | bytes 1572872 | tf_op jit(solution)/shard_map/ppermute | solution.py:19
  144.6 37.8 %collective-permute-start.11 = (bf16[4,128,4,128]{1,3,2,0:T(8,128)(2,1)}, bf16[4,128,4,128]{1,3,2,0:T(8,128)(2,1)}, u32[]{:S(2)}, u32[]{:S(2)}) collective-permute-start(bf16[4,128,4,128]{1,3,2,0:T(8,128)(2,1)} %get-tuple-element.11), channel_id=1, source_target_pairs={{16,0},{20,4},{24,8},{28,12},{17,1},{21,5},{25,9},{29,13},{18,2},{... | collective-permute-start | bytes 1572872 | tf_op jit(solution)/shard_map/ppermute | solution.py:19
  145.9 13.3 %slice-start.2 = ((s8[9437184]{0:T(1024)(128)(4,1)}), s8[1048576]{0:T(1024)(128)(4,1)S(1)}, s32[]{:S(2)}) async-start(s8[9437184]{0:T(1024)(128)(4,1)} %bitcast.195), calls=%async_computation.5 | async-start | bytes 2097152
  148.2 19.1 %copy-start.4 = (f32[8,128,4,128]{1,3,2,0:T(8,128)}, f32[8,128,4,128]{1,3,2,0:T(8,128)S(1)}, u32[]{:S(2)}) copy-start(f32[8,128,4,128]{1,3,2,0:T(8,128)S(1)} %pad_add_fusion) | copy-start | bytes 6291460
  151.2 56.9 %collective-permute-start.9 = (bf16[4,128,4,128]{1,3,2,0:T(8,128)(2,1)}, bf16[4,128,4,128]{1,3,2,0:T(8,128)(2,1)}, u32[]{:S(2)}, u32[]{:S(2)}) collective-permute-start(bf16[4,128,4,128]{1,3,2,0:T(8,128)(2,1)} %fusion.7), channel_id=1, source_target_pairs={{4,0},{8,4},{12,8},{16,12},{20,16},{24,20},{28,24},{5,1},{9,5},{13... | collective-permute-start | bytes 1572872 | tf_op jit(solution)/shard_map/ppermute | solution.py:19
  159.2 8.2 %copy-start.9 = (bf16[4,128,4,128]{3,2,1,0:T(4,128)(2,1)S(1)}, bf16[4,128,4,128]{3,2,1,0:T(4,128)(2,1)}, u32[]{:S(2)}) copy-start(bf16[4,128,4,128]{3,2,1,0:T(4,128)(2,1)} %reshape.105) | copy-start | bytes 1572868
  170.6 5.4 %copy-start.3 = (f32[4,9,128,4,128]{4,2,1,3,0:T(8,128)}, f32[4,9,128,4,128]{4,2,1,3,0:T(8,128)S(1)}, u32[]{:S(2)}) copy-start(f32[4,9,128,4,128]{4,2,1,3,0:T(8,128)S(1)} %get-tuple-element.27) | copy-start | bytes 28311556
  170.6 8.9 %slice-start.5 = ((s8[4718592]{0:T(1024)(128)(4,1)}), s8[4194304]{0:T(1024)(128)(4,1)S(1)}, s32[]{:S(2)}) async-start(s8[4718592]{0:T(1024)(128)(4,1)} %bitcast.199), calls=%async_computation.8 | async-start | bytes 8388608
  171.6 40.1 %collective-permute-start.7 = (bf16[4,128,4,128]{3,1,2,0:T(8,128)(2,1)}, bf16[4,128,4,128]{3,1,2,0:T(8,128)(2,1)}, u32[]{:S(2)}, u32[]{:S(2)}) collective-permute-start(bf16[4,128,4,128]{3,1,2,0:T(8,128)(2,1)} %get-tuple-element.12), channel_id=1, source_target_pairs={{8,0},{12,4},{16,8},{20,12},{24,16},{28,20},{9,1},{13,5},{17,9},{2... | collective-permute-start | bytes 1572872 | tf_op jit(solution)/shard_map/ppermute | solution.py:19
  174.0 37.8 %collective-permute-start.8 = (bf16[4,128,4,128]{3,1,2,0:T(8,128)(2,1)}, bf16[4,128,4,128]{3,1,2,0:T(8,128)(2,1)}, u32[]{:S(2)}, u32[]{:S(2)}) collective-permute-start(bf16[4,128,4,128]{3,1,2,0:T(8,128)(2,1)} %get-tuple-element.13), channel_id=1, source_target_pairs={{16,0},{20,4},{24,8},{28,12},{17,1},{21,5},{25,9},{29,13},{18,2},{... | collective-permute-start | bytes 1572872 | tf_op jit(solution)/shard_map/ppermute | solution.py:19
  175.5 3.9 %slice-start.3 = ((s8[4718592]{0:T(1024)(128)(4,1)}), s8[4194304]{0:T(1024)(128)(4,1)S(1)}, s32[]{:S(2)}) async-start(s8[4718592]{0:T(1024)(128)(4,1)} %bitcast.197), calls=%async_computation.6 | async-start | bytes 8388608
  175.5 3.9 %slice-start.6 = ((s8[4718592]{0:T(1024)(128)(4,1)}), s8[524288]{0:T(1024)(128)(4,1)S(1)}, s32[]{:S(2)}) async-start(s8[4718592]{0:T(1024)(128)(4,1)} %bitcast.199), calls=%async_computation.9 | async-start | bytes 1048576
  175.8 3.7 %slice-start.4 = ((s8[4718592]{0:T(1024)(128)(4,1)}), s8[524288]{0:T(1024)(128)(4,1)S(1)}, s32[]{:S(2)}) async-start(s8[4718592]{0:T(1024)(128)(4,1)} %bitcast.197), calls=%async_computation.7 | async-start | bytes 1048576
  176.0 5.1 %copy-start.5 = (f32[8,128,4,128]{3,1,2,0:T(8,128)}, f32[8,128,4,128]{3,1,2,0:T(8,128)S(1)}, u32[]{:S(2)}) copy-start(f32[8,128,4,128]{3,1,2,0:T(8,128)S(1)} %pad_add_fusion.1) | copy-start | bytes 6291460
  176.9 63.8 %collective-permute-start.6 = (bf16[4,128,4,128]{3,1,2,0:T(8,128)(2,1)}, bf16[4,128,4,128]{3,1,2,0:T(8,128)(2,1)}, u32[]{:S(2)}, u32[]{:S(2)}) collective-permute-start(bf16[4,128,4,128]{3,1,2,0:T(8,128)(2,1)} %fusion.13), channel_id=1, source_target_pairs={{4,0},{8,4},{12,8},{16,12},{20,16},{24,20},{28,24},{5,1},{9,5},{13... | collective-permute-start | bytes 1572872 | tf_op jit(solution)/shard_map/ppermute | solution.py:19
  208.1 36.3 %copy-start.1 = (bf16[512,2048]{1,0:T(8,128)(2,1)S(1)}, bf16[512,2048]{1,0:T(8,128)(2,1)}, u32[]{:S(2)}) copy-start(bf16[512,2048]{1,0:T(8,128)(2,1)} %param.10) | copy-start | bytes 6291460
Sparse Core Ops, SparseCore 0:
  25.3 23.3 all-gather.1
  131.2 35.9 reduce-scatter.1
where the time goes:
time: 252 us; the launch traced here: 251 us
  waiting for transfers between devices  111 us (44%)
  matrix products  41.6 us (17%)
  local copies, waits for them, and re-layouts  39.9 us (16%)
  starting transfers between devices  32.6 us (13%)
  between operations  14.7 us (6%)
  other arithmetic  11.7 us (5%)
    ppermute x12, waiting for transfers between devices, passed_along(): return lax.ppermute(block, axis, route)  111 us
    ppermute x12, starting transfers between devices, passed_along(): return lax.ppermute(block, axis, route)  32.5 us
    unnamed x68, local copies, waits for them, and re-layouts  17.3 us
    dot_general x1, matrix products, attend_grads(): jnp.einsum('nhqck,nqhe->nckhe', weights, d_att, preferred_element_type=jn...  10.4 us
    dot_general x1, matrix products, attend(): jnp.einsum('nhqck,nckhe->nqhe', weights, values, preferred_element_type=j...  8.83 us
    dot_general x1, matrix products, attend_grads(): jnp.einsum('nqhe,nckhe->nhqck', d_att, values, preferred_element_type=jnp...  8.16 us
  transfers between devices with their start and end apart: 14, of which 3 were waited for; matrix products, arithmetic and copies ran while one was open for 27% of the time, Pallas kernels for 0%

commit v1 on v0

v1 whole, which is shorter than its diff:
```python
import jax
import jax.numpy as jnp
from jax import lax
from jax.sharding import PartitionSpec as P

HD = 128
BLK = 128
WIN_MAX = 3
LEVELS = 5
NB = 4


neg_large = -1e30


def passed_along(block, axis, distance):
    devices = range(lax.axis_size(axis))
    route = [(i - distance, i) for i in devices if i - distance in devices]
    return lax.ppermute(block, axis, route)


def causal_first(valid):
    grid_shape = (BLK, valid.shape[1], BLK)
    query_pos = lax.broadcasted_iota(jnp.int32, grid_shape, 0)
    key_pos = lax.broadcasted_iota(jnp.int32, grid_shape, 2)
    candidate = lax.broadcasted_iota(jnp.int32, grid_shape, 1)
    inside = (key_pos <= query_pos) | (candidate > 0)
    return valid[:, None, None, :, None] & inside[None, None]


def causal_first_keyside(valid):
    grid_shape = (valid.shape[1], BLK, BLK)
    candidate = lax.broadcasted_iota(jnp.int32, grid_shape, 0)
    query_pos = lax.broadcasted_iota(jnp.int32, grid_shape, 1)
    key_pos = lax.broadcasted_iota(jnp.int32, grid_shape, 2)
    inside = (key_pos <= query_pos) | (candidate > 0)
    return valid[:, None, :, None, None] & inside[None, None]


def query_side(q, g, cand_k, cand_v, allowed):
    scale = HD ** (-0.5)
    raw = jnp.einsum("nqhe,nckhe->nhqck", q, cand_k, preferred_element_type=jnp.float32) * scale
    scores = jnp.where(allowed, raw, neg_large)
    row_max = jnp.max(scores, axis=(3, 4), keepdims=True)
    row_total = jnp.sum(jnp.exp(scores - row_max), axis=(3, 4), keepdims=True)
    log_total = row_max + jnp.log(row_total)
    probabilities = jnp.exp(scores - log_total)
    weights = probabilities.astype(jnp.bfloat16)
    attended = jnp.einsum(
        "nhqck,nckhe->nqhe", weights, cand_v, preferred_element_type=jnp.float32
    ).astype(jnp.bfloat16)
    delta = jnp.transpose(
        jnp.sum(g.astype(jnp.float32) * attended.astype(jnp.float32), axis=3), (0, 2, 1)
    )
    d_prob = jnp.einsum("nqhe,nckhe->nhqck", g, cand_v, preferred_element_type=jnp.float32)
    d_score = (probabilities * (d_prob - delta[:, :, :, None, None]) * scale).astype(jnp.bfloat16)
    query_grad = jnp.einsum("nhqck,nckhe->nqhe", d_score, cand_k, preferred_element_type=jnp.float32)
    return attended, log_total[:, :, :, 0, 0], delta, query_grad


def key_side(k, v, cand_q, cand_g, cand_lse, cand_delta, allowed):
    scale = HD ** (-0.5)
    raw = jnp.einsum("ncqhe,nkhe->nhcqk", cand_q, k, preferred_element_type=jnp.float32) * scale
    scores = jnp.where(allowed, raw, neg_large)
    lse = jnp.transpose(cand_lse, (0, 2, 1, 3))[..., None]
    delta = jnp.transpose(cand_delta, (0, 2, 1, 3))[..., None]
    probabilities = jnp.exp(scores - lse)
    weights = probabilities.astype(jnp.bfloat16)
    value_grad = jnp.einsum("nhcqk,ncqhe->nkhe", weights, cand_g, preferred_element_type=jnp.float32)
    d_prob = jnp.einsum("ncqhe,nkhe->nhcqk", cand_g, v, preferred_element_type=jnp.float32)
    d_score = (probabilities * (d_prob - delta) * scale).astype(jnp.bfloat16)
    key_grad = jnp.einsum("nhcqk,ncqhe->nkhe", d_score, cand_q, preferred_element_type=jnp.float32)
    return key_grad, value_grad


def local(queries, keys, values, out_weight, d_out, window, far_select):
    tokens_local = queries.shape[0]
    heads_local = queries.shape[1] // HD
    assert tokens_local == NB * BLK
    ctx_count = lax.axis_size("ctx")
    ctx_index = lax.axis_index("ctx")
    nblocks = ctx_count * NB
    block_shape = (NB, BLK, heads_local, HD)
    q = queries.reshape(block_shape)
    k = keys.reshape(block_shape)
    v = values.reshape(block_shape)
    local_ids = jnp.arange(NB, dtype=jnp.int32)
    block_ids = ctx_index * NB + local_ids
    levels = [m for m in range(LEVELS) if 2**m < ctx_count]

    from_below = {m: passed_along((k, v), "ctx", 2**m) for m in levels}
    q_above = {m: passed_along(q, "ctx", -(2**m)) for m in levels}

    grad_att = lax.dot_general(
        lax.all_gather(d_out, "head", axis=1, tiled=True),
        out_weight,
        (((1,), (1,)), ((), ())),
        preferred_element_type=jnp.float32,
    )
    g = grad_att.astype(jnp.bfloat16).reshape(block_shape)
    g_above = {m: passed_along(g, "ctx", -(2**m)) for m in levels}

    prev_k, prev_v = from_below[0]
    ext_k = jnp.concatenate([prev_k, k], axis=0)
    ext_v = jnp.concatenate([prev_v, v], axis=0)
    cand_k = jnp.stack(
        [k]
        + [ext_k[NB - o : 2 * NB - o] for o in range(1, WIN_MAX + 1)]
        + [from_below[m][0] for m in levels],
        axis=1,
    )
    cand_v = jnp.stack(
        [v]
        + [ext_v[NB - o : 2 * NB - o] for o in range(1, WIN_MAX + 1)]
        + [from_below[m][1] for m in levels],
        axis=1,
    )
    own_window = lax.dynamic_slice_in_dim(window, ctx_index * NB, NB, 0)
    own_select = lax.dynamic_slice_in_dim(far_select, ctx_index * NB, NB, 0)
    valid_cols = [block_ids >= 0]
    for offset in range(1, WIN_MAX + 1):
        valid_cols.append((offset <= own_window) & (block_ids - offset >= 0))
    for m in levels:
        valid_cols.append((own_select[:, m] == 1) & (block_ids - NB * 2**m >= 0))
    allowed_q = causal_first(jnp.stack(valid_cols, axis=1))
    attended, log_total, delta, query_grad = query_side(q, g, cand_k, cand_v, allowed_q)

    attended_flat = attended.reshape(tokens_local, heads_local * HD)
    partial_out = jnp.dot(attended_flat, out_weight, preferred_element_type=jnp.float32)
    output = lax.psum_scatter(
        partial_out.astype(jnp.bfloat16), "head", scatter_dimension=1, tiled=True
    )

    stats_above = {m: passed_along((log_total, delta), "ctx", -(2**m)) for m in levels}

    def key_candidates(own, above):
        ext = jnp.concatenate([own, above[0]], axis=0)
        return jnp.stack(
            [own] + [ext[o : o + NB] for o in range(1, WIN_MAX + 1)] + [above[m] for m in levels],
            axis=1,
        )

    cand_q = key_candidates(q, q_above)
    cand_g = key_candidates(g, g_above)
    cand_lse = key_candidates(log_total, {m: stats_above[m][0] for m in levels})
    cand_delta = key_candidates(delta, {m: stats_above[m][1] for m in levels})
    last = nblocks - 1
    key_cols = [block_ids >= 0]
    for offset in range(1, WIN_MAX + 1):
        qb = block_ids + offset
        key_cols.append((qb <= last) & (offset <= jnp.take(window, jnp.minimum(qb, last))))
    for m in levels:
        qb = block_ids + NB * 2**m
        key_cols.append((qb <= last) & (jnp.take(far_select[:, m], jnp.minimum(qb, last)) == 1))
    allowed_k = causal_first_keyside(jnp.stack(key_cols, axis=1))
    key_grad, value_grad = key_side(k, v, cand_q, cand_g, cand_lse, cand_delta, allowed_k)

    flat_shape = (tokens_local, heads_local * HD)
    return (
        output,
        query_grad.reshape(flat_shape).astype(jnp.bfloat16),
        key_grad.reshape(flat_shape).astype(jnp.bfloat16),
        value_grad.reshape(flat_shape).astype(jnp.bfloat16),
    )


def solution(mesh):
    return jax.shard_map(
        local,
        mesh=mesh,
        in_specs=(
            P("ctx", "head"),
            P("ctx", "head"),
            P("ctx", "head"),
            P("head", None),
            P("ctx", "head"),
            P(),
            P(),
        ),
        out_specs=(P("ctx", "head"), P("ctx", "head"), P("ctx", "head"), P("ctx", "head")),
        check_vma=False,
    )
```

time: 252 us -> 252 us (level)
  the two profiles are of different devices: /device:TPU:10 before, /device:TPU:0 now
where the time goes in v1:
time: 252 us; the launch traced here: 250 us
  starting transfers between devices  66.8 us (27%)
  local copies, waits for them, and re-layouts  58.8 us (23%)
  waiting for transfers between devices  56.2 us (22%)
  matrix products  45.9 us (18%)
  between operations  14.8 us (6%)
  other arithmetic  7.35 us (3%)
    ppermute x18, starting transfers between devices, passed_along(): return lax.ppermute(block, axis, route)  66.7 us
    ppermute x18, waiting for transfers between devices, passed_along(): return lax.ppermute(block, axis, route)  56.1 us
    unnamed x53, local copies, waits for them, and re-layouts  23.2 us
    dot_general x1, matrix products, key_side(): jnp.einsum('nhcqk,ncqhe->nkhe', d_score, cand_q, preferred_element_type=j...  10.5 us
    dot_general x1, matrix products, query_side(): jnp.einsum('nhqck,nckhe->nqhe', d_score, cand_k, preferred_element_type=j...  10.4 us
    dot_general x1, matrix products, query_side(): jnp.einsum('nhqck,nckhe->nqhe', weights, cand_v, preferred_element_type=j...  7.42 us
    another operation x7, local copies, waits for them, and re-layouts, key_candidates(): jnp.stack([own] + [ext[o:o + NB] for o in range(1, WIN_MAX + 1)] + [above...  7 us
    dot_general x1, matrix products, key_side(): jnp.einsum('nhcqk,ncqhe->nkhe', weights, cand_g, preferred_element_type=j...  5.67 us
  transfers between devices with their start and end apart: 20, of which 4 were waited for; matrix products, arithmetic and copies ran while one was open for 38% of the time, Pallas kernels for 0%

profile of v1, /device:TPU:0, one launch (start us, length us, event | category | flops | bytes accessed | tf_op | source)
XLA Modules:
  0.0 249.8 jit_solution(8265758932786215978)
XLA Ops:
  7.2 1.3 reshape.123
  8.9 4.9 %collective-permute-start = (bf16[4,128,4,128]{1,3,2,0:T(8,128)(2,1)S(1)}, bf16[4,128,4,128]{1,3,2,0:T(8,128)(2,1)S(1)}, u32[]{:S(2)}, u32[]{:S(2)}) collective-permute-start(bf16[4,128,4,128]{1,3,2,0:T(8,128)(2,1)S(1)} %copy.35), channel_id=1, source_target_pairs={{0,4},{4,8},{8,12},{12,16},{16,20},{20,24},{24,28},{1,5},{5,9},{9,... | collective-permute-start | bytes 1572872 | tf_op jit(solution)/shard_map/ppermute | solution.py:19
  13.7 4.3 %collective-permute-start.1 = (bf16[4,128,4,128]{1,3,2,0:T(8,128)(2,1)S(1)}, bf16[4,128,4,128]{1,3,2,0:T(8,128)(2,1)}, u32[]{:S(2)}, u32[]{:S(2)}) collective-permute-start(bf16[4,128,4,128]{1,3,2,0:T(8,128)(2,1)S(1)} %copy.35), channel_id=1, source_target_pairs={{0,8},{4,12},{8,16},{12,20},{16,24},{20,28},{1,9},{5,13},{9,17},{1... | collective-permute-start | bytes 1572872 | tf_op jit(solution)/shard_map/ppermute | solution.py:19
  18.0 4.5 %collective-permute-start.2 = (bf16[4,128,4,128]{1,3,2,0:T(8,128)(2,1)S(1)}, bf16[4,128,4,128]{1,3,2,0:T(8,128)(2,1)}, u32[]{:S(2)}, u32[]{:S(2)}) collective-permute-start(bf16[4,128,4,128]{1,3,2,0:T(8,128)(2,1)S(1)} %copy.35), channel_id=1, source_target_pairs={{0,16},{4,20},{8,24},{12,28},{1,17},{5,21},{9,25},{13,29},{2,18},{... | collective-permute-start | bytes 1572872 | tf_op jit(solution)/shard_map/ppermute | solution.py:19
  22.5 2.0 reshape.124
  24.5 2.0 copy.44
  26.4 2.7 %collective-permute-start.3 = (bf16[4,128,4,128]{3,1,2,0:T(8,128)(2,1)}, bf16[4,128,4,128]{3,1,2,0:T(8,128)(2,1)}, u32[]{:S(2)}, u32[]{:S(2)}) collective-permute-start(bf16[4,128,4,128]{3,1,2,0:T(8,128)(2,1)} %copy.44), channel_id=1, source_target_pairs={{0,4},{4,8},{8,12},{12,16},{16,20},{20,24},{24,28},{1,5},{5,9},{9,... | collective-permute-start | bytes 1572872 | tf_op jit(solution)/shard_map/ppermute | solution.py:19
  29.1 2.1 collective-permute-start.4
  31.3 2.0 stack_reshape.12
  33.2 2.0 stack_reshape.13
  35.5 2.1 copy.39
  37.9 1.9 copy_dynamic-update-slice_fusion.1
  44.0 1.1 broadcast_and_fusion.1
  45.1 1.1 broadcast_and_fusion
  46.2 2.0 constant_dynamic-update-slice_fusion
  48.1 2.0 reshape.125
  50.1 2.0 stack_reshape.14
  52.1 1.9 reshape.199
  54.0 1.3 copy_dynamic-update-slice_fusion
  55.3 1.4 fusion.106
  56.7 32.1 %collective-permute-start.5 = (bf16[4,128,4,128]{3,1,2,0:T(8,128)(2,1)}, bf16[4,128,4,128]{3,1,2,0:T(8,128)(2,1)S(1)}, u32[]{:S(2)}, u32[]{:S(2)}) collective-permute-start(bf16[4,128,4,128]{3,1,2,0:T(8,128)(2,1)} %copy.44), channel_id=1, source_target_pairs={{0,16},{4,20},{8,24},{12,28},{1,17},{5,21},{9,25},{13,29},{2,18},{... | collective-permute-start | bytes 1572872 | tf_op jit(solution)/shard_map/ppermute | solution.py:19
  88.8 1.1 constant_dynamic-update-slice_fusion.2
  90.3 1.1 bitcast_dynamic-update-slice_fusion.8
  91.4 1.3 collective-permute-start.6
  92.7 1.1 bitcast_dynamic-update-slice_fusion.7
  93.9 1.9 collective-permute-done.5
  95.7 1.3 collective-permute-start.7
  97.1 1.4 fusion.2
  99.0 1.6 exponential_reduce_fusion
  100.5 1.4 copy-done.3
  102.5 1.4 collective-permute-start.8
  104.3 1.3 collective-permute-start.9
  106.0 1.3 collective-permute-start.10
  107.3 1.1 bitcast_dynamic-update-slice_fusion.10
  108.5 1.5 collective-permute-start.11
  110.0 33.2 %collective-permute-done.8 = bf16[4,128,4,128]{3,1,2,0:T(8,128)(2,1)S(1)} collective-permute-done((bf16[4,128,4,128]{3,1,2,0:T(8,128)(2,1)S(1)}, bf16[4,128,4,128]{3,1,2,0:T(8,128)(2,1)S(1)}, u32[]{:S(2)}, u32[]{:S(2)}) %collective-permute-start.8) | collective-permute-done | bytes 524320 | tf_op jit(solution)/shard_map/ppermute | solution.py:19
  143.3 4.0 %fusion.71 = f32[4,4,7,128,128]{4,3,2,1,0:T(8,128)} fusion(bf16[4,7,128,4,128]{4,2,1,3,0:T(8,128)(2,1)S(1)} %bitcast_dynamic-update-slice_fusion.3, bf16[4,128,4,128,1]{3,2,1,0,4:T(4,128)(2,1)S(1)} %bitcast.260), kind=kOutput, calls=%fused_computation.94 | convolution fusion | flops 469762048 | bytes 11534336 | tf_op jit(solution)/shard_map/ncqhe,nkhe->nhcqk/dot_general | solution.py:63
  147.4 1.1 bitcast_dynamic-update-slice_fusion.9
  148.6 1.7 copy-done.9
  150.4 2.9 %convolution_convert_fusion.1 = bf16[512,512]{1,0:T(8,128)(2,1)S(1)} fusion(bf16[512,2048]{1,0:T(8,128)(2,1)} %all-gather.2.cloned.1.call-done, bf16[512,2048]{1,0:T(8,128)(2,1)S(1)} %copy-done), kind=kOutput, calls=%fused_computation.40 | convolution fusion | flops 1074003968 | bytes 4718592 | tf_op jit(solution)/shard_map/dot_general | solution.py:94
  154.1 0.9 reshape.196
  155.3 7.4 %multiply_reduce_fusion = (f32[4,128,4]{1,2,0:T(4,128)S(1)}, bf16[4,128,4,128]{1,3,2,0:T(8,128)(2,1)}) fusion(bf16[4,128,4,128]{1,3,2,0:T(8,128)(2,1)S(1)} %copy.55, bf16[4,7,128,4,128]{2,4,1,3,0:T(8,128)(2,1)} %copy-done.9, f32[4,4,7,128,128]{4,3,2,1,0:T(8,128)} %copy-done.3, f32[4,4,128]{2,1,0:T(4,128)S(1)} %get-tuple-element.6, ...), kind=kOutput, calls=%fused_computation.53 | convolution fusion | flops 478410752 | bytes 12533760 | tf_op jit(solution)/shard_map/nhqck,nckhe->nqhe/dot_general | solution.py:49
  162.8 1.3 collective-permute-start.15
  164.0 1.3 collective-permute-start.16
  165.3 1.3 collective-permute-start.17
  166.6 1.3 collective-permute-start.12
  167.9 1.5 collective-permute-start.13
  169.5 2.1 copy.54
  171.6 3.6 %convolution_convert_fusion = bf16[512,2048]{1,0:T(8,128)(2,1)} fusion(bf16[512,2048]{1,0:T(8,128)(2,1)S(1)} %copy-done, bf16[64,8,4,128]{3,2,1,0:T(4,128)(2,1)} %bitcast.268), kind=kOutput, calls=%fused_computation.29 | convolution fusion | flops 1074790400 | bytes 4718592 | tf_op jit(solution)/shard_map/dot_general | solution.py:129
  175.2 10.4 %fusion.40 = bf16[4,128,4,128]{1,3,2,0:T(8,128)(2,1)} fusion(bf16[4,7,128,4,128]{4,2,1,3,0:T(8,128)(2,1)} %copy-done.11, f32[4,4,7,128,128]{4,3,2,1,0:T(8,128)} %copy-done.3, f32[4,4,128]{2,1,0:T(4,128)S(1)} %bitcast.272, f32[4,4,128]{2,1,0:T(4,128)S(1)} %get-tuple-element.6, pred[4,128,7,128]{1,3,2,0:T(8,128)(4,1)} %broadcast_and_fusion.1, ...), kind=kOutput, calls=%fused_computation.42 | convolution fusion | flops 952631296 | bytes 16203776 | tf_op jit(solution)/shard_map/nhqck,nckhe->nqhe/dot_general | solution.py:57
  185.6 2.0 stack_reshape.15
  187.6 2.1 copy.74
  189.6 2.0 constant_dynamic-update-slice_fusion.12
  191.6 2.1 copy.58
  193.7 1.9 copy.128
  195.6 1.5 collective-permute-start.14
  197.3 1.0 fusion.52
  198.3 0.9 fusion.49
  200.1 0.9 bitcast_dynamic-update-slice_fusion.2
  201.0 2.0 bitcast_dynamic-update-slice_fusion.1
  203.0 20.4 %collective-permute-done.14 = bf16[4,128,4,128]{1,3,2,0:T(8,128)(2,1)S(1)} collective-permute-done((bf16[4,128,4,128]{1,3,2,0:T(8,128)(2,1)S(1)}, bf16[4,128,4,128]{1,3,2,0:T(8,128)(2,1)S(1)}, u32[]{:S(2)}, u32[]{:S(2)}) %collective-permute-start.14) | collective-permute-done | bytes 524320 | tf_op jit(solution)/shard_map/ppermute | solution.py:19
  223.5 0.9 bitcast_dynamic-update-slice_fusion
  224.4 10.5 %fusion.39 = bf16[4,128,4,128]{1,3,2,0:T(8,128)(2,1)S(1)} fusion(bf16[4,7,128,4,128]{4,2,1,3,0:T(8,128)(2,1)} %copy-done.4, f32[4,4,7,128,128]{4,3,2,1,0:T(8,128)} %fusion.71, f32[4,4,7,128]{3,2,1,0:T(8,128)S(1)} %copy.78, f32[4,4,7,128]{3,2,1,0:T(8,128)S(1)} %copy.69, pred[4,7,128,128]{3,2,1,0:T(8,128)(4,1)} %broadcast_and_fusion, ...), kind=kOutput, calls=%fused_computation.41 | convolution fusion | flops 952631296 | bytes 16302080 | tf_op jit(solution)/shard_map/nhcqk,ncqhe->nkhe/dot_general | solution.py:72
  236.1 5.7 %fusion.44 = bf16[4,128,4,128]{1,3,2,0:T(8,128)(2,1)S(1)} fusion(bf16[4,7,128,4,128]{2,4,1,3,0:T(8,128)(2,1)} %bitcast_dynamic-update-slice_fusion, f32[4,4,7,128,128]{4,3,2,1,0:T(8,128)} %fusion.71, f32[4,4,7,128]{3,2,1,0:T(8,128)S(1)} %copy.69, pred[4,7,128,128]{3,2,1,0:T(8,128)(4,1)} %broadcast_and_fusion), kind=kOutput, calls=%fused_computation.44 | convolution fusion | flops 477364224 | bytes 12050432 | tf_op jit(solution)/shard_map/nhcqk,ncqhe->nkhe/dot_general | solution.py:69
  (117 shorter events, 12.0 us)
Async XLA Ops:
  7.2 143.3 %copy-start = (bf16[512,2048]{1,0:T(8,128)(2,1)S(1)}, bf16[512,2048]{1,0:T(8,128)(2,1)}, u32[]{:S(2)}) copy-start(bf16[512,2048]{1,0:T(8,128)(2,1)} %param.12) | copy-start | bytes 6291460
  7.2 143.2 %all-gather.2.cloned.1.call-start = ((), (), s32[]{:S(2)}) async-start(), calls=%async_computation.2 | async-start | bytes 2621440 | tf_op jit(solution)/shard_map/all_gather | solution.py:95
  8.5 29.0 %copy-start.12 = (s32[32,5]{0,1:T(8,128)S(1)}, s32[32,5]{0,1:T(8,128)}, u32[]{:S(2)}) copy-start(s32[32,5]{0,1:T(8,128)} %param.15) | copy-start | bytes 1924
  8.5 29.1 %copy-start.1 = (s32[32]{0:T(128)S(1)}, s32[32]{0:T(128)}, u32[]{:S(2)}) copy-start(s32[32]{0:T(128)} %param.14) | copy-start | bytes 388
  8.9 95.4 %collective-permute-start = (bf16[4,128,4,128]{1,3,2,0:T(8,128)(2,1)S(1)}, bf16[4,128,4,128]{1,3,2,0:T(8,128)(2,1)S(1)}, u32[]{:S(2)}, u32[]{:S(2)}) collective-permute-start(bf16[4,128,4,128]{1,3,2,0:T(8,128)(2,1)S(1)} %copy.35), channel_id=1, source_target_pairs={{0,4},{4,8},{8,12},{12,16},{16,20},{20,24},{24,28},{1,5},{5,9},{9,... | collective-permute-start | bytes 1572872 | tf_op jit(solution)/shard_map/ppermute | solution.py:19
  13.7 92.3 %collective-permute-start.1 = (bf16[4,128,4,128]{1,3,2,0:T(8,128)(2,1)S(1)}, bf16[4,128,4,128]{1,3,2,0:T(8,128)(2,1)}, u32[]{:S(2)}, u32[]{:S(2)}) collective-permute-start(bf16[4,128,4,128]{1,3,2,0:T(8,128)(2,1)S(1)} %copy.35), channel_id=1, source_target_pairs={{0,8},{4,12},{8,16},{12,20},{16,24},{20,28},{1,9},{5,13},{9,17},{1... | collective-permute-start | bytes 1572872 | tf_op jit(solution)/shard_map/ppermute | solution.py:19
  18.0 129.4 %collective-permute-start.2 = (bf16[4,128,4,128]{1,3,2,0:T(8,128)(2,1)S(1)}, bf16[4,128,4,128]{1,3,2,0:T(8,128)(2,1)}, u32[]{:S(2)}, u32[]{:S(2)}) collective-permute-start(bf16[4,128,4,128]{1,3,2,0:T(8,128)(2,1)S(1)} %copy.35), channel_id=1, source_target_pairs={{0,16},{4,20},{8,24},{12,28},{1,17},{5,21},{9,25},{13,29},{2,18},{... | collective-permute-start | bytes 1572872 | tf_op jit(solution)/shard_map/ppermute | solution.py:19
  26.4 30.3 %collective-permute-start.3 = (bf16[4,128,4,128]{3,1,2,0:T(8,128)(2,1)}, bf16[4,128,4,128]{3,1,2,0:T(8,128)(2,1)}, u32[]{:S(2)}, u32[]{:S(2)}) collective-permute-start(bf16[4,128,4,128]{3,1,2,0:T(8,128)(2,1)} %copy.44), channel_id=1, source_target_pairs={{0,4},{4,8},{8,12},{12,16},{16,20},{20,24},{24,28},{1,5},{5,9},{9,... | collective-permute-start | bytes 1572872 | tf_op jit(solution)/shard_map/ppermute | solution.py:19
  29.1 62.3 %collective-permute-start.4 = (bf16[4,128,4,128]{3,1,2,0:T(8,128)(2,1)}, bf16[4,128,4,128]{3,1,2,0:T(8,128)(2,1)}, u32[]{:S(2)}, u32[]{:S(2)}) collective-permute-start(bf16[4,128,4,128]{3,1,2,0:T(8,128)(2,1)} %copy.44), channel_id=1, source_target_pairs={{0,8},{4,12},{8,16},{12,20},{16,24},{20,28},{1,9},{5,13},{9,17},{1... | collective-permute-start | bytes 1572872 | tf_op jit(solution)/shard_map/ppermute | solution.py:19
  31.2 211.8 %reduce-scatter.2.cloned.1.call-start = ((), (), s32[]{:S(2)}) async-start(), calls=%async_computation.1 | async-start | bytes 2621440 | tf_op jit(solution)/shard_map/reduce_scatter | solution.py:130
  54.0 35.8 %copy-start.2 = (bf16[4,128,4,128]{3,2,1,0:T(4,128)(2,1)S(1)}, bf16[4,128,4,128]{3,2,1,0:T(4,128)(2,1)}, u32[]{:S(2)}) copy-start(bf16[4,128,4,128]{3,2,1,0:T(4,128)(2,1)} %reshape.124) | copy-start | bytes 1572868
  54.0 36.0 %copy-start.10 = (bf16[4,7,128,4,128]{4,2,1,3,0:T(8,128)(2,1)S(1)}, bf16[4,7,128,4,128]{4,2,1,3,0:T(8,128)(2,1)}, u32[]{:S(2)}) copy-start(bf16[4,7,128,4,128]{4,2,1,3,0:T(8,128)(2,1)} %copy_dynamic-update-slice_fusion.1) | copy-start | bytes 11010052
  56.7 39.0 %collective-permute-start.5 = (bf16[4,128,4,128]{3,1,2,0:T(8,128)(2,1)}, bf16[4,128,4,128]{3,1,2,0:T(8,128)(2,1)S(1)}, u32[]{:S(2)}, u32[]{:S(2)}) collective-permute-start(bf16[4,128,4,128]{3,1,2,0:T(8,128)(2,1)} %copy.44), channel_id=1, source_target_pairs={{0,16},{4,20},{8,24},{12,28},{1,17},{5,21},{9,25},{13,29},{2,18},{... | collective-permute-start | bytes 1572872 | tf_op jit(solution)/shard_map/ppermute | solution.py:19
  89.9 7.3 %copy-start.6 = (bf16[4,128,4,128]{3,2,1,0:T(4,128)(2,1)S(1)}, bf16[4,128,4,128]{3,2,1,0:T(4,128)(2,1)}, u32[]{:S(2)}) copy-start(bf16[4,128,4,128]{3,2,1,0:T(4,128)(2,1)} %reshape.125) | copy-start | bytes 1572868
  89.9 7.2 %copy-start.7 = (pred[4,128,7,128]{1,3,2,0:T(8,128)(4,1)S(1)}, pred[4,128,7,128]{1,3,2,0:T(8,128)(4,1)}, u32[]{:S(2)}) copy-start(pred[4,128,7,128]{1,3,2,0:T(8,128)(4,1)} %broadcast_and_fusion.1) | copy-start | bytes 1376260
  91.4 11.1 %collective-permute-start.6 = (bf16[4,128,4,128]{3,1,2,0:T(8,128)(2,1)S(1)}, bf16[4,128,4,128]{3,1,2,0:T(8,128)(2,1)S(1)}, u32[]{:S(2)}, u32[]{:S(2)}) collective-permute-start(bf16[4,128,4,128]{3,1,2,0:T(8,128)(2,1)S(1)} %get-tuple-element.7), channel_id=1, source_target_pairs={{4,0},{8,4},{12,8},{16,12},{20,16},{24,20},{28,24},{5,1},{9,5},{13... | collective-permute-start | bytes 1572872 | tf_op jit(solution)/shard_map/ppermute | solution.py:19
  95.7 12.7 %collective-permute-start.7 = (bf16[4,128,4,128]{3,1,2,0:T(8,128)(2,1)S(1)}, bf16[4,128,4,128]{3,1,2,0:T(8,128)(2,1)S(1)}, u32[]{:S(2)}, u32[]{:S(2)}) collective-permute-start(bf16[4,128,4,128]{3,1,2,0:T(8,128)(2,1)S(1)} %get-tuple-element.7), channel_id=1, source_target_pairs={{8,0},{12,4},{16,8},{20,12},{24,16},{28,20},{9,1},{13,5},{17,9},{2... | collective-permute-start | bytes 1572872 | tf_op jit(solution)/shard_map/ppermute | solution.py:19
  97.1 1.9 copy-start.11
  99.0 3.0 %copy-start.3 = (f32[4,4,7,128,128]{4,3,2,1,0:T(8,128)}, f32[4,4,7,128,128]{4,3,2,1,0:T(8,128)S(1)}, u32[]{:S(2)}) copy-start(f32[4,4,7,128,128]{4,3,2,1,0:T(8,128)S(1)} %get-tuple-element.19) | copy-start | bytes 22020100
  102.0 3.6 %copy-start.8 = (bf16[4,7,128,4,128]{2,4,1,3,0:T(8,128)(2,1)S(1)}, bf16[4,7,128,4,128]{2,4,1,3,0:T(8,128)(2,1)}, u32[]{:S(2)}) copy-start(bf16[4,7,128,4,128]{2,4,1,3,0:T(8,128)(2,1)} %constant_dynamic-update-slice_fusion) | copy-start | bytes 11010052
  102.5 40.8 %collective-permute-start.8 = (bf16[4,128,4,128]{3,1,2,0:T(8,128)(2,1)S(1)}, bf16[4,128,4,128]{3,1,2,0:T(8,128)(2,1)S(1)}, u32[]{:S(2)}, u32[]{:S(2)}) collective-permute-start(bf16[4,128,4,128]{3,1,2,0:T(8,128)(2,1)S(1)} %get-tuple-element.7), channel_id=1, source_target_pairs={{16,0},{20,4},{24,8},{28,12},{17,1},{21,5},{25,9},{29,13},{18,2},{... | collective-permute-start | bytes 1572872 | tf_op jit(solution)/shard_map/ppermute | solution.py:19
  104.3 44.3 %collective-permute-start.9 = (f32[4,4,128]{2,1,0:T(4,128)S(1)}, f32[4,4,128]{2,1,0:T(4,128)S(1)}, u32[]{:S(2)}, u32[]{:S(2)}) collective-permute-start(f32[4,4,128]{2,1,0:T(4,128)S(1)} %get-tuple-element.6), channel_id=1, source_target_pairs={{4,0},{8,4},{12,8},{16,12},{20,16},{24,20},{28,24},{5,1},{9,5},{13... | collective-permute-start | bytes 24584 | tf_op jit(solution)/shard_map/ppermute | solution.py:19
  106.0 42.6 %collective-permute-start.10 = (f32[4,4,128]{2,1,0:T(4,128)S(1)}, f32[4,4,128]{2,1,0:T(4,128)S(1)}, u32[]{:S(2)}, u32[]{:S(2)}) collective-permute-start(f32[4,4,128]{2,1,0:T(4,128)S(1)} %get-tuple-element.6), channel_id=1, source_target_pairs={{8,0},{12,4},{16,8},{20,12},{24,16},{28,20},{9,1},{13,5},{17,9},{2... | collective-permute-start | bytes 24584 | tf_op jit(solution)/shard_map/ppermute | solution.py:19
  108.5 40.2 %collective-permute-start.11 = (f32[4,4,128]{2,1,0:T(4,128)S(1)}, f32[4,4,128]{2,1,0:T(4,128)S(1)}, u32[]{:S(2)}, u32[]{:S(2)}) collective-permute-start(f32[4,4,128]{2,1,0:T(4,128)S(1)} %get-tuple-element.6), channel_id=1, source_target_pairs={{16,0},{20,4},{24,8},{28,12},{17,1},{21,5},{25,9},{29,13},{18,2},{... | collective-permute-start | bytes 24584 | tf_op jit(solution)/shard_map/ppermute | solution.py:19
  143.3 4.0 %copy-start.4 = (bf16[4,7,128,4,128]{4,2,1,3,0:T(8,128)(2,1)}, bf16[4,7,128,4,128]{4,2,1,3,0:T(8,128)(2,1)S(1)}, u32[]{:S(2)}) copy-start(bf16[4,7,128,4,128]{4,2,1,3,0:T(8,128)(2,1)S(1)} %bitcast_dynamic-update-slice_fusion.3) | copy-start | bytes 11010052
  148.5 1.9 copy-start.9
  153.3 0.8 copy-start.5
  162.8 32.9 %collective-permute-start.15 = (f32[4,4,128]{2,1,0:T(4,128)S(1)}, f32[4,4,128]{2,1,0:T(4,128)S(1)}, u32[]{:S(2)}, u32[]{:S(2)}) collective-permute-start(f32[4,4,128]{2,1,0:T(4,128)S(1)} %bitcast.269), channel_id=1, source_target_pairs={{4,0},{8,4},{12,8},{16,12},{20,16},{24,20},{28,24},{5,1},{9,5},{13... | collective-permute-start | bytes 24584 | tf_op jit(solution)/shard_map/ppermute | solution.py:19
  164.0 33.2 %collective-permute-start.16 = (f32[4,4,128]{2,1,0:T(4,128)S(1)}, f32[4,4,128]{2,1,0:T(4,128)S(1)}, u32[]{:S(2)}, u32[]{:S(2)}) collective-permute-start(f32[4,4,128]{2,1,0:T(4,128)S(1)} %bitcast.270), channel_id=1, source_target_pairs={{8,0},{12,4},{16,8},{20,12},{24,16},{28,20},{9,1},{13,5},{17,9},{2... | collective-permute-start | bytes 24584 | tf_op jit(solution)/shard_map/ppermute | solution.py:19
  165.3 31.9 %collective-permute-start.17 = (f32[4,4,128]{2,1,0:T(4,128)S(1)}, f32[4,4,128]{2,1,0:T(4,128)S(1)}, u32[]{:S(2)}, u32[]{:S(2)}) collective-permute-start(f32[4,4,128]{2,1,0:T(4,128)S(1)} %bitcast.271), channel_id=1, source_target_pairs={{16,0},{20,4},{24,8},{28,12},{17,1},{21,5},{25,9},{29,13},{18,2},{... | collective-permute-start | bytes 24584 | tf_op jit(solution)/shard_map/ppermute | solution.py:19
  166.6 30.7 %collective-permute-start.12 = (bf16[4,128,4,128]{1,3,2,0:T(8,128)(2,1)S(1)}, bf16[4,128,4,128]{1,3,2,0:T(8,128)(2,1)S(1)}, u32[]{:S(2)}, u32[]{:S(2)}) collective-permute-start(bf16[4,128,4,128]{1,3,2,0:T(8,128)(2,1)S(1)} %copy.55), channel_id=1, source_target_pairs={{4,0},{8,4},{12,8},{16,12},{20,16},{24,20},{28,24},{5,1},{9,5},{13... | collective-permute-start | bytes 1572872 | tf_op jit(solution)/shard_map/ppermute | solution.py:19
  167.9 33.1 %collective-permute-start.13 = (bf16[4,128,4,128]{1,3,2,0:T(8,128)(2,1)S(1)}, bf16[4,128,4,128]{1,3,2,0:T(8,128)(2,1)}, u32[]{:S(2)}, u32[]{:S(2)}) collective-permute-start(bf16[4,128,4,128]{1,3,2,0:T(8,128)(2,1)S(1)} %copy.55), channel_id=1, source_target_pairs={{8,0},{12,4},{16,8},{20,12},{24,16},{28,20},{9,1},{13,5},{17,9},{2... | collective-permute-start | bytes 1572872 | tf_op jit(solution)/shard_map/ppermute | solution.py:19
  195.6 27.8 %collective-permute-start.14 = (bf16[4,128,4,128]{1,3,2,0:T(8,128)(2,1)S(1)}, bf16[4,128,4,128]{1,3,2,0:T(8,128)(2,1)S(1)}, u32[]{:S(2)}, u32[]{:S(2)}) collective-permute-start(bf16[4,128,4,128]{1,3,2,0:T(8,128)(2,1)S(1)} %copy.55), channel_id=1, source_target_pairs={{16,0},{20,4},{24,8},{28,12},{17,1},{21,5},{25,9},{29,13},{18,2},{... | collective-permute-start | bytes 1572872 | tf_op jit(solution)/shard_map/ppermute | solution.py:19
Sparse Core Ops, SparseCore 0:
  31.4 19.8 all-gather.1
  175.3 37.5 reduce-scatter.1

commit v2 on v1

v2 whole, which is shorter than its diff:
```python
import functools

import jax
import jax.numpy as jnp
from jax import lax
from jax.experimental import pallas as pl
from jax.experimental.pallas import tpu as pltpu
from jax.sharding import PartitionSpec as P

HD = 128
BLK = 128
WIN_MAX = 3
LEVELS = 5
NB = 4


neg_large = -1e30


def passed_along(block, axis, distance):
    devices = range(lax.axis_size(axis))
    route = [(i - distance, i) for i in devices if i - distance in devices]
    return lax.ppermute(block, axis, route)


def dot_nt(a, b):
    return lax.dot_general(a, b, (((1,), (1,)), ((), ())), preferred_element_type=jnp.float32)


def dot_nn(a, b):
    return jnp.dot(a, b, preferred_element_type=jnp.float32)


def col_to_row(col):
    eye = lax.broadcasted_iota(jnp.int32, (BLK, BLK), 0) == lax.broadcasted_iota(
        jnp.int32, (BLK, BLK), 1
    )
    return jnp.sum(jnp.where(eye, col, 0.0), axis=0, keepdims=True)


def query_kernel(n_levels, valid_ref, q_ref, g_ref, k_ref, v_ref, *rest):
    kf = rest[0 : 2 * n_levels : 2]
    vf = rest[1 : 2 * n_levels : 2]
    att_ref, dq_ref, st_ref = rest[2 * n_levels :]
    n_cand = 1 + WIN_MAX + n_levels
    scale = HD ** (-0.5)
    causal = lax.broadcasted_iota(jnp.int32, (BLK, BLK), 1) <= lax.broadcasted_iota(
        jnp.int32, (BLK, BLK), 0
    )
    for n in range(NB):
        rows = pl.ds(n * BLK, BLK)
        qn = q_ref[rows, :]
        gn = g_ref[rows, :]
        cands = [(k_ref, v_ref, n)]
        for o in range(1, WIN_MAX + 1):
            j = n - o
            cands.append((k_ref, v_ref, j) if j >= 0 else (kf[0], vf[0], NB + j))
        for mi in range(n_levels):
            cands.append((kf[mi], vf[mi], n))
        scores = []
        for ci, (kr, _, j) in enumerate(cands):
            s = dot_nt(qn, kr[pl.ds(j * BLK, BLK), :]) * scale
            if ci == 0:
                s = jnp.where(causal, s, neg_large)
            else:
                s = jnp.where(valid_ref[n * n_cand + ci] != 0, s, neg_large)
            scores.append(s)
        row_max = scores[0].max(axis=1, keepdims=True)
        for s in scores[1:]:
            row_max = jnp.maximum(row_max, s.max(axis=1, keepdims=True))
        row_total = None
        for s in scores:
            part = jnp.sum(jnp.exp(s - row_max), axis=1, keepdims=True)
            row_total = part if row_total is None else row_total + part
        log_total = row_max + jnp.log(row_total)
        probs = [jnp.exp(s - log_total) for s in scores]
        att = None
        for p, (_, vr, j) in zip(probs, cands):
            part = dot_nn(p.astype(jnp.bfloat16), vr[pl.ds(j * BLK, BLK), :])
            att = part if att is None else att + part
        att_b = att.astype(jnp.bfloat16)
        att_ref[rows, :] = att_b
        delta = jnp.sum(gn.astype(jnp.float32) * att_b.astype(jnp.float32), axis=1, keepdims=True)
        dq = None
        for p, (kr, vr, j) in zip(probs, cands):
            d_prob = dot_nt(gn, vr[pl.ds(j * BLK, BLK), :])
            d_score = (p * (d_prob - delta) * scale).astype(jnp.bfloat16)
            part = dot_nn(d_score, kr[pl.ds(j * BLK, BLK), :])
            dq = part if dq is None else dq + part
        dq_ref[rows, :] = dq.astype(jnp.bfloat16)
        st_ref[0, 0, pl.ds(n, 1), :] = col_to_row(log_total)
        st_ref[1, 0, pl.ds(n, 1), :] = col_to_row(delta)


def key_kernel(n_levels, valid_ref, k_ref, v_ref, q_ref, g_ref, st_ref, *rest):
    qf = rest[0 : 3 * n_levels : 3]
    gf = rest[1 : 3 * n_levels : 3]
    sf = rest[2 : 3 * n_levels : 3]
    dk_ref, dv_ref = rest[3 * n_levels :]
    n_cand = 1 + WIN_MAX + n_levels
    scale = HD ** (-0.5)
    causal = lax.broadcasted_iota(jnp.int32, (BLK, BLK), 0) <= lax.broadcasted_iota(
        jnp.int32, (BLK, BLK), 1
    )
    for j in range(NB):
        rows = pl.ds(j * BLK, BLK)
        kj = k_ref[rows, :]
        vj = v_ref[rows, :]
        cands = [(q_ref, g_ref, st_ref, j)]
        for o in range(1, WIN_MAX + 1):
            i = j + o
            cands.append((q_ref, g_ref, st_ref, i) if i < NB else (qf[0], gf[0], sf[0], i - NB))
        for mi in range(n_levels):
            cands.append((qf[mi], gf[mi], sf[mi], j))
        dk = None
        dv = None
        for ci, (qr, gr, sr, i) in enumerate(cands):
            qc = qr[pl.ds(i * BLK, BLK), :]
            gc = gr[pl.ds(i * BLK, BLK), :]
            lse = sr[0, 0, pl.ds(i, 1), :]
            delta = sr[1, 0, pl.ds(i, 1), :]
            s = dot_nt(kj, qc) * scale
            if ci == 0:
                s = jnp.where(causal, s, neg_large)
            else:
                s = jnp.where(valid_ref[j * n_cand + ci] != 0, s, neg_large)
            p = jnp.exp(s - lse)
            part_v = dot_nn(p.astype(jnp.bfloat16), gc)
            d_prob = dot_nt(vj, gc)
            d_score = (p * (d_prob - delta) * scale).astype(jnp.bfloat16)
            part_k = dot_nn(d_score, qc)
            dv = part_v if dv is None else dv + part_v
            dk = part_k if dk is None else dk + part_k
        dk_ref[rows, :] = dk.astype(jnp.bfloat16)
        dv_ref[rows, :] = dv.astype(jnp.bfloat16)


def head_block(part):
    return pl.BlockSpec((NB * BLK, HD), lambda h, valid: (part, h))


def stats_block(heads):
    return pl.BlockSpec((2, 1, NB, BLK), lambda h, valid: (0, h, 0, 0))


def query_call(valid, q, g, k, v, kv_from, heads, n_levels):
    tokens, features = q.shape
    in_specs = [head_block(0)] * 4
    args = [q, g, k, v]
    for kv in kv_from:
        in_specs += [head_block(0), head_block(1)]
        args += [kv, kv]
    grid_spec = pltpu.PrefetchScalarGridSpec(
        num_scalar_prefetch=1,
        grid=(heads,),
        in_specs=in_specs,
        out_specs=[head_block(0), head_block(0), stats_block(heads)],
    )
    return pl.pallas_call(
        functools.partial(query_kernel, n_levels),
        grid_spec=grid_spec,
        out_shape=[
            jax.ShapeDtypeStruct((tokens, features), jnp.bfloat16),
            jax.ShapeDtypeStruct((tokens, features), jnp.bfloat16),
            jax.ShapeDtypeStruct((2, heads, NB, BLK), jnp.float32),
        ],
        name="query_side",
    )(valid, *args)


def key_call(valid, k, v, q, g, stats, qg_from, st_from, heads, n_levels):
    tokens, features = q.shape
    in_specs = [head_block(0)] * 4 + [stats_block(heads)]
    args = [k, v, q, g, stats]
    for qg, st in zip(qg_from, st_from):
        in_specs += [head_block(0), head_block(1), stats_block(heads)]
        args += [qg, qg, st]
    grid_spec = pltpu.PrefetchScalarGridSpec(
        num_scalar_prefetch=1,
        grid=(heads,),
        in_specs=in_specs,
        out_specs=[head_block(0), head_block(0)],
    )
    return pl.pallas_call(
        functools.partial(key_kernel, n_levels),
        grid_spec=grid_spec,
        out_shape=[
            jax.ShapeDtypeStruct((tokens, features), jnp.bfloat16),
            jax.ShapeDtypeStruct((tokens, features), jnp.bfloat16),
        ],
        name="key_side",
    )(valid, *args)


def local(queries, keys, values, out_weight, d_out, window, far_select):
    tokens_local = queries.shape[0]
    heads_local = queries.shape[1] // HD
    assert tokens_local == NB * BLK
    ctx_count = lax.axis_size("ctx")
    ctx_index = lax.axis_index("ctx")
    nblocks = ctx_count * NB
    last = nblocks - 1
    levels = [m for m in range(LEVELS) if 2**m < ctx_count]
    n_levels = len(levels)
    block_ids = ctx_index * NB + jnp.arange(NB, dtype=jnp.int32)

    kv = jnp.concatenate([keys, values], axis=0)
    kv_from = [passed_along(kv, "ctx", 2**m) for m in levels]

    grad_att = lax.dot_general(
        lax.all_gather(d_out, "head", axis=1, tiled=True),
        out_weight,
        (((1,), (1,)), ((), ())),
        preferred_element_type=jnp.float32,
    )
    g = grad_att.astype(jnp.bfloat16)
    qg = jnp.concatenate([queries, g], axis=0)
    qg_from = [passed_along(qg, "ctx", -(2**m)) for m in levels]

    own_window = lax.dynamic_slice_in_dim(window, ctx_index * NB, NB, 0)
    own_select = lax.dynamic_slice_in_dim(far_select, ctx_index * NB, NB, 0)
    valid_cols = [block_ids >= 0]
    for offset in range(1, WIN_MAX + 1):
        valid_cols.append((offset <= own_window) & (block_ids - offset >= 0))
    for m in levels:
        valid_cols.append((own_select[:, m] == 1) & (block_ids - NB * 2**m >= 0))
    valid_q = jnp.stack(valid_cols, axis=1).astype(jnp.int32).reshape(-1)

    key_cols = [block_ids >= 0]
    for offset in range(1, WIN_MAX + 1):
        qb = block_ids + offset
        key_cols.append((qb <= last) & (offset <= jnp.take(window, jnp.minimum(qb, last))))
    for m in levels:
        qb = block_ids + NB * 2**m
        key_cols.append((qb <= last) & (jnp.take(far_select[:, m], jnp.minimum(qb, last)) == 1))
    valid_k = jnp.stack(key_cols, axis=1).astype(jnp.int32).reshape(-1)

    attended, query_grad, stats = query_call(
        valid_q, queries, g, keys, values, kv_from, heads_local, n_levels
    )
    partial_out = jnp.dot(attended, out_weight, preferred_element_type=jnp.float32)
    output = lax.psum_scatter(
        partial_out.astype(jnp.bfloat16), "head", scatter_dimension=1, tiled=True
    )

    st_from = [passed_along(stats, "ctx", -(2**m)) for m in levels]
    key_grad, value_grad = key_call(
        valid_k, keys, values, queries, g, stats, qg_from, st_from, heads_local, n_levels
    )
    return output, query_grad, key_grad, value_grad


def solution(mesh):
    return jax.shard_map(
        local,
        mesh=mesh,
        in_specs=(
            P("ctx", "head"),
            P("ctx", "head"),
            P("ctx", "head"),
            P("head", None),
            P("ctx", "head"),
            P(),
            P(),
        ),
        out_specs=(P("ctx", "head"), P("ctx", "head"), P("ctx", "head"), P("ctx", "head")),
        check_vma=False,
    )
```

time: 252 us -> 278 us (1.10)
  waiting for transfers between devices: 56.2 us -> 165 us
  Pallas kernels: 0 us -> 55.7 us
  local copies, waits for them, and re-layouts: 58.8 us -> 10.2 us
  starting transfers between devices: 66.8 us -> 21.6 us
  matrix products: 45.9 us -> 7.34 us
  other arithmetic: 7.35 us -> 1.3 us
    ppermute x18 -> x9, waiting for transfers between devices: 56.1 us -> 156 us  [passed_along(): return lax.ppermute(block, axis, route)]
    pallas_call x0 -> x2, Pallas kernels: none -> 55.7 us  [the longest x1 34.6 us: key_call(): pl.pallas_call(functools.partial(key_kernel, n_levels), grid_spec=grid_sp...]
    ppermute x18 -> x9, starting transfers between devices: 66.7 us -> 21.5 us  [passed_along(): return lax.ppermute(block, axis, route)]
    dot_general x7 -> x1, matrix products: 43.1 us -> 3.65 us  [local(): jnp.dot(attended, out_weight, preferred_element_type=jnp.float32)]
    unnamed x53 -> x23, local copies, waits for them, and re-layouts: 23.2 us -> 2.89 us
    another operation x16 -> x2, local copies, waits for them, and re-layouts: 14.5 us -> 0.07 us  [the longest x1 0.03 us: local(): valid_q = jnp.stack(valid_cols, axis=1).astype(jnp.int32).reshape(-1)]
    reshape x10 -> x0, local copies, waits for them, and re-layouts: 12.1 us -> none  [the longest x2 3.92 us: local(): k = keys.reshape(block_shape)]
    all_gather x1, waiting for transfers between devices: 0.02 us -> 8.46 us  [local(): lax.all_gather(d_out, 'head', axis=1, tiled=True)]
  transfers between devices with their start and end apart: 20 -> 11, of which waited for: 4 -> 7; matrix products, arithmetic and copies ran while one was open for 38% -> 5% of each run, Pallas kernels for 0% -> 13%
where the time goes in v2:
time: 278 us; the launch traced here: 276 us
  waiting for transfers between devices  165 us (59%)
  Pallas kernels  55.7 us (20%)
  starting transfers between devices  21.6 us (8%)
  between operations  14.3 us (5%)
  local copies, waits for them, and re-layouts  10.2 us (4%)
  matrix products  7.34 us (3%)
    ppermute x9, waiting for transfers between devices, passed_along(): return lax.ppermute(block, axis, route)  156 us
    pallas_call x1, Pallas kernels, key_call(): pl.pallas_call(functools.partial(key_kernel, n_levels), grid_spec=grid_sp...  34.6 us
    ppermute x9, starting transfers between devices, passed_along(): return lax.ppermute(block, axis, route)  21.5 us
    pallas_call x1, Pallas kernels, query_call(): pl.pallas_call(functools.partial(query_kernel, n_levels), grid_spec=grid_...  21.1 us
    all_gather x1, waiting for transfers between devices, local(): lax.all_gather(d_out, 'head', axis=1, tiled=True)  8.46 us
  transfers between devices with their start and end apart: 11, of which 7 were waited for; matrix products, arithmetic and copies ran while one was open for 5% of the time, Pallas kernels for 13%

profile of v2, /device:TPU:0, one launch (start us, length us, event | category | flops | bytes accessed | tf_op | source)
XLA Modules:
  0.0 275.6 jit_solution(5515890873459204490)
XLA Ops:
  7.2 0.0 copy-start
  7.2 0.0 copy-start.1
  7.2 0.0 copy-start.10
  7.2 0.0 all-gather.2.cloned.1.call-start
  7.2 0.7 all-gather.2.cloned.1.call-update
  7.9 0.0 reduce-scatter.2.cloned.1.call-start
  8.0 1.9 constant_dynamic-update-slice_fusion.1
  9.9 1.9 constant_dynamic-update-slice_fusion
  11.8 4.9 %collective-permute-start = (bf16[1024,512]{1,0:T(8,128)(2,1)}, bf16[1024,512]{1,0:T(8,128)(2,1)S(1)}, u32[]{:S(2)}, u32[]{:S(2)}) collective-permute-start(bf16[1024,512]{1,0:T(8,128)(2,1)} %constant_dynamic-update-slice_fusion), channel_id=1, source_target_pairs={{0,4},{4,8},{8,12},{12,16},{16,20},{20,24},{24,28},{1,5},{5,9},{9,... | collective-permute-start | bytes 3145736 | tf_op jit(solution)/shard_map/ppermute | solution.py:23
  16.7 4.4 %collective-permute-start.1 = (bf16[1024,512]{1,0:T(8,128)(2,1)}, bf16[1024,512]{1,0:T(8,128)(2,1)}, u32[]{:S(2)}, u32[]{:S(2)}) collective-permute-start(bf16[1024,512]{1,0:T(8,128)(2,1)} %constant_dynamic-update-slice_fusion), channel_id=1, source_target_pairs={{0,8},{4,12},{8,16},{12,20},{16,24},{20,28},{1,9},{5,13},{9,17},{1... | collective-permute-start | bytes 3145736 | tf_op jit(solution)/shard_map/ppermute | solution.py:23
  21.1 4.5 %collective-permute-start.2 = (bf16[1024,512]{1,0:T(8,128)(2,1)}, bf16[1024,512]{1,0:T(8,128)(2,1)}, u32[]{:S(2)}, u32[]{:S(2)}) collective-permute-start(bf16[1024,512]{1,0:T(8,128)(2,1)} %constant_dynamic-update-slice_fusion), channel_id=1, source_target_pairs={{0,16},{4,20},{8,24},{12,28},{1,17},{5,21},{9,25},{13,29},{2,18},{... | collective-permute-start | bytes 3145736 | tf_op jit(solution)/shard_map/ppermute | solution.py:23
  25.6 0.0 copy-done.1
  25.6 0.1 and_bitcast_fusion.6
  25.6 0.0 copy-done.10
  25.6 0.1 constant_dynamic-slice_fusion
  25.8 0.1 copy.13
  25.9 0.6 reshape.52.valid_ref
  26.5 8.5 %all-gather.2.cloned.1.call-done = bf16[512,2048]{1,0:T(8,128)(2,1)} async-done(((bf16[512,512]{1,0:T(8,128)(2,1)}), bf16[512,2048]{1,0:T(8,128)(2,1)}) %all-gather.2.cloned.1.call-update) | async-done | bytes 2097168 | tf_op jit(solution)/shard_map/all_gather | solution.py:211
  34.9 0.0 copy-done
  34.9 3.7 %convolution_convert_fusion.1.g_ref = bf16[512,512]{1,0:T(8,128)(2,1)} fusion(bf16[512,2048]{1,0:T(8,128)(2,1)} %all-gather.2.cloned.1.call-done, bf16[512,2048]{1,0:T(8,128)(2,1)S(1)} %copy-done), kind=kOutput, calls=%fused_computation.7 | convolution fusion | flops 1074003968 | bytes 4718592 | tf_op jit(solution)/shard_map/dot_general | solution.py:210
  38.6 0.7 collective-permute-done.rest_0_.rest_1_
  39.3 0.0 copy-start.5
  39.3 4.7 %collective-permute-done.1.rest_2_.rest_3_ = bf16[1024,512]{1,0:T(8,128)(2,1)} collective-permute-done((bf16[1024,512]{1,0:T(8,128)(2,1)}, bf16[1024,512]{1,0:T(8,128)(2,1)}, u32[]{:S(2)}, u32[]{:S(2)}) %collective-permute-start.1) | collective-permute-done | bytes 1048608 | tf_op jit(solution)/shard_map/ppermute | solution.py:23
  44.0 21.1 %collective-permute-done.2.rest_4_.rest_5_ = bf16[1024,512]{1,0:T(8,128)(2,1)} collective-permute-done((bf16[1024,512]{1,0:T(8,128)(2,1)}, bf16[1024,512]{1,0:T(8,128)(2,1)}, u32[]{:S(2)}, u32[]{:S(2)}) %collective-permute-start.2) | collective-permute-done | bytes 1048608 | tf_op jit(solution)/shard_map/ppermute | solution.py:23
  65.0 0.0 copy-done.5
  65.0 21.1 %query_side.1 = (bf16[512,512]{1,0:T(8,128)(2,1)}, bf16[512,512]{1,0:T(8,128)(2,1)}, f32[2,4,4,128]{3,2,1,0:T(4,128)}) custom-call(s32[28]{0:T(128)} %reshape.52.valid_ref, bf16[512,512]{1,0:T(8,128)(2,1)} %q_ref.3, bf16[512,512]{1,0:T(8,128)(2,1)} %convolution_convert_fusion.1.g_ref, bf16[512,512]{1,0:T(8,128)(2,1)} %k_ref.3, bf16[512,512]{1,0:T(8,128)(2,1)} %v_ref.3, ...), custom_call_target="tpu_custom_call" | custom-call | tf_op jit(solution)/shard_map/query_side/pallas_call | solution.py:159
  86.2 3.7 %convolution_convert_fusion = bf16[512,2048]{1,0:T(8,128)(2,1)} fusion(bf16[512,512]{1,0:T(8,128)(2,1)} %get-tuple-element.10, bf16[512,2048]{1,0:T(8,128)(2,1)S(1)} %copy-done), kind=kOutput, calls=%fused_computation.6 | convolution fusion | flops 1074790400 | bytes 4718592 | tf_op jit(solution)/shard_map/dot_general | solution.py:241
  89.8 0.0 copy-start.2
  89.8 0.0 copy-start.3
  89.8 0.0 reduce-scatter.2.cloned.1.call-update
  89.9 0.6 gather_fusion
  90.5 0.0 copy-start.6
  90.5 0.6 gather_fusion.1
  91.2 0.0 copy-done.2
  91.3 0.0 copy-done.3
  91.3 1.1 pad_maximum_fusion
  92.3 1.3 collective-permute-start.3
  93.6 1.3 collective-permute-start.5
  94.9 1.3 collective-permute-start.7
  96.2 0.6 gather_fusion.2
  96.9 0.6 gather_fusion.3
  97.5 0.6 gather_fusion.4
  98.2 0.0 copy-done.6
  98.2 1.3 collective-permute-start.4
  99.5 0.6 gather_fusion.5
  100.2 1.3 collective-permute-start.6
  101.5 36.4 %collective-permute-done.4.rest_2_ = f32[2,4,4,128]{3,2,1,0:T(4,128)S(1)} collective-permute-done((f32[2,4,4,128]{3,2,1,0:T(4,128)S(1)}, f32[2,4,4,128]{3,2,1,0:T(4,128)S(1)}, u32[]{:S(2)}, u32[]{:S(2)}) %collective-permute-start.4) | collective-permute-done | bytes 16416 | tf_op jit(solution)/shard_map/ppermute | solution.py:23
  137.9 0.0 copy-start.7
  137.9 1.3 collective-permute-start.8
  139.2 0.1 copy.14
  139.3 0.7 reshape.53.valid_ref
  140.0 23.6 %collective-permute-done.6.rest_5_ = f32[2,4,4,128]{3,2,1,0:T(4,128)S(1)} collective-permute-done((f32[2,4,4,128]{3,2,1,0:T(4,128)S(1)}, f32[2,4,4,128]{3,2,1,0:T(4,128)S(1)}, u32[]{:S(2)}, u32[]{:S(2)}) %collective-permute-start.6) | collective-permute-done | bytes 16416 | tf_op jit(solution)/shard_map/ppermute | solution.py:23
  163.6 0.0 copy-start.8
  163.6 69.6 %collective-permute-done.8.rest_8_ = f32[2,4,4,128]{3,2,1,0:T(4,128)S(1)} collective-permute-done((f32[2,4,4,128]{3,2,1,0:T(4,128)S(1)}, f32[2,4,4,128]{3,2,1,0:T(4,128)S(1)}, u32[]{:S(2)}, u32[]{:S(2)}) %collective-permute-start.8) | collective-permute-done | bytes 16416 | tf_op jit(solution)/shard_map/ppermute | solution.py:23
  233.1 0.0 copy-start.9
  233.1 0.0 collective-permute-done.3.rest_0_.rest_1_
  233.1 0.0 collective-permute-done.5.rest_3_.rest_4_
  233.1 0.0 collective-permute-done.7.rest_6_.rest_7_
  233.1 0.0 copy-done.7
  233.2 0.0 copy-done.8
  233.2 0.6 copy-done.9
  233.7 0.4 copy-done.4
  234.1 34.6 %key_side.1 = (bf16[512,512]{1,0:T(8,128)(2,1)}, bf16[512,512]{1,0:T(8,128)(2,1)}) custom-call(s32[28]{0:T(128)} %reshape.53.valid_ref, bf16[512,512]{1,0:T(8,128)(2,1)} %k_ref.3, bf16[512,512]{1,0:T(8,128)(2,1)} %v_ref.3, bf16[512,512]{1,0:T(8,128)(2,1)} %q_ref.3, bf16[512,512]{1,0:T(8,128)(2,1)} %convolution_convert_fusion.1.g_ref, ...), custom_call_target="tpu_custom_call" | custom-call | tf_op jit(solution)/shard_map/key_side/pallas_call | solution.py:184
  268.7 0.0 reduce-scatter.2.cloned.1.call-done
  (22 shorter events, 0.2 us)
Async XLA Ops:
  7.2 27.8 %copy-start = (bf16[512,2048]{1,0:T(8,128)(2,1)S(1)}, bf16[512,2048]{1,0:T(8,128)(2,1)}, u32[]{:S(2)}) copy-start(bf16[512,2048]{1,0:T(8,128)(2,1)} %param.12) | copy-start | bytes 6291460
  7.2 18.4 %copy-start.1 = (s32[32]{0:T(128)S(1)}, s32[32]{0:T(128)}, u32[]{:S(2)}) copy-start(s32[32]{0:T(128)} %param.14) | copy-start | bytes 388
  7.2 18.5 %copy-start.10 = (s32[32,5]{0,1:T(8,128)S(1)}, s32[32,5]{0,1:T(8,128)}, u32[]{:S(2)}) copy-start(s32[32,5]{0,1:T(8,128)} %param.15) | copy-start | bytes 1924
  7.2 27.7 %all-gather.2.cloned.1.call-start = ((), (), s32[]{:S(2)}) async-start(), calls=%async_computation.1 | async-start | bytes 2621440 | tf_op jit(solution)/shard_map/all_gather | solution.py:211
  7.9 260.8 %reduce-scatter.2.cloned.1.call-start = ((), (), s32[]{:S(2)}) async-start(), calls=%async_computation.2 | async-start | bytes 2621440 | tf_op jit(solution)/shard_map/reduce_scatter | solution.py:242
  11.8 27.6 %collective-permute-start = (bf16[1024,512]{1,0:T(8,128)(2,1)}, bf16[1024,512]{1,0:T(8,128)(2,1)S(1)}, u32[]{:S(2)}, u32[]{:S(2)}) collective-permute-start(bf16[1024,512]{1,0:T(8,128)(2,1)} %constant_dynamic-update-slice_fusion), channel_id=1, source_target_pairs={{0,4},{4,8},{8,12},{12,16},{16,20},{20,24},{24,28},{1,5},{5,9},{9,... | collective-permute-start | bytes 3145736 | tf_op jit(solution)/shard_map/ppermute | solution.py:23
  16.7 27.3 %collective-permute-start.1 = (bf16[1024,512]{1,0:T(8,128)(2,1)}, bf16[1024,512]{1,0:T(8,128)(2,1)}, u32[]{:S(2)}, u32[]{:S(2)}) collective-permute-start(bf16[1024,512]{1,0:T(8,128)(2,1)} %constant_dynamic-update-slice_fusion), channel_id=1, source_target_pairs={{0,8},{4,12},{8,16},{12,20},{16,24},{20,28},{1,9},{5,13},{9,17},{1... | collective-permute-start | bytes 3145736 | tf_op jit(solution)/shard_map/ppermute | solution.py:23
  21.1 44.0 %collective-permute-start.2 = (bf16[1024,512]{1,0:T(8,128)(2,1)}, bf16[1024,512]{1,0:T(8,128)(2,1)}, u32[]{:S(2)}, u32[]{:S(2)}) collective-permute-start(bf16[1024,512]{1,0:T(8,128)(2,1)} %constant_dynamic-update-slice_fusion), channel_id=1, source_target_pairs={{0,16},{4,20},{8,24},{12,28},{1,17},{5,21},{9,25},{13,29},{2,18},{... | collective-permute-start | bytes 3145736 | tf_op jit(solution)/shard_map/ppermute | solution.py:23
  39.3 25.7 %copy-start.5 = (bf16[1024,512]{1,0:T(8,128)(2,1)}, bf16[1024,512]{1,0:T(8,128)(2,1)S(1)}, u32[]{:S(2)}) copy-start(bf16[1024,512]{1,0:T(8,128)(2,1)S(1)} %collective-permute-done.rest_0_.rest_1_) | copy-start | bytes 3145732
  89.8 1.4 copy-start.2
  89.8 1.5 copy-start.3
  90.5 7.7 %copy-start.6 = (f32[2,4,4,128]{3,2,1,0:T(4,128)S(1)}, f32[2,4,4,128]{3,2,1,0:T(4,128)}, u32[]{:S(2)}) copy-start(f32[2,4,4,128]{3,2,1,0:T(4,128)} %get-tuple-element.12.st_ref) | copy-start | bytes 49156
  92.3 140.8 %collective-permute-start.3 = (bf16[1024,512]{1,0:T(8,128)(2,1)}, bf16[1024,512]{1,0:T(8,128)(2,1)S(1)}, u32[]{:S(2)}, u32[]{:S(2)}) collective-permute-start(bf16[1024,512]{1,0:T(8,128)(2,1)} %pad_maximum_fusion), channel_id=1, source_target_pairs={{4,0},{8,4},{12,8},{16,12},{20,16},{24,20},{28,24},{5,1},{9,5},{13... | collective-permute-start | bytes 3145736 | tf_op jit(solution)/shard_map/ppermute | solution.py:23
  93.6 139.5 %collective-permute-start.5 = (bf16[1024,512]{1,0:T(8,128)(2,1)}, bf16[1024,512]{1,0:T(8,128)(2,1)}, u32[]{:S(2)}, u32[]{:S(2)}) collective-permute-start(bf16[1024,512]{1,0:T(8,128)(2,1)} %pad_maximum_fusion), channel_id=1, source_target_pairs={{8,0},{12,4},{16,8},{20,12},{24,16},{28,20},{9,1},{13,5},{17,9},{2... | collective-permute-start | bytes 3145736 | tf_op jit(solution)/shard_map/ppermute | solution.py:23
  94.9 138.2 %collective-permute-start.7 = (bf16[1024,512]{1,0:T(8,128)(2,1)}, bf16[1024,512]{1,0:T(8,128)(2,1)}, u32[]{:S(2)}, u32[]{:S(2)}) collective-permute-start(bf16[1024,512]{1,0:T(8,128)(2,1)} %pad_maximum_fusion), channel_id=1, source_target_pairs={{16,0},{20,4},{24,8},{28,12},{17,1},{21,5},{25,9},{29,13},{18,2},{... | collective-permute-start | bytes 3145736 | tf_op jit(solution)/shard_map/ppermute | solution.py:23
  98.2 39.7 %collective-permute-start.4 = (f32[2,4,4,128]{3,2,1,0:T(4,128)S(1)}, f32[2,4,4,128]{3,2,1,0:T(4,128)S(1)}, u32[]{:S(2)}, u32[]{:S(2)}) collective-permute-start(f32[2,4,4,128]{3,2,1,0:T(4,128)S(1)} %copy-done.6), channel_id=1, source_target_pairs={{4,0},{8,4},{12,8},{16,12},{20,16},{24,20},{28,24},{5,1},{9,5},{13... | collective-permute-start | bytes 49160 | tf_op jit(solution)/shard_map/ppermute | solution.py:23
  100.2 63.4 %collective-permute-start.6 = (f32[2,4,4,128]{3,2,1,0:T(4,128)S(1)}, f32[2,4,4,128]{3,2,1,0:T(4,128)S(1)}, u32[]{:S(2)}, u32[]{:S(2)}) collective-permute-start(f32[2,4,4,128]{3,2,1,0:T(4,128)S(1)} %copy-done.6), channel_id=1, source_target_pairs={{8,0},{12,4},{16,8},{20,12},{24,16},{28,20},{9,1},{13,5},{17,9},{2... | collective-permute-start | bytes 49160 | tf_op jit(solution)/shard_map/ppermute | solution.py:23
  137.9 95.3 %copy-start.7 = (f32[2,4,4,128]{3,2,1,0:T(4,128)}, f32[2,4,4,128]{3,2,1,0:T(4,128)S(1)}, u32[]{:S(2)}) copy-start(f32[2,4,4,128]{3,2,1,0:T(4,128)S(1)} %collective-permute-done.4.rest_2_) | copy-start | bytes 49156
  137.9 95.2 %collective-permute-start.8 = (f32[2,4,4,128]{3,2,1,0:T(4,128)S(1)}, f32[2,4,4,128]{3,2,1,0:T(4,128)S(1)}, u32[]{:S(2)}, u32[]{:S(2)}) collective-permute-start(f32[2,4,4,128]{3,2,1,0:T(4,128)S(1)} %copy-done.6), channel_id=1, source_target_pairs={{16,0},{20,4},{24,8},{28,12},{17,1},{21,5},{25,9},{29,13},{18,2},{... | collective-permute-start | bytes 49160 | tf_op jit(solution)/shard_map/ppermute | solution.py:23
  163.6 69.6 %copy-start.8 = (f32[2,4,4,128]{3,2,1,0:T(4,128)}, f32[2,4,4,128]{3,2,1,0:T(4,128)S(1)}, u32[]{:S(2)}) copy-start(f32[2,4,4,128]{3,2,1,0:T(4,128)S(1)} %collective-permute-done.6.rest_5_) | copy-start | bytes 49156
  233.1 0.6 copy-start.9
  233.1 1.0 copy-start.4
Sparse Core Ops, SparseCore 0:
  9.6 25.2 all-gather.1
  90.0 75.2 reduce-scatter.1

commit v3 on v2

--- a/solution.py
+++ b/solution.py
@@ -216,6 +216,7 @@
     g = grad_att.astype(jnp.bfloat16)
     qg = jnp.concatenate([queries, g], axis=0)
     qg_from = [passed_along(qg, "ctx", -(2**m)) for m in levels]
+    kv_from, qg_from = lax.optimization_barrier((kv_from, qg_from))
 
     own_window = lax.dynamic_slice_in_dim(window, ctx_index * NB, NB, 0)
     own_select = lax.dynamic_slice_in_dim(far_select, ctx_index * NB, NB, 0)

time: 278 us -> 214 us (0.77)
  the two profiles are of different devices: /device:TPU:0 before, /device:TPU:18 now
where the time goes in v3:
time: 214 us; the launch traced here: 213 us
  waiting for transfers between devices  82.9 us (39%)
  Pallas kernels  55.8 us (26%)
  starting transfers between devices  42.8 us (20%)
  between operations  14.3 us (7%)
  local copies, waits for them, and re-layouts  9.82 us (5%)
  matrix products  6.5 us (3%)
    ppermute x9, waiting for transfers between devices, passed_along(): return lax.ppermute(block, axis, route)  67.5 us
    ppermute x9, starting transfers between devices, passed_along(): return lax.ppermute(block, axis, route)  42.7 us
    pallas_call x1, Pallas kernels, key_call(): pl.pallas_call(functools.partial(key_kernel, n_levels), grid_spec=grid_sp...  34.6 us
    pallas_call x1, Pallas kernels, query_call(): pl.pallas_call(functools.partial(query_kernel, n_levels), grid_spec=grid_...  21.1 us
    all_gather x1, waiting for transfers between devices, local(): lax.all_gather(d_out, 'head', axis=1, tiled=True)  14.7 us
  transfers between devices with their start and end apart: 11, of which 7 were waited for; matrix products, arithmetic and copies ran while one was open for 6% of the time, Pallas kernels for 16%

profile of v3, /device:TPU:18, one launch (start us, length us, event | category | flops | bytes accessed | tf_op | source)
XLA Modules:
  0.0 213.5 jit_solution(1728131862844497283)
XLA Ops:
  7.2 0.0 copy-start
  7.2 0.0 all-gather.2.cloned.1.call-start
  7.2 0.7 all-gather.2.cloned.1.call-update
  7.9 0.0 reduce-scatter.2.cloned.1.call-start
  8.0 1.9 constant_dynamic-update-slice_fusion.1
  9.8 1.9 constant_dynamic-update-slice_fusion
  11.7 0.0 copy-start.2
  11.7 1.4 collective-permute-start.2
  13.1 3.5 %collective-permute-start.1 = (bf16[1024,512]{1,0:T(8,128)(2,1)}, bf16[1024,512]{1,0:T(8,128)(2,1)}, u32[]{:S(2)}, u32[]{:S(2)}) collective-permute-start(bf16[1024,512]{1,0:T(8,128)(2,1)} %constant_dynamic-update-slice_fusion), channel_id=1, source_target_pairs={{0,8},{4,12},{8,16},{12,20},{16,24},{20,28},{1,9},{5,13},{9,17},{1... | collective-permute-start | bytes 3145736 | tf_op jit(solution)/shard_map/ppermute | solution.py:23
  16.6 1.9 collective-permute-start
  18.6 14.7 %all-gather.2.cloned.1.call-done = bf16[512,2048]{1,0:T(8,128)(2,1)} async-done(((bf16[512,512]{1,0:T(8,128)(2,1)}), bf16[512,2048]{1,0:T(8,128)(2,1)}) %all-gather.2.cloned.1.call-update) | async-done | bytes 2097168 | tf_op jit(solution)/shard_map/all_gather | solution.py:211
  33.2 0.0 copy-done
  33.3 2.9 %convolution_convert_fusion.1.g_ref = bf16[512,512]{1,0:T(8,128)(2,1)S(1)} fusion(bf16[512,2048]{1,0:T(8,128)(2,1)} %all-gather.2.cloned.1.call-done, bf16[512,2048]{1,0:T(8,128)(2,1)S(1)} %copy-done), kind=kOutput, calls=%fused_computation.7 | convolution fusion | flops 1074003968 | bytes 4718592 | tf_op jit(solution)/shard_map/dot_general | solution.py:210
  36.1 0.0 copy-done.2
  36.1 0.0 copy-start.3
  36.1 0.0 copy-start.1
  36.2 0.0 copy-start.8
  36.2 1.1 pad_maximum_fusion
  37.3 3.4 %collective-permute-start.5 = (bf16[1024,512]{1,0:T(8,128)(2,1)}, bf16[1024,512]{1,0:T(8,128)(2,1)}, u32[]{:S(2)}, u32[]{:S(2)}) collective-permute-start(bf16[1024,512]{1,0:T(8,128)(2,1)} %pad_maximum_fusion), channel_id=1, source_target_pairs={{16,0},{20,4},{24,8},{28,12},{17,1},{21,5},{25,9},{29,13},{18,2},{... | collective-permute-start | bytes 3145736 | tf_op jit(solution)/shard_map/ppermute | solution.py:23
  40.7 1.9 collective-permute-start.4
  42.6 0.0 collective-permute-done.2.rest_4_.rest_5_
  42.6 2.5 %collective-permute-start.3 = (bf16[1024,512]{1,0:T(8,128)(2,1)}, bf16[1024,512]{1,0:T(8,128)(2,1)}, u32[]{:S(2)}, u32[]{:S(2)}) collective-permute-start(bf16[1024,512]{1,0:T(8,128)(2,1)} %pad_maximum_fusion), channel_id=1, source_target_pairs={{4,0},{8,4},{12,8},{16,12},{20,16},{24,20},{28,24},{5,1},{9,5},{13... | collective-permute-start | bytes 3145736 | tf_op jit(solution)/shard_map/ppermute | solution.py:23
  45.1 0.0 copy-done.1
  45.1 0.1 and_bitcast_fusion.6
  45.2 0.0 copy-done.8
  45.2 0.1 constant_dynamic-slice_fusion
  45.3 0.1 copy.13
  45.4 0.6 reshape.52.valid_ref
  46.0 38.9 %collective-permute-done.1.rest_2_.rest_3_ = bf16[1024,512]{1,0:T(8,128)(2,1)} collective-permute-done((bf16[1024,512]{1,0:T(8,128)(2,1)}, bf16[1024,512]{1,0:T(8,128)(2,1)}, u32[]{:S(2)}, u32[]{:S(2)}) %collective-permute-start.1) | collective-permute-done | bytes 1048608 | tf_op jit(solution)/shard_map/ppermute | solution.py:23
  84.9 0.0 collective-permute-done.rest_0_.rest_1_
  84.9 1.1 collective-permute-done.5.rest_6_.rest_7_
  86.0 21.8 %collective-permute-done.4.rest_3_.rest_4_ = bf16[1024,512]{1,0:T(8,128)(2,1)} collective-permute-done((bf16[1024,512]{1,0:T(8,128)(2,1)}, bf16[1024,512]{1,0:T(8,128)(2,1)}, u32[]{:S(2)}, u32[]{:S(2)}) %collective-permute-start.4) | collective-permute-done | bytes 1048608 | tf_op jit(solution)/shard_map/ppermute | solution.py:23
  107.8 2.0 collective-permute-done.3.rest_0_.rest_1_
  109.8 0.0 copy-done.3
  109.8 21.1 %query_side.1 = (bf16[512,512]{1,0:T(8,128)(2,1)}, bf16[512,512]{1,0:T(8,128)(2,1)}, f32[2,4,4,128]{3,2,1,0:T(4,128)}) custom-call(s32[28]{0:T(128)} %reshape.52.valid_ref, bf16[512,512]{1,0:T(8,128)(2,1)} %q_ref.3, bf16[512,512]{1,0:T(8,128)(2,1)} %copy-done.3, bf16[512,512]{1,0:T(8,128)(2,1)} %k_ref.3, bf16[512,512]{1,0:T(8,128)(2,1)} %v_ref.3, ...), custom_call_target="tpu_custom_call" | custom-call | tf_op jit(solution)/shard_map/query_side/pallas_call | solution.py:159
  130.9 3.6 %convolution_convert_fusion = bf16[512,2048]{1,0:T(8,128)(2,1)} fusion(bf16[512,512]{1,0:T(8,128)(2,1)} %get-tuple-element.19, bf16[512,2048]{1,0:T(8,128)(2,1)S(1)} %copy-done), kind=kOutput, calls=%fused_computation.6 | convolution fusion | flops 1074790400 | bytes 4718592 | tf_op jit(solution)/shard_map/dot_general | solution.py:242
  134.5 0.0 reduce-scatter.2.cloned.1.call-update
  134.5 0.0 copy-start.4
  134.6 0.6 gather_fusion.1
  135.2 0.6 gather_fusion.2
  135.9 0.6 gather_fusion
  136.6 0.6 gather_fusion.5
  137.2 0.6 gather_fusion.3
  137.8 0.6 gather_fusion.4
  138.6 0.0 copy-done.4
  138.6 3.3 %collective-permute-start.8 = (f32[2,4,4,128]{3,2,1,0:T(4,128)S(1)}, f32[2,4,4,128]{3,2,1,0:T(4,128)S(1)}, u32[]{:S(2)}, u32[]{:S(2)}) collective-permute-start(f32[2,4,4,128]{3,2,1,0:T(4,128)S(1)} %copy-done.4), channel_id=1, source_target_pairs={{16,0},{20,4},{24,8},{28,12},{17,1},{21,5},{25,9},{29,13},{18,2},{... | collective-permute-start | bytes 49160 | tf_op jit(solution)/shard_map/ppermute | solution.py:23
  141.9 22.9 %collective-permute-start.7 = (f32[2,4,4,128]{3,2,1,0:T(4,128)S(1)}, f32[2,4,4,128]{3,2,1,0:T(4,128)S(1)}, u32[]{:S(2)}, u32[]{:S(2)}) collective-permute-start(f32[2,4,4,128]{3,2,1,0:T(4,128)S(1)} %copy-done.4), channel_id=1, source_target_pairs={{8,0},{12,4},{16,8},{20,12},{24,16},{28,20},{9,1},{13,5},{17,9},{2... | collective-permute-start | bytes 49160 | tf_op jit(solution)/shard_map/ppermute | solution.py:23
  164.8 1.9 collective-permute-start.6
  166.8 0.1 copy.14
  166.9 0.7 reshape.53.valid_ref
  167.6 0.0 collective-permute-done.8.rest_8_
  167.6 0.0 copy-start.5
  167.6 0.4 collective-permute-done.7.rest_5_
  168.0 0.0 copy-start.6
  168.0 3.4 %collective-permute-done.6.rest_2_ = f32[2,4,4,128]{3,2,1,0:T(4,128)S(1)} collective-permute-done((f32[2,4,4,128]{3,2,1,0:T(4,128)S(1)}, f32[2,4,4,128]{3,2,1,0:T(4,128)S(1)}, u32[]{:S(2)}, u32[]{:S(2)}) %collective-permute-start.6) | collective-permute-done | bytes 16416 | tf_op jit(solution)/shard_map/ppermute | solution.py:23
  171.3 0.0 copy-done.5
  171.3 0.0 copy-done.6
  171.3 0.0 copy-start.7
  171.4 0.6 copy-done.7
  172.0 34.6 %key_side.1 = (bf16[512,512]{1,0:T(8,128)(2,1)}, bf16[512,512]{1,0:T(8,128)(2,1)}) custom-call(s32[28]{0:T(128)} %reshape.53.valid_ref, bf16[512,512]{1,0:T(8,128)(2,1)} %k_ref.3, bf16[512,512]{1,0:T(8,128)(2,1)} %v_ref.3, bf16[512,512]{1,0:T(8,128)(2,1)} %q_ref.3, bf16[512,512]{1,0:T(8,128)(2,1)} %copy-done.3, f32[2,4,4,128]{3,2,1,0:T(4,128)} %get-tuple-element.21.st_ref, ...), custom_call_target="tpu_custom_call" | custom-call | tf_op jit(solution)/shard_map/key_side/pallas_call | solution.py:184
  206.6 0.0 reduce-scatter.2.cloned.1.call-done
  (21 shorter events, 0.2 us)
Async XLA Ops:
  7.2 26.1 %copy-start = (bf16[512,2048]{1,0:T(8,128)(2,1)S(1)}, bf16[512,2048]{1,0:T(8,128)(2,1)}, u32[]{:S(2)}) copy-start(bf16[512,2048]{1,0:T(8,128)(2,1)} %param.12) | copy-start | bytes 6291460
  7.2 26.1 %all-gather.2.cloned.1.call-start = ((), (), s32[]{:S(2)}) async-start(), calls=%async_computation.1 | async-start | bytes 2621440 | tf_op jit(solution)/shard_map/all_gather | solution.py:211
  7.9 198.7 %reduce-scatter.2.cloned.1.call-start = ((), (), s32[]{:S(2)}) async-start(), calls=%async_computation.2 | async-start | bytes 2621440 | tf_op jit(solution)/shard_map/reduce_scatter | solution.py:243
  11.7 24.4 %copy-start.2 = (bf16[512,512]{1,0:T(8,128)(2,1)S(1)}, bf16[512,512]{1,0:T(8,128)(2,1)}, u32[]{:S(2)}) copy-start(bf16[512,512]{1,0:T(8,128)(2,1)} %q_ref.3) | copy-start | bytes 1572868
  11.7 30.9 %collective-permute-start.2 = (bf16[1024,512]{1,0:T(8,128)(2,1)}, bf16[1024,512]{1,0:T(8,128)(2,1)}, u32[]{:S(2)}, u32[]{:S(2)}) collective-permute-start(bf16[1024,512]{1,0:T(8,128)(2,1)} %constant_dynamic-update-slice_fusion), channel_id=1, source_target_pairs={{0,16},{4,20},{8,24},{12,28},{1,17},{5,21},{9,25},{13,29},{2,18},{... | collective-permute-start | bytes 3145736 | tf_op jit(solution)/shard_map/ppermute | solution.py:23
  13.1 71.8 %collective-permute-start.1 = (bf16[1024,512]{1,0:T(8,128)(2,1)}, bf16[1024,512]{1,0:T(8,128)(2,1)}, u32[]{:S(2)}, u32[]{:S(2)}) collective-permute-start(bf16[1024,512]{1,0:T(8,128)(2,1)} %constant_dynamic-update-slice_fusion), channel_id=1, source_target_pairs={{0,8},{4,12},{8,16},{12,20},{16,24},{20,28},{1,9},{5,13},{9,17},{1... | collective-permute-start | bytes 3145736 | tf_op jit(solution)/shard_map/ppermute | solution.py:23
  16.6 68.3 %collective-permute-start = (bf16[1024,512]{1,0:T(8,128)(2,1)}, bf16[1024,512]{1,0:T(8,128)(2,1)}, u32[]{:S(2)}, u32[]{:S(2)}) collective-permute-start(bf16[1024,512]{1,0:T(8,128)(2,1)} %constant_dynamic-update-slice_fusion), channel_id=1, source_target_pairs={{0,4},{4,8},{8,12},{12,16},{16,20},{20,24},{24,28},{1,5},{5,9},{9,... | collective-permute-start | bytes 3145736 | tf_op jit(solution)/shard_map/ppermute | solution.py:23
  36.1 73.6 %copy-start.3 = (bf16[512,512]{1,0:T(8,128)(2,1)}, bf16[512,512]{1,0:T(8,128)(2,1)S(1)}, u32[]{:S(2)}) copy-start(bf16[512,512]{1,0:T(8,128)(2,1)S(1)} %convolution_convert_fusion.1.g_ref) | copy-start | bytes 1572868
  36.1 9.0 %copy-start.1 = (s32[32]{0:T(128)S(1)}, s32[32]{0:T(128)}, u32[]{:S(2)}) copy-start(s32[32]{0:T(128)} %param.14) | copy-start | bytes 388
  36.2 9.1 %copy-start.8 = (s32[32,5]{0,1:T(8,128)S(1)}, s32[32,5]{0,1:T(8,128)}, u32[]{:S(2)}) copy-start(s32[32,5]{0,1:T(8,128)} %param.15) | copy-start | bytes 1924
  37.3 48.7 %collective-permute-start.5 = (bf16[1024,512]{1,0:T(8,128)(2,1)}, bf16[1024,512]{1,0:T(8,128)(2,1)}, u32[]{:S(2)}, u32[]{:S(2)}) collective-permute-start(bf16[1024,512]{1,0:T(8,128)(2,1)} %pad_maximum_fusion), channel_id=1, source_target_pairs={{16,0},{20,4},{24,8},{28,12},{17,1},{21,5},{25,9},{29,13},{18,2},{... | collective-permute-start | bytes 3145736 | tf_op jit(solution)/shard_map/ppermute | solution.py:23
  40.7 67.1 %collective-permute-start.4 = (bf16[1024,512]{1,0:T(8,128)(2,1)}, bf16[1024,512]{1,0:T(8,128)(2,1)}, u32[]{:S(2)}, u32[]{:S(2)}) collective-permute-start(bf16[1024,512]{1,0:T(8,128)(2,1)} %pad_maximum_fusion), channel_id=1, source_target_pairs={{8,0},{12,4},{16,8},{20,12},{24,16},{28,20},{9,1},{13,5},{17,9},{2... | collective-permute-start | bytes 3145736 | tf_op jit(solution)/shard_map/ppermute | solution.py:23
  42.6 67.1 %collective-permute-start.3 = (bf16[1024,512]{1,0:T(8,128)(2,1)}, bf16[1024,512]{1,0:T(8,128)(2,1)}, u32[]{:S(2)}, u32[]{:S(2)}) collective-permute-start(bf16[1024,512]{1,0:T(8,128)(2,1)} %pad_maximum_fusion), channel_id=1, source_target_pairs={{4,0},{8,4},{12,8},{16,12},{20,16},{24,20},{28,24},{5,1},{9,5},{13... | collective-permute-start | bytes 3145736 | tf_op jit(solution)/shard_map/ppermute | solution.py:23
  134.5 4.0 %copy-start.4 = (f32[2,4,4,128]{3,2,1,0:T(4,128)S(1)}, f32[2,4,4,128]{3,2,1,0:T(4,128)}, u32[]{:S(2)}) copy-start(f32[2,4,4,128]{3,2,1,0:T(4,128)} %get-tuple-element.21.st_ref) | copy-start | bytes 49156
  138.6 29.0 %collective-permute-start.8 = (f32[2,4,4,128]{3,2,1,0:T(4,128)S(1)}, f32[2,4,4,128]{3,2,1,0:T(4,128)S(1)}, u32[]{:S(2)}, u32[]{:S(2)}) collective-permute-start(f32[2,4,4,128]{3,2,1,0:T(4,128)S(1)} %copy-done.4), channel_id=1, source_target_pairs={{16,0},{20,4},{24,8},{28,12},{17,1},{21,5},{25,9},{29,13},{18,2},{... | collective-permute-start | bytes 49160 | tf_op jit(solution)/shard_map/ppermute | solution.py:23
  141.9 26.1 %collective-permute-start.7 = (f32[2,4,4,128]{3,2,1,0:T(4,128)S(1)}, f32[2,4,4,128]{3,2,1,0:T(4,128)S(1)}, u32[]{:S(2)}, u32[]{:S(2)}) collective-permute-start(f32[2,4,4,128]{3,2,1,0:T(4,128)S(1)} %copy-done.4), channel_id=1, source_target_pairs={{8,0},{12,4},{16,8},{20,12},{24,16},{28,20},{9,1},{13,5},{17,9},{2... | collective-permute-start | bytes 49160 | tf_op jit(solution)/shard_map/ppermute | solution.py:23
  164.8 6.5 %collective-permute-start.6 = (f32[2,4,4,128]{3,2,1,0:T(4,128)S(1)}, f32[2,4,4,128]{3,2,1,0:T(4,128)S(1)}, u32[]{:S(2)}, u32[]{:S(2)}) collective-permute-start(f32[2,4,4,128]{3,2,1,0:T(4,128)S(1)} %copy-done.4), channel_id=1, source_target_pairs={{4,0},{8,4},{12,8},{16,12},{20,16},{24,20},{28,24},{5,1},{9,5},{13... | collective-permute-start | bytes 49160 | tf_op jit(solution)/shard_map/ppermute | solution.py:23
  167.6 3.8 %copy-start.5 = (f32[2,4,4,128]{3,2,1,0:T(4,128)}, f32[2,4,4,128]{3,2,1,0:T(4,128)S(1)}, u32[]{:S(2)}) copy-start(f32[2,4,4,128]{3,2,1,0:T(4,128)S(1)} %collective-permute-done.8.rest_8_) | copy-start | bytes 49156
  168.0 3.4 %copy-start.6 = (f32[2,4,4,128]{3,2,1,0:T(4,128)}, f32[2,4,4,128]{3,2,1,0:T(4,128)S(1)}, u32[]{:S(2)}) copy-start(f32[2,4,4,128]{3,2,1,0:T(4,128)S(1)} %collective-permute-done.7.rest_5_) | copy-start | bytes 49156
  171.3 0.6 copy-start.7
Sparse Core Ops, SparseCore 0:
  9.6 23.6 all-gather.1
  134.7 52.2 reduce-scatter.1

commit v4 on v3

--- a/solution.py
+++ b/solution.py
@@ -38,15 +38,26 @@
     return jnp.sum(jnp.where(eye, col, 0.0), axis=0, keepdims=True)
 
 
+def candidate_mask(valid_ref, base, n_cand, diag):
+    width = n_cand * BLK
+    col = lax.broadcasted_iota(jnp.int32, (BLK, width), 1)
+    allowed = (col < BLK) & diag
+    for ci in range(1, n_cand):
+        inside = (col >= ci * BLK) & (col < (ci + 1) * BLK)
+        allowed = allowed | (inside & (valid_ref[base + ci] != 0))
+    return allowed
+
+
 def query_kernel(n_levels, valid_ref, q_ref, g_ref, k_ref, v_ref, *rest):
     kf = rest[0 : 2 * n_levels : 2]
     vf = rest[1 : 2 * n_levels : 2]
     att_ref, dq_ref, st_ref = rest[2 * n_levels :]
     n_cand = 1 + WIN_MAX + n_levels
+    width = n_cand * BLK
     scale = HD ** (-0.5)
-    causal = lax.broadcasted_iota(jnp.int32, (BLK, BLK), 1) <= lax.broadcasted_iota(
-        jnp.int32, (BLK, BLK), 0
-    )
+    col = lax.broadcasted_iota(jnp.int32, (BLK, width), 1)
+    row = lax.broadcasted_iota(jnp.int32, (BLK, width), 0)
+    diag = col <= row
     for n in range(NB):
         rows = pl.ds(n * BLK, BLK)
         qn = q_ref[rows, :]
@@ -57,37 +68,20 @@
             cands.append((k_ref, v_ref, j) if j >= 0 else (kf[0], vf[0], NB + j))
         for mi in range(n_levels):
             cands.append((kf[mi], vf[mi], n))
-        scores = []
-        for ci, (kr, _, j) in enumerate(cands):
-            s = dot_nt(qn, kr[pl.ds(j * BLK, BLK), :]) * scale
-            if ci == 0:
-                s = jnp.where(causal, s, neg_large)
-            else:
-                s = jnp.where(valid_ref[n * n_cand + ci] != 0, s, neg_large)
-            scores.append(s)
-        row_max = scores[0].max(axis=1, keepdims=True)
-        for s in scores[1:]:
-            row_max = jnp.maximum(row_max, s.max(axis=1, keepdims=True))
-        row_total = None
-        for s in scores:
-            part = jnp.sum(jnp.exp(s - row_max), axis=1, keepdims=True)
-            row_total = part if row_total is None else row_total + part
+        kcat = jnp.concatenate([kr[pl.ds(j * BLK, BLK), :] for kr, _, j in cands], axis=0)
+        vcat = jnp.concatenate([vr[pl.ds(j * BLK, BLK), :] for _, vr, j in cands], axis=0)
+        allowed = candidate_mask(valid_ref, n * n_cand, n_cand, diag)
+        scores = jnp.where(allowed, dot_nt(qn, kcat) * scale, neg_large)
+        row_max = scores.max(axis=1, keepdims=True)
+        row_total = jnp.sum(jnp.exp(scores - row_max), axis=1, keepdims=True)
         log_total = row_max + jnp.log(row_total)
-        probs = [jnp.exp(s - log_total) for s in scores]
-        att = None
-        for p, (_, vr, j) in zip(probs, cands):
-            part = dot_nn(p.astype(jnp.bfloat16), vr[pl.ds(j * BLK, BLK), :])
-            att = part if att is None else att + part
-        att_b = att.astype(jnp.bfloat16)
+        probs = jnp.exp(scores - log_total)
+        att_b = dot_nn(probs.astype(jnp.bfloat16), vcat).astype(jnp.bfloat16)
         att_ref[rows, :] = att_b
         delta = jnp.sum(gn.astype(jnp.float32) * att_b.astype(jnp.float32), axis=1, keepdims=True)
-        dq = None
-        for p, (kr, vr, j) in zip(probs, cands):
-            d_prob = dot_nt(gn, vr[pl.ds(j * BLK, BLK), :])
-            d_score = (p * (d_prob - delta) * scale).astype(jnp.bfloat16)
-            part = dot_nn(d_score, kr[pl.ds(j * BLK, BLK), :])
-            dq = part if dq is None else dq + part
-        dq_ref[rows, :] = dq.astype(jnp.bfloat16)
+        d_prob = dot_nt(gn, vcat)
+        d_score = (probs * (d_prob - delta) * scale).astype(jnp.bfloat16)
+        dq_ref[rows, :] = dot_nn(d_score, kcat).astype(jnp.bfloat16)
         st_ref[0, 0, pl.ds(n, 1), :] = col_to_row(log_total)
         st_ref[1, 0, pl.ds(n, 1), :] = col_to_row(delta)
 
@@ -98,10 +92,11 @@
     sf = rest[2 : 3 * n_levels : 3]
     dk_ref, dv_ref = rest[3 * n_levels :]
     n_cand = 1 + WIN_MAX + n_levels
+    width = n_cand * BLK
     scale = HD ** (-0.5)
-    causal = lax.broadcasted_iota(jnp.int32, (BLK, BLK), 0) <= lax.broadcasted_iota(
-        jnp.int32, (BLK, BLK), 1
-    )
+    col = lax.broadcasted_iota(jnp.int32, (BLK, width), 1)
+    row = lax.broadcasted_iota(jnp.int32, (BLK, width), 0)
+    diag = row <= col
     for j in range(NB):
         rows = pl.ds(j * BLK, BLK)
         kj = k_ref[rows, :]
@@ -112,27 +107,17 @@
             cands.append((q_ref, g_ref, st_ref, i) if i < NB else (qf[0], gf[0], sf[0], i - NB))
         for mi in range(n_levels):
             cands.append((qf[mi], gf[mi], sf[mi], j))
-        dk = None
-        dv = None
-        for ci, (qr, gr, sr, i) in enumerate(cands):
-            qc = qr[pl.ds(i * BLK, BLK), :]
-            gc = gr[pl.ds(i * BLK, BLK), :]
-            lse = sr[0, 0, pl.ds(i, 1), :]
-            delta = sr[1, 0, pl.ds(i, 1), :]
-            s = dot_nt(kj, qc) * scale
-            if ci == 0:
-                s = jnp.where(causal, s, neg_large)
-            else:
-                s = jnp.where(valid_ref[j * n_cand + ci] != 0, s, neg_large)
-            p = jnp.exp(s - lse)
-            part_v = dot_nn(p.astype(jnp.bfloat16), gc)
-            d_prob = dot_nt(vj, gc)
-            d_score = (p * (d_prob - delta) * scale).astype(jnp.bfloat16)
-            part_k = dot_nn(d_score, qc)
-            dv = part_v if dv is None else dv + part_v
-            dk = part_k if dk is None else dk + part_k
-        dk_ref[rows, :] = dk.astype(jnp.bfloat16)
-        dv_ref[rows, :] = dv.astype(jnp.bfloat16)
+        qcat = jnp.concatenate([qr[pl.ds(i * BLK, BLK), :] for qr, _, _, i in cands], axis=0)
+        gcat = jnp.concatenate([gr[pl.ds(i * BLK, BLK), :] for _, gr, _, i in cands], axis=0)
+        lse = jnp.concatenate([sr[0, 0, pl.ds(i, 1), :] for _, _, sr, i in cands], axis=1)
+        delta = jnp.concatenate([sr[1, 0, pl.ds(i, 1), :] for _, _, sr, i in cands], axis=1)
+        allowed = candidate_mask(valid_ref, j * n_cand, n_cand, diag)
+        scores = jnp.where(allowed, dot_nt(kj, qcat) * scale, neg_large)
+        probs = jnp.exp(scores - lse)
+        dv_ref[rows, :] = dot_nn(probs.astype(jnp.bfloat16), gcat).astype(jnp.bfloat16)
+        d_prob = dot_nt(vj, gcat)
+        d_score = (probs * (d_prob - delta) * scale).astype(jnp.bfloat16)
+        dk_ref[rows, :] = dot_nn(d_score, qcat).astype(jnp.bfloat16)
 
 
 def head_block(part):

time: 214 us -> 190 us (0.89)
  the two profiles are of different devices: /device:TPU:18 before, /device:TPU:0 now
where the time goes in v4:
time: 190 us; the launch traced here: 189 us
  waiting for transfers between devices  107 us (56%)
  Pallas kernels  25.9 us (14%)
  starting transfers between devices  23.7 us (12%)
  between operations  14.2 us (7%)
  local copies, waits for them, and re-layouts  10.4 us (5%)
  matrix products  6.51 us (3%)
    ppermute x9, waiting for transfers between devices, passed_along(): return lax.ppermute(block, axis, route)  88.9 us
    ppermute x9, starting transfers between devices, passed_along(): return lax.ppermute(block, axis, route)  23.6 us
    pallas_call x1, Pallas kernels, query_call(): pl.pallas_call(functools.partial(query_kernel, n_levels), grid_spec=grid_...  15.2 us
    pallas_call x1, Pallas kernels, key_call(): pl.pallas_call(functools.partial(key_kernel, n_levels), grid_spec=grid_sp...  10.6 us
    reduce_scatter x1, waiting for transfers between devices, local(): lax.psum_scatter(partial_out.astype(jnp.bfloat16), 'head', scatter_dimens...  10.4 us
    all_gather x1, waiting for transfers between devices, local(): lax.all_gather(d_out, 'head', axis=1, tiled=True)  7.28 us
  transfers between devices with their start and end apart: 11, of which 6 were waited for; matrix products, arithmetic and copies ran while one was open for 7% of the time, Pallas kernels for 6%

profile of v4, /device:TPU:0, one launch (start us, length us, event | category | flops | bytes accessed | tf_op | source)
XLA Modules:
  0.0 189.4 jit_solution(15620756530909365036)
XLA Ops:
  7.2 0.0 copy-start
  7.2 0.0 all-gather.2.cloned.1.call-start
  7.2 0.7 all-gather.2.cloned.1.call-update
  7.9 0.0 reduce-scatter.2.cloned.1.call-start
  8.0 1.9 constant_dynamic-update-slice_fusion.1
  9.8 1.9 constant_dynamic-update-slice_fusion
  11.7 0.0 copy-start.2
  11.7 7.0 %collective-permute-start.2 = (bf16[1024,512]{1,0:T(8,128)(2,1)}, bf16[1024,512]{1,0:T(8,128)(2,1)}, u32[]{:S(2)}, u32[]{:S(2)}) collective-permute-start(bf16[1024,512]{1,0:T(8,128)(2,1)} %constant_dynamic-update-slice_fusion), channel_id=1, source_target_pairs={{0,16},{4,20},{8,24},{12,28},{1,17},{5,21},{9,25},{13,29},{2,18},{... | collective-permute-start | bytes 3145736 | tf_op jit(solution)/shard_map/ppermute | solution.py:23
  18.8 4.5 %collective-permute-start.1 = (bf16[1024,512]{1,0:T(8,128)(2,1)}, bf16[1024,512]{1,0:T(8,128)(2,1)}, u32[]{:S(2)}, u32[]{:S(2)}) collective-permute-start(bf16[1024,512]{1,0:T(8,128)(2,1)} %constant_dynamic-update-slice_fusion), channel_id=1, source_target_pairs={{0,8},{4,12},{8,16},{12,20},{16,24},{20,28},{1,9},{5,13},{9,17},{1... | collective-permute-start | bytes 3145736 | tf_op jit(solution)/shard_map/ppermute | solution.py:23
  23.2 4.4 %collective-permute-start = (bf16[1024,512]{1,0:T(8,128)(2,1)}, bf16[1024,512]{1,0:T(8,128)(2,1)}, u32[]{:S(2)}, u32[]{:S(2)}) collective-permute-start(bf16[1024,512]{1,0:T(8,128)(2,1)} %constant_dynamic-update-slice_fusion), channel_id=1, source_target_pairs={{0,4},{4,8},{8,12},{12,16},{16,20},{20,24},{24,28},{1,5},{5,9},{9,... | collective-permute-start | bytes 3145736 | tf_op jit(solution)/shard_map/ppermute | solution.py:23
  27.6 7.3 %all-gather.2.cloned.1.call-done = bf16[512,2048]{1,0:T(8,128)(2,1)} async-done(((bf16[512,512]{1,0:T(8,128)(2,1)}), bf16[512,2048]{1,0:T(8,128)(2,1)}) %all-gather.2.cloned.1.call-update) | async-done | bytes 2097168 | tf_op jit(solution)/shard_map/all_gather | solution.py:196
  34.9 0.0 copy-done
  34.9 2.9 %convolution_convert_fusion.1.g_ref = bf16[512,512]{1,0:T(8,128)(2,1)S(1)} fusion(bf16[512,2048]{1,0:T(8,128)(2,1)} %all-gather.2.cloned.1.call-done, bf16[512,2048]{1,0:T(8,128)(2,1)S(1)} %copy-done), kind=kOutput, calls=%fused_computation.7 | convolution fusion | flops 1074003968 | bytes 4718592 | tf_op jit(solution)/shard_map/dot_general | solution.py:195
  37.8 0.0 copy-done.2
  37.8 0.0 copy-start.3
  37.8 0.0 copy-start.1
  37.8 0.0 copy-start.8
  37.8 1.1 pad_maximum_fusion
  39.0 1.3 collective-permute-start.5
  40.3 1.3 collective-permute-start.4
  41.6 0.1 collective-permute-done.2.rest_4_.rest_5_
  41.7 1.3 collective-permute-start.3
  43.0 0.0 copy-done.1
  43.0 0.1 and_bitcast_fusion.6
  43.1 0.0 copy-done.8
  43.1 0.1 constant_dynamic-slice_fusion
  43.2 0.1 copy.13
  43.3 0.6 reshape.52.valid_ref
  43.9 19.1 %collective-permute-done.1.rest_2_.rest_3_ = bf16[1024,512]{1,0:T(8,128)(2,1)} collective-permute-done((bf16[1024,512]{1,0:T(8,128)(2,1)}, bf16[1024,512]{1,0:T(8,128)(2,1)}, u32[]{:S(2)}, u32[]{:S(2)}) %collective-permute-start.1) | collective-permute-done | bytes 1048608 | tf_op jit(solution)/shard_map/ppermute | solution.py:23
  63.0 0.0 collective-permute-done.rest_0_.rest_1_
  63.0 27.6 %collective-permute-done.5.rest_6_.rest_7_ = bf16[1024,512]{1,0:T(8,128)(2,1)} collective-permute-done((bf16[1024,512]{1,0:T(8,128)(2,1)}, bf16[1024,512]{1,0:T(8,128)(2,1)}, u32[]{:S(2)}, u32[]{:S(2)}) %collective-permute-start.5) | collective-permute-done | bytes 1048608 | tf_op jit(solution)/shard_map/ppermute | solution.py:23
  90.6 0.0 collective-permute-done.4.rest_3_.rest_4_
  90.6 0.0 collective-permute-done.3.rest_0_.rest_1_
  90.6 0.0 copy-done.3
  90.6 15.2 %query_side.1 = (bf16[512,512]{1,0:T(8,128)(2,1)}, bf16[512,512]{1,0:T(8,128)(2,1)}, f32[2,4,4,128]{3,2,1,0:T(4,128)}) custom-call(s32[28]{0:T(128)} %reshape.52.valid_ref, bf16[512,512]{1,0:T(8,128)(2,1)} %q_ref.3, bf16[512,512]{1,0:T(8,128)(2,1)} %copy-done.3, bf16[512,512]{1,0:T(8,128)(2,1)} %k_ref.3, bf16[512,512]{1,0:T(8,128)(2,1)} %v_ref.3, ...), custom_call_target="tpu_custom_call" | custom-call | tf_op jit(solution)/shard_map/query_side/pallas_call | solution.py:144
  105.8 3.6 %convolution_convert_fusion = bf16[512,2048]{1,0:T(8,128)(2,1)} fusion(bf16[512,512]{1,0:T(8,128)(2,1)} %get-tuple-element.19, bf16[512,2048]{1,0:T(8,128)(2,1)S(1)} %copy-done), kind=kOutput, calls=%fused_computation.6 | convolution fusion | flops 1074790400 | bytes 4718592 | tf_op jit(solution)/shard_map/dot_general | solution.py:227
  109.5 0.0 reduce-scatter.2.cloned.1.call-update
  109.5 0.0 copy-start.4
  109.5 0.6 gather_fusion.1
  110.2 0.6 gather_fusion.2
  110.8 0.6 gather_fusion
  111.5 0.6 gather_fusion.5
  112.1 0.6 gather_fusion.3
  112.8 0.6 gather_fusion.4
  113.5 0.0 copy-done.4
  113.5 1.3 collective-permute-start.8
  114.8 1.3 collective-permute-start.7
  116.1 1.3 collective-permute-start.6
  117.5 0.1 copy.14
  117.6 0.7 reshape.53.valid_ref
  118.2 42.0 %collective-permute-done.8.rest_8_ = f32[2,4,4,128]{3,2,1,0:T(4,128)S(1)} collective-permute-done((f32[2,4,4,128]{3,2,1,0:T(4,128)S(1)}, f32[2,4,4,128]{3,2,1,0:T(4,128)S(1)}, u32[]{:S(2)}, u32[]{:S(2)}) %collective-permute-start.8) | collective-permute-done | bytes 16416 | tf_op jit(solution)/shard_map/ppermute | solution.py:23
  160.3 0.0 copy-start.5
  160.3 0.0 collective-permute-done.7.rest_5_
  160.3 0.0 copy-start.6
  160.3 0.0 collective-permute-done.6.rest_2_
  160.3 0.6 copy-done.5
  160.9 0.0 copy-done.6
  160.9 0.0 copy-start.7
  160.9 0.6 copy-done.7
  161.5 10.6 %key_side.1 = (bf16[512,512]{1,0:T(8,128)(2,1)}, bf16[512,512]{1,0:T(8,128)(2,1)}) custom-call(s32[28]{0:T(128)} %reshape.53.valid_ref, bf16[512,512]{1,0:T(8,128)(2,1)} %k_ref.3, bf16[512,512]{1,0:T(8,128)(2,1)} %v_ref.3, bf16[512,512]{1,0:T(8,128)(2,1)} %q_ref.3, bf16[512,512]{1,0:T(8,128)(2,1)} %copy-done.3, f32[2,4,4,128]{3,2,1,0:T(4,128)} %get-tuple-element.21.st_ref, ...), custom_call_target="tpu_custom_call" | custom-call | tf_op jit(solution)/shard_map/key_side/pallas_call | solution.py:169
  172.1 10.4 %reduce-scatter.2.cloned.1.call-done = bf16[512,512]{1,0:T(8,128)(2,1)} async-done(((bf16[512,2048]{1,0:T(8,128)(2,1)}), bf16[512,512]{1,0:T(8,128)(2,1)}) %reduce-scatter.2.cloned.1.call-update) | async-done | bytes 524304 | tf_op jit(solution)/shard_map/reduce_scatter | solution.py:228
  (21 shorter events, 0.2 us)
Async XLA Ops:
  7.2 27.7 %copy-start = (bf16[512,2048]{1,0:T(8,128)(2,1)S(1)}, bf16[512,2048]{1,0:T(8,128)(2,1)}, u32[]{:S(2)}) copy-start(bf16[512,2048]{1,0:T(8,128)(2,1)} %param.12) | copy-start | bytes 6291460
  7.2 27.7 %all-gather.2.cloned.1.call-start = ((), (), s32[]{:S(2)}) async-start(), calls=%async_computation.1 | async-start | bytes 2621440 | tf_op jit(solution)/shard_map/all_gather | solution.py:196
  7.9 174.6 %reduce-scatter.2.cloned.1.call-start = ((), (), s32[]{:S(2)}) async-start(), calls=%async_computation.2 | async-start | bytes 2621440 | tf_op jit(solution)/shard_map/reduce_scatter | solution.py:228
  11.7 26.1 %copy-start.2 = (bf16[512,512]{1,0:T(8,128)(2,1)S(1)}, bf16[512,512]{1,0:T(8,128)(2,1)}, u32[]{:S(2)}) copy-start(bf16[512,512]{1,0:T(8,128)(2,1)} %q_ref.3) | copy-start | bytes 1572868
  11.7 30.0 %collective-permute-start.2 = (bf16[1024,512]{1,0:T(8,128)(2,1)}, bf16[1024,512]{1,0:T(8,128)(2,1)}, u32[]{:S(2)}, u32[]{:S(2)}) collective-permute-start(bf16[1024,512]{1,0:T(8,128)(2,1)} %constant_dynamic-update-slice_fusion), channel_id=1, source_target_pairs={{0,16},{4,20},{8,24},{12,28},{1,17},{5,21},{9,25},{13,29},{2,18},{... | collective-permute-start | bytes 3145736 | tf_op jit(solution)/shard_map/ppermute | solution.py:23
  18.8 44.3 %collective-permute-start.1 = (bf16[1024,512]{1,0:T(8,128)(2,1)}, bf16[1024,512]{1,0:T(8,128)(2,1)}, u32[]{:S(2)}, u32[]{:S(2)}) collective-permute-start(bf16[1024,512]{1,0:T(8,128)(2,1)} %constant_dynamic-update-slice_fusion), channel_id=1, source_target_pairs={{0,8},{4,12},{8,16},{12,20},{16,24},{20,28},{1,9},{5,13},{9,17},{1... | collective-permute-start | bytes 3145736 | tf_op jit(solution)/shard_map/ppermute | solution.py:23
  23.2 39.8 %collective-permute-start = (bf16[1024,512]{1,0:T(8,128)(2,1)}, bf16[1024,512]{1,0:T(8,128)(2,1)}, u32[]{:S(2)}, u32[]{:S(2)}) collective-permute-start(bf16[1024,512]{1,0:T(8,128)(2,1)} %constant_dynamic-update-slice_fusion), channel_id=1, source_target_pairs={{0,4},{4,8},{8,12},{12,16},{16,20},{20,24},{24,28},{1,5},{5,9},{9,... | collective-permute-start | bytes 3145736 | tf_op jit(solution)/shard_map/ppermute | solution.py:23
  37.8 52.8 %copy-start.3 = (bf16[512,512]{1,0:T(8,128)(2,1)}, bf16[512,512]{1,0:T(8,128)(2,1)S(1)}, u32[]{:S(2)}) copy-start(bf16[512,512]{1,0:T(8,128)(2,1)S(1)} %convolution_convert_fusion.1.g_ref) | copy-start | bytes 1572868
  37.8 5.2 %copy-start.1 = (s32[32]{0:T(128)S(1)}, s32[32]{0:T(128)}, u32[]{:S(2)}) copy-start(s32[32]{0:T(128)} %param.14) | copy-start | bytes 388
  37.8 5.3 %copy-start.8 = (s32[32,5]{0,1:T(8,128)S(1)}, s32[32,5]{0,1:T(8,128)}, u32[]{:S(2)}) copy-start(s32[32,5]{0,1:T(8,128)} %param.15) | copy-start | bytes 1924
  39.0 51.6 %collective-permute-start.5 = (bf16[1024,512]{1,0:T(8,128)(2,1)}, bf16[1024,512]{1,0:T(8,128)(2,1)}, u32[]{:S(2)}, u32[]{:S(2)}) collective-permute-start(bf16[1024,512]{1,0:T(8,128)(2,1)} %pad_maximum_fusion), channel_id=1, source_target_pairs={{16,0},{20,4},{24,8},{28,12},{17,1},{21,5},{25,9},{29,13},{18,2},{... | collective-permute-start | bytes 3145736 | tf_op jit(solution)/shard_map/ppermute | solution.py:23
  40.3 50.3 %collective-permute-start.4 = (bf16[1024,512]{1,0:T(8,128)(2,1)}, bf16[1024,512]{1,0:T(8,128)(2,1)}, u32[]{:S(2)}, u32[]{:S(2)}) collective-permute-start(bf16[1024,512]{1,0:T(8,128)(2,1)} %pad_maximum_fusion), channel_id=1, source_target_pairs={{8,0},{12,4},{16,8},{20,12},{24,16},{28,20},{9,1},{13,5},{17,9},{2... | collective-permute-start | bytes 3145736 | tf_op jit(solution)/shard_map/ppermute | solution.py:23
  41.7 48.9 %collective-permute-start.3 = (bf16[1024,512]{1,0:T(8,128)(2,1)}, bf16[1024,512]{1,0:T(8,128)(2,1)}, u32[]{:S(2)}, u32[]{:S(2)}) collective-permute-start(bf16[1024,512]{1,0:T(8,128)(2,1)} %pad_maximum_fusion), channel_id=1, source_target_pairs={{4,0},{8,4},{12,8},{16,12},{20,16},{24,20},{28,24},{5,1},{9,5},{13... | collective-permute-start | bytes 3145736 | tf_op jit(solution)/shard_map/ppermute | solution.py:23
  109.5 4.0 %copy-start.4 = (f32[2,4,4,128]{3,2,1,0:T(4,128)S(1)}, f32[2,4,4,128]{3,2,1,0:T(4,128)}, u32[]{:S(2)}) copy-start(f32[2,4,4,128]{3,2,1,0:T(4,128)} %get-tuple-element.21.st_ref) | copy-start | bytes 49156
  113.5 46.8 %collective-permute-start.8 = (f32[2,4,4,128]{3,2,1,0:T(4,128)S(1)}, f32[2,4,4,128]{3,2,1,0:T(4,128)S(1)}, u32[]{:S(2)}, u32[]{:S(2)}) collective-permute-start(f32[2,4,4,128]{3,2,1,0:T(4,128)S(1)} %copy-done.4), channel_id=1, source_target_pairs={{16,0},{20,4},{24,8},{28,12},{17,1},{21,5},{25,9},{29,13},{18,2},{... | collective-permute-start | bytes 49160 | tf_op jit(solution)/shard_map/ppermute | solution.py:23
  114.8 45.5 %collective-permute-start.7 = (f32[2,4,4,128]{3,2,1,0:T(4,128)S(1)}, f32[2,4,4,128]{3,2,1,0:T(4,128)S(1)}, u32[]{:S(2)}, u32[]{:S(2)}) collective-permute-start(f32[2,4,4,128]{3,2,1,0:T(4,128)S(1)} %copy-done.4), channel_id=1, source_target_pairs={{8,0},{12,4},{16,8},{20,12},{24,16},{28,20},{9,1},{13,5},{17,9},{2... | collective-permute-start | bytes 49160 | tf_op jit(solution)/shard_map/ppermute | solution.py:23
  116.1 44.2 %collective-permute-start.6 = (f32[2,4,4,128]{3,2,1,0:T(4,128)S(1)}, f32[2,4,4,128]{3,2,1,0:T(4,128)S(1)}, u32[]{:S(2)}, u32[]{:S(2)}) collective-permute-start(f32[2,4,4,128]{3,2,1,0:T(4,128)S(1)} %copy-done.4), channel_id=1, source_target_pairs={{4,0},{8,4},{12,8},{16,12},{20,16},{24,20},{28,24},{5,1},{9,5},{13... | collective-permute-start | bytes 49160 | tf_op jit(solution)/shard_map/ppermute | solution.py:23
  160.3 0.6 copy-start.5
  160.3 0.6 copy-start.6
  160.9 0.6 copy-start.7
Sparse Core Ops, SparseCore 0:
  9.6 25.2 all-gather.1
  109.6 72.8 reduce-scatter.1

commit v5 on v4

--- a/solution.py
+++ b/solution.py
@@ -153,13 +153,13 @@
     )(valid, *args)
 
 
-def key_call(valid, k, v, q, g, stats, qg_from, st_from, heads, n_levels):
+def key_call(valid, k, v, q, g, stats, q_from, g_from, st_from, heads, n_levels):
     tokens, features = q.shape
     in_specs = [head_block(0)] * 4 + [stats_block(heads)]
     args = [k, v, q, g, stats]
-    for qg, st in zip(qg_from, st_from):
-        in_specs += [head_block(0), head_block(1), stats_block(heads)]
-        args += [qg, qg, st]
+    for qa, ga, st in zip(q_from, g_from, st_from):
+        in_specs += [head_block(0), head_block(0), stats_block(heads)]
+        args += [qa, ga, st]
     grid_spec = pltpu.PrefetchScalarGridSpec(
         num_scalar_prefetch=1,
         grid=(heads,),
@@ -189,20 +189,6 @@
     n_levels = len(levels)
     block_ids = ctx_index * NB + jnp.arange(NB, dtype=jnp.int32)
 
-    kv = jnp.concatenate([keys, values], axis=0)
-    kv_from = [passed_along(kv, "ctx", 2**m) for m in levels]
-
-    grad_att = lax.dot_general(
-        lax.all_gather(d_out, "head", axis=1, tiled=True),
-        out_weight,
-        (((1,), (1,)), ((), ())),
-        preferred_element_type=jnp.float32,
-    )
-    g = grad_att.astype(jnp.bfloat16)
-    qg = jnp.concatenate([queries, g], axis=0)
-    qg_from = [passed_along(qg, "ctx", -(2**m)) for m in levels]
-    kv_from, qg_from = lax.optimization_barrier((kv_from, qg_from))
-
     own_window = lax.dynamic_slice_in_dim(window, ctx_index * NB, NB, 0)
     own_select = lax.dynamic_slice_in_dim(far_select, ctx_index * NB, NB, 0)
     valid_cols = [block_ids >= 0]
@@ -221,6 +207,22 @@
         key_cols.append((qb <= last) & (jnp.take(far_select[:, m], jnp.minimum(qb, last)) == 1))
     valid_k = jnp.stack(key_cols, axis=1).astype(jnp.int32).reshape(-1)
 
+    kv = jnp.concatenate([keys, values], axis=0)
+    kv_from = [passed_along(kv, "ctx", 2**m) for m in levels]
+    q_from = [passed_along(queries, "ctx", -(2**m)) for m in levels]
+
+    grad_att = lax.dot_general(
+        lax.all_gather(d_out, "head", axis=1, tiled=True),
+        out_weight,
+        (((1,), (1,)), ((), ())),
+        preferred_element_type=jnp.float32,
+    )
+    g = grad_att.astype(jnp.bfloat16)
+    g_from = [passed_along(g, "ctx", -(2**m)) for m in levels]
+    kv_from, q_from, g_from, valid_q, valid_k = lax.optimization_barrier(
+        (kv_from, q_from, g_from, valid_q, valid_k)
+    )
+
     attended, query_grad, stats = query_call(
         valid_q, queries, g, keys, values, kv_from, heads_local, n_levels
     )
@@ -231,7 +233,7 @@
 
     st_from = [passed_along(stats, "ctx", -(2**m)) for m in levels]
     key_grad, value_grad = key_call(
-        valid_k, keys, values, queries, g, stats, qg_from, st_from, heads_local, n_levels
+        valid_k, keys, values, queries, g, stats, q_from, g_from, st_from, heads_local, n_levels
     )
     return output, query_grad, key_grad, value_grad
 

time: 190 us -> 174 us (0.916)
  waiting for transfers between devices: 107 us -> 82.4 us
  starting transfers between devices: 23.7 us -> 32 us
    ppermute x9 -> x12, waiting for transfers between devices: 88.9 us -> 68.7 us  [passed_along(): return lax.ppermute(block, axis, route)]
    ppermute x9 -> x12, starting transfers between devices: 23.6 us -> 31.9 us  [passed_along(): return lax.ppermute(block, axis, route)]
    all_gather x1, waiting for transfers between devices: 7.28 us -> 0.01 us  [local(): lax.all_gather(d_out, 'head', axis=1, tiled=True)]
    reduce_scatter x1, waiting for transfers between devices: 10.4 us -> 13 us  [local(): lax.psum_scatter(partial_out.astype(jnp.bfloat16), 'head', scatter_dimens...]
    unnamed x19 -> x17, local copies, waits for them, and re-layouts: 3.09 us -> 3.8 us
  transfers between devices with their start and end apart: 11 -> 14, of which waited for: 6 -> 6; matrix products, arithmetic and copies ran while one was open for 7% -> 8% of each run, Pallas kernels for 6% -> 6%
where the time goes in v5:
time: 174 us; the launch traced here: 173 us
  waiting for transfers between devices  82.4 us (47%)
  starting transfers between devices  32 us (18%)
  Pallas kernels  25.9 us (15%)
  between operations  14.3 us (8%)
  local copies, waits for them, and re-layouts  11.1 us (6%)
  matrix products  7.31 us (4%)
    ppermute x12, waiting for transfers between devices, passed_along(): return lax.ppermute(block, axis, route)  68.7 us
    ppermute x12, starting transfers between devices, passed_along(): return lax.ppermute(block, axis, route)  31.9 us
    pallas_call x1, Pallas kernels, query_call(): pl.pallas_call(functools.partial(query_kernel, n_levels), grid_spec=grid_...  15.2 us
    reduce_scatter x1, waiting for transfers between devices, local(): lax.psum_scatter(partial_out.astype(jnp.bfloat16), 'head', scatter_dimens...  13 us
    pallas_call x1, Pallas kernels, key_call(): pl.pallas_call(functools.partial(key_kernel, n_levels), grid_spec=grid_sp...  10.7 us
    unnamed x17, local copies, waits for them, and re-layouts  3.8 us
    dot_general x1, matrix products, local(): lax.dot_general(lax.all_gather(d_out, 'head', axis=1, tiled=True), out_we...  3.66 us
    dot_general x1, matrix products, local(): jnp.dot(attended, out_weight, preferred_element_type=jnp.float32)  3.65 us
  transfers between devices with their start and end apart: 14, of which 6 were waited for; matrix products, arithmetic and copies ran while one was open for 8% of the time, Pallas kernels for 6%

profile of v5, /device:TPU:0, one launch (start us, length us, event | category | flops | bytes accessed | tf_op | source)
XLA Modules:
  0.0 173.2 jit_solution(15152707907765104619)
XLA Ops:
  7.2 0.0 copy-start
  7.2 0.0 copy-start.7
  7.2 0.0 copy-start.1
  7.2 0.0 all-gather.2.cloned.1.call-start
  7.2 0.7 all-gather.2.cloned.1.call-update
  7.9 0.0 reduce-scatter.2.cloned.1.call-start
  8.0 1.3 collective-permute-start.5
  9.3 1.3 collective-permute-start.4
  10.6 1.3 collective-permute-start.3
  11.9 1.9 %constant_dynamic-update-slice_fusion.1 = bf16[1024,512]{1,0:T(8,128)(2,1)} fusion(bf16[512,512]{1,0:T(8,128)(2,1)} %k_ref.3), kind=kLoop, calls=%fused_computation.15 | loop fusion | bytes 1048576
  13.8 1.9 %constant_dynamic-update-slice_fusion = bf16[1024,512]{1,0:T(8,128)(2,1)} fusion(bf16[1024,512]{1,0:T(8,128)(2,1)} %constant_dynamic-update-slice_fusion.1, bf16[512,512]{1,0:T(8,128)(2,1)} %v_ref.3), kind=kLoop, calls=%fused_computation.14 | loop fusion | bytes 1048576 | tf_op jit(solution)/shard_map/concatenate | solution.py:210
  15.7 9.1 %collective-permute-start.2 = (bf16[1024,512]{1,0:T(8,128)(2,1)}, bf16[1024,512]{1,0:T(8,128)(2,1)S(1)}, u32[]{:S(2)}, u32[]{:S(2)}) collective-permute-start(bf16[1024,512]{1,0:T(8,128)(2,1)} %constant_dynamic-update-slice_fusion), channel_id=1, source_target_pairs={{0,16},{4,20},{8,24},{12,28},{1,17},{5,21},{9,25},{13,29},{2,18},{... | collective-permute-start | bytes 3145736 | tf_op jit(solution)/shard_map/ppermute | solution.py:23
  24.8 5.9 %collective-permute-start.1 = (bf16[1024,512]{1,0:T(8,128)(2,1)}, bf16[1024,512]{1,0:T(8,128)(2,1)}, u32[]{:S(2)}, u32[]{:S(2)}) collective-permute-start(bf16[1024,512]{1,0:T(8,128)(2,1)} %constant_dynamic-update-slice_fusion), channel_id=1, source_target_pairs={{0,8},{4,12},{8,16},{12,20},{16,24},{20,28},{1,9},{5,13},{9,17},{1... | collective-permute-start | bytes 3145736 | tf_op jit(solution)/shard_map/ppermute | solution.py:23
  30.7 0.0 copy-done.7
  30.7 0.6 gather_fusion.5
  31.4 0.6 gather_fusion.3
  32.0 0.0 copy-done.1
  32.0 0.6 gather_fusion.1
  32.7 0.6 gather_fusion.4
  33.3 0.1 constant_dynamic-slice_fusion
  33.5 0.1 and_bitcast_fusion.6
  33.6 0.1 copy.13
  33.7 0.6 reshape.52.valid_ref
  34.3 3.4 %collective-permute-done.5.rest_6_ = bf16[512,512]{1,0:T(8,128)(2,1)} collective-permute-done((bf16[512,512]{1,0:T(8,128)(2,1)}, bf16[512,512]{1,0:T(8,128)(2,1)}, u32[]{:S(2)}, u32[]{:S(2)}) %collective-permute-start.5) | collective-permute-done | bytes 524320 | tf_op jit(solution)/shard_map/ppermute | solution.py:23
  37.6 5.3 %collective-permute-start = (bf16[1024,512]{1,0:T(8,128)(2,1)}, bf16[1024,512]{1,0:T(8,128)(2,1)}, u32[]{:S(2)}, u32[]{:S(2)}) collective-permute-start(bf16[1024,512]{1,0:T(8,128)(2,1)} %constant_dynamic-update-slice_fusion), channel_id=1, source_target_pairs={{0,4},{4,8},{8,12},{12,16},{16,20},{20,24},{24,28},{1,5},{5,9},{9,... | collective-permute-start | bytes 3145736 | tf_op jit(solution)/shard_map/ppermute | solution.py:23
  43.0 0.6 gather_fusion.2
  43.6 0.0 all-gather.2.cloned.1.call-done
  43.6 0.0 copy-done
  43.6 3.7 %convolution_convert_fusion.1.g_ref = bf16[512,512]{1,0:T(8,128)(2,1)} fusion(bf16[512,2048]{1,0:T(8,128)(2,1)} %all-gather.2.cloned.1.call-done, bf16[512,2048]{1,0:T(8,128)(2,1)S(1)} %copy-done), kind=kOutput, calls=%fused_computation.7 | convolution fusion | flops 1074003968 | bytes 4718592 | tf_op jit(solution)/shard_map/dot_general | solution.py:214
  47.3 0.0 collective-permute-done.4.rest_3_
  47.3 1.3 collective-permute-start.8
  48.6 0.0 collective-permute-done.3.rest_0_
  48.6 1.3 collective-permute-start.7
  49.9 0.0 collective-permute-done.2.rest_4_.rest_5_
  49.9 0.0 copy-start.2
  49.9 1.3 collective-permute-start.6
  51.2 0.6 gather_fusion
  51.9 0.1 copy.14
  52.0 0.6 reshape.53.valid_ref
  52.7 16.7 %collective-permute-done.1.rest_2_.rest_3_ = bf16[1024,512]{1,0:T(8,128)(2,1)} collective-permute-done((bf16[1024,512]{1,0:T(8,128)(2,1)}, bf16[1024,512]{1,0:T(8,128)(2,1)}, u32[]{:S(2)}, u32[]{:S(2)}) %collective-permute-start.1) | collective-permute-done | bytes 1048608 | tf_op jit(solution)/shard_map/ppermute | solution.py:23
  69.4 0.1 collective-permute-done.rest_0_.rest_1_
  69.5 13.2 %collective-permute-done.8.rest_7_ = bf16[512,512]{1,0:T(8,128)(2,1)} collective-permute-done((bf16[512,512]{1,0:T(8,128)(2,1)}, bf16[512,512]{1,0:T(8,128)(2,1)}, u32[]{:S(2)}, u32[]{:S(2)}) %collective-permute-start.8) | collective-permute-done | bytes 524320 | tf_op jit(solution)/shard_map/ppermute | solution.py:23
  82.7 0.0 collective-permute-done.7.rest_4_
  82.7 0.0 collective-permute-done.6.rest_1_
  82.7 0.0 copy-done.2
  82.7 15.2 %query_side.1 = (bf16[512,512]{1,0:T(8,128)(2,1)}, bf16[512,512]{1,0:T(8,128)(2,1)}, f32[2,4,4,128]{3,2,1,0:T(4,128)}) custom-call(s32[28]{0:T(128)} %reshape.52.valid_ref, bf16[512,512]{1,0:T(8,128)(2,1)} %q_ref.3, bf16[512,512]{1,0:T(8,128)(2,1)} %convolution_convert_fusion.1.g_ref, bf16[512,512]{1,0:T(8,128)(2,1)} %k_ref.3, bf16[512,512]{1,0:T(8,128)(2,1)} %v_ref.3, ...), custom_call_target="tpu_custom_call" | custom-call | tf_op jit(solution)/shard_map/query_side/pallas_call | solution.py:144
  97.9 3.6 %convolution_convert_fusion = bf16[512,2048]{1,0:T(8,128)(2,1)} fusion(bf16[512,512]{1,0:T(8,128)(2,1)} %get-tuple-element.25, bf16[512,2048]{1,0:T(8,128)(2,1)S(1)} %copy-done), kind=kOutput, calls=%fused_computation.6 | convolution fusion | flops 1074790400 | bytes 4718592 | tf_op jit(solution)/shard_map/dot_general | solution.py:229
  101.6 0.0 copy-start.3
  101.6 0.0 reduce-scatter.2.cloned.1.call-update
  101.6 0.7 copy-done.3
  102.3 1.3 collective-permute-start.11
  103.6 1.3 collective-permute-start.10
  104.9 1.3 collective-permute-start.9
  106.2 35.3 %collective-permute-done.11.rest_8_ = f32[2,4,4,128]{3,2,1,0:T(4,128)S(1)} collective-permute-done((f32[2,4,4,128]{3,2,1,0:T(4,128)S(1)}, f32[2,4,4,128]{3,2,1,0:T(4,128)S(1)}, u32[]{:S(2)}, u32[]{:S(2)}) %collective-permute-start.11) | collective-permute-done | bytes 16416 | tf_op jit(solution)/shard_map/ppermute | solution.py:23
  141.5 0.0 copy-start.4
  141.5 0.0 collective-permute-done.10.rest_5_
  141.5 0.0 copy-start.5
  141.5 0.0 collective-permute-done.9.rest_2_
  141.5 0.6 copy-done.4
  142.1 0.0 copy-done.5
  142.1 0.0 copy-start.6
  142.1 0.6 copy-done.6
  142.7 10.7 %key_side.1 = (bf16[512,512]{1,0:T(8,128)(2,1)}, bf16[512,512]{1,0:T(8,128)(2,1)}) custom-call(s32[28]{0:T(128)} %reshape.53.valid_ref, bf16[512,512]{1,0:T(8,128)(2,1)} %k_ref.3, bf16[512,512]{1,0:T(8,128)(2,1)} %v_ref.3, bf16[512,512]{1,0:T(8,128)(2,1)} %q_ref.3, bf16[512,512]{1,0:T(8,128)(2,1)} %convolution_convert_fusion.1.g_ref, ...), custom_call_target="tpu_custom_call" | custom-call | tf_op jit(solution)/shard_map/key_side/pallas_call | solution.py:169
  153.4 13.0 %reduce-scatter.2.cloned.1.call-done = bf16[512,512]{1,0:T(8,128)(2,1)} async-done(((bf16[512,2048]{1,0:T(8,128)(2,1)}), bf16[512,512]{1,0:T(8,128)(2,1)}) %reduce-scatter.2.cloned.1.call-update) | async-done | bytes 524304 | tf_op jit(solution)/shard_map/reduce_scatter | solution.py:230
  (21 shorter events, 0.2 us)
Async XLA Ops:
  7.2 36.4 %copy-start = (bf16[512,2048]{1,0:T(8,128)(2,1)S(1)}, bf16[512,2048]{1,0:T(8,128)(2,1)}, u32[]{:S(2)}) copy-start(bf16[512,2048]{1,0:T(8,128)(2,1)} %param.12) | copy-start | bytes 6291460
  7.2 23.5 %copy-start.7 = (s32[32,5]{0,1:T(8,128)S(1)}, s32[32,5]{0,1:T(8,128)}, u32[]{:S(2)}) copy-start(s32[32,5]{0,1:T(8,128)} %param.15) | copy-start | bytes 1924
  7.2 24.8 %copy-start.1 = (s32[32]{0:T(128)S(1)}, s32[32]{0:T(128)}, u32[]{:S(2)}) copy-start(s32[32]{0:T(128)} %param.14) | copy-start | bytes 388
  7.2 36.4 %all-gather.2.cloned.1.call-start = ((), (), s32[]{:S(2)}) async-start(), calls=%async_computation.1 | async-start | bytes 2621440 | tf_op jit(solution)/shard_map/all_gather | solution.py:215
  7.9 158.4 %reduce-scatter.2.cloned.1.call-start = ((), (), s32[]{:S(2)}) async-start(), calls=%async_computation.2 | async-start | bytes 2621440 | tf_op jit(solution)/shard_map/reduce_scatter | solution.py:230
  8.0 29.7 %collective-permute-start.5 = (bf16[512,512]{1,0:T(8,128)(2,1)}, bf16[512,512]{1,0:T(8,128)(2,1)}, u32[]{:S(2)}, u32[]{:S(2)}) collective-permute-start(bf16[512,512]{1,0:T(8,128)(2,1)} %q_ref.3), channel_id=1, source_target_pairs={{16,0},{20,4},{24,8},{28,12},{17,1},{21,5},{25,9},{29,13},{18,2},{... | collective-permute-start | bytes 1572872 | tf_op jit(solution)/shard_map/ppermute | solution.py:23
  9.3 38.0 %collective-permute-start.4 = (bf16[512,512]{1,0:T(8,128)(2,1)}, bf16[512,512]{1,0:T(8,128)(2,1)}, u32[]{:S(2)}, u32[]{:S(2)}) collective-permute-start(bf16[512,512]{1,0:T(8,128)(2,1)} %q_ref.3), channel_id=1, source_target_pairs={{8,0},{12,4},{16,8},{20,12},{24,16},{28,20},{9,1},{13,5},{17,9},{2... | collective-permute-start | bytes 1572872 | tf_op jit(solution)/shard_map/ppermute | solution.py:23
  10.6 38.0 %collective-permute-start.3 = (bf16[512,512]{1,0:T(8,128)(2,1)}, bf16[512,512]{1,0:T(8,128)(2,1)}, u32[]{:S(2)}, u32[]{:S(2)}) collective-permute-start(bf16[512,512]{1,0:T(8,128)(2,1)} %q_ref.3), channel_id=1, source_target_pairs={{4,0},{8,4},{12,8},{16,12},{20,16},{24,20},{28,24},{5,1},{9,5},{13... | collective-permute-start | bytes 1572872 | tf_op jit(solution)/shard_map/ppermute | solution.py:23
  15.7 34.2 %collective-permute-start.2 = (bf16[1024,512]{1,0:T(8,128)(2,1)}, bf16[1024,512]{1,0:T(8,128)(2,1)S(1)}, u32[]{:S(2)}, u32[]{:S(2)}) collective-permute-start(bf16[1024,512]{1,0:T(8,128)(2,1)} %constant_dynamic-update-slice_fusion), channel_id=1, source_target_pairs={{0,16},{4,20},{8,24},{12,28},{1,17},{5,21},{9,25},{13,29},{2,18},{... | collective-permute-start | bytes 3145736 | tf_op jit(solution)/shard_map/ppermute | solution.py:23
  24.8 44.6 %collective-permute-start.1 = (bf16[1024,512]{1,0:T(8,128)(2,1)}, bf16[1024,512]{1,0:T(8,128)(2,1)}, u32[]{:S(2)}, u32[]{:S(2)}) collective-permute-start(bf16[1024,512]{1,0:T(8,128)(2,1)} %constant_dynamic-update-slice_fusion), channel_id=1, source_target_pairs={{0,8},{4,12},{8,16},{12,20},{16,24},{20,28},{1,9},{5,13},{9,17},{1... | collective-permute-start | bytes 3145736 | tf_op jit(solution)/shard_map/ppermute | solution.py:23
  37.6 31.8 %collective-permute-start = (bf16[1024,512]{1,0:T(8,128)(2,1)}, bf16[1024,512]{1,0:T(8,128)(2,1)}, u32[]{:S(2)}, u32[]{:S(2)}) collective-permute-start(bf16[1024,512]{1,0:T(8,128)(2,1)} %constant_dynamic-update-slice_fusion), channel_id=1, source_target_pairs={{0,4},{4,8},{8,12},{12,16},{16,20},{20,24},{24,28},{1,5},{5,9},{9,... | collective-permute-start | bytes 3145736 | tf_op jit(solution)/shard_map/ppermute | solution.py:23
  47.3 35.4 %collective-permute-start.8 = (bf16[512,512]{1,0:T(8,128)(2,1)}, bf16[512,512]{1,0:T(8,128)(2,1)}, u32[]{:S(2)}, u32[]{:S(2)}) collective-permute-start(bf16[512,512]{1,0:T(8,128)(2,1)} %convolution_convert_fusion.1.g_ref), channel_id=1, source_target_pairs={{16,0},{20,4},{24,8},{28,12},{17,1},{21,5},{25,9},{29,13},{18,2},{... | collective-permute-start | bytes 1572872 | tf_op jit(solution)/shard_map/ppermute | solution.py:23
  48.6 34.1 %collective-permute-start.7 = (bf16[512,512]{1,0:T(8,128)(2,1)}, bf16[512,512]{1,0:T(8,128)(2,1)}, u32[]{:S(2)}, u32[]{:S(2)}) collective-permute-start(bf16[512,512]{1,0:T(8,128)(2,1)} %convolution_convert_fusion.1.g_ref), channel_id=1, source_target_pairs={{8,0},{12,4},{16,8},{20,12},{24,16},{28,20},{9,1},{13,5},{17,9},{2... | collective-permute-start | bytes 1572872 | tf_op jit(solution)/shard_map/ppermute | solution.py:23
  49.9 32.8 %copy-start.2 = (bf16[1024,512]{1,0:T(8,128)(2,1)}, bf16[1024,512]{1,0:T(8,128)(2,1)S(1)}, u32[]{:S(2)}) copy-start(bf16[1024,512]{1,0:T(8,128)(2,1)S(1)} %collective-permute-done.2.rest_4_.rest_5_) | copy-start | bytes 3145732
  49.9 32.8 %collective-permute-start.6 = (bf16[512,512]{1,0:T(8,128)(2,1)}, bf16[512,512]{1,0:T(8,128)(2,1)}, u32[]{:S(2)}, u32[]{:S(2)}) collective-permute-start(bf16[512,512]{1,0:T(8,128)(2,1)} %convolution_convert_fusion.1.g_ref), channel_id=1, source_target_pairs={{4,0},{8,4},{12,8},{16,12},{20,16},{24,20},{28,24},{5,1},{9,5},{13... | collective-permute-start | bytes 1572872 | tf_op jit(solution)/shard_map/ppermute | solution.py:23
  101.6 0.7 copy-start.3
  102.3 39.2 %collective-permute-start.11 = (f32[2,4,4,128]{3,2,1,0:T(4,128)S(1)}, f32[2,4,4,128]{3,2,1,0:T(4,128)S(1)}, u32[]{:S(2)}, u32[]{:S(2)}) collective-permute-start(f32[2,4,4,128]{3,2,1,0:T(4,128)S(1)} %copy-done.3), channel_id=1, source_target_pairs={{16,0},{20,4},{24,8},{28,12},{17,1},{21,5},{25,9},{29,13},{18,2},{... | collective-permute-start | bytes 49160 | tf_op jit(solution)/shard_map/ppermute | solution.py:23
  103.6 37.9 %collective-permute-start.10 = (f32[2,4,4,128]{3,2,1,0:T(4,128)S(1)}, f32[2,4,4,128]{3,2,1,0:T(4,128)S(1)}, u32[]{:S(2)}, u32[]{:S(2)}) collective-permute-start(f32[2,4,4,128]{3,2,1,0:T(4,128)S(1)} %copy-done.3), channel_id=1, source_target_pairs={{8,0},{12,4},{16,8},{20,12},{24,16},{28,20},{9,1},{13,5},{17,9},{2... | collective-permute-start | bytes 49160 | tf_op jit(solution)/shard_map/ppermute | solution.py:23
  104.9 36.6 %collective-permute-start.9 = (f32[2,4,4,128]{3,2,1,0:T(4,128)S(1)}, f32[2,4,4,128]{3,2,1,0:T(4,128)S(1)}, u32[]{:S(2)}, u32[]{:S(2)}) collective-permute-start(f32[2,4,4,128]{3,2,1,0:T(4,128)S(1)} %copy-done.3), channel_id=1, source_target_pairs={{4,0},{8,4},{12,8},{16,12},{20,16},{24,20},{28,24},{5,1},{9,5},{13... | collective-permute-start | bytes 49160 | tf_op jit(solution)/shard_map/ppermute | solution.py:23
  141.5 0.6 copy-start.4
  141.5 0.6 copy-start.5
  142.1 0.6 copy-start.6
Sparse Core Ops, SparseCore 0:
  9.6 25.3 all-gather.1
  101.7 64.5 reduce-scatter.1

commit v6 on v5

--- a/solution.py
+++ b/solution.py
@@ -219,17 +219,19 @@
     )
     g = grad_att.astype(jnp.bfloat16)
     g_from = [passed_along(g, "ctx", -(2**m)) for m in levels]
-    kv_from, q_from, g_from, valid_q, valid_k = lax.optimization_barrier(
-        (kv_from, q_from, g_from, valid_q, valid_k)
+    weight_cols = lax.all_to_all(out_weight, "head", 1, 0, tiled=True)
+    kv_from, q_from, g_from, valid_q, valid_k, weight_cols = lax.optimization_barrier(
+        (kv_from, q_from, g_from, valid_q, valid_k, weight_cols)
     )
 
     attended, query_grad, stats = query_call(
         valid_q, queries, g, keys, values, kv_from, heads_local, n_levels
     )
-    partial_out = jnp.dot(attended, out_weight, preferred_element_type=jnp.float32)
-    output = lax.psum_scatter(
-        partial_out.astype(jnp.bfloat16), "head", scatter_dimension=1, tiled=True
-    )
+    output = jnp.dot(
+        lax.all_gather(attended, "head", axis=1, tiled=True),
+        weight_cols,
+        preferred_element_type=jnp.float32,
+    ).astype(jnp.bfloat16)
 
     st_from = [passed_along(stats, "ctx", -(2**m)) for m in levels]
     key_grad, value_grad = key_call(

time: 174 us -> 163 us (0.937)
  waiting for transfers between devices: 82.4 us -> 52.3 us
  starting transfers between devices: 32 us -> 46.4 us
  local copies, waits for them, and re-layouts: 11.1 us -> 14.9 us
    ppermute x12, waiting for transfers between devices: 68.7 us -> 51.6 us  [passed_along(): return lax.ppermute(block, axis, route)]
    reduce_scatter x1 -> x0, waiting for transfers between devices: 13 us -> none  [local(): lax.psum_scatter(partial_out.astype(jnp.bfloat16), 'head', scatter_dimens...]
    ppermute x12, starting transfers between devices: 31.9 us -> 42.6 us  [passed_along(): return lax.ppermute(block, axis, route)]
    all_to_all x0 -> x1, starting transfers between devices: none -> 3.74 us  [local(): weight_cols = lax.all_to_all(out_weight, 'head', 1, 0, tiled=True)]
    all_to_all x0 -> x1, local copies, waits for them, and re-layouts: none -> 2.37 us  [local(): weight_cols = lax.all_to_all(out_weight, 'head', 1, 0, tiled=True)]
    unnamed x17 -> x18, local copies, waits for them, and re-layouts: 3.8 us -> 5.24 us
  transfers between devices with their start and end apart: 14 -> 15, of which waited for: 6 -> 8; matrix products, arithmetic and copies ran while one was open for 8% -> 11% of each run, Pallas kernels for 6% -> 7%
where the time goes in v6:
time: 163 us; the launch traced here: 162 us
  waiting for transfers between devices  52.3 us (32%)
  starting transfers between devices  46.4 us (28%)
  Pallas kernels  25.8 us (16%)
  local copies, waits for them, and re-layouts  14.9 us (9%)
  between operations  14.3 us (9%)
  matrix products  7.93 us (5%)
    ppermute x12, waiting for transfers between devices, passed_along(): return lax.ppermute(block, axis, route)  51.6 us
    ppermute x12, starting transfers between devices, passed_along(): return lax.ppermute(block, axis, route)  42.6 us
    pallas_call x1, Pallas kernels, query_call(): pl.pallas_call(functools.partial(query_kernel, n_levels), grid_spec=grid_...  15.2 us
    pallas_call x1, Pallas kernels, key_call(): pl.pallas_call(functools.partial(key_kernel, n_levels), grid_spec=grid_sp...  10.6 us
    unnamed x18, local copies, waits for them, and re-layouts  5.24 us
    dot_general x1, matrix products, local(): lax.dot_general(lax.all_gather(d_out, 'head', axis=1, tiled=True), out_we...  4.3 us
    all_to_all x1, starting transfers between devices, local(): weight_cols = lax.all_to_all(out_weight, 'head', 1, 0, tiled=True)  3.74 us
    dot_general x1, matrix products, local(): jnp.dot(lax.all_gather(attended, 'head', axis=1, tiled=True), weight_cols...  3.63 us
  transfers between devices with their start and end apart: 15, of which 8 were waited for; matrix products, arithmetic and copies ran while one was open for 11% of the time, Pallas kernels for 7%

profile of v6, /device:TPU:0, one launch (start us, length us, event | category | flops | bytes accessed | tf_op | source)
XLA Modules:
  0.0 161.9 jit_solution(12823573103119095153)
XLA Ops:
  7.2 0.0 copy-start.2
  7.2 0.0 all-gather.3.cloned.1.call-start
  7.2 0.7 all-gather.3.cloned.1.call-update
  7.9 1.9 %constant_dynamic-update-slice_fusion.1 = bf16[1024,512]{1,0:T(8,128)(2,1)} fusion(bf16[512,512]{1,0:T(8,128)(2,1)} %k_ref.3), kind=kLoop, calls=%fused_computation.15 | loop fusion | bytes 1048576
  9.8 1.9 %constant_dynamic-update-slice_fusion = bf16[1024,512]{1,0:T(8,128)(2,1)} fusion(bf16[1024,512]{1,0:T(8,128)(2,1)} %constant_dynamic-update-slice_fusion.1, bf16[512,512]{1,0:T(8,128)(2,1)} %v_ref.3), kind=kLoop, calls=%fused_computation.14 | loop fusion | bytes 1048576 | tf_op jit(solution)/shard_map/concatenate | solution.py:210
  11.7 4.9 %collective-permute-start = (bf16[1024,512]{1,0:T(8,128)(2,1)}, bf16[1024,512]{1,0:T(8,128)(2,1)S(1)}, u32[]{:S(2)}, u32[]{:S(2)}) collective-permute-start(bf16[1024,512]{1,0:T(8,128)(2,1)} %constant_dynamic-update-slice_fusion), channel_id=1, source_target_pairs={{0,4},{4,8},{8,12},{12,16},{16,20},{20,24},{24,28},{1,5},{5,9},{9,... | collective-permute-start | bytes 3145736 | tf_op jit(solution)/shard_map/ppermute | solution.py:23
  16.6 4.5 %collective-permute-start.1 = (bf16[1024,512]{1,0:T(8,128)(2,1)}, bf16[1024,512]{1,0:T(8,128)(2,1)}, u32[]{:S(2)}, u32[]{:S(2)}) collective-permute-start(bf16[1024,512]{1,0:T(8,128)(2,1)} %constant_dynamic-update-slice_fusion), channel_id=1, source_target_pairs={{0,8},{4,12},{8,16},{12,20},{16,24},{20,28},{1,9},{5,13},{9,17},{1... | collective-permute-start | bytes 3145736 | tf_op jit(solution)/shard_map/ppermute | solution.py:23
  21.1 1.3 collective-permute-start.3
  22.4 1.3 collective-permute-start.4
  23.7 1.3 collective-permute-start.5
  25.0 0.0 copy-done.2
  25.0 2.5 %copy.17 = bf16[512,2048]{0,1:T(8,128)(2,1)} copy(bf16[512,2048]{1,0:T(8,128)(2,1)S(1)} %copy-done.2) | data formatting | bytes 4194304 | tf_op args[3]
  27.5 0.0 copy-start
  27.5 3.7 %all-to-all-start = ((bf16[512,4,512]{0,2,1:T(8,128)(2,1)}), bf16[512,4,512]{0,2,1:T(8,128)(2,1)S(1)}, u32[]{:S(2)}, u32[]{:S(2)}) async-start(bf16[512,4,512]{0,2,1:T(8,128)(2,1)} %bitcast.32), calls=%async_computation | async-start | bytes 4194304 | tf_op jit(solution)/shard_map/all_to_all | solution.py:222
  31.3 0.0 all-gather.5.cloned.1.call-start
  31.3 0.0 copy-done.7
  31.4 0.6 gather_fusion.5
  32.0 0.6 gather_fusion.4
  32.7 0.6 gather_fusion.3
  33.3 0.0 copy-done
  33.3 0.6 gather_fusion.2
  34.0 0.1 and_bitcast_fusion.6
  34.1 0.1 constant_dynamic-slice_fusion
  34.3 0.1 copy.15
  34.4 0.6 reshape.55.valid_ref
  34.9 1.5 collective-permute-done.3.rest_0_
  36.4 21.5 %collective-permute-start.2 = (bf16[1024,512]{1,0:T(8,128)(2,1)}, bf16[1024,512]{1,0:T(8,128)(2,1)}, u32[]{:S(2)}, u32[]{:S(2)}) collective-permute-start(bf16[1024,512]{1,0:T(8,128)(2,1)} %constant_dynamic-update-slice_fusion), channel_id=1, source_target_pairs={{0,16},{4,20},{8,24},{12,28},{1,17},{5,21},{9,25},{13,29},{2,18},{... | collective-permute-start | bytes 3145736 | tf_op jit(solution)/shard_map/ppermute | solution.py:23
  57.9 0.6 gather_fusion.1
  58.5 0.0 all-gather.3.cloned.1.call-done
  58.5 4.3 %convolution_convert_fusion.1.g_ref = bf16[512,512]{1,0:T(8,128)(2,1)} fusion(bf16[512,2048]{1,0:T(8,128)(2,1)} %all-gather.3.cloned.1.call-done, bf16[512,2048]{1,0:T(8,128)(2,1)} %param.12), kind=kOutput, calls=%fused_computation.7 | convolution fusion | flops 1074003968 | bytes 4718592 | tf_op jit(solution)/shard_map/dot_general | solution.py:214
  62.8 0.0 collective-permute-done.4.rest_3_
  62.8 1.3 collective-permute-start.6
  64.1 8.8 %collective-permute-done.5.rest_6_ = bf16[512,512]{1,0:T(8,128)(2,1)} collective-permute-done((bf16[512,512]{1,0:T(8,128)(2,1)}, bf16[512,512]{1,0:T(8,128)(2,1)}, u32[]{:S(2)}, u32[]{:S(2)}) %collective-permute-start.5) | collective-permute-done | bytes 524320 | tf_op jit(solution)/shard_map/ppermute | solution.py:23
  72.9 1.3 collective-permute-start.7
  74.2 0.0 collective-permute-done.rest_0_.rest_1_
  74.2 0.0 copy-start.1
  74.2 1.3 collective-permute-start.8
  75.5 0.6 gather_fusion
  76.2 0.1 copy.16
  76.3 0.6 reshape.56.valid_ref
  76.9 0.0 all-to-all-done
  76.9 2.4 %copy.18 = bf16[4,512,512]{2,1,0:T(8,128)(2,1)} copy(bf16[4,512,512]{1,2,0:T(8,128)(2,1)S(1)} %bitcast.31) | data formatting | bytes 4194304 | tf_op jit(solution)/shard_map/all_to_all | solution.py:222
  79.3 0.0 copy-done.1
  79.3 0.0 collective-permute-done.1.rest_2_.rest_3_
  79.3 0.5 collective-permute-done.2.rest_4_.rest_5_
  79.8 0.0 collective-permute-done.6.rest_1_
  79.8 13.8 %collective-permute-done.7.rest_4_ = bf16[512,512]{1,0:T(8,128)(2,1)} collective-permute-done((bf16[512,512]{1,0:T(8,128)(2,1)}, bf16[512,512]{1,0:T(8,128)(2,1)}, u32[]{:S(2)}, u32[]{:S(2)}) %collective-permute-start.7) | collective-permute-done | bytes 524320 | tf_op jit(solution)/shard_map/ppermute | solution.py:23
  93.6 22.5 %collective-permute-done.8.rest_7_ = bf16[512,512]{1,0:T(8,128)(2,1)} collective-permute-done((bf16[512,512]{1,0:T(8,128)(2,1)}, bf16[512,512]{1,0:T(8,128)(2,1)}, u32[]{:S(2)}, u32[]{:S(2)}) %collective-permute-start.8) | collective-permute-done | bytes 524320 | tf_op jit(solution)/shard_map/ppermute | solution.py:23
  116.1 15.2 %query_side.1 = (bf16[512,512]{1,0:T(8,128)(2,1)}, bf16[512,512]{1,0:T(8,128)(2,1)}, f32[2,4,4,128]{3,2,1,0:T(4,128)}) custom-call(s32[28]{0:T(128)} %reshape.55.valid_ref, bf16[512,512]{1,0:T(8,128)(2,1)} %q_ref.3, bf16[512,512]{1,0:T(8,128)(2,1)} %convolution_convert_fusion.1.g_ref, bf16[512,512]{1,0:T(8,128)(2,1)} %k_ref.3, bf16[512,512]{1,0:T(8,128)(2,1)} %v_ref.3, ...), custom_call_target="tpu_custom_call" | custom-call | tf_op jit(solution)/shard_map/query_side/pallas_call | solution.py:144
  131.3 0.0 all-gather.5.cloned.1.call-update
  131.4 0.0 copy-start.3
  131.4 1.4 collective-permute-start.10
  132.8 1.3 collective-permute-start.11
  134.1 1.3 collective-permute-start.9
  135.4 1.9 %collective-permute-done.10.rest_5_ = f32[2,4,4,128]{3,2,1,0:T(4,128)S(1)} collective-permute-done((f32[2,4,4,128]{3,2,1,0:T(4,128)}, f32[2,4,4,128]{3,2,1,0:T(4,128)S(1)}, u32[]{:S(2)}, u32[]{:S(2)}) %collective-permute-start.10) | collective-permute-done | bytes 16416 | tf_op jit(solution)/shard_map/ppermute | solution.py:23
  137.4 2.2 %collective-permute-done.11.rest_8_ = f32[2,4,4,128]{3,2,1,0:T(4,128)S(1)} collective-permute-done((f32[2,4,4,128]{3,2,1,0:T(4,128)}, f32[2,4,4,128]{3,2,1,0:T(4,128)S(1)}, u32[]{:S(2)}, u32[]{:S(2)}) %collective-permute-start.11) | collective-permute-done | bytes 16416 | tf_op jit(solution)/shard_map/ppermute | solution.py:23
  139.6 0.4 collective-permute-done.9.rest_2_
  140.0 0.0 copy-done.4
  140.0 0.2 copy-done.5
  140.2 0.6 copy-done.6
  140.7 10.6 %key_side.1 = (bf16[512,512]{1,0:T(8,128)(2,1)}, bf16[512,512]{1,0:T(8,128)(2,1)}) custom-call(s32[28]{0:T(128)} %reshape.56.valid_ref, bf16[512,512]{1,0:T(8,128)(2,1)} %k_ref.3, bf16[512,512]{1,0:T(8,128)(2,1)} %v_ref.3, bf16[512,512]{1,0:T(8,128)(2,1)} %q_ref.3, bf16[512,512]{1,0:T(8,128)(2,1)} %convolution_convert_fusion.1.g_ref, ...), custom_call_target="tpu_custom_call" | custom-call | tf_op jit(solution)/shard_map/key_side/pallas_call | solution.py:169
  151.4 0.0 all-gather.5.cloned.1.call-done
  151.4 0.0 copy-done.3
  151.4 3.6 %convolution_convert_fusion = bf16[512,512]{1,0:T(8,128)(2,1)} fusion(bf16[512,2048]{1,0:T(8,128)(2,1)} %all-gather.5.cloned.1.call-done, bf16[2048,512]{1,0:T(8,128)(2,1)S(1)} %bitcast.33), kind=kOutput, calls=%fused_computation.6 | convolution fusion | flops 1074003968 | bytes 4718592 | tf_op jit(solution)/shard_map/dot_general | solution.py:230
  (25 shorter events, 0.2 us)
Async XLA Ops:
  7.2 17.8 %copy-start.2 = (bf16[512,2048]{1,0:T(8,128)(2,1)S(1)}, bf16[512,2048]{1,0:T(8,128)(2,1)}, u32[]{:S(2)}) copy-start(bf16[512,2048]{1,0:T(8,128)(2,1)} %param.12) | copy-start | bytes 6291460
  7.2 51.4 %all-gather.3.cloned.1.call-start = ((), (), s32[]{:S(2)}) async-start(), calls=%async_computation.1 | async-start | bytes 2621440 | tf_op jit(solution)/shard_map/all_gather | solution.py:215
  11.7 62.4 %collective-permute-start = (bf16[1024,512]{1,0:T(8,128)(2,1)}, bf16[1024,512]{1,0:T(8,128)(2,1)S(1)}, u32[]{:S(2)}, u32[]{:S(2)}) collective-permute-start(bf16[1024,512]{1,0:T(8,128)(2,1)} %constant_dynamic-update-slice_fusion), channel_id=1, source_target_pairs={{0,4},{4,8},{8,12},{12,16},{16,20},{20,24},{24,28},{1,5},{5,9},{9,... | collective-permute-start | bytes 3145736 | tf_op jit(solution)/shard_map/ppermute | solution.py:23
  16.6 62.7 %collective-permute-start.1 = (bf16[1024,512]{1,0:T(8,128)(2,1)}, bf16[1024,512]{1,0:T(8,128)(2,1)}, u32[]{:S(2)}, u32[]{:S(2)}) collective-permute-start(bf16[1024,512]{1,0:T(8,128)(2,1)} %constant_dynamic-update-slice_fusion), channel_id=1, source_target_pairs={{0,8},{4,12},{8,16},{12,20},{16,24},{20,28},{1,9},{5,13},{9,17},{1... | collective-permute-start | bytes 3145736 | tf_op jit(solution)/shard_map/ppermute | solution.py:23
  21.1 15.3 %collective-permute-start.3 = (bf16[512,512]{1,0:T(8,128)(2,1)}, bf16[512,512]{1,0:T(8,128)(2,1)}, u32[]{:S(2)}, u32[]{:S(2)}) collective-permute-start(bf16[512,512]{1,0:T(8,128)(2,1)} %q_ref.3), channel_id=1, source_target_pairs={{4,0},{8,4},{12,8},{16,12},{20,16},{24,20},{28,24},{5,1},{9,5},{13... | collective-permute-start | bytes 1572872 | tf_op jit(solution)/shard_map/ppermute | solution.py:23
  22.4 40.5 %collective-permute-start.4 = (bf16[512,512]{1,0:T(8,128)(2,1)}, bf16[512,512]{1,0:T(8,128)(2,1)}, u32[]{:S(2)}, u32[]{:S(2)}) collective-permute-start(bf16[512,512]{1,0:T(8,128)(2,1)} %q_ref.3), channel_id=1, source_target_pairs={{8,0},{12,4},{16,8},{20,12},{24,16},{28,20},{9,1},{13,5},{17,9},{2... | collective-permute-start | bytes 1572872 | tf_op jit(solution)/shard_map/ppermute | solution.py:23
  23.7 49.2 %collective-permute-start.5 = (bf16[512,512]{1,0:T(8,128)(2,1)}, bf16[512,512]{1,0:T(8,128)(2,1)}, u32[]{:S(2)}, u32[]{:S(2)}) collective-permute-start(bf16[512,512]{1,0:T(8,128)(2,1)} %q_ref.3), channel_id=1, source_target_pairs={{16,0},{20,4},{24,8},{28,12},{17,1},{21,5},{25,9},{29,13},{18,2},{... | collective-permute-start | bytes 1572872 | tf_op jit(solution)/shard_map/ppermute | solution.py:23
  27.5 3.8 %copy-start.7 = (s32[32,5]{0,1:T(8,128)S(1)}, s32[32,5]{0,1:T(8,128)}, u32[]{:S(2)}) copy-start(s32[32,5]{0,1:T(8,128)} %param.15) | copy-start | bytes 1924
  27.5 5.8 %copy-start = (s32[32]{0:T(128)S(1)}, s32[32]{0:T(128)}, u32[]{:S(2)}) copy-start(s32[32]{0:T(128)} %param.14) | copy-start | bytes 388
  27.5 49.4 %all-to-all-start = ((bf16[512,4,512]{0,2,1:T(8,128)(2,1)}), bf16[512,4,512]{0,2,1:T(8,128)(2,1)S(1)}, u32[]{:S(2)}, u32[]{:S(2)}) async-start(bf16[512,4,512]{0,2,1:T(8,128)(2,1)} %bitcast.32), calls=%async_computation | async-start | bytes 4194304 | tf_op jit(solution)/shard_map/all_to_all | solution.py:222
  31.3 120.1 %all-gather.5.cloned.1.call-start = ((), (), s32[]{:S(2)}) async-start(), calls=%async_computation.2 | async-start | bytes 2621440 | tf_op jit(solution)/shard_map/all_gather | solution.py:231
  36.4 43.4 %collective-permute-start.2 = (bf16[1024,512]{1,0:T(8,128)(2,1)}, bf16[1024,512]{1,0:T(8,128)(2,1)}, u32[]{:S(2)}, u32[]{:S(2)}) collective-permute-start(bf16[1024,512]{1,0:T(8,128)(2,1)} %constant_dynamic-update-slice_fusion), channel_id=1, source_target_pairs={{0,16},{4,20},{8,24},{12,28},{1,17},{5,21},{9,25},{13,29},{2,18},{... | collective-permute-start | bytes 3145736 | tf_op jit(solution)/shard_map/ppermute | solution.py:23
  62.8 17.0 %collective-permute-start.6 = (bf16[512,512]{1,0:T(8,128)(2,1)}, bf16[512,512]{1,0:T(8,128)(2,1)}, u32[]{:S(2)}, u32[]{:S(2)}) collective-permute-start(bf16[512,512]{1,0:T(8,128)(2,1)} %convolution_convert_fusion.1.g_ref), channel_id=1, source_target_pairs={{4,0},{8,4},{12,8},{16,12},{20,16},{24,20},{28,24},{5,1},{9,5},{13... | collective-permute-start | bytes 1572872 | tf_op jit(solution)/shard_map/ppermute | solution.py:23
  72.9 20.7 %collective-permute-start.7 = (bf16[512,512]{1,0:T(8,128)(2,1)}, bf16[512,512]{1,0:T(8,128)(2,1)}, u32[]{:S(2)}, u32[]{:S(2)}) collective-permute-start(bf16[512,512]{1,0:T(8,128)(2,1)} %convolution_convert_fusion.1.g_ref), channel_id=1, source_target_pairs={{8,0},{12,4},{16,8},{20,12},{24,16},{28,20},{9,1},{13,5},{17,9},{2... | collective-permute-start | bytes 1572872 | tf_op jit(solution)/shard_map/ppermute | solution.py:23
  74.2 5.1 %copy-start.1 = (bf16[1024,512]{1,0:T(8,128)(2,1)}, bf16[1024,512]{1,0:T(8,128)(2,1)S(1)}, u32[]{:S(2)}) copy-start(bf16[1024,512]{1,0:T(8,128)(2,1)S(1)} %collective-permute-done.rest_0_.rest_1_) | copy-start | bytes 3145732
  74.2 41.9 %collective-permute-start.8 = (bf16[512,512]{1,0:T(8,128)(2,1)}, bf16[512,512]{1,0:T(8,128)(2,1)}, u32[]{:S(2)}, u32[]{:S(2)}) collective-permute-start(bf16[512,512]{1,0:T(8,128)(2,1)} %convolution_convert_fusion.1.g_ref), channel_id=1, source_target_pairs={{16,0},{20,4},{24,8},{28,12},{17,1},{21,5},{25,9},{29,13},{18,2},{... | collective-permute-start | bytes 1572872 | tf_op jit(solution)/shard_map/ppermute | solution.py:23
  131.4 20.0 %copy-start.3 = (bf16[4,512,512]{2,1,0:T(8,128)(2,1)S(1)}, bf16[4,512,512]{2,1,0:T(8,128)(2,1)}, u32[]{:S(2)}) copy-start(bf16[4,512,512]{2,1,0:T(8,128)(2,1)} %copy.18) | copy-start | bytes 6291460
  131.4 6.0 %collective-permute-start.10 = (f32[2,4,4,128]{3,2,1,0:T(4,128)}, f32[2,4,4,128]{3,2,1,0:T(4,128)S(1)}, u32[]{:S(2)}, u32[]{:S(2)}) collective-permute-start(f32[2,4,4,128]{3,2,1,0:T(4,128)} %get-tuple-element.30.st_ref), channel_id=1, source_target_pairs={{8,0},{12,4},{16,8},{20,12},{24,16},{28,20},{9,1},{13,5},{17,9},{2... | collective-permute-start | bytes 49160 | tf_op jit(solution)/shard_map/ppermute | solution.py:23
  132.8 6.7 %collective-permute-start.11 = (f32[2,4,4,128]{3,2,1,0:T(4,128)}, f32[2,4,4,128]{3,2,1,0:T(4,128)S(1)}, u32[]{:S(2)}, u32[]{:S(2)}) collective-permute-start(f32[2,4,4,128]{3,2,1,0:T(4,128)} %get-tuple-element.30.st_ref), channel_id=1, source_target_pairs={{16,0},{20,4},{24,8},{28,12},{17,1},{21,5},{25,9},{29,13},{18,2},{... | collective-permute-start | bytes 49160 | tf_op jit(solution)/shard_map/ppermute | solution.py:23
  134.1 5.8 %collective-permute-start.9 = (f32[2,4,4,128]{3,2,1,0:T(4,128)}, f32[2,4,4,128]{3,2,1,0:T(4,128)S(1)}, u32[]{:S(2)}, u32[]{:S(2)}) collective-permute-start(f32[2,4,4,128]{3,2,1,0:T(4,128)} %get-tuple-element.30.st_ref), channel_id=1, source_target_pairs={{4,0},{8,4},{12,8},{16,12},{20,16},{24,20},{28,24},{5,1},{9,5},{13... | collective-permute-start | bytes 49160 | tf_op jit(solution)/shard_map/ppermute | solution.py:23
  137.4 2.6 %copy-start.4 = (f32[2,4,4,128]{3,2,1,0:T(4,128)}, f32[2,4,4,128]{3,2,1,0:T(4,128)S(1)}, u32[]{:S(2)}) copy-start(f32[2,4,4,128]{3,2,1,0:T(4,128)S(1)} %collective-permute-done.10.rest_5_) | copy-start | bytes 49156
  139.6 0.6 copy-start.5
  140.2 0.6 copy-start.6
Sparse Core Ops, SparseCore 0:
  9.6 25.2 all-gather.2
  131.5 19.8 all-gather.4

commit v7 on v6

--- a/solution.py
+++ b/solution.py
@@ -48,20 +48,24 @@
     return allowed
 
 
-def query_kernel(n_levels, valid_ref, q_ref, g_ref, k_ref, v_ref, *rest):
-    kf = rest[0 : 2 * n_levels : 2]
-    vf = rest[1 : 2 * n_levels : 2]
-    att_ref, dq_ref, st_ref = rest[2 * n_levels :]
+def row_to_col(row):
+    eye = lax.broadcasted_iota(jnp.int32, (BLK, BLK), 0) == lax.broadcasted_iota(
+        jnp.int32, (BLK, BLK), 1
+    )
+    return jnp.sum(jnp.where(eye, row, 0.0), axis=1, keepdims=True)
+
+
+def query_blocks(n_levels, valid_ref, q_ref, k_ref, v_ref, kv_refs):
+    kf = kv_refs[0::2]
+    vf = kv_refs[1::2]
     n_cand = 1 + WIN_MAX + n_levels
-    width = n_cand * BLK
     scale = HD ** (-0.5)
-    col = lax.broadcasted_iota(jnp.int32, (BLK, width), 1)
-    row = lax.broadcasted_iota(jnp.int32, (BLK, width), 0)
+    col = lax.broadcasted_iota(jnp.int32, (BLK, n_cand * BLK), 1)
+    row = lax.broadcasted_iota(jnp.int32, (BLK, n_cand * BLK), 0)
     diag = col <= row
     for n in range(NB):
         rows = pl.ds(n * BLK, BLK)
         qn = q_ref[rows, :]
-        gn = g_ref[rows, :]
         cands = [(k_ref, v_ref, n)]
         for o in range(1, WIN_MAX + 1):
             j = n - o
@@ -72,18 +76,36 @@
         vcat = jnp.concatenate([vr[pl.ds(j * BLK, BLK), :] for _, vr, j in cands], axis=0)
         allowed = candidate_mask(valid_ref, n * n_cand, n_cand, diag)
         scores = jnp.where(allowed, dot_nt(qn, kcat) * scale, neg_large)
+        yield n, rows, kcat, vcat, scores
+
+
+def query_fwd_kernel(n_levels, valid_ref, q_ref, g_ref, k_ref, v_ref, *rest):
+    att_ref, st_ref = rest[2 * n_levels :]
+    blocks = query_blocks(n_levels, valid_ref, q_ref, k_ref, v_ref, rest[: 2 * n_levels])
+    for n, rows, kcat, vcat, scores in blocks:
         row_max = scores.max(axis=1, keepdims=True)
         row_total = jnp.sum(jnp.exp(scores - row_max), axis=1, keepdims=True)
         log_total = row_max + jnp.log(row_total)
         probs = jnp.exp(scores - log_total)
         att_b = dot_nn(probs.astype(jnp.bfloat16), vcat).astype(jnp.bfloat16)
         att_ref[rows, :] = att_b
+        gn = g_ref[rows, :]
         delta = jnp.sum(gn.astype(jnp.float32) * att_b.astype(jnp.float32), axis=1, keepdims=True)
-        d_prob = dot_nt(gn, vcat)
+        st_ref[0, 0, pl.ds(n, 1), :] = col_to_row(log_total)
+        st_ref[1, 0, pl.ds(n, 1), :] = col_to_row(delta)
+
+
+def query_bwd_kernel(n_levels, valid_ref, q_ref, g_ref, k_ref, v_ref, st_ref, *rest):
+    dq_ref = rest[2 * n_levels]
+    scale = HD ** (-0.5)
+    blocks = query_blocks(n_levels, valid_ref, q_ref, k_ref, v_ref, rest[: 2 * n_levels])
+    for n, rows, kcat, vcat, scores in blocks:
+        log_total = row_to_col(st_ref[0, 0, pl.ds(n, 1), :])
+        delta = row_to_col(st_ref[1, 0, pl.ds(n, 1), :])
+        probs = jnp.exp(scores - log_total)
+        d_prob = dot_nt(g_ref[rows, :], vcat)
         d_score = (probs * (d_prob - delta) * scale).astype(jnp.bfloat16)
         dq_ref[rows, :] = dot_nn(d_score, kcat).astype(jnp.bfloat16)
-        st_ref[0, 0, pl.ds(n, 1), :] = col_to_row(log_total)
-        st_ref[1, 0, pl.ds(n, 1), :] = col_to_row(delta)
 
 
 def key_kernel(n_levels, valid_ref, k_ref, v_ref, q_ref, g_ref, st_ref, *rest):
@@ -128,10 +150,9 @@
     return pl.BlockSpec((2, 1, NB, BLK), lambda h, valid: (0, h, 0, 0))
 
 
-def query_call(valid, q, g, k, v, kv_from, heads, n_levels):
-    tokens, features = q.shape
-    in_specs = [head_block(0)] * 4
-    args = [q, g, k, v]
+def query_call(kernel, valid, q, g, k, v, kv_from, extra, heads, n_levels, out_specs, out_shape, name):
+    in_specs = [head_block(0)] * 4 + [stats_block(heads)] * len(extra)
+    args = [q, g, k, v] + list(extra)
     for kv in kv_from:
         in_specs += [head_block(0), head_block(1)]
         args += [kv, kv]
@@ -139,17 +160,13 @@
         num_scalar_prefetch=1,
         grid=(heads,),
         in_specs=in_specs,
-        out_specs=[head_block(0), head_block(0), stats_block(heads)],
+        out_specs=out_specs,
     )
     return pl.pallas_call(
-        functools.partial(query_kernel, n_levels),
+        functools.partial(kernel, n_levels),
         grid_spec=grid_spec,
-        out_shape=[
-            jax.ShapeDtypeStruct((tokens, features), jnp.bfloat16),
-            jax.ShapeDtypeStruct((tokens, features), jnp.bfloat16),
-            jax.ShapeDtypeStruct((2, heads, NB, BLK), jnp.float32),
-        ],
-        name="query_side",
+        out_shape=out_shape,
+        name=name,
     )(valid, *args)
 
 
@@ -224,8 +241,15 @@
         (kv_from, q_from, g_from, valid_q, valid_k, weight_cols)
     )
 
-    attended, query_grad, stats = query_call(
-        valid_q, queries, g, keys, values, kv_from, heads_local, n_levels
+    flat = jax.ShapeDtypeStruct(queries.shape, jnp.bfloat16)
+    stats_shape = jax.ShapeDtypeStruct((2, heads_local, NB, BLK), jnp.float32)
+    attended, stats = query_call(
+        query_fwd_kernel, valid_q, queries, g, keys, values, kv_from, [], heads_local, n_levels,
+        [head_block(0), stats_block(heads_local)], [flat, stats_shape], "query_forward",
+    )
+    (query_grad,) = query_call(
+        query_bwd_kernel, valid_q, queries, g, keys, values, kv_from, [stats], heads_local,
+        n_levels, [head_block(0)], [flat], "query_backward",
     )
     output = jnp.dot(
         lax.all_gather(attended, "head", axis=1, tiled=True),

time: 163 us -> 165 us (1.012); the launches traced: 162 us -> 162 us
  waiting for transfers between devices: 52.3 us -> 45.4 us
  Pallas kernels: 25.8 us -> 30.4 us
  local copies, waits for them, and re-layouts: 14.9 us -> 18.5 us
    ppermute x12, waiting for transfers between devices: 51.6 us -> 44.7 us  [passed_along(): return lax.ppermute(block, axis, route)]
    pallas_call x1 -> x2, Pallas kernels: 15.2 us -> 19.8 us  [query_call(): pl.pallas_call(functools.partial(kernel, n_levels), grid_spec=grid_spec,...]
    ppermute x12, starting transfers between devices: 42.6 us -> 40.7 us  [passed_along(): return lax.ppermute(block, axis, route)]
    unnamed x18 -> x20, local copies, waits for them, and re-layouts: 5.24 us -> 7.08 us
    all_to_all x1, local copies, waits for them, and re-layouts: 2.37 us -> 4.13 us  [local(): weight_cols = lax.all_to_all(out_weight, 'head', 1, 0, tiled=True)]
  transfers between devices with their start and end apart: 15 -> 15, of which waited for: 8 -> 3; matrix products, arithmetic and copies ran while one was open for 11% -> 13% of each run, Pallas kernels for 7% -> 12%
where the time goes in v7:
time: 165 us; the launch traced here: 162 us
  waiting for transfers between devices  45.4 us (28%)
  starting transfers between devices  45.3 us (27%)
  Pallas kernels  30.4 us (18%)
  local copies, waits for them, and re-layouts  18.5 us (11%)
  between operations  14.4 us (9%)
  matrix products  7.94 us (5%)
    ppermute x12, waiting for transfers between devices, passed_along(): return lax.ppermute(block, axis, route)  44.7 us
    ppermute x12, starting transfers between devices, passed_along(): return lax.ppermute(block, axis, route)  40.7 us
    pallas_call x2, Pallas kernels, query_call(): pl.pallas_call(functools.partial(kernel, n_levels), grid_spec=grid_spec,...  19.8 us
    pallas_call x1, Pallas kernels, key_call(): pl.pallas_call(functools.partial(key_kernel, n_levels), grid_spec=grid_sp...  10.6 us
    unnamed x20, local copies, waits for them, and re-layouts  7.08 us
    all_to_all x1, starting transfers between devices, local(): weight_cols = lax.all_to_all(out_weight, 'head', 1, 0, tiled=True)  4.59 us
    dot_general x1, matrix products, local(): lax.dot_general(lax.all_gather(d_out, 'head', axis=1, tiled=True), out_we...  4.3 us
    all_to_all x1, local copies, waits for them, and re-layouts, local(): weight_cols = lax.all_to_all(out_weight, 'head', 1, 0, tiled=True)  4.13 us
  transfers between devices with their start and end apart: 15, of which 3 were waited for; matrix products, arithmetic and copies ran while one was open for 13% of the time, Pallas kernels for 12%

profile of v7, /device:TPU:0, one launch (start us, length us, event | category | flops | bytes accessed | tf_op | source)
XLA Modules:
  0.0 162.2 jit_solution(3770498378945331135)
XLA Ops:
  7.2 0.0 all-gather.3.cloned.1.call-start
  7.2 0.7 all-gather.3.cloned.1.call-update
  7.9 1.9 %constant_dynamic-update-slice_fusion.1 = bf16[1024,512]{1,0:T(8,128)(2,1)} fusion(bf16[512,512]{1,0:T(8,128)(2,1)} %k_ref.5), kind=kLoop, calls=%fused_computation.15 | loop fusion | bytes 1048576
  9.8 1.9 %constant_dynamic-update-slice_fusion = bf16[1024,512]{1,0:T(8,128)(2,1)} fusion(bf16[1024,512]{1,0:T(8,128)(2,1)} %constant_dynamic-update-slice_fusion.1, bf16[512,512]{1,0:T(8,128)(2,1)} %v_ref.5), kind=kLoop, calls=%fused_computation.14 | loop fusion | bytes 1048576 | tf_op jit(solution)/shard_map/concatenate | solution.py:227
  11.7 4.9 %collective-permute-start = (bf16[1024,512]{1,0:T(8,128)(2,1)}, bf16[1024,512]{1,0:T(8,128)(2,1)S(1)}, u32[]{:S(2)}, u32[]{:S(2)}) collective-permute-start(bf16[1024,512]{1,0:T(8,128)(2,1)} %constant_dynamic-update-slice_fusion), channel_id=1, source_target_pairs={{0,4},{4,8},{8,12},{12,16},{16,20},{20,24},{24,28},{1,5},{5,9},{9,... | collective-permute-start | bytes 3145736 | tf_op jit(solution)/shard_map/ppermute | solution.py:23
  16.6 3.5 %collective-permute-start.1 = (bf16[1024,512]{1,0:T(8,128)(2,1)}, bf16[1024,512]{1,0:T(8,128)(2,1)S(1)}, u32[]{:S(2)}, u32[]{:S(2)}) collective-permute-start(bf16[1024,512]{1,0:T(8,128)(2,1)} %constant_dynamic-update-slice_fusion), channel_id=1, source_target_pairs={{0,8},{4,12},{8,16},{12,20},{16,24},{20,28},{1,9},{5,13},{9,17},{1... | collective-permute-start | bytes 3145736 | tf_op jit(solution)/shard_map/ppermute | solution.py:23
  20.1 1.3 collective-permute-start.3
  21.4 1.3 collective-permute-start.4
  22.7 1.3 collective-permute-start.5
  24.0 4.0 %copy.17 = bf16[512,2048]{0,1:T(8,128)(2,1)} copy(bf16[512,2048]{1,0:T(8,128)(2,1)} %param.12) | data formatting | bytes 4194304 | tf_op args[3]
  28.0 4.6 %all-to-all-start = ((bf16[512,4,512]{0,2,1:T(8,128)(2,1)}), bf16[512,4,512]{0,2,1:T(8,128)(2,1)}, u32[]{:S(2)}, u32[]{:S(2)}) async-start(bf16[512,4,512]{0,2,1:T(8,128)(2,1)} %bitcast.31), calls=%async_computation | async-start | bytes 4194304 | tf_op jit(solution)/shard_map/all_to_all | solution.py:239
  32.6 0.0 all-gather.5.cloned.1.call-start
  32.7 0.0 copy-done.8
  32.7 0.6 gather_fusion.5
  33.4 0.6 gather_fusion.4
  34.0 0.6 gather_fusion.3
  34.7 0.0 copy-done
  34.7 0.6 gather_fusion.2
  35.4 0.1 and_bitcast_fusion.6
  35.5 0.1 constant_dynamic-slice_fusion
  35.6 0.1 copy.15
  35.7 0.6 reshape.55.valid_ref
  36.3 0.0 collective-permute-done.3.rest_0_
  36.3 20.7 %collective-permute-start.2 = (bf16[1024,512]{1,0:T(8,128)(2,1)}, bf16[1024,512]{1,0:T(8,128)(2,1)S(1)}, u32[]{:S(2)}, u32[]{:S(2)}) collective-permute-start(bf16[1024,512]{1,0:T(8,128)(2,1)} %constant_dynamic-update-slice_fusion), channel_id=1, source_target_pairs={{0,16},{4,20},{8,24},{12,28},{1,17},{5,21},{9,25},{13,29},{2,18},{... | collective-permute-start | bytes 3145736 | tf_op jit(solution)/shard_map/ppermute | solution.py:23
  57.0 0.6 gather_fusion.1
  57.6 4.3 %convolution_convert_fusion.1.g_ref = bf16[512,512]{1,0:T(8,128)(2,1)} fusion(bf16[512,2048]{1,0:T(8,128)(2,1)} %all-gather.3.cloned.1.call-done, bf16[512,2048]{1,0:T(8,128)(2,1)} %param.12), kind=kOutput, calls=%fused_computation.7 | convolution fusion | flops 1074003968 | bytes 4718592 | tf_op jit(solution)/shard_map/dot_general | solution.py:231
  61.9 0.0 collective-permute-done.4.rest_3_
  61.9 1.3 collective-permute-start.6
  63.2 9.7 %collective-permute-done.5.rest_6_ = bf16[512,512]{1,0:T(8,128)(2,1)} collective-permute-done((bf16[512,512]{1,0:T(8,128)(2,1)}, bf16[512,512]{1,0:T(8,128)(2,1)}, u32[]{:S(2)}, u32[]{:S(2)}) %collective-permute-start.5) | collective-permute-done | bytes 524320 | tf_op jit(solution)/shard_map/ppermute | solution.py:23
  72.9 1.3 collective-permute-start.7
  74.2 0.0 collective-permute-done.rest_0_.rest_1_
  74.2 0.0 copy-start.1
  74.2 1.3 collective-permute-start.8
  75.5 0.6 gather_fusion
  76.2 0.1 copy.16
  76.3 0.6 reshape.56.valid_ref
  76.9 0.0 all-to-all-done
  76.9 4.1 %copy.18 = bf16[4,512,512]{2,1,0:T(8,128)(2,1)} copy(bf16[4,512,512]{1,2,0:T(8,128)(2,1)} %bitcast.13) | data formatting | bytes 4194304 | tf_op jit(solution)/shard_map/all_to_all | solution.py:239
  81.1 0.0 copy-done.1
  81.1 0.0 collective-permute-done.1.rest_2_.rest_3_
  81.1 0.0 collective-permute-done.2.rest_4_.rest_5_
  81.1 0.0 copy-start.3
  81.1 0.0 collective-permute-done.6.rest_1_
  81.1 12.5 %collective-permute-done.7.rest_4_ = bf16[512,512]{1,0:T(8,128)(2,1)} collective-permute-done((bf16[512,512]{1,0:T(8,128)(2,1)}, bf16[512,512]{1,0:T(8,128)(2,1)}, u32[]{:S(2)}, u32[]{:S(2)}) %collective-permute-start.7) | collective-permute-done | bytes 524320 | tf_op jit(solution)/shard_map/ppermute | solution.py:23
  93.6 22.5 %collective-permute-done.8.rest_7_ = bf16[512,512]{1,0:T(8,128)(2,1)} collective-permute-done((bf16[512,512]{1,0:T(8,128)(2,1)}, bf16[512,512]{1,0:T(8,128)(2,1)}, u32[]{:S(2)}, u32[]{:S(2)}) %collective-permute-start.8) | collective-permute-done | bytes 524320 | tf_op jit(solution)/shard_map/ppermute | solution.py:23
  116.1 0.0 copy-done.2
  116.1 0.0 copy-done.3
  116.1 11.1 %query_forward.1 = (bf16[512,512]{1,0:T(8,128)(2,1)}, f32[2,4,4,128]{3,2,1,0:T(4,128)}) custom-call(s32[28]{0:T(128)} %reshape.55.valid_ref, bf16[512,512]{1,0:T(8,128)(2,1)} %q_ref.5, bf16[512,512]{1,0:T(8,128)(2,1)} %convolution_convert_fusion.1.g_ref, bf16[512,512]{1,0:T(8,128)(2,1)} %k_ref.5, bf16[512,512]{1,0:T(8,128)(2,1)} %v_ref.5, ...), custom_call_target="tpu_custom_call" | custom-call | tf_op jit(solution)/shard_map/query_forward/pallas_call | solution.py:165
  127.2 0.0 all-gather.5.cloned.1.call-update
  127.2 1.3 collective-permute-start.10
  128.5 1.3 collective-permute-start.11
  129.8 1.3 collective-permute-start.9
  131.1 8.7 %query_backward.1 = bf16[512,512]{1,0:T(8,128)(2,1)} custom-call(s32[28]{0:T(128)} %reshape.55.valid_ref, bf16[512,512]{1,0:T(8,128)(2,1)} %q_ref.5, bf16[512,512]{1,0:T(8,128)(2,1)} %convolution_convert_fusion.1.g_ref, bf16[512,512]{1,0:T(8,128)(2,1)} %k_ref.5, bf16[512,512]{1,0:T(8,128)(2,1)} %v_ref.5, f32[2,4,4,128]{3,2,1,0:T(4,128)} %get-tuple-element.27.st_ref, ...), custom_call_target="tpu_custom_call" | custom-call | tf_op jit(solution)/shard_map/query_backward/pallas_call | solution.py:165
  139.8 0.0 collective-permute-done.10.rest_5_
  139.8 0.0 copy-start.5
  139.8 0.0 collective-permute-done.11.rest_8_
  139.8 0.0 copy-start.6
  139.9 0.0 collective-permute-done.9.rest_2_
  139.9 0.6 copy-done.5
  140.4 0.0 copy-done.6
  140.4 0.6 copy-done.7
  141.0 10.6 %key_side.1 = (bf16[512,512]{1,0:T(8,128)(2,1)}, bf16[512,512]{1,0:T(8,128)(2,1)}) custom-call(s32[28]{0:T(128)} %reshape.56.valid_ref, bf16[512,512]{1,0:T(8,128)(2,1)} %k_ref.5, bf16[512,512]{1,0:T(8,128)(2,1)} %v_ref.5, bf16[512,512]{1,0:T(8,128)(2,1)} %q_ref.5, bf16[512,512]{1,0:T(8,128)(2,1)} %convolution_convert_fusion.1.g_ref, ...), custom_call_target="tpu_custom_call" | custom-call | tf_op jit(solution)/shard_map/key_side/pallas_call | solution.py:186
  151.7 0.0 all-gather.5.cloned.1.call-done
  151.7 3.6 %convolution_convert_fusion = bf16[512,512]{1,0:T(8,128)(2,1)} fusion(bf16[512,2048]{1,0:T(8,128)(2,1)} %all-gather.5.cloned.1.call-done, bf16[2048,512]{1,0:T(8,128)(2,1)S(1)} %bitcast.32), kind=kOutput, calls=%fused_computation.6 | convolution fusion | flops 1074003968 | bytes 4718592 | tf_op jit(solution)/shard_map/dot_general | solution.py:254
  (28 shorter events, 0.2 us)
Async XLA Ops:
  7.2 50.5 %all-gather.3.cloned.1.call-start = ((), (), s32[]{:S(2)}) async-start(), calls=%async_computation.1 | async-start | bytes 2621440 | tf_op jit(solution)/shard_map/all_gather | solution.py:232
  11.7 62.4 %collective-permute-start = (bf16[1024,512]{1,0:T(8,128)(2,1)}, bf16[1024,512]{1,0:T(8,128)(2,1)S(1)}, u32[]{:S(2)}, u32[]{:S(2)}) collective-permute-start(bf16[1024,512]{1,0:T(8,128)(2,1)} %constant_dynamic-update-slice_fusion), channel_id=1, source_target_pairs={{0,4},{4,8},{8,12},{12,16},{16,20},{20,24},{24,28},{1,5},{5,9},{9,... | collective-permute-start | bytes 3145736 | tf_op jit(solution)/shard_map/ppermute | solution.py:23
  16.6 64.5 %collective-permute-start.1 = (bf16[1024,512]{1,0:T(8,128)(2,1)}, bf16[1024,512]{1,0:T(8,128)(2,1)S(1)}, u32[]{:S(2)}, u32[]{:S(2)}) collective-permute-start(bf16[1024,512]{1,0:T(8,128)(2,1)} %constant_dynamic-update-slice_fusion), channel_id=1, source_target_pairs={{0,8},{4,12},{8,16},{12,20},{16,24},{20,28},{1,9},{5,13},{9,17},{1... | collective-permute-start | bytes 3145736 | tf_op jit(solution)/shard_map/ppermute | solution.py:23
  20.1 16.2 %collective-permute-start.3 = (bf16[512,512]{1,0:T(8,128)(2,1)}, bf16[512,512]{1,0:T(8,128)(2,1)}, u32[]{:S(2)}, u32[]{:S(2)}) collective-permute-start(bf16[512,512]{1,0:T(8,128)(2,1)} %q_ref.5), channel_id=1, source_target_pairs={{4,0},{8,4},{12,8},{16,12},{20,16},{24,20},{28,24},{5,1},{9,5},{13... | collective-permute-start | bytes 1572872 | tf_op jit(solution)/shard_map/ppermute | solution.py:23
  21.4 40.5 %collective-permute-start.4 = (bf16[512,512]{1,0:T(8,128)(2,1)}, bf16[512,512]{1,0:T(8,128)(2,1)}, u32[]{:S(2)}, u32[]{:S(2)}) collective-permute-start(bf16[512,512]{1,0:T(8,128)(2,1)} %q_ref.5), channel_id=1, source_target_pairs={{8,0},{12,4},{16,8},{20,12},{24,16},{28,20},{9,1},{13,5},{17,9},{2... | collective-permute-start | bytes 1572872 | tf_op jit(solution)/shard_map/ppermute | solution.py:23
  22.7 50.2 %collective-permute-start.5 = (bf16[512,512]{1,0:T(8,128)(2,1)}, bf16[512,512]{1,0:T(8,128)(2,1)}, u32[]{:S(2)}, u32[]{:S(2)}) collective-permute-start(bf16[512,512]{1,0:T(8,128)(2,1)} %q_ref.5), channel_id=1, source_target_pairs={{16,0},{20,4},{24,8},{28,12},{17,1},{21,5},{25,9},{29,13},{18,2},{... | collective-permute-start | bytes 1572872 | tf_op jit(solution)/shard_map/ppermute | solution.py:23
  28.0 4.7 %copy-start.8 = (s32[32,5]{0,1:T(8,128)S(1)}, s32[32,5]{0,1:T(8,128)}, u32[]{:S(2)}) copy-start(s32[32,5]{0,1:T(8,128)} %param.15) | copy-start | bytes 1924
  28.0 6.7 %copy-start = (s32[32]{0:T(128)S(1)}, s32[32]{0:T(128)}, u32[]{:S(2)}) copy-start(s32[32]{0:T(128)} %param.14) | copy-start | bytes 388
  28.0 48.9 %all-to-all-start = ((bf16[512,4,512]{0,2,1:T(8,128)(2,1)}), bf16[512,4,512]{0,2,1:T(8,128)(2,1)}, u32[]{:S(2)}, u32[]{:S(2)}) async-start(bf16[512,4,512]{0,2,1:T(8,128)(2,1)} %bitcast.31), calls=%async_computation | async-start | bytes 4194304 | tf_op jit(solution)/shard_map/all_to_all | solution.py:239
  32.6 119.1 %all-gather.5.cloned.1.call-start = ((), (), s32[]{:S(2)}) async-start(), calls=%async_computation.2 | async-start | bytes 2621440 | tf_op jit(solution)/shard_map/all_gather | solution.py:255
  36.3 44.8 %collective-permute-start.2 = (bf16[1024,512]{1,0:T(8,128)(2,1)}, bf16[1024,512]{1,0:T(8,128)(2,1)S(1)}, u32[]{:S(2)}, u32[]{:S(2)}) collective-permute-start(bf16[1024,512]{1,0:T(8,128)(2,1)} %constant_dynamic-update-slice_fusion), channel_id=1, source_target_pairs={{0,16},{4,20},{8,24},{12,28},{1,17},{5,21},{9,25},{13,29},{2,18},{... | collective-permute-start | bytes 3145736 | tf_op jit(solution)/shard_map/ppermute | solution.py:23
  61.9 19.2 %collective-permute-start.6 = (bf16[512,512]{1,0:T(8,128)(2,1)}, bf16[512,512]{1,0:T(8,128)(2,1)}, u32[]{:S(2)}, u32[]{:S(2)}) collective-permute-start(bf16[512,512]{1,0:T(8,128)(2,1)} %convolution_convert_fusion.1.g_ref), channel_id=1, source_target_pairs={{4,0},{8,4},{12,8},{16,12},{20,16},{24,20},{28,24},{5,1},{9,5},{13... | collective-permute-start | bytes 1572872 | tf_op jit(solution)/shard_map/ppermute | solution.py:23
  72.9 20.7 %collective-permute-start.7 = (bf16[512,512]{1,0:T(8,128)(2,1)}, bf16[512,512]{1,0:T(8,128)(2,1)}, u32[]{:S(2)}, u32[]{:S(2)}) collective-permute-start(bf16[512,512]{1,0:T(8,128)(2,1)} %convolution_convert_fusion.1.g_ref), channel_id=1, source_target_pairs={{8,0},{12,4},{16,8},{20,12},{24,16},{28,20},{9,1},{13,5},{17,9},{2... | collective-permute-start | bytes 1572872 | tf_op jit(solution)/shard_map/ppermute | solution.py:23
  74.2 6.9 %copy-start.1 = (bf16[1024,512]{1,0:T(8,128)(2,1)}, bf16[1024,512]{1,0:T(8,128)(2,1)S(1)}, u32[]{:S(2)}) copy-start(bf16[1024,512]{1,0:T(8,128)(2,1)S(1)} %collective-permute-done.rest_0_.rest_1_) | copy-start | bytes 3145732
  74.2 41.9 %collective-permute-start.8 = (bf16[512,512]{1,0:T(8,128)(2,1)}, bf16[512,512]{1,0:T(8,128)(2,1)}, u32[]{:S(2)}, u32[]{:S(2)}) collective-permute-start(bf16[512,512]{1,0:T(8,128)(2,1)} %convolution_convert_fusion.1.g_ref), channel_id=1, source_target_pairs={{16,0},{20,4},{24,8},{28,12},{17,1},{21,5},{25,9},{29,13},{18,2},{... | collective-permute-start | bytes 1572872 | tf_op jit(solution)/shard_map/ppermute | solution.py:23
  81.1 35.0 %copy-start.2 = (bf16[1024,512]{1,0:T(8,128)(2,1)}, bf16[1024,512]{1,0:T(8,128)(2,1)S(1)}, u32[]{:S(2)}) copy-start(bf16[1024,512]{1,0:T(8,128)(2,1)S(1)} %collective-permute-done.1.rest_2_.rest_3_) | copy-start | bytes 3145732
  81.1 35.0 %copy-start.3 = (bf16[1024,512]{1,0:T(8,128)(2,1)}, bf16[1024,512]{1,0:T(8,128)(2,1)S(1)}, u32[]{:S(2)}) copy-start(bf16[1024,512]{1,0:T(8,128)(2,1)S(1)} %collective-permute-done.2.rest_4_.rest_5_) | copy-start | bytes 3145732
  127.2 12.6 %collective-permute-start.10 = (f32[2,4,4,128]{3,2,1,0:T(4,128)}, f32[2,4,4,128]{3,2,1,0:T(4,128)S(1)}, u32[]{:S(2)}, u32[]{:S(2)}) collective-permute-start(f32[2,4,4,128]{3,2,1,0:T(4,128)} %get-tuple-element.27.st_ref), channel_id=1, source_target_pairs={{8,0},{12,4},{16,8},{20,12},{24,16},{28,20},{9,1},{13,5},{17,9},{2... | collective-permute-start | bytes 49160 | tf_op jit(solution)/shard_map/ppermute | solution.py:23
  128.5 11.3 %collective-permute-start.11 = (f32[2,4,4,128]{3,2,1,0:T(4,128)}, f32[2,4,4,128]{3,2,1,0:T(4,128)S(1)}, u32[]{:S(2)}, u32[]{:S(2)}) collective-permute-start(f32[2,4,4,128]{3,2,1,0:T(4,128)} %get-tuple-element.27.st_ref), channel_id=1, source_target_pairs={{16,0},{20,4},{24,8},{28,12},{17,1},{21,5},{25,9},{29,13},{18,2},{... | collective-permute-start | bytes 49160 | tf_op jit(solution)/shard_map/ppermute | solution.py:23
  129.8 10.0 %collective-permute-start.9 = (f32[2,4,4,128]{3,2,1,0:T(4,128)}, f32[2,4,4,128]{3,2,1,0:T(4,128)S(1)}, u32[]{:S(2)}, u32[]{:S(2)}) collective-permute-start(f32[2,4,4,128]{3,2,1,0:T(4,128)} %get-tuple-element.27.st_ref), channel_id=1, source_target_pairs={{4,0},{8,4},{12,8},{16,12},{20,16},{24,20},{28,24},{5,1},{9,5},{13... | collective-permute-start | bytes 49160 | tf_op jit(solution)/shard_map/ppermute | solution.py:23
  139.8 11.9 %copy-start.4 = (bf16[4,512,512]{2,1,0:T(8,128)(2,1)S(1)}, bf16[4,512,512]{2,1,0:T(8,128)(2,1)}, u32[]{:S(2)}) copy-start(bf16[4,512,512]{2,1,0:T(8,128)(2,1)} %copy.18) | copy-start | bytes 6291460
  139.8 0.6 copy-start.5
  139.8 0.6 copy-start.6
  140.4 0.6 copy-start.7
Sparse Core Ops, SparseCore 0:
  9.6 25.2 all-gather.2
  127.3 19.8 all-gather.4

commit v8 on v6

--- a/solution.py
+++ b/solution.py
@@ -38,14 +38,48 @@
     return jnp.sum(jnp.where(eye, col, 0.0), axis=0, keepdims=True)
 
 
-def candidate_mask(valid_ref, base, n_cand, diag):
-    width = n_cand * BLK
+SLOTS = 3
+
+
+def candidate_mask(oks, diag):
+    width = (1 + len(oks)) * BLK
     col = lax.broadcasted_iota(jnp.int32, (BLK, width), 1)
-    allowed = (col < BLK) & diag
+    allowed = (col < BLK) & diag[:, :width]
+    for ci, ok in enumerate(oks, start=1):
+        inside = (col >= ci * BLK) & (col < (ci + 1) * BLK)
+        allowed = allowed | (inside & ok)
+    return allowed
+
+
+def compacted(valid_ref, base, n_cand):
+    oks, ranks = [], []
+    count = jnp.int32(0)
     for ci in range(1, n_cand):
-        inside = (col >= ci * BLK) & (col < (ci + 1) * BLK)
-        allowed = allowed | (inside & (valid_ref[base + ci] != 0))
-    return allowed
+        ok = valid_ref[base + ci] != 0
+        oks.append(ok)
+        ranks.append(count)
+        count = count + ok.astype(jnp.int32)
+    return oks, ranks, count
+
+
+def pick(blocks, oks, ranks, slot):
+    out = jnp.zeros_like(blocks[0])
+    for block, ok, rank in zip(blocks, oks, ranks):
+        out = jnp.where(ok & (rank == slot), block, out)
+    return out
+
+
+def narrow_or_full(valid_ref, base, n_cand, body):
+    oks, ranks, count = compacted(valid_ref, base, n_cand)
+
+    @pl.when(count <= SLOTS)
+    def _():
+        body(lambda blocks: [pick(blocks, oks, ranks, p) for p in range(SLOTS)],
+             [count > p for p in range(SLOTS)])
+
+    @pl.when(count > SLOTS)
+    def _():
+        body(lambda blocks: blocks, oks)
 
 
 def query_kernel(n_levels, valid_ref, q_ref, g_ref, k_ref, v_ref, *rest):
@@ -60,30 +94,36 @@
     diag = col <= row
     for n in range(NB):
         rows = pl.ds(n * BLK, BLK)
-        qn = q_ref[rows, :]
-        gn = g_ref[rows, :]
         cands = [(k_ref, v_ref, n)]
         for o in range(1, WIN_MAX + 1):
             j = n - o
             cands.append((k_ref, v_ref, j) if j >= 0 else (kf[0], vf[0], NB + j))
         for mi in range(n_levels):
             cands.append((kf[mi], vf[mi], n))
-        kcat = jnp.concatenate([kr[pl.ds(j * BLK, BLK), :] for kr, _, j in cands], axis=0)
-        vcat = jnp.concatenate([vr[pl.ds(j * BLK, BLK), :] for _, vr, j in cands], axis=0)
-        allowed = candidate_mask(valid_ref, n * n_cand, n_cand, diag)
-        scores = jnp.where(allowed, dot_nt(qn, kcat) * scale, neg_large)
-        row_max = scores.max(axis=1, keepdims=True)
-        row_total = jnp.sum(jnp.exp(scores - row_max), axis=1, keepdims=True)
-        log_total = row_max + jnp.log(row_total)
-        probs = jnp.exp(scores - log_total)
-        att_b = dot_nn(probs.astype(jnp.bfloat16), vcat).astype(jnp.bfloat16)
-        att_ref[rows, :] = att_b
-        delta = jnp.sum(gn.astype(jnp.float32) * att_b.astype(jnp.float32), axis=1, keepdims=True)
-        d_prob = dot_nt(gn, vcat)
-        d_score = (probs * (d_prob - delta) * scale).astype(jnp.bfloat16)
-        dq_ref[rows, :] = dot_nn(d_score, kcat).astype(jnp.bfloat16)
-        st_ref[0, 0, pl.ds(n, 1), :] = col_to_row(log_total)
-        st_ref[1, 0, pl.ds(n, 1), :] = col_to_row(delta)
+
+        def body(select, oks, rows=rows, cands=cands, n=n):
+            qn = q_ref[rows, :]
+            gn = g_ref[rows, :]
+            ks = [kr[pl.ds(j * BLK, BLK), :] for kr, _, j in cands]
+            vs = [vr[pl.ds(j * BLK, BLK), :] for _, vr, j in cands]
+            kcat = jnp.concatenate([ks[0]] + select(ks[1:]), axis=0)
+            vcat = jnp.concatenate([vs[0]] + select(vs[1:]), axis=0)
+            allowed = candidate_mask(oks, diag)
+            scores = jnp.where(allowed, dot_nt(qn, kcat) * scale, neg_large)
+            row_max = scores.max(axis=1, keepdims=True)
+            row_total = jnp.sum(jnp.exp(scores - row_max), axis=1, keepdims=True)
+            log_total = row_max + jnp.log(row_total)
+            probs = jnp.exp(scores - log_total)
+            att_b = dot_nn(probs.astype(jnp.bfloat16), vcat).astype(jnp.bfloat16)
+            att_ref[rows, :] = att_b
+            delta = jnp.sum(gn.astype(jnp.float32) * att_b.astype(jnp.float32), axis=1, keepdims=True)
+            d_prob = dot_nt(gn, vcat)
+            d_score = (probs * (d_prob - delta) * scale).astype(jnp.bfloat16)
+            dq_ref[rows, :] = dot_nn(d_score, kcat).astype(jnp.bfloat16)
+            st_ref[0, 0, pl.ds(n, 1), :] = col_to_row(log_total)
+            st_ref[1, 0, pl.ds(n, 1), :] = col_to_row(delta)
+
+        narrow_or_full(valid_ref, n * n_cand, n_cand, body)
 
 
 def key_kernel(n_levels, valid_ref, k_ref, v_ref, q_ref, g_ref, st_ref, *rest):
@@ -99,25 +139,33 @@
     diag = row <= col
     for j in range(NB):
         rows = pl.ds(j * BLK, BLK)
-        kj = k_ref[rows, :]
-        vj = v_ref[rows, :]
         cands = [(q_ref, g_ref, st_ref, j)]
         for o in range(1, WIN_MAX + 1):
             i = j + o
             cands.append((q_ref, g_ref, st_ref, i) if i < NB else (qf[0], gf[0], sf[0], i - NB))
         for mi in range(n_levels):
             cands.append((qf[mi], gf[mi], sf[mi], j))
-        qcat = jnp.concatenate([qr[pl.ds(i * BLK, BLK), :] for qr, _, _, i in cands], axis=0)
-        gcat = jnp.concatenate([gr[pl.ds(i * BLK, BLK), :] for _, gr, _, i in cands], axis=0)
-        lse = jnp.concatenate([sr[0, 0, pl.ds(i, 1), :] for _, _, sr, i in cands], axis=1)
-        delta = jnp.concatenate([sr[1, 0, pl.ds(i, 1), :] for _, _, sr, i in cands], axis=1)
-        allowed = candidate_mask(valid_ref, j * n_cand, n_cand, diag)
-        scores = jnp.where(allowed, dot_nt(kj, qcat) * scale, neg_large)
-        probs = jnp.exp(scores - lse)
-        dv_ref[rows, :] = dot_nn(probs.astype(jnp.bfloat16), gcat).astype(jnp.bfloat16)
-        d_prob = dot_nt(vj, gcat)
-        d_score = (probs * (d_prob - delta) * scale).astype(jnp.bfloat16)
-        dk_ref[rows, :] = dot_nn(d_score, qcat).astype(jnp.bfloat16)
+
+        def body(select, oks, rows=rows, cands=cands):
+            kj = k_ref[rows, :]
+            vj = v_ref[rows, :]
+            qs = [qr[pl.ds(i * BLK, BLK), :] for qr, _, _, i in cands]
+            gs = [gr[pl.ds(i * BLK, BLK), :] for _, gr, _, i in cands]
+            ls = [sr[0, 0, pl.ds(i, 1), :] for _, _, sr, i in cands]
+            ds = [sr[1, 0, pl.ds(i, 1), :] for _, _, sr, i in cands]
+            qcat = jnp.concatenate([qs[0]] + select(qs[1:]), axis=0)
+            gcat = jnp.concatenate([gs[0]] + select(gs[1:]), axis=0)
+            lse = jnp.concatenate([ls[0]] + select(ls[1:]), axis=1)
+            delta = jnp.concatenate([ds[0]] + select(ds[1:]), axis=1)
+            allowed = candidate_mask(oks, diag)
+            scores = jnp.where(allowed, dot_nt(kj, qcat) * scale, neg_large)
+            probs = jnp.exp(scores - lse)
+            dv_ref[rows, :] = dot_nn(probs.astype(jnp.bfloat16), gcat).astype(jnp.bfloat16)
+            d_prob = dot_nt(vj, gcat)
+            d_score = (probs * (d_prob - delta) * scale).astype(jnp.bfloat16)
+            dk_ref[rows, :] = dot_nn(d_score, qcat).astype(jnp.bfloat16)
+
+        narrow_or_full(valid_ref, j * n_cand, n_cand, body)
 
 
 def head_block(part):

time: 163 us -> 164 us (level)
  no operation moved by 1% of the time
where the time goes in v8:
time: 164 us; the launch traced here: 163 us
  waiting for transfers between devices  52.1 us (32%)
  starting transfers between devices  46.6 us (28%)
  Pallas kernels  27.2 us (17%)
  local copies, waits for them, and re-layouts  14.9 us (9%)
  between operations  14.3 us (9%)
  matrix products  7.93 us (5%)
    ppermute x12, waiting for transfers between devices, passed_along(): return lax.ppermute(block, axis, route)  51.4 us
    ppermute x12, starting transfers between devices, passed_along(): return lax.ppermute(block, axis, route)  42.8 us
    pallas_call x1, Pallas kernels, query_call(): pl.pallas_call(functools.partial(query_kernel, n_levels), grid_spec=grid_...  15.2 us
    pallas_call x1, Pallas kernels, key_call(): pl.pallas_call(functools.partial(key_kernel, n_levels), grid_spec=grid_sp...  12 us
    unnamed x18, local copies, waits for them, and re-layouts  5.24 us
    dot_general x1, matrix products, local(): lax.dot_general(lax.all_gather(d_out, 'head', axis=1, tiled=True), out_we...  4.3 us
    all_to_all x1, starting transfers between devices, local(): weight_cols = lax.all_to_all(out_weight, 'head', 1, 0, tiled=True)  3.74 us
    dot_general x1, matrix products, local(): jnp.dot(lax.all_gather(attended, 'head', axis=1, tiled=True), weight_cols...  3.63 us
  transfers between devices with their start and end apart: 15, of which 8 were waited for; matrix products, arithmetic and copies ran while one was open for 11% of the time, Pallas kernels for 7%

profile of v8, /device:TPU:0, one launch (start us, length us, event | category | flops | bytes accessed | tf_op | source)
XLA Modules:
  0.0 163.2 jit_solution(18040698179719917792)
XLA Ops:
  7.2 0.0 copy-start.2
  7.2 0.0 all-gather.3.cloned.1.call-start
  7.2 0.7 all-gather.3.cloned.1.call-update
  7.9 1.9 %constant_dynamic-update-slice_fusion.1 = bf16[1024,512]{1,0:T(8,128)(2,1)} fusion(bf16[512,512]{1,0:T(8,128)(2,1)} %k_ref.3), kind=kLoop, calls=%fused_computation.15 | loop fusion | bytes 1048576
  9.8 1.9 %constant_dynamic-update-slice_fusion = bf16[1024,512]{1,0:T(8,128)(2,1)} fusion(bf16[1024,512]{1,0:T(8,128)(2,1)} %constant_dynamic-update-slice_fusion.1, bf16[512,512]{1,0:T(8,128)(2,1)} %v_ref.3), kind=kLoop, calls=%fused_computation.14 | loop fusion | bytes 1048576 | tf_op jit(solution)/shard_map/concatenate | solution.py:258
  11.7 4.9 %collective-permute-start = (bf16[1024,512]{1,0:T(8,128)(2,1)}, bf16[1024,512]{1,0:T(8,128)(2,1)S(1)}, u32[]{:S(2)}, u32[]{:S(2)}) collective-permute-start(bf16[1024,512]{1,0:T(8,128)(2,1)} %constant_dynamic-update-slice_fusion), channel_id=1, source_target_pairs={{0,4},{4,8},{8,12},{12,16},{16,20},{20,24},{24,28},{1,5},{5,9},{9,... | collective-permute-start | bytes 3145736 | tf_op jit(solution)/shard_map/ppermute | solution.py:23
  16.6 4.5 %collective-permute-start.1 = (bf16[1024,512]{1,0:T(8,128)(2,1)}, bf16[1024,512]{1,0:T(8,128)(2,1)}, u32[]{:S(2)}, u32[]{:S(2)}) collective-permute-start(bf16[1024,512]{1,0:T(8,128)(2,1)} %constant_dynamic-update-slice_fusion), channel_id=1, source_target_pairs={{0,8},{4,12},{8,16},{12,20},{16,24},{20,28},{1,9},{5,13},{9,17},{1... | collective-permute-start | bytes 3145736 | tf_op jit(solution)/shard_map/ppermute | solution.py:23
  21.1 1.3 collective-permute-start.3
  22.4 1.3 collective-permute-start.4
  23.7 1.3 collective-permute-start.5
  25.0 0.0 copy-done.2
  25.0 2.5 %copy.17 = bf16[512,2048]{0,1:T(8,128)(2,1)} copy(bf16[512,2048]{1,0:T(8,128)(2,1)S(1)} %copy-done.2) | data formatting | bytes 4194304 | tf_op args[3]
  27.5 0.0 copy-start.7
  27.5 3.7 %all-to-all-start = ((bf16[512,4,512]{0,2,1:T(8,128)(2,1)}), bf16[512,4,512]{0,2,1:T(8,128)(2,1)S(1)}, u32[]{:S(2)}, u32[]{:S(2)}) async-start(bf16[512,4,512]{0,2,1:T(8,128)(2,1)} %bitcast.32), calls=%async_computation | async-start | bytes 4194304 | tf_op jit(solution)/shard_map/all_to_all | solution.py:270
  31.3 0.0 all-gather.5.cloned.1.call-start
  31.3 0.0 copy-done.7
  31.4 0.6 gather_fusion.5
  32.0 0.6 gather_fusion.4
  32.7 0.6 gather_fusion.3
  33.3 0.0 copy-done
  33.3 0.6 gather_fusion.2
  34.0 0.1 and_bitcast_fusion.6
  34.1 0.1 constant_dynamic-slice_fusion
  34.3 0.1 copy.15
  34.4 0.6 reshape.55.valid_ref
  34.9 1.5 collective-permute-done.3.rest_0_
  36.4 21.5 %collective-permute-start.2 = (bf16[1024,512]{1,0:T(8,128)(2,1)}, bf16[1024,512]{1,0:T(8,128)(2,1)}, u32[]{:S(2)}, u32[]{:S(2)}) collective-permute-start(bf16[1024,512]{1,0:T(8,128)(2,1)} %constant_dynamic-update-slice_fusion), channel_id=1, source_target_pairs={{0,16},{4,20},{8,24},{12,28},{1,17},{5,21},{9,25},{13,29},{2,18},{... | collective-permute-start | bytes 3145736 | tf_op jit(solution)/shard_map/ppermute | solution.py:23
  57.9 0.6 gather_fusion.1
  58.5 0.0 all-gather.3.cloned.1.call-done
  58.5 4.3 %convolution_convert_fusion.1.g_ref = bf16[512,512]{1,0:T(8,128)(2,1)} fusion(bf16[512,2048]{1,0:T(8,128)(2,1)} %all-gather.3.cloned.1.call-done, bf16[512,2048]{1,0:T(8,128)(2,1)} %param.12), kind=kOutput, calls=%fused_computation.7 | convolution fusion | flops 1074003968 | bytes 4718592 | tf_op jit(solution)/shard_map/dot_general | solution.py:262
  62.8 0.0 collective-permute-done.4.rest_3_
  62.8 1.3 collective-permute-start.6
  64.1 8.8 %collective-permute-done.5.rest_6_ = bf16[512,512]{1,0:T(8,128)(2,1)} collective-permute-done((bf16[512,512]{1,0:T(8,128)(2,1)}, bf16[512,512]{1,0:T(8,128)(2,1)}, u32[]{:S(2)}, u32[]{:S(2)}) %collective-permute-start.5) | collective-permute-done | bytes 524320 | tf_op jit(solution)/shard_map/ppermute | solution.py:23
  72.9 1.3 collective-permute-start.7
  74.2 0.0 collective-permute-done.rest_0_.rest_1_
  74.2 0.0 copy-start.1
  74.2 1.3 collective-permute-start.8
  75.5 0.6 gather_fusion
  76.2 0.1 copy.16
  76.3 0.6 reshape.56.valid_ref
  76.9 0.0 all-to-all-done
  76.9 2.4 %copy.18 = bf16[4,512,512]{2,1,0:T(8,128)(2,1)} copy(bf16[4,512,512]{1,2,0:T(8,128)(2,1)S(1)} %bitcast.31) | data formatting | bytes 4194304 | tf_op jit(solution)/shard_map/all_to_all | solution.py:270
  79.3 0.0 copy-done.1
  79.3 0.0 collective-permute-done.1.rest_2_.rest_3_
  79.3 0.5 collective-permute-done.2.rest_4_.rest_5_
  79.8 0.0 collective-permute-done.6.rest_1_
  79.8 13.8 %collective-permute-done.7.rest_4_ = bf16[512,512]{1,0:T(8,128)(2,1)} collective-permute-done((bf16[512,512]{1,0:T(8,128)(2,1)}, bf16[512,512]{1,0:T(8,128)(2,1)}, u32[]{:S(2)}, u32[]{:S(2)}) %collective-permute-start.7) | collective-permute-done | bytes 524320 | tf_op jit(solution)/shard_map/ppermute | solution.py:23
  93.6 22.5 %collective-permute-done.8.rest_7_ = bf16[512,512]{1,0:T(8,128)(2,1)} collective-permute-done((bf16[512,512]{1,0:T(8,128)(2,1)}, bf16[512,512]{1,0:T(8,128)(2,1)}, u32[]{:S(2)}, u32[]{:S(2)}) %collective-permute-start.8) | collective-permute-done | bytes 524320 | tf_op jit(solution)/shard_map/ppermute | solution.py:23
  116.1 15.2 %query_side.1 = (bf16[512,512]{1,0:T(8,128)(2,1)}, bf16[512,512]{1,0:T(8,128)(2,1)}, f32[2,4,4,128]{3,2,1,0:T(4,128)}) custom-call(s32[28]{0:T(128)} %reshape.55.valid_ref, bf16[512,512]{1,0:T(8,128)(2,1)} %q_ref.3, bf16[512,512]{1,0:T(8,128)(2,1)} %convolution_convert_fusion.1.g_ref, bf16[512,512]{1,0:T(8,128)(2,1)} %k_ref.3, bf16[512,512]{1,0:T(8,128)(2,1)} %v_ref.3, ...), custom_call_target="tpu_custom_call" | custom-call | tf_op jit(solution)/shard_map/query_side/pallas_call | solution.py:192
  131.3 0.0 all-gather.5.cloned.1.call-update
  131.3 0.0 copy-start.3
  131.3 1.4 collective-permute-start.10
  132.7 1.3 collective-permute-start.11
  134.0 1.5 collective-permute-start.9
  135.5 1.8 %collective-permute-done.10.rest_5_ = f32[2,4,4,128]{3,2,1,0:T(4,128)S(1)} collective-permute-done((f32[2,4,4,128]{3,2,1,0:T(4,128)}, f32[2,4,4,128]{3,2,1,0:T(4,128)S(1)}, u32[]{:S(2)}, u32[]{:S(2)}) %collective-permute-start.10) | collective-permute-done | bytes 16416 | tf_op jit(solution)/shard_map/ppermute | solution.py:23
  137.3 2.2 %collective-permute-done.11.rest_8_ = f32[2,4,4,128]{3,2,1,0:T(4,128)S(1)} collective-permute-done((f32[2,4,4,128]{3,2,1,0:T(4,128)}, f32[2,4,4,128]{3,2,1,0:T(4,128)S(1)}, u32[]{:S(2)}, u32[]{:S(2)}) %collective-permute-start.11) | collective-permute-done | bytes 16416 | tf_op jit(solution)/shard_map/ppermute | solution.py:23
  139.5 0.4 collective-permute-done.9.rest_2_
  139.9 0.0 copy-done.4
  139.9 0.2 copy-done.5
  140.1 0.6 copy-done.6
  140.7 12.0 %key_side.1 = (bf16[512,512]{1,0:T(8,128)(2,1)}, bf16[512,512]{1,0:T(8,128)(2,1)}) custom-call(s32[28]{0:T(128)} %reshape.56.valid_ref, bf16[512,512]{1,0:T(8,128)(2,1)} %k_ref.3, bf16[512,512]{1,0:T(8,128)(2,1)} %v_ref.3, bf16[512,512]{1,0:T(8,128)(2,1)} %q_ref.3, bf16[512,512]{1,0:T(8,128)(2,1)} %convolution_convert_fusion.1.g_ref, ...), custom_call_target="tpu_custom_call" | custom-call | tf_op jit(solution)/shard_map/key_side/pallas_call | solution.py:217
  152.7 0.0 all-gather.5.cloned.1.call-done
  152.8 0.0 copy-done.3
  152.8 3.6 %convolution_convert_fusion = bf16[512,512]{1,0:T(8,128)(2,1)} fusion(bf16[512,2048]{1,0:T(8,128)(2,1)} %all-gather.5.cloned.1.call-done, bf16[2048,512]{1,0:T(8,128)(2,1)S(1)} %bitcast.33), kind=kOutput, calls=%fused_computation.6 | convolution fusion | flops 1074003968 | bytes 4718592 | tf_op jit(solution)/shard_map/dot_general | solution.py:278
  (25 shorter events, 0.2 us)
Async XLA Ops:
  7.2 17.8 %copy-start.2 = (bf16[512,2048]{1,0:T(8,128)(2,1)S(1)}, bf16[512,2048]{1,0:T(8,128)(2,1)}, u32[]{:S(2)}) copy-start(bf16[512,2048]{1,0:T(8,128)(2,1)} %param.12) | copy-start | bytes 6291460
  7.2 51.4 %all-gather.3.cloned.1.call-start = ((), (), s32[]{:S(2)}) async-start(), calls=%async_computation.1 | async-start | bytes 2621440 | tf_op jit(solution)/shard_map/all_gather | solution.py:263
  11.7 62.4 %collective-permute-start = (bf16[1024,512]{1,0:T(8,128)(2,1)}, bf16[1024,512]{1,0:T(8,128)(2,1)S(1)}, u32[]{:S(2)}, u32[]{:S(2)}) collective-permute-start(bf16[1024,512]{1,0:T(8,128)(2,1)} %constant_dynamic-update-slice_fusion), channel_id=1, source_target_pairs={{0,4},{4,8},{8,12},{12,16},{16,20},{20,24},{24,28},{1,5},{5,9},{9,... | collective-permute-start | bytes 3145736 | tf_op jit(solution)/shard_map/ppermute | solution.py:23
  16.6 62.7 %collective-permute-start.1 = (bf16[1024,512]{1,0:T(8,128)(2,1)}, bf16[1024,512]{1,0:T(8,128)(2,1)}, u32[]{:S(2)}, u32[]{:S(2)}) collective-permute-start(bf16[1024,512]{1,0:T(8,128)(2,1)} %constant_dynamic-update-slice_fusion), channel_id=1, source_target_pairs={{0,8},{4,12},{8,16},{12,20},{16,24},{20,28},{1,9},{5,13},{9,17},{1... | collective-permute-start | bytes 3145736 | tf_op jit(solution)/shard_map/ppermute | solution.py:23
  21.1 15.3 %collective-permute-start.3 = (bf16[512,512]{1,0:T(8,128)(2,1)}, bf16[512,512]{1,0:T(8,128)(2,1)}, u32[]{:S(2)}, u32[]{:S(2)}) collective-permute-start(bf16[512,512]{1,0:T(8,128)(2,1)} %q_ref.3), channel_id=1, source_target_pairs={{4,0},{8,4},{12,8},{16,12},{20,16},{24,20},{28,24},{5,1},{9,5},{13... | collective-permute-start | bytes 1572872 | tf_op jit(solution)/shard_map/ppermute | solution.py:23
  22.4 40.5 %collective-permute-start.4 = (bf16[512,512]{1,0:T(8,128)(2,1)}, bf16[512,512]{1,0:T(8,128)(2,1)}, u32[]{:S(2)}, u32[]{:S(2)}) collective-permute-start(bf16[512,512]{1,0:T(8,128)(2,1)} %q_ref.3), channel_id=1, source_target_pairs={{8,0},{12,4},{16,8},{20,12},{24,16},{28,20},{9,1},{13,5},{17,9},{2... | collective-permute-start | bytes 1572872 | tf_op jit(solution)/shard_map/ppermute | solution.py:23
  23.7 49.2 %collective-permute-start.5 = (bf16[512,512]{1,0:T(8,128)(2,1)}, bf16[512,512]{1,0:T(8,128)(2,1)}, u32[]{:S(2)}, u32[]{:S(2)}) collective-permute-start(bf16[512,512]{1,0:T(8,128)(2,1)} %q_ref.3), channel_id=1, source_target_pairs={{16,0},{20,4},{24,8},{28,12},{17,1},{21,5},{25,9},{29,13},{18,2},{... | collective-permute-start | bytes 1572872 | tf_op jit(solution)/shard_map/ppermute | solution.py:23
  27.5 3.8 %copy-start.7 = (s32[32,5]{0,1:T(8,128)S(1)}, s32[32,5]{0,1:T(8,128)}, u32[]{:S(2)}) copy-start(s32[32,5]{0,1:T(8,128)} %param.15) | copy-start | bytes 1924
  27.5 5.8 %copy-start = (s32[32]{0:T(128)S(1)}, s32[32]{0:T(128)}, u32[]{:S(2)}) copy-start(s32[32]{0:T(128)} %param.14) | copy-start | bytes 388
  27.5 49.4 %all-to-all-start = ((bf16[512,4,512]{0,2,1:T(8,128)(2,1)}), bf16[512,4,512]{0,2,1:T(8,128)(2,1)S(1)}, u32[]{:S(2)}, u32[]{:S(2)}) async-start(bf16[512,4,512]{0,2,1:T(8,128)(2,1)} %bitcast.32), calls=%async_computation | async-start | bytes 4194304 | tf_op jit(solution)/shard_map/all_to_all | solution.py:270
  31.3 121.5 %all-gather.5.cloned.1.call-start = ((), (), s32[]{:S(2)}) async-start(), calls=%async_computation.2 | async-start | bytes 2621440 | tf_op jit(solution)/shard_map/all_gather | solution.py:279
  36.4 43.4 %collective-permute-start.2 = (bf16[1024,512]{1,0:T(8,128)(2,1)}, bf16[1024,512]{1,0:T(8,128)(2,1)}, u32[]{:S(2)}, u32[]{:S(2)}) collective-permute-start(bf16[1024,512]{1,0:T(8,128)(2,1)} %constant_dynamic-update-slice_fusion), channel_id=1, source_target_pairs={{0,16},{4,20},{8,24},{12,28},{1,17},{5,21},{9,25},{13,29},{2,18},{... | collective-permute-start | bytes 3145736 | tf_op jit(solution)/shard_map/ppermute | solution.py:23
  62.8 17.0 %collective-permute-start.6 = (bf16[512,512]{1,0:T(8,128)(2,1)}, bf16[512,512]{1,0:T(8,128)(2,1)}, u32[]{:S(2)}, u32[]{:S(2)}) collective-permute-start(bf16[512,512]{1,0:T(8,128)(2,1)} %convolution_convert_fusion.1.g_ref), channel_id=1, source_target_pairs={{4,0},{8,4},{12,8},{16,12},{20,16},{24,20},{28,24},{5,1},{9,5},{13... | collective-permute-start | bytes 1572872 | tf_op jit(solution)/shard_map/ppermute | solution.py:23
  72.9 20.7 %collective-permute-start.7 = (bf16[512,512]{1,0:T(8,128)(2,1)}, bf16[512,512]{1,0:T(8,128)(2,1)}, u32[]{:S(2)}, u32[]{:S(2)}) collective-permute-start(bf16[512,512]{1,0:T(8,128)(2,1)} %convolution_convert_fusion.1.g_ref), channel_id=1, source_target_pairs={{8,0},{12,4},{16,8},{20,12},{24,16},{28,20},{9,1},{13,5},{17,9},{2... | collective-permute-start | bytes 1572872 | tf_op jit(solution)/shard_map/ppermute | solution.py:23
  74.2 5.1 %copy-start.1 = (bf16[1024,512]{1,0:T(8,128)(2,1)}, bf16[1024,512]{1,0:T(8,128)(2,1)S(1)}, u32[]{:S(2)}) copy-start(bf16[1024,512]{1,0:T(8,128)(2,1)S(1)} %collective-permute-done.rest_0_.rest_1_) | copy-start | bytes 3145732
  74.2 41.9 %collective-permute-start.8 = (bf16[512,512]{1,0:T(8,128)(2,1)}, bf16[512,512]{1,0:T(8,128)(2,1)}, u32[]{:S(2)}, u32[]{:S(2)}) collective-permute-start(bf16[512,512]{1,0:T(8,128)(2,1)} %convolution_convert_fusion.1.g_ref), channel_id=1, source_target_pairs={{16,0},{20,4},{24,8},{28,12},{17,1},{21,5},{25,9},{29,13},{18,2},{... | collective-permute-start | bytes 1572872 | tf_op jit(solution)/shard_map/ppermute | solution.py:23
  131.3 21.5 %copy-start.3 = (bf16[4,512,512]{2,1,0:T(8,128)(2,1)S(1)}, bf16[4,512,512]{2,1,0:T(8,128)(2,1)}, u32[]{:S(2)}) copy-start(bf16[4,512,512]{2,1,0:T(8,128)(2,1)} %copy.18) | copy-start | bytes 6291460
  131.3 6.0 %collective-permute-start.10 = (f32[2,4,4,128]{3,2,1,0:T(4,128)}, f32[2,4,4,128]{3,2,1,0:T(4,128)S(1)}, u32[]{:S(2)}, u32[]{:S(2)}) collective-permute-start(f32[2,4,4,128]{3,2,1,0:T(4,128)} %get-tuple-element.30.st_ref), channel_id=1, source_target_pairs={{8,0},{12,4},{16,8},{20,12},{24,16},{28,20},{9,1},{13,5},{17,9},{2... | collective-permute-start | bytes 49160 | tf_op jit(solution)/shard_map/ppermute | solution.py:23
  132.7 6.7 %collective-permute-start.11 = (f32[2,4,4,128]{3,2,1,0:T(4,128)}, f32[2,4,4,128]{3,2,1,0:T(4,128)S(1)}, u32[]{:S(2)}, u32[]{:S(2)}) collective-permute-start(f32[2,4,4,128]{3,2,1,0:T(4,128)} %get-tuple-element.30.st_ref), channel_id=1, source_target_pairs={{16,0},{20,4},{24,8},{28,12},{17,1},{21,5},{25,9},{29,13},{18,2},{... | collective-permute-start | bytes 49160 | tf_op jit(solution)/shard_map/ppermute | solution.py:23
  134.0 5.8 %collective-permute-start.9 = (f32[2,4,4,128]{3,2,1,0:T(4,128)}, f32[2,4,4,128]{3,2,1,0:T(4,128)S(1)}, u32[]{:S(2)}, u32[]{:S(2)}) collective-permute-start(f32[2,4,4,128]{3,2,1,0:T(4,128)} %get-tuple-element.30.st_ref), channel_id=1, source_target_pairs={{4,0},{8,4},{12,8},{16,12},{20,16},{24,20},{28,24},{5,1},{9,5},{13... | collective-permute-start | bytes 49160 | tf_op jit(solution)/shard_map/ppermute | solution.py:23
  137.3 2.6 %copy-start.4 = (f32[2,4,4,128]{3,2,1,0:T(4,128)}, f32[2,4,4,128]{3,2,1,0:T(4,128)S(1)}, u32[]{:S(2)}) copy-start(f32[2,4,4,128]{3,2,1,0:T(4,128)S(1)} %collective-permute-done.10.rest_5_) | copy-start | bytes 49156
  139.5 0.6 copy-start.5
  140.1 0.6 copy-start.6
Sparse Core Ops, SparseCore 0:
  9.6 25.2 all-gather.2
  131.4 19.9 all-gather.4

commit v9 on v6

--- a/solution.py
+++ b/solution.py
@@ -209,7 +209,7 @@
 
     kv = jnp.concatenate([keys, values], axis=0)
     kv_from = [passed_along(kv, "ctx", 2**m) for m in levels]
-    q_from = [passed_along(queries, "ctx", -(2**m)) for m in levels]
+    q_near = passed_along(queries, "ctx", -1)
 
     grad_att = lax.dot_general(
         lax.all_gather(d_out, "head", axis=1, tiled=True),
@@ -218,7 +218,11 @@
         preferred_element_type=jnp.float32,
     )
     g = grad_att.astype(jnp.bfloat16)
-    g_from = [passed_along(g, "ctx", -(2**m)) for m in levels]
+    g_near = passed_along(g, "ctx", -1)
+    qg = jnp.concatenate([queries, g], axis=0)
+    qg_far = [passed_along(qg, "ctx", -(2**m)) for m in levels[1:]]
+    q_from = [q_near] + [pair[: queries.shape[0]] for pair in qg_far]
+    g_from = [g_near] + [pair[queries.shape[0] :] for pair in qg_far]
     weight_cols = lax.all_to_all(out_weight, "head", 1, 0, tiled=True)
     kv_from, q_from, g_from, valid_q, valid_k, weight_cols = lax.optimization_barrier(
         (kv_from, q_from, g_from, valid_q, valid_k, weight_cols)

time: 163 us -> 186 us (1.14)
  waiting for transfers between devices: 52.3 us -> 89.5 us
  starting transfers between devices: 46.4 us -> 26.8 us
  local copies, waits for them, and re-layouts: 14.9 us -> 20 us
    ppermute x12 -> x10, waiting for transfers between devices: 51.6 us -> 76.3 us  [passed_along(): return lax.ppermute(block, axis, route)]
    ppermute x12 -> x10, starting transfers between devices: 42.6 us -> 23 us  [passed_along(): return lax.ppermute(block, axis, route)]
    all_to_all x1, waiting for transfers between devices: 0.01 us -> 10.9 us  [local(): weight_cols = lax.all_to_all(out_weight, 'head', 1, 0, tiled=True)]
    slice x0 -> x2, local copies, waits for them, and re-layouts: none -> 4.54 us  [local(): g_from = [g_near] + [pair[queries.shape[0]:] for pair in qg_far]]
    unnamed x18 -> x24, local copies, waits for them, and re-layouts: 5.24 us -> 5.81 us
  transfers between devices with their start and end apart: 15 -> 13, of which waited for: 8 -> 8; matrix products, arithmetic and copies ran while one was open for 11% -> 13% of each run, Pallas kernels for 7% -> 6%
where the time goes in v9:
time: 186 us; the launch traced here: 185 us
  waiting for transfers between devices  89.5 us (48%)
  starting transfers between devices  26.8 us (14%)
  Pallas kernels  25.8 us (14%)
  local copies, waits for them, and re-layouts  20 us (11%)
  between operations  14.3 us (8%)
  matrix products  7.13 us (4%)
    ppermute x10, waiting for transfers between devices, passed_along(): return lax.ppermute(block, axis, route)  76.3 us
    ppermute x10, starting transfers between devices, passed_along(): return lax.ppermute(block, axis, route)  23 us
    pallas_call x1, Pallas kernels, query_call(): pl.pallas_call(functools.partial(query_kernel, n_levels), grid_spec=grid_...  15.2 us
    all_to_all x1, waiting for transfers between devices, local(): weight_cols = lax.all_to_all(out_weight, 'head', 1, 0, tiled=True)  10.9 us
    pallas_call x1, Pallas kernels, key_call(): pl.pallas_call(functools.partial(key_kernel, n_levels), grid_spec=grid_sp...  10.6 us
    unnamed x24, local copies, waits for them, and re-layouts  5.81 us
    slice x2, local copies, waits for them, and re-layouts, local(): g_from = [g_near] + [pair[queries.shape[0]:] for pair in qg_far]  4.54 us
    all_to_all x1, starting transfers between devices, local(): weight_cols = lax.all_to_all(out_weight, 'head', 1, 0, tiled=True)  3.74 us
  transfers between devices with their start and end apart: 13, of which 8 were waited for; matrix products, arithmetic and copies ran while one was open for 13% of the time, Pallas kernels for 6%

profile of v9, /device:TPU:0, one launch (start us, length us, event | category | flops | bytes accessed | tf_op | source)
XLA Modules:
  0.0 185.0 jit_solution(9873702720366482949)
XLA Ops:
  7.2 0.0 copy-start.3
  7.2 0.0 all-gather.3.cloned.1.call-start
  7.2 0.7 all-gather.3.cloned.1.call-update
  7.9 1.9 %constant_dynamic-update-slice_fusion.1 = bf16[1024,512]{1,0:T(8,128)(2,1)} fusion(bf16[512,512]{1,0:T(8,128)(2,1)} %k_ref.3), kind=kLoop, calls=%fused_computation.16 | loop fusion | bytes 1048576
  9.8 1.9 %constant_dynamic-update-slice_fusion = bf16[1024,512]{1,0:T(8,128)(2,1)} fusion(bf16[1024,512]{1,0:T(8,128)(2,1)} %constant_dynamic-update-slice_fusion.1, bf16[512,512]{1,0:T(8,128)(2,1)} %v_ref.3), kind=kLoop, calls=%fused_computation.15 | loop fusion | bytes 1048576 | tf_op jit(solution)/shard_map/concatenate | solution.py:210
  11.6 5.9 %collective-permute-start = (bf16[1024,512]{1,0:T(8,128)(2,1)}, bf16[1024,512]{1,0:T(8,128)(2,1)}, u32[]{:S(2)}, u32[]{:S(2)}) collective-permute-start(bf16[1024,512]{1,0:T(8,128)(2,1)} %constant_dynamic-update-slice_fusion), channel_id=1, source_target_pairs={{0,4},{4,8},{8,12},{12,16},{16,20},{20,24},{24,28},{1,5},{5,9},{9,... | collective-permute-start | bytes 3145736 | tf_op jit(solution)/shard_map/ppermute | solution.py:23
  17.5 3.5 %collective-permute-start.1 = (bf16[1024,512]{1,0:T(8,128)(2,1)}, bf16[1024,512]{1,0:T(8,128)(2,1)}, u32[]{:S(2)}, u32[]{:S(2)}) collective-permute-start(bf16[1024,512]{1,0:T(8,128)(2,1)} %constant_dynamic-update-slice_fusion), channel_id=1, source_target_pairs={{0,8},{4,12},{8,16},{12,20},{16,24},{20,28},{1,9},{5,13},{9,17},{1... | collective-permute-start | bytes 3145736 | tf_op jit(solution)/shard_map/ppermute | solution.py:23
  21.0 4.5 %collective-permute-start.2 = (bf16[1024,512]{1,0:T(8,128)(2,1)}, bf16[1024,512]{1,0:T(8,128)(2,1)}, u32[]{:S(2)}, u32[]{:S(2)}) collective-permute-start(bf16[1024,512]{1,0:T(8,128)(2,1)} %constant_dynamic-update-slice_fusion), channel_id=1, source_target_pairs={{0,16},{4,20},{8,24},{12,28},{1,17},{5,21},{9,25},{13,29},{2,18},{... | collective-permute-start | bytes 3145736 | tf_op jit(solution)/shard_map/ppermute | solution.py:23
  25.4 0.0 copy-done.3
  25.4 2.5 %copy.17 = bf16[512,2048]{0,1:T(8,128)(2,1)} copy(bf16[512,2048]{1,0:T(8,128)(2,1)S(1)} %copy-done.3) | data formatting | bytes 4194304 | tf_op args[3]
  28.0 3.7 %all-to-all-start = ((bf16[512,4,512]{0,2,1:T(8,128)(2,1)}), bf16[512,4,512]{0,2,1:T(8,128)(2,1)S(1)}, u32[]{:S(2)}, u32[]{:S(2)}) async-start(bf16[512,4,512]{0,2,1:T(8,128)(2,1)} %bitcast.32), calls=%async_computation | async-start | bytes 4194304 | tf_op jit(solution)/shard_map/all_to_all | solution.py:226
  31.7 0.0 all-gather.5.cloned.1.call-start
  31.8 0.0 copy-done.10
  31.8 0.6 gather_fusion.5
  32.4 0.6 gather_fusion.4
  33.1 0.1 constant_dynamic-slice_fusion
  33.3 0.0 copy-start.1
  33.3 1.6 all-gather.3.cloned.1.call-done
  34.9 3.5 %convolution_convert_fusion.1.g_ref = bf16[512,512]{1,0:T(8,128)(2,1)S(1)} fusion(bf16[512,2048]{1,0:T(8,128)(2,1)} %all-gather.3.cloned.1.call-done, bf16[512,2048]{1,0:T(8,128)(2,1)} %param.12), kind=kOutput, calls=%fused_computation.7 | convolution fusion | flops 1074003968 | bytes 4718592 | tf_op jit(solution)/shard_map/dot_general | solution.py:214
  38.4 0.0 copy-done.1
  38.4 0.0 copy-start.2
  38.4 0.0 copy-start
  38.4 1.1 pad_maximum_fusion
  39.6 1.3 collective-permute-start.5
  40.9 1.3 collective-permute-start.4
  42.2 0.0 copy-done
  42.2 0.1 and_bitcast_fusion.6
  42.3 0.1 copy.15
  42.4 0.6 reshape.55.valid_ref
  43.0 0.6 gather_fusion.2
  43.6 0.6 gather_fusion.1
  44.3 0.6 gather_fusion.3
  45.0 0.6 gather_fusion
  45.7 0.1 copy.16
  45.8 0.7 reshape.56.valid_ref
  46.4 10.9 %all-to-all-done = bf16[512,4,512]{0,2,1:T(8,128)(2,1)S(1)} async-done(((bf16[512,4,512]{0,2,1:T(8,128)(2,1)}), bf16[512,4,512]{0,2,1:T(8,128)(2,1)S(1)}, u32[]{:S(2)}, u32[]{:S(2)}) %all-to-all-start) | async-done | bytes 2097184 | tf_op jit(solution)/shard_map/all_to_all | solution.py:226
  57.4 2.4 %copy.18 = bf16[4,512,512]{2,1,0:T(8,128)(2,1)} copy(bf16[4,512,512]{1,2,0:T(8,128)(2,1)S(1)} %bitcast.31) | data formatting | bytes 4194304 | tf_op jit(solution)/shard_map/all_to_all | solution.py:226
  59.7 32.8 %collective-permute-done.5 = bf16[1024,512]{1,0:T(8,128)(2,1)} collective-permute-done((bf16[1024,512]{1,0:T(8,128)(2,1)}, bf16[1024,512]{1,0:T(8,128)(2,1)}, u32[]{:S(2)}, u32[]{:S(2)}) %collective-permute-start.5) | collective-permute-done | bytes 1048608 | tf_op jit(solution)/shard_map/ppermute | solution.py:23
  92.5 1.3 collective-permute-start.3
  93.8 0.0 collective-permute-done.4
  93.8 0.0 copy-done.2
  93.8 1.3 collective-permute-start.6
  95.1 2.3 %fusion.7 = (bf16[512,512]{1,0:T(8,128)(2,1)}, bf16[512,512]{1,0:T(8,128)(2,1)}) fusion(bf16[1024,512]{1,0:T(8,128)(2,1)} %collective-permute-done.5), kind=kLoop, calls=%fused_computation.54 | loop fusion | bytes 2097152 | tf_op jit(solution)/shard_map/slice | solution.py:225
  97.4 2.3 %fusion.8 = (bf16[512,512]{1,0:T(8,128)(2,1)}, bf16[512,512]{1,0:T(8,128)(2,1)}) fusion(bf16[1024,512]{1,0:T(8,128)(2,1)} %collective-permute-done.4), kind=kLoop, calls=%fused_computation.55 | loop fusion | bytes 2097152 | tf_op jit(solution)/shard_map/slice | solution.py:225
  99.7 10.5 %collective-permute-done.3.rest_0_ = bf16[512,512]{1,0:T(8,128)(2,1)S(1)} collective-permute-done((bf16[512,512]{1,0:T(8,128)(2,1)S(1)}, bf16[512,512]{1,0:T(8,128)(2,1)S(1)}, u32[]{:S(2)}, u32[]{:S(2)}) %collective-permute-start.3) | collective-permute-done | bytes 524320 | tf_op jit(solution)/shard_map/ppermute | solution.py:23
  110.2 0.0 collective-permute-done.rest_0_.rest_1_
  110.2 0.0 collective-permute-done.1.rest_2_.rest_3_
  110.2 0.0 collective-permute-done.2.rest_4_.rest_5_
  110.2 9.8 %collective-permute-done.6.rest_1_ = bf16[512,512]{1,0:T(8,128)(2,1)S(1)} collective-permute-done((bf16[512,512]{1,0:T(8,128)(2,1)S(1)}, bf16[512,512]{1,0:T(8,128)(2,1)S(1)}, u32[]{:S(2)}, u32[]{:S(2)}) %collective-permute-start.6) | collective-permute-done | bytes 524320 | tf_op jit(solution)/shard_map/ppermute | solution.py:23
  120.0 0.0 copy-done.5
  120.1 0.8 copy-done.6
  120.8 15.2 %query_side.1 = (bf16[512,512]{1,0:T(8,128)(2,1)}, bf16[512,512]{1,0:T(8,128)(2,1)}, f32[2,4,4,128]{3,2,1,0:T(4,128)}) custom-call(s32[28]{0:T(128)} %reshape.55.valid_ref, bf16[512,512]{1,0:T(8,128)(2,1)} %q_ref.3, bf16[512,512]{1,0:T(8,128)(2,1)} %copy-done.2, bf16[512,512]{1,0:T(8,128)(2,1)} %k_ref.3, bf16[512,512]{1,0:T(8,128)(2,1)} %v_ref.3, ...), custom_call_target="tpu_custom_call" | custom-call | tf_op jit(solution)/shard_map/query_side/pallas_call | solution.py:144
  136.1 0.0 all-gather.5.cloned.1.call-update
  136.1 0.0 copy-start.4
  136.1 1.4 collective-permute-start.7
  137.5 1.3 collective-permute-start.8
  138.8 1.3 collective-permute-start.9
  140.1 10.3 %collective-permute-done.7.rest_2_ = f32[2,4,4,128]{3,2,1,0:T(4,128)S(1)} collective-permute-done((f32[2,4,4,128]{3,2,1,0:T(4,128)}, f32[2,4,4,128]{3,2,1,0:T(4,128)S(1)}, u32[]{:S(2)}, u32[]{:S(2)}) %collective-permute-start.7) | collective-permute-done | bytes 16416 | tf_op jit(solution)/shard_map/ppermute | solution.py:23
  150.4 3.4 %collective-permute-done.8.rest_5_ = f32[2,4,4,128]{3,2,1,0:T(4,128)S(1)} collective-permute-done((f32[2,4,4,128]{3,2,1,0:T(4,128)}, f32[2,4,4,128]{3,2,1,0:T(4,128)S(1)}, u32[]{:S(2)}, u32[]{:S(2)}) %collective-permute-start.8) | collective-permute-done | bytes 16416 | tf_op jit(solution)/shard_map/ppermute | solution.py:23
  153.8 9.5 %collective-permute-done.9.rest_8_ = f32[2,4,4,128]{3,2,1,0:T(4,128)S(1)} collective-permute-done((f32[2,4,4,128]{3,2,1,0:T(4,128)}, f32[2,4,4,128]{3,2,1,0:T(4,128)S(1)}, u32[]{:S(2)}, u32[]{:S(2)}) %collective-permute-start.9) | collective-permute-done | bytes 16416 | tf_op jit(solution)/shard_map/ppermute | solution.py:23
  163.3 0.6 copy-done.9
  163.9 10.6 %key_side.1 = (bf16[512,512]{1,0:T(8,128)(2,1)}, bf16[512,512]{1,0:T(8,128)(2,1)}) custom-call(s32[28]{0:T(128)} %reshape.56.valid_ref, bf16[512,512]{1,0:T(8,128)(2,1)} %k_ref.3, bf16[512,512]{1,0:T(8,128)(2,1)} %v_ref.3, bf16[512,512]{1,0:T(8,128)(2,1)} %q_ref.3, bf16[512,512]{1,0:T(8,128)(2,1)} %copy-done.2, f32[2,4,4,128]{3,2,1,0:T(4,128)} %get-tuple-element.30.st_ref, ...), custom_call_target="tpu_custom_call" | custom-call | tf_op jit(solution)/shard_map/key_side/pallas_call | solution.py:169
  174.5 0.0 all-gather.5.cloned.1.call-done
  174.5 3.6 %convolution_convert_fusion = bf16[512,512]{1,0:T(8,128)(2,1)} fusion(bf16[512,2048]{1,0:T(8,128)(2,1)} %all-gather.5.cloned.1.call-done, bf16[2048,512]{1,0:T(8,128)(2,1)S(1)} %bitcast.33), kind=kOutput, calls=%fused_computation.6 | convolution fusion | flops 1074003968 | bytes 4718592 | tf_op jit(solution)/shard_map/dot_general | solution.py:234
  (30 shorter events, 0.2 us)
Async XLA Ops:
  7.2 18.3 %copy-start.3 = (bf16[512,2048]{1,0:T(8,128)(2,1)S(1)}, bf16[512,2048]{1,0:T(8,128)(2,1)}, u32[]{:S(2)}) copy-start(bf16[512,2048]{1,0:T(8,128)(2,1)} %param.12) | copy-start | bytes 6291460
  7.2 27.7 %all-gather.3.cloned.1.call-start = ((), (), s32[]{:S(2)}) async-start(), calls=%async_computation.1 | async-start | bytes 2621440 | tf_op jit(solution)/shard_map/all_gather | solution.py:215
  11.6 98.6 %collective-permute-start = (bf16[1024,512]{1,0:T(8,128)(2,1)}, bf16[1024,512]{1,0:T(8,128)(2,1)}, u32[]{:S(2)}, u32[]{:S(2)}) collective-permute-start(bf16[1024,512]{1,0:T(8,128)(2,1)} %constant_dynamic-update-slice_fusion), channel_id=1, source_target_pairs={{0,4},{4,8},{8,12},{12,16},{16,20},{20,24},{24,28},{1,5},{5,9},{9,... | collective-permute-start | bytes 3145736 | tf_op jit(solution)/shard_map/ppermute | solution.py:23
  17.5 92.7 %collective-permute-start.1 = (bf16[1024,512]{1,0:T(8,128)(2,1)}, bf16[1024,512]{1,0:T(8,128)(2,1)}, u32[]{:S(2)}, u32[]{:S(2)}) collective-permute-start(bf16[1024,512]{1,0:T(8,128)(2,1)} %constant_dynamic-update-slice_fusion), channel_id=1, source_target_pairs={{0,8},{4,12},{8,16},{12,20},{16,24},{20,28},{1,9},{5,13},{9,17},{1... | collective-permute-start | bytes 3145736 | tf_op jit(solution)/shard_map/ppermute | solution.py:23
  21.0 89.2 %collective-permute-start.2 = (bf16[1024,512]{1,0:T(8,128)(2,1)}, bf16[1024,512]{1,0:T(8,128)(2,1)}, u32[]{:S(2)}, u32[]{:S(2)}) collective-permute-start(bf16[1024,512]{1,0:T(8,128)(2,1)} %constant_dynamic-update-slice_fusion), channel_id=1, source_target_pairs={{0,16},{4,20},{8,24},{12,28},{1,17},{5,21},{9,25},{13,29},{2,18},{... | collective-permute-start | bytes 3145736 | tf_op jit(solution)/shard_map/ppermute | solution.py:23
  27.9 3.8 %copy-start.10 = (s32[32,5]{0,1:T(8,128)S(1)}, s32[32,5]{0,1:T(8,128)}, u32[]{:S(2)}) copy-start(s32[32,5]{0,1:T(8,128)} %param.15) | copy-start | bytes 1924
  28.0 29.4 %all-to-all-start = ((bf16[512,4,512]{0,2,1:T(8,128)(2,1)}), bf16[512,4,512]{0,2,1:T(8,128)(2,1)S(1)}, u32[]{:S(2)}, u32[]{:S(2)}) async-start(bf16[512,4,512]{0,2,1:T(8,128)(2,1)} %bitcast.32), calls=%async_computation | async-start | bytes 4194304 | tf_op jit(solution)/shard_map/all_to_all | solution.py:226
  31.7 142.8 %all-gather.5.cloned.1.call-start = ((), (), s32[]{:S(2)}) async-start(), calls=%async_computation.2 | async-start | bytes 2621440 | tf_op jit(solution)/shard_map/all_gather | solution.py:235
  33.3 5.1 %copy-start.1 = (bf16[512,512]{1,0:T(8,128)(2,1)S(1)}, bf16[512,512]{1,0:T(8,128)(2,1)}, u32[]{:S(2)}) copy-start(bf16[512,512]{1,0:T(8,128)(2,1)} %q_ref.3) | copy-start | bytes 1572868
  38.4 55.4 %copy-start.2 = (bf16[512,512]{1,0:T(8,128)(2,1)}, bf16[512,512]{1,0:T(8,128)(2,1)S(1)}, u32[]{:S(2)}) copy-start(bf16[512,512]{1,0:T(8,128)(2,1)S(1)} %convolution_convert_fusion.1.g_ref) | copy-start | bytes 1572868
  38.4 3.7 %copy-start = (s32[32]{0:T(128)S(1)}, s32[32]{0:T(128)}, u32[]{:S(2)}) copy-start(s32[32]{0:T(128)} %param.14) | copy-start | bytes 388
  39.6 52.9 %collective-permute-start.5 = (bf16[1024,512]{1,0:T(8,128)(2,1)}, bf16[1024,512]{1,0:T(8,128)(2,1)}, u32[]{:S(2)}, u32[]{:S(2)}) collective-permute-start(bf16[1024,512]{1,0:T(8,128)(2,1)} %pad_maximum_fusion), channel_id=1, source_target_pairs={{16,0},{20,4},{24,8},{28,12},{17,1},{21,5},{25,9},{29,13},{18,2},{... | collective-permute-start | bytes 3145736 | tf_op jit(solution)/shard_map/ppermute | solution.py:23
  40.9 52.9 %collective-permute-start.4 = (bf16[1024,512]{1,0:T(8,128)(2,1)}, bf16[1024,512]{1,0:T(8,128)(2,1)}, u32[]{:S(2)}, u32[]{:S(2)}) collective-permute-start(bf16[1024,512]{1,0:T(8,128)(2,1)} %pad_maximum_fusion), channel_id=1, source_target_pairs={{8,0},{12,4},{16,8},{20,12},{24,16},{28,20},{9,1},{13,5},{17,9},{2... | collective-permute-start | bytes 3145736 | tf_op jit(solution)/shard_map/ppermute | solution.py:23
  92.5 17.7 %collective-permute-start.3 = (bf16[512,512]{1,0:T(8,128)(2,1)S(1)}, bf16[512,512]{1,0:T(8,128)(2,1)S(1)}, u32[]{:S(2)}, u32[]{:S(2)}) collective-permute-start(bf16[512,512]{1,0:T(8,128)(2,1)S(1)} %copy-done.1), channel_id=1, source_target_pairs={{4,0},{8,4},{12,8},{16,12},{20,16},{24,20},{28,24},{5,1},{9,5},{13... | collective-permute-start | bytes 1572872 | tf_op jit(solution)/shard_map/ppermute | solution.py:23
  93.8 26.2 %collective-permute-start.6 = (bf16[512,512]{1,0:T(8,128)(2,1)S(1)}, bf16[512,512]{1,0:T(8,128)(2,1)S(1)}, u32[]{:S(2)}, u32[]{:S(2)}) collective-permute-start(bf16[512,512]{1,0:T(8,128)(2,1)S(1)} %convolution_convert_fusion.1.g_ref), channel_id=1, source_target_pairs={{4,0},{8,4},{12,8},{16,12},{20,16},{24,20},{28,24},{5,1},{9,5},{13... | collective-permute-start | bytes 1572872 | tf_op jit(solution)/shard_map/ppermute | solution.py:23
  110.2 9.9 %copy-start.5 = (bf16[512,512]{1,0:T(8,128)(2,1)}, bf16[512,512]{1,0:T(8,128)(2,1)S(1)}, u32[]{:S(2)}) copy-start(bf16[512,512]{1,0:T(8,128)(2,1)S(1)} %collective-permute-done.3.rest_0_) | copy-start | bytes 1572868
  120.0 0.8 copy-start.6
  136.1 38.4 %copy-start.4 = (bf16[4,512,512]{2,1,0:T(8,128)(2,1)S(1)}, bf16[4,512,512]{2,1,0:T(8,128)(2,1)}, u32[]{:S(2)}) copy-start(bf16[4,512,512]{2,1,0:T(8,128)(2,1)} %copy.18) | copy-start | bytes 6291460
  136.1 14.3 %collective-permute-start.7 = (f32[2,4,4,128]{3,2,1,0:T(4,128)}, f32[2,4,4,128]{3,2,1,0:T(4,128)S(1)}, u32[]{:S(2)}, u32[]{:S(2)}) collective-permute-start(f32[2,4,4,128]{3,2,1,0:T(4,128)} %get-tuple-element.30.st_ref), channel_id=1, source_target_pairs={{4,0},{8,4},{12,8},{16,12},{20,16},{24,20},{28,24},{5,1},{9,5},{13... | collective-permute-start | bytes 49160 | tf_op jit(solution)/shard_map/ppermute | solution.py:23
  137.5 16.3 %collective-permute-start.8 = (f32[2,4,4,128]{3,2,1,0:T(4,128)}, f32[2,4,4,128]{3,2,1,0:T(4,128)S(1)}, u32[]{:S(2)}, u32[]{:S(2)}) collective-permute-start(f32[2,4,4,128]{3,2,1,0:T(4,128)} %get-tuple-element.30.st_ref), channel_id=1, source_target_pairs={{8,0},{12,4},{16,8},{20,12},{24,16},{28,20},{9,1},{13,5},{17,9},{2... | collective-permute-start | bytes 49160 | tf_op jit(solution)/shard_map/ppermute | solution.py:23
  138.8 24.4 %collective-permute-start.9 = (f32[2,4,4,128]{3,2,1,0:T(4,128)}, f32[2,4,4,128]{3,2,1,0:T(4,128)S(1)}, u32[]{:S(2)}, u32[]{:S(2)}) collective-permute-start(f32[2,4,4,128]{3,2,1,0:T(4,128)} %get-tuple-element.30.st_ref), channel_id=1, source_target_pairs={{16,0},{20,4},{24,8},{28,12},{17,1},{21,5},{25,9},{29,13},{18,2},{... | collective-permute-start | bytes 49160 | tf_op jit(solution)/shard_map/ppermute | solution.py:23
  150.4 12.9 %copy-start.7 = (f32[2,4,4,128]{3,2,1,0:T(4,128)}, f32[2,4,4,128]{3,2,1,0:T(4,128)S(1)}, u32[]{:S(2)}) copy-start(f32[2,4,4,128]{3,2,1,0:T(4,128)S(1)} %collective-permute-done.7.rest_2_) | copy-start | bytes 49156
  153.8 9.5 %copy-start.8 = (f32[2,4,4,128]{3,2,1,0:T(4,128)}, f32[2,4,4,128]{3,2,1,0:T(4,128)S(1)}, u32[]{:S(2)}) copy-start(f32[2,4,4,128]{3,2,1,0:T(4,128)S(1)} %collective-permute-done.8.rest_5_) | copy-start | bytes 49156
  163.3 0.6 copy-start.9
Sparse Core Ops, SparseCore 0:
  9.6 25.2 all-gather.2
  136.2 37.0 all-gather.4

commit v10 on v6

--- a/solution.py
+++ b/solution.py
@@ -233,7 +233,13 @@
         preferred_element_type=jnp.float32,
     ).astype(jnp.bfloat16)
 
-    st_from = [passed_along(stats, "ctx", -(2**m)) for m in levels]
+    every = lax.all_to_all(
+        jnp.broadcast_to(stats[None], (ctx_count,) + stats.shape), "ctx", 0, 0, tiled=False
+    )
+    st_from = [
+        lax.dynamic_index_in_dim(every, jnp.minimum(ctx_index + 2**m, ctx_count - 1), 0, False)
+        for m in levels
+    ]
     key_grad, value_grad = key_call(
         valid_k, keys, values, queries, g, stats, q_from, g_from, st_from, heads_local, n_levels
     )

time: 163 us -> 166 us (1.018)
  waiting for transfers between devices: 52.3 us -> 55 us
    all_to_all x0 -> x1, waiting for transfers between devices: none -> 7.27 us  [local(): lax.all_to_all(jnp.broadcast_to(stats[None], (ctx_count,) + stats.shape),...]
    ppermute x12 -> x9, waiting for transfers between devices: 51.6 us -> 47 us  [passed_along(): return lax.ppermute(block, axis, route)]
    ppermute x12 -> x9, starting transfers between devices: 42.6 us -> 38.6 us  [passed_along(): return lax.ppermute(block, axis, route)]
    all_to_all x0 -> x1, starting transfers between devices: none -> 3.38 us  [local(): lax.all_to_all(jnp.broadcast_to(stats[None], (ctx_count,) + stats.shape),...]
    unnamed x18 -> x12, local copies, waits for them, and re-layouts: 5.24 us -> 4.43 us
  transfers between devices with their start and end apart: 15 -> 13, of which waited for: 8 -> 6; matrix products, arithmetic and copies ran while one was open for 11% -> 13% of each run, Pallas kernels for 7% -> 7%
where the time goes in v10:
time: 166 us; the launch traced here: 165 us
  waiting for transfers between devices  55 us (33%)
  starting transfers between devices  45.8 us (28%)
  Pallas kernels  26 us (16%)
  local copies, waits for them, and re-layouts  16.2 us (10%)
  between operations  14.3 us (9%)
  matrix products  7.93 us (5%)
    ppermute x9, waiting for transfers between devices, passed_along(): return lax.ppermute(block, axis, route)  47 us
    ppermute x9, starting transfers between devices, passed_along(): return lax.ppermute(block, axis, route)  38.6 us
    pallas_call x1, Pallas kernels, query_call(): pl.pallas_call(functools.partial(query_kernel, n_levels), grid_spec=grid_...  15.2 us
    pallas_call x1, Pallas kernels, key_call(): pl.pallas_call(functools.partial(key_kernel, n_levels), grid_spec=grid_sp...  10.8 us
    all_to_all x1, waiting for transfers between devices, local(): lax.all_to_all(jnp.broadcast_to(stats[None], (ctx_count,) + stats.shape),...  7.27 us
    unnamed x12, local copies, waits for them, and re-layouts  4.43 us
    dot_general x1, matrix products, local(): lax.dot_general(lax.all_gather(d_out, 'head', axis=1, tiled=True), out_we...  4.3 us
    all_to_all x1, starting transfers between devices, local(): weight_cols = lax.all_to_all(out_weight, 'head', 1, 0, tiled=True)  3.74 us
  transfers between devices with their start and end apart: 13, of which 6 were waited for; matrix products, arithmetic and copies ran while one was open for 13% of the time, Pallas kernels for 7%

profile of v10, /device:TPU:0, one launch (start us, length us, event | category | flops | bytes accessed | tf_op | source)
XLA Modules:
  0.0 165.3 jit_solution(2416889821551382481)
XLA Ops:
  7.2 0.0 copy-start.2
  7.2 0.0 all-gather.3.cloned.1.call-start
  7.2 0.7 all-gather.3.cloned.1.call-update
  7.9 1.9 %constant_dynamic-update-slice_fusion.1 = bf16[1024,512]{1,0:T(8,128)(2,1)} fusion(bf16[512,512]{1,0:T(8,128)(2,1)} %k_ref.3), kind=kLoop, calls=%fused_computation.18 | loop fusion | bytes 1048576
  9.8 1.9 %constant_dynamic-update-slice_fusion = bf16[1024,512]{1,0:T(8,128)(2,1)} fusion(bf16[1024,512]{1,0:T(8,128)(2,1)} %constant_dynamic-update-slice_fusion.1, bf16[512,512]{1,0:T(8,128)(2,1)} %v_ref.3), kind=kLoop, calls=%fused_computation.17 | loop fusion | bytes 1048576 | tf_op jit(solution)/shard_map/concatenate | solution.py:210
  11.7 4.9 %collective-permute-start = (bf16[1024,512]{1,0:T(8,128)(2,1)}, bf16[1024,512]{1,0:T(8,128)(2,1)S(1)}, u32[]{:S(2)}, u32[]{:S(2)}) collective-permute-start(bf16[1024,512]{1,0:T(8,128)(2,1)} %constant_dynamic-update-slice_fusion), channel_id=1, source_target_pairs={{0,4},{4,8},{8,12},{12,16},{16,20},{20,24},{24,28},{1,5},{5,9},{9,... | collective-permute-start | bytes 3145736 | tf_op jit(solution)/shard_map/ppermute | solution.py:23
  16.6 4.4 %collective-permute-start.1 = (bf16[1024,512]{1,0:T(8,128)(2,1)}, bf16[1024,512]{1,0:T(8,128)(2,1)}, u32[]{:S(2)}, u32[]{:S(2)}) collective-permute-start(bf16[1024,512]{1,0:T(8,128)(2,1)} %constant_dynamic-update-slice_fusion), channel_id=1, source_target_pairs={{0,8},{4,12},{8,16},{12,20},{16,24},{20,28},{1,9},{5,13},{9,17},{1... | collective-permute-start | bytes 3145736 | tf_op jit(solution)/shard_map/ppermute | solution.py:23
  21.1 1.3 collective-permute-start.3
  22.4 1.3 collective-permute-start.4
  23.7 1.3 collective-permute-start.5
  25.0 0.0 copy-done.2
  25.0 2.5 %copy.17 = bf16[512,2048]{0,1:T(8,128)(2,1)} copy(bf16[512,2048]{1,0:T(8,128)(2,1)S(1)} %copy-done.2) | data formatting | bytes 4194304 | tf_op args[3]
  27.5 0.0 copy-start.4
  27.5 0.0 copy-start
  27.5 3.7 %all-to-all-start = ((bf16[512,4,512]{0,2,1:T(8,128)(2,1)}), bf16[512,4,512]{0,2,1:T(8,128)(2,1)S(1)}, u32[]{:S(2)}, u32[]{:S(2)}) async-start(bf16[512,4,512]{0,2,1:T(8,128)(2,1)} %bitcast.38), calls=%async_computation | async-start | bytes 4194304 | tf_op jit(solution)/shard_map/all_to_all | solution.py:222
  31.2 0.0 all-gather.5.cloned.1.call-start
  31.3 0.0 copy-done.4
  31.3 0.6 gather_fusion.5
  32.0 0.6 gather_fusion.4
  32.6 0.6 gather_fusion.3
  33.3 0.0 copy-done
  33.3 0.6 gather_fusion.2
  34.0 0.1 and_bitcast_fusion.6
  34.1 0.1 constant_dynamic-slice_fusion
  34.2 0.1 copy.15
  34.3 0.6 reshape.56.valid_ref
  34.9 1.5 collective-permute-done.3.rest_0_
  36.4 21.5 %collective-permute-start.2 = (bf16[1024,512]{1,0:T(8,128)(2,1)}, bf16[1024,512]{1,0:T(8,128)(2,1)}, u32[]{:S(2)}, u32[]{:S(2)}) collective-permute-start(bf16[1024,512]{1,0:T(8,128)(2,1)} %constant_dynamic-update-slice_fusion), channel_id=1, source_target_pairs={{0,16},{4,20},{8,24},{12,28},{1,17},{5,21},{9,25},{13,29},{2,18},{... | collective-permute-start | bytes 3145736 | tf_op jit(solution)/shard_map/ppermute | solution.py:23
  57.9 0.6 gather_fusion.1
  58.5 0.0 all-gather.3.cloned.1.call-done
  58.5 4.3 %convolution_convert_fusion.1.g_ref = bf16[512,512]{1,0:T(8,128)(2,1)} fusion(bf16[512,2048]{1,0:T(8,128)(2,1)} %all-gather.3.cloned.1.call-done, bf16[512,2048]{1,0:T(8,128)(2,1)} %param.12), kind=kOutput, calls=%fused_computation.7 | convolution fusion | flops 1074003968 | bytes 4718592 | tf_op jit(solution)/shard_map/dot_general | solution.py:214
  62.8 0.0 collective-permute-done.4.rest_3_
  62.8 1.3 collective-permute-start.6
  64.1 8.8 %collective-permute-done.5.rest_6_ = bf16[512,512]{1,0:T(8,128)(2,1)} collective-permute-done((bf16[512,512]{1,0:T(8,128)(2,1)}, bf16[512,512]{1,0:T(8,128)(2,1)}, u32[]{:S(2)}, u32[]{:S(2)}) %collective-permute-start.5) | collective-permute-done | bytes 524320 | tf_op jit(solution)/shard_map/ppermute | solution.py:23
  72.9 1.3 collective-permute-start.7
  74.2 0.0 collective-permute-done.rest_0_.rest_1_
  74.2 0.0 copy-start.1
  74.2 1.3 collective-permute-start.8
  75.5 0.6 gather_fusion
  76.2 0.1 copy.16
  76.3 0.7 reshape.57.valid_ref
  77.0 0.0 all-to-all-done
  77.0 2.4 %copy.18 = bf16[4,512,512]{2,1,0:T(8,128)(2,1)} copy(bf16[4,512,512]{1,2,0:T(8,128)(2,1)S(1)} %bitcast.37) | data formatting | bytes 4194304 | tf_op jit(solution)/shard_map/all_to_all | solution.py:222
  79.4 0.0 copy-done.1
  79.4 0.0 collective-permute-done.1.rest_2_.rest_3_
  79.4 0.5 collective-permute-done.2.rest_4_.rest_5_
  79.8 0.0 collective-permute-done.6.rest_1_
  79.8 13.8 %collective-permute-done.7.rest_4_ = bf16[512,512]{1,0:T(8,128)(2,1)} collective-permute-done((bf16[512,512]{1,0:T(8,128)(2,1)}, bf16[512,512]{1,0:T(8,128)(2,1)}, u32[]{:S(2)}, u32[]{:S(2)}) %collective-permute-start.7) | collective-permute-done | bytes 524320 | tf_op jit(solution)/shard_map/ppermute | solution.py:23
  93.6 22.5 %collective-permute-done.8.rest_7_ = bf16[512,512]{1,0:T(8,128)(2,1)} collective-permute-done((bf16[512,512]{1,0:T(8,128)(2,1)}, bf16[512,512]{1,0:T(8,128)(2,1)}, u32[]{:S(2)}, u32[]{:S(2)}) %collective-permute-start.8) | collective-permute-done | bytes 524320 | tf_op jit(solution)/shard_map/ppermute | solution.py:23
  116.1 15.2 %query_side.1 = (bf16[512,512]{1,0:T(8,128)(2,1)}, bf16[512,512]{1,0:T(8,128)(2,1)}, f32[2,4,4,128]{3,2,1,0:T(4,128)}) custom-call(s32[28]{0:T(128)} %reshape.56.valid_ref, bf16[512,512]{1,0:T(8,128)(2,1)} %q_ref.3, bf16[512,512]{1,0:T(8,128)(2,1)} %convolution_convert_fusion.1.g_ref, bf16[512,512]{1,0:T(8,128)(2,1)} %k_ref.3, bf16[512,512]{1,0:T(8,128)(2,1)} %v_ref.3, ...), custom_call_target="tpu_custom_call" | custom-call | tf_op jit(solution)/shard_map/query_side/pallas_call | solution.py:144
  131.3 0.0 all-gather.5.cloned.1.call-update
  131.4 1.4 broadcast_in_dim.5
  132.8 3.4 %all-to-all-start.1 = ((f32[8,2,4,4,128]{4,3,2,1,0:T(4,128)}), f32[8,2,4,4,128]{4,3,2,1,0:T(4,128)S(1)}, u32[]{:S(2)}, u32[]{:S(2)}) async-start(f32[8,2,4,4,128]{4,3,2,1,0:T(4,128)} %broadcast_in_dim.5), calls=%async_computation.1 | async-start | bytes 262144 | tf_op jit(solution)/shard_map/all_to_all | solution.py:236
  136.2 7.3 %all-to-all-done.1 = f32[8,2,4,4,128]{4,3,2,1,0:T(4,128)S(1)} async-done(((f32[8,2,4,4,128]{4,3,2,1,0:T(4,128)}), f32[8,2,4,4,128]{4,3,2,1,0:T(4,128)S(1)}, u32[]{:S(2)}, u32[]{:S(2)}) %all-to-all-start.1) | async-done | bytes 131104 | tf_op jit(solution)/shard_map/all_to_all | solution.py:236
  143.4 0.6 dynamic-slice_bitcast_fusion
  144.1 0.0 copy-start.3
  144.1 10.8 %key_side.1 = (bf16[512,512]{1,0:T(8,128)(2,1)}, bf16[512,512]{1,0:T(8,128)(2,1)}) custom-call(s32[28]{0:T(128)} %reshape.57.valid_ref, bf16[512,512]{1,0:T(8,128)(2,1)} %k_ref.3, bf16[512,512]{1,0:T(8,128)(2,1)} %v_ref.3, bf16[512,512]{1,0:T(8,128)(2,1)} %q_ref.3, bf16[512,512]{1,0:T(8,128)(2,1)} %convolution_convert_fusion.1.g_ref, ...), custom_call_target="tpu_custom_call" | custom-call | tf_op jit(solution)/shard_map/key_side/pallas_call | solution.py:169
  154.8 0.0 all-gather.5.cloned.1.call-done
  154.9 0.0 copy-done.3
  154.9 3.6 %convolution_convert_fusion = bf16[512,512]{1,0:T(8,128)(2,1)} fusion(bf16[512,2048]{1,0:T(8,128)(2,1)} %all-gather.5.cloned.1.call-done, bf16[2048,512]{1,0:T(8,128)(2,1)S(1)} %bitcast.39), kind=kOutput, calls=%fused_computation.6 | convolution fusion | flops 1074003968 | bytes 4718592 | tf_op jit(solution)/shard_map/dot_general | solution.py:230
  (21 shorter events, 0.2 us)
Async XLA Ops:
  7.2 17.8 %copy-start.2 = (bf16[512,2048]{1,0:T(8,128)(2,1)S(1)}, bf16[512,2048]{1,0:T(8,128)(2,1)}, u32[]{:S(2)}) copy-start(bf16[512,2048]{1,0:T(8,128)(2,1)} %param.12) | copy-start | bytes 6291460
  7.2 51.4 %all-gather.3.cloned.1.call-start = ((), (), s32[]{:S(2)}) async-start(), calls=%async_computation.2 | async-start | bytes 2621440 | tf_op jit(solution)/shard_map/all_gather | solution.py:215
  11.7 62.4 %collective-permute-start = (bf16[1024,512]{1,0:T(8,128)(2,1)}, bf16[1024,512]{1,0:T(8,128)(2,1)S(1)}, u32[]{:S(2)}, u32[]{:S(2)}) collective-permute-start(bf16[1024,512]{1,0:T(8,128)(2,1)} %constant_dynamic-update-slice_fusion), channel_id=1, source_target_pairs={{0,4},{4,8},{8,12},{12,16},{16,20},{20,24},{24,28},{1,5},{5,9},{9,... | collective-permute-start | bytes 3145736 | tf_op jit(solution)/shard_map/ppermute | solution.py:23
  16.6 62.7 %collective-permute-start.1 = (bf16[1024,512]{1,0:T(8,128)(2,1)}, bf16[1024,512]{1,0:T(8,128)(2,1)}, u32[]{:S(2)}, u32[]{:S(2)}) collective-permute-start(bf16[1024,512]{1,0:T(8,128)(2,1)} %constant_dynamic-update-slice_fusion), channel_id=1, source_target_pairs={{0,8},{4,12},{8,16},{12,20},{16,24},{20,28},{1,9},{5,13},{9,17},{1... | collective-permute-start | bytes 3145736 | tf_op jit(solution)/shard_map/ppermute | solution.py:23
  21.1 15.3 %collective-permute-start.3 = (bf16[512,512]{1,0:T(8,128)(2,1)}, bf16[512,512]{1,0:T(8,128)(2,1)}, u32[]{:S(2)}, u32[]{:S(2)}) collective-permute-start(bf16[512,512]{1,0:T(8,128)(2,1)} %q_ref.3), channel_id=1, source_target_pairs={{4,0},{8,4},{12,8},{16,12},{20,16},{24,20},{28,24},{5,1},{9,5},{13... | collective-permute-start | bytes 1572872 | tf_op jit(solution)/shard_map/ppermute | solution.py:23
  22.4 40.5 %collective-permute-start.4 = (bf16[512,512]{1,0:T(8,128)(2,1)}, bf16[512,512]{1,0:T(8,128)(2,1)}, u32[]{:S(2)}, u32[]{:S(2)}) collective-permute-start(bf16[512,512]{1,0:T(8,128)(2,1)} %q_ref.3), channel_id=1, source_target_pairs={{8,0},{12,4},{16,8},{20,12},{24,16},{28,20},{9,1},{13,5},{17,9},{2... | collective-permute-start | bytes 1572872 | tf_op jit(solution)/shard_map/ppermute | solution.py:23
  23.7 49.2 %collective-permute-start.5 = (bf16[512,512]{1,0:T(8,128)(2,1)}, bf16[512,512]{1,0:T(8,128)(2,1)}, u32[]{:S(2)}, u32[]{:S(2)}) collective-permute-start(bf16[512,512]{1,0:T(8,128)(2,1)} %q_ref.3), channel_id=1, source_target_pairs={{16,0},{20,4},{24,8},{28,12},{17,1},{21,5},{25,9},{29,13},{18,2},{... | collective-permute-start | bytes 1572872 | tf_op jit(solution)/shard_map/ppermute | solution.py:23
  27.5 3.8 %copy-start.4 = (s32[32,5]{0,1:T(8,128)S(1)}, s32[32,5]{0,1:T(8,128)}, u32[]{:S(2)}) copy-start(s32[32,5]{0,1:T(8,128)} %param.15) | copy-start | bytes 1924
  27.5 5.8 %copy-start = (s32[32]{0:T(128)S(1)}, s32[32]{0:T(128)}, u32[]{:S(2)}) copy-start(s32[32]{0:T(128)} %param.14) | copy-start | bytes 388
  27.5 49.5 %all-to-all-start = ((bf16[512,4,512]{0,2,1:T(8,128)(2,1)}), bf16[512,4,512]{0,2,1:T(8,128)(2,1)S(1)}, u32[]{:S(2)}, u32[]{:S(2)}) async-start(bf16[512,4,512]{0,2,1:T(8,128)(2,1)} %bitcast.38), calls=%async_computation | async-start | bytes 4194304 | tf_op jit(solution)/shard_map/all_to_all | solution.py:222
  31.2 123.6 %all-gather.5.cloned.1.call-start = ((), (), s32[]{:S(2)}) async-start(), calls=%async_computation.3 | async-start | bytes 2621440 | tf_op jit(solution)/shard_map/all_gather | solution.py:231
  36.4 43.5 %collective-permute-start.2 = (bf16[1024,512]{1,0:T(8,128)(2,1)}, bf16[1024,512]{1,0:T(8,128)(2,1)}, u32[]{:S(2)}, u32[]{:S(2)}) collective-permute-start(bf16[1024,512]{1,0:T(8,128)(2,1)} %constant_dynamic-update-slice_fusion), channel_id=1, source_target_pairs={{0,16},{4,20},{8,24},{12,28},{1,17},{5,21},{9,25},{13,29},{2,18},{... | collective-permute-start | bytes 3145736 | tf_op jit(solution)/shard_map/ppermute | solution.py:23
  62.8 17.0 %collective-permute-start.6 = (bf16[512,512]{1,0:T(8,128)(2,1)}, bf16[512,512]{1,0:T(8,128)(2,1)}, u32[]{:S(2)}, u32[]{:S(2)}) collective-permute-start(bf16[512,512]{1,0:T(8,128)(2,1)} %convolution_convert_fusion.1.g_ref), channel_id=1, source_target_pairs={{4,0},{8,4},{12,8},{16,12},{20,16},{24,20},{28,24},{5,1},{9,5},{13... | collective-permute-start | bytes 1572872 | tf_op jit(solution)/shard_map/ppermute | solution.py:23
  72.9 20.7 %collective-permute-start.7 = (bf16[512,512]{1,0:T(8,128)(2,1)}, bf16[512,512]{1,0:T(8,128)(2,1)}, u32[]{:S(2)}, u32[]{:S(2)}) collective-permute-start(bf16[512,512]{1,0:T(8,128)(2,1)} %convolution_convert_fusion.1.g_ref), channel_id=1, source_target_pairs={{8,0},{12,4},{16,8},{20,12},{24,16},{28,20},{9,1},{13,5},{17,9},{2... | collective-permute-start | bytes 1572872 | tf_op jit(solution)/shard_map/ppermute | solution.py:23
  74.2 5.2 %copy-start.1 = (bf16[1024,512]{1,0:T(8,128)(2,1)}, bf16[1024,512]{1,0:T(8,128)(2,1)S(1)}, u32[]{:S(2)}) copy-start(bf16[1024,512]{1,0:T(8,128)(2,1)S(1)} %collective-permute-done.rest_0_.rest_1_) | copy-start | bytes 3145732
  74.2 41.9 %collective-permute-start.8 = (bf16[512,512]{1,0:T(8,128)(2,1)}, bf16[512,512]{1,0:T(8,128)(2,1)}, u32[]{:S(2)}, u32[]{:S(2)}) collective-permute-start(bf16[512,512]{1,0:T(8,128)(2,1)} %convolution_convert_fusion.1.g_ref), channel_id=1, source_target_pairs={{16,0},{20,4},{24,8},{28,12},{17,1},{21,5},{25,9},{29,13},{18,2},{... | collective-permute-start | bytes 1572872 | tf_op jit(solution)/shard_map/ppermute | solution.py:23
  132.8 10.7 %all-to-all-start.1 = ((f32[8,2,4,4,128]{4,3,2,1,0:T(4,128)}), f32[8,2,4,4,128]{4,3,2,1,0:T(4,128)S(1)}, u32[]{:S(2)}, u32[]{:S(2)}) async-start(f32[8,2,4,4,128]{4,3,2,1,0:T(4,128)} %broadcast_in_dim.5), calls=%async_computation.1 | async-start | bytes 262144 | tf_op jit(solution)/shard_map/all_to_all | solution.py:236
  144.1 10.8 %copy-start.3 = (bf16[4,512,512]{2,1,0:T(8,128)(2,1)S(1)}, bf16[4,512,512]{2,1,0:T(8,128)(2,1)}, u32[]{:S(2)}) copy-start(bf16[4,512,512]{2,1,0:T(8,128)(2,1)} %copy.18) | copy-start | bytes 6291460
Sparse Core Ops, SparseCore 0:
  9.6 25.2 all-gather.2
  131.5 19.8 all-gather.4

commit v11 on v7

--- a/solution.py
+++ b/solution.py
@@ -257,7 +257,13 @@
         preferred_element_type=jnp.float32,
     ).astype(jnp.bfloat16)
 
-    st_from = [passed_along(stats, "ctx", -(2**m)) for m in levels]
+    every = lax.all_to_all(
+        jnp.broadcast_to(stats[None], (ctx_count,) + stats.shape), "ctx", 0, 0, tiled=False
+    )
+    st_from = [
+        lax.dynamic_index_in_dim(every, jnp.minimum(ctx_index + 2**m, ctx_count - 1), 0, False)
+        for m in levels
+    ]
     key_grad, value_grad = key_call(
         valid_k, keys, values, queries, g, stats, q_from, g_from, st_from, heads_local, n_levels
     )

time: 165 us -> 163 us (0.988); the launches traced: 162 us -> 162 us
    ppermute x12 -> x9, starting transfers between devices: 40.7 us -> 36.8 us  [passed_along(): return lax.ppermute(block, axis, route)]
    all_to_all x0 -> x1, starting transfers between devices: none -> 3.38 us  [local(): lax.all_to_all(jnp.broadcast_to(stats[None], (ctx_count,) + stats.shape),...]
    unnamed x20 -> x14, local copies, waits for them, and re-layouts: 7.08 us -> 5.88 us
    ppermute x12 -> x9, waiting for transfers between devices: 44.7 us -> 44.6 us  [passed_along(): return lax.ppermute(block, axis, route)]
  transfers between devices with their start and end apart: 15 -> 13, of which waited for: 3 -> 3; matrix products, arithmetic and copies ran while one was open for 13% -> 15% of each run, Pallas kernels for 12% -> 12%
where the time goes in v11:
time: 163 us; the launch traced here: 162 us
  waiting for transfers between devices  45.4 us (28%)
  starting transfers between devices  44.8 us (27%)
  Pallas kernels  30.2 us (19%)
  local copies, waits for them, and re-layouts  19.4 us (12%)
  between operations  14.3 us (9%)
  matrix products  7.93 us (5%)
    ppermute x9, waiting for transfers between devices, passed_along(): return lax.ppermute(block, axis, route)  44.6 us
    ppermute x9, starting transfers between devices, passed_along(): return lax.ppermute(block, axis, route)  36.8 us
    pallas_call x2, Pallas kernels, query_call(): pl.pallas_call(functools.partial(kernel, n_levels), grid_spec=grid_spec,...  19.4 us
    pallas_call x1, Pallas kernels, key_call(): pl.pallas_call(functools.partial(key_kernel, n_levels), grid_spec=grid_sp...  10.8 us
    unnamed x14, local copies, waits for them, and re-layouts  5.88 us
    all_to_all x1, starting transfers between devices, local(): weight_cols = lax.all_to_all(out_weight, 'head', 1, 0, tiled=True)  4.59 us
    dot_general x1, matrix products, local(): lax.dot_general(lax.all_gather(d_out, 'head', axis=1, tiled=True), out_we...  4.3 us
    all_to_all x1, local copies, waits for them, and re-layouts, local(): weight_cols = lax.all_to_all(out_weight, 'head', 1, 0, tiled=True)  4.12 us
  transfers between devices with their start and end apart: 13, of which 3 were waited for; matrix products, arithmetic and copies ran while one was open for 15% of the time, Pallas kernels for 12%

profile of v11, /device:TPU:0, one launch (start us, length us, event | category | flops | bytes accessed | tf_op | source)
XLA Modules:
  0.0 162.3 jit_solution(2883553795829646235)
XLA Ops:
  7.2 0.0 all-gather.3.cloned.1.call-start
  7.2 0.7 all-gather.3.cloned.1.call-update
  7.9 1.9 %constant_dynamic-update-slice_fusion.1 = bf16[1024,512]{1,0:T(8,128)(2,1)} fusion(bf16[512,512]{1,0:T(8,128)(2,1)} %k_ref.5), kind=kLoop, calls=%fused_computation.18 | loop fusion | bytes 1048576
  9.8 1.9 %constant_dynamic-update-slice_fusion = bf16[1024,512]{1,0:T(8,128)(2,1)} fusion(bf16[1024,512]{1,0:T(8,128)(2,1)} %constant_dynamic-update-slice_fusion.1, bf16[512,512]{1,0:T(8,128)(2,1)} %v_ref.5), kind=kLoop, calls=%fused_computation.17 | loop fusion | bytes 1048576 | tf_op jit(solution)/shard_map/concatenate | solution.py:227
  11.7 4.9 %collective-permute-start = (bf16[1024,512]{1,0:T(8,128)(2,1)}, bf16[1024,512]{1,0:T(8,128)(2,1)S(1)}, u32[]{:S(2)}, u32[]{:S(2)}) collective-permute-start(bf16[1024,512]{1,0:T(8,128)(2,1)} %constant_dynamic-update-slice_fusion), channel_id=1, source_target_pairs={{0,4},{4,8},{8,12},{12,16},{16,20},{20,24},{24,28},{1,5},{5,9},{9,... | collective-permute-start | bytes 3145736 | tf_op jit(solution)/shard_map/ppermute | solution.py:23
  16.6 3.5 %collective-permute-start.1 = (bf16[1024,512]{1,0:T(8,128)(2,1)}, bf16[1024,512]{1,0:T(8,128)(2,1)S(1)}, u32[]{:S(2)}, u32[]{:S(2)}) collective-permute-start(bf16[1024,512]{1,0:T(8,128)(2,1)} %constant_dynamic-update-slice_fusion), channel_id=1, source_target_pairs={{0,8},{4,12},{8,16},{12,20},{16,24},{20,28},{1,9},{5,13},{9,17},{1... | collective-permute-start | bytes 3145736 | tf_op jit(solution)/shard_map/ppermute | solution.py:23
  20.1 1.3 collective-permute-start.3
  21.4 1.3 collective-permute-start.4
  22.7 1.3 collective-permute-start.5
  24.0 4.0 %copy.17 = bf16[512,2048]{0,1:T(8,128)(2,1)} copy(bf16[512,2048]{1,0:T(8,128)(2,1)} %param.12) | data formatting | bytes 4194304 | tf_op args[3]
  28.0 0.0 copy-start.5
  28.0 0.0 copy-start
  28.0 4.6 %all-to-all-start = ((bf16[512,4,512]{0,2,1:T(8,128)(2,1)}), bf16[512,4,512]{0,2,1:T(8,128)(2,1)}, u32[]{:S(2)}, u32[]{:S(2)}) async-start(bf16[512,4,512]{0,2,1:T(8,128)(2,1)} %bitcast.37), calls=%async_computation | async-start | bytes 4194304 | tf_op jit(solution)/shard_map/all_to_all | solution.py:239
  32.6 0.0 all-gather.5.cloned.1.call-start
  32.7 0.0 copy-done.5
  32.7 0.6 gather_fusion.5
  33.3 0.6 gather_fusion.4
  34.0 0.6 gather_fusion.3
  34.6 0.0 copy-done
  34.6 0.6 gather_fusion.2
  35.3 0.1 and_bitcast_fusion.6
  35.4 0.1 constant_dynamic-slice_fusion
  35.6 0.1 copy.15
  35.7 0.6 reshape.56.valid_ref
  36.3 0.0 collective-permute-done.3.rest_0_
  36.3 20.7 %collective-permute-start.2 = (bf16[1024,512]{1,0:T(8,128)(2,1)}, bf16[1024,512]{1,0:T(8,128)(2,1)S(1)}, u32[]{:S(2)}, u32[]{:S(2)}) collective-permute-start(bf16[1024,512]{1,0:T(8,128)(2,1)} %constant_dynamic-update-slice_fusion), channel_id=1, source_target_pairs={{0,16},{4,20},{8,24},{12,28},{1,17},{5,21},{9,25},{13,29},{2,18},{... | collective-permute-start | bytes 3145736 | tf_op jit(solution)/shard_map/ppermute | solution.py:23
  57.0 0.6 gather_fusion.1
  57.6 0.0 all-gather.3.cloned.1.call-done
  57.6 4.3 %convolution_convert_fusion.1.g_ref = bf16[512,512]{1,0:T(8,128)(2,1)} fusion(bf16[512,2048]{1,0:T(8,128)(2,1)} %all-gather.3.cloned.1.call-done, bf16[512,2048]{1,0:T(8,128)(2,1)} %param.12), kind=kOutput, calls=%fused_computation.7 | convolution fusion | flops 1074003968 | bytes 4718592 | tf_op jit(solution)/shard_map/dot_general | solution.py:231
  61.9 0.0 collective-permute-done.4.rest_3_
  61.9 1.3 collective-permute-start.6
  63.2 9.7 %collective-permute-done.5.rest_6_ = bf16[512,512]{1,0:T(8,128)(2,1)} collective-permute-done((bf16[512,512]{1,0:T(8,128)(2,1)}, bf16[512,512]{1,0:T(8,128)(2,1)}, u32[]{:S(2)}, u32[]{:S(2)}) %collective-permute-start.5) | collective-permute-done | bytes 524320 | tf_op jit(solution)/shard_map/ppermute | solution.py:23
  72.9 1.3 collective-permute-start.7
  74.2 0.0 collective-permute-done.rest_0_.rest_1_
  74.2 0.0 copy-start.1
  74.2 1.3 collective-permute-start.8
  75.5 0.6 gather_fusion
  76.2 0.1 copy.16
  76.3 0.7 reshape.57.valid_ref
  77.0 0.0 all-to-all-done
  77.0 4.1 %copy.18 = bf16[4,512,512]{2,1,0:T(8,128)(2,1)} copy(bf16[4,512,512]{1,2,0:T(8,128)(2,1)} %bitcast.13) | data formatting | bytes 4194304 | tf_op jit(solution)/shard_map/all_to_all | solution.py:239
  81.1 0.0 copy-done.1
  81.1 0.0 collective-permute-done.1.rest_2_.rest_3_
  81.1 0.0 copy-start.2
  81.1 0.0 collective-permute-done.2.rest_4_.rest_5_
  81.1 0.0 copy-start.3
  81.2 0.0 collective-permute-done.6.rest_1_
  81.2 12.4 %collective-permute-done.7.rest_4_ = bf16[512,512]{1,0:T(8,128)(2,1)} collective-permute-done((bf16[512,512]{1,0:T(8,128)(2,1)}, bf16[512,512]{1,0:T(8,128)(2,1)}, u32[]{:S(2)}, u32[]{:S(2)}) %collective-permute-start.7) | collective-permute-done | bytes 524320 | tf_op jit(solution)/shard_map/ppermute | solution.py:23
  93.6 22.5 %collective-permute-done.8.rest_7_ = bf16[512,512]{1,0:T(8,128)(2,1)} collective-permute-done((bf16[512,512]{1,0:T(8,128)(2,1)}, bf16[512,512]{1,0:T(8,128)(2,1)}, u32[]{:S(2)}, u32[]{:S(2)}) %collective-permute-start.8) | collective-permute-done | bytes 524320 | tf_op jit(solution)/shard_map/ppermute | solution.py:23
  116.1 0.0 copy-done.2
  116.1 0.0 copy-done.3
  116.1 11.1 %query_forward.1 = (bf16[512,512]{1,0:T(8,128)(2,1)}, f32[2,4,4,128]{3,2,1,0:T(4,128)}) custom-call(s32[28]{0:T(128)} %reshape.56.valid_ref, bf16[512,512]{1,0:T(8,128)(2,1)} %q_ref.5, bf16[512,512]{1,0:T(8,128)(2,1)} %convolution_convert_fusion.1.g_ref, bf16[512,512]{1,0:T(8,128)(2,1)} %k_ref.5, bf16[512,512]{1,0:T(8,128)(2,1)} %v_ref.5, ...), custom_call_target="tpu_custom_call" | custom-call | tf_op jit(solution)/shard_map/query_forward/pallas_call | solution.py:165
  127.2 0.0 all-gather.5.cloned.1.call-update
  127.2 1.4 broadcast_in_dim.5
  128.6 3.4 %all-to-all-start.1 = ((f32[8,2,4,4,128]{4,3,2,1,0:T(4,128)}), f32[8,2,4,4,128]{4,3,2,1,0:T(4,128)S(1)}, u32[]{:S(2)}, u32[]{:S(2)}) async-start(f32[8,2,4,4,128]{4,3,2,1,0:T(4,128)} %broadcast_in_dim.5), calls=%async_computation.1 | async-start | bytes 262144 | tf_op jit(solution)/shard_map/all_to_all | solution.py:260
  132.0 8.4 %query_backward.1 = bf16[512,512]{1,0:T(8,128)(2,1)} custom-call(s32[28]{0:T(128)} %reshape.56.valid_ref, bf16[512,512]{1,0:T(8,128)(2,1)} %q_ref.5, bf16[512,512]{1,0:T(8,128)(2,1)} %convolution_convert_fusion.1.g_ref, bf16[512,512]{1,0:T(8,128)(2,1)} %k_ref.5, bf16[512,512]{1,0:T(8,128)(2,1)} %v_ref.5, f32[2,4,4,128]{3,2,1,0:T(4,128)} %get-tuple-element.27.st_ref, ...), custom_call_target="tpu_custom_call" | custom-call | tf_op jit(solution)/shard_map/query_backward/pallas_call | solution.py:165
  140.3 0.0 all-to-all-done.1
  140.3 0.6 dynamic-slice_bitcast_fusion
  141.0 0.0 copy-start.4
  141.0 10.8 %key_side.1 = (bf16[512,512]{1,0:T(8,128)(2,1)}, bf16[512,512]{1,0:T(8,128)(2,1)}) custom-call(s32[28]{0:T(128)} %reshape.57.valid_ref, bf16[512,512]{1,0:T(8,128)(2,1)} %k_ref.5, bf16[512,512]{1,0:T(8,128)(2,1)} %v_ref.5, bf16[512,512]{1,0:T(8,128)(2,1)} %q_ref.5, bf16[512,512]{1,0:T(8,128)(2,1)} %convolution_convert_fusion.1.g_ref, ...), custom_call_target="tpu_custom_call" | custom-call | tf_op jit(solution)/shard_map/key_side/pallas_call | solution.py:186
  151.8 0.0 all-gather.5.cloned.1.call-done
  151.8 0.0 copy-done.4
  151.8 3.6 %convolution_convert_fusion = bf16[512,512]{1,0:T(8,128)(2,1)} fusion(bf16[512,2048]{1,0:T(8,128)(2,1)} %all-gather.5.cloned.1.call-done, bf16[2048,512]{1,0:T(8,128)(2,1)S(1)} %bitcast.38), kind=kOutput, calls=%fused_computation.6 | convolution fusion | flops 1074003968 | bytes 4718592 | tf_op jit(solution)/shard_map/dot_general | solution.py:254
  (21 shorter events, 0.2 us)
Async XLA Ops:
  7.2 50.4 %all-gather.3.cloned.1.call-start = ((), (), s32[]{:S(2)}) async-start(), calls=%async_computation.2 | async-start | bytes 2621440 | tf_op jit(solution)/shard_map/all_gather | solution.py:232
  11.7 62.4 %collective-permute-start = (bf16[1024,512]{1,0:T(8,128)(2,1)}, bf16[1024,512]{1,0:T(8,128)(2,1)S(1)}, u32[]{:S(2)}, u32[]{:S(2)}) collective-permute-start(bf16[1024,512]{1,0:T(8,128)(2,1)} %constant_dynamic-update-slice_fusion), channel_id=1, source_target_pairs={{0,4},{4,8},{8,12},{12,16},{16,20},{20,24},{24,28},{1,5},{5,9},{9,... | collective-permute-start | bytes 3145736 | tf_op jit(solution)/shard_map/ppermute | solution.py:23
  16.6 64.5 %collective-permute-start.1 = (bf16[1024,512]{1,0:T(8,128)(2,1)}, bf16[1024,512]{1,0:T(8,128)(2,1)S(1)}, u32[]{:S(2)}, u32[]{:S(2)}) collective-permute-start(bf16[1024,512]{1,0:T(8,128)(2,1)} %constant_dynamic-update-slice_fusion), channel_id=1, source_target_pairs={{0,8},{4,12},{8,16},{12,20},{16,24},{20,28},{1,9},{5,13},{9,17},{1... | collective-permute-start | bytes 3145736 | tf_op jit(solution)/shard_map/ppermute | solution.py:23
  20.1 16.1 %collective-permute-start.3 = (bf16[512,512]{1,0:T(8,128)(2,1)}, bf16[512,512]{1,0:T(8,128)(2,1)}, u32[]{:S(2)}, u32[]{:S(2)}) collective-permute-start(bf16[512,512]{1,0:T(8,128)(2,1)} %q_ref.5), channel_id=1, source_target_pairs={{4,0},{8,4},{12,8},{16,12},{20,16},{24,20},{28,24},{5,1},{9,5},{13... | collective-permute-start | bytes 1572872 | tf_op jit(solution)/shard_map/ppermute | solution.py:23
  21.4 40.5 %collective-permute-start.4 = (bf16[512,512]{1,0:T(8,128)(2,1)}, bf16[512,512]{1,0:T(8,128)(2,1)}, u32[]{:S(2)}, u32[]{:S(2)}) collective-permute-start(bf16[512,512]{1,0:T(8,128)(2,1)} %q_ref.5), channel_id=1, source_target_pairs={{8,0},{12,4},{16,8},{20,12},{24,16},{28,20},{9,1},{13,5},{17,9},{2... | collective-permute-start | bytes 1572872 | tf_op jit(solution)/shard_map/ppermute | solution.py:23
  22.7 50.2 %collective-permute-start.5 = (bf16[512,512]{1,0:T(8,128)(2,1)}, bf16[512,512]{1,0:T(8,128)(2,1)}, u32[]{:S(2)}, u32[]{:S(2)}) collective-permute-start(bf16[512,512]{1,0:T(8,128)(2,1)} %q_ref.5), channel_id=1, source_target_pairs={{16,0},{20,4},{24,8},{28,12},{17,1},{21,5},{25,9},{29,13},{18,2},{... | collective-permute-start | bytes 1572872 | tf_op jit(solution)/shard_map/ppermute | solution.py:23
  28.0 4.7 %copy-start.5 = (s32[32,5]{0,1:T(8,128)S(1)}, s32[32,5]{0,1:T(8,128)}, u32[]{:S(2)}) copy-start(s32[32,5]{0,1:T(8,128)} %param.15) | copy-start | bytes 1924
  28.0 6.7 %copy-start = (s32[32]{0:T(128)S(1)}, s32[32]{0:T(128)}, u32[]{:S(2)}) copy-start(s32[32]{0:T(128)} %param.14) | copy-start | bytes 388
  28.0 49.0 %all-to-all-start = ((bf16[512,4,512]{0,2,1:T(8,128)(2,1)}), bf16[512,4,512]{0,2,1:T(8,128)(2,1)}, u32[]{:S(2)}, u32[]{:S(2)}) async-start(bf16[512,4,512]{0,2,1:T(8,128)(2,1)} %bitcast.37), calls=%async_computation | async-start | bytes 4194304 | tf_op jit(solution)/shard_map/all_to_all | solution.py:239
  32.6 119.2 %all-gather.5.cloned.1.call-start = ((), (), s32[]{:S(2)}) async-start(), calls=%async_computation.3 | async-start | bytes 2621440 | tf_op jit(solution)/shard_map/all_gather | solution.py:255
  36.3 44.9 %collective-permute-start.2 = (bf16[1024,512]{1,0:T(8,128)(2,1)}, bf16[1024,512]{1,0:T(8,128)(2,1)S(1)}, u32[]{:S(2)}, u32[]{:S(2)}) collective-permute-start(bf16[1024,512]{1,0:T(8,128)(2,1)} %constant_dynamic-update-slice_fusion), channel_id=1, source_target_pairs={{0,16},{4,20},{8,24},{12,28},{1,17},{5,21},{9,25},{13,29},{2,18},{... | collective-permute-start | bytes 3145736 | tf_op jit(solution)/shard_map/ppermute | solution.py:23
  61.9 19.2 %collective-permute-start.6 = (bf16[512,512]{1,0:T(8,128)(2,1)}, bf16[512,512]{1,0:T(8,128)(2,1)}, u32[]{:S(2)}, u32[]{:S(2)}) collective-permute-start(bf16[512,512]{1,0:T(8,128)(2,1)} %convolution_convert_fusion.1.g_ref), channel_id=1, source_target_pairs={{4,0},{8,4},{12,8},{16,12},{20,16},{24,20},{28,24},{5,1},{9,5},{13... | collective-permute-start | bytes 1572872 | tf_op jit(solution)/shard_map/ppermute | solution.py:23
  72.9 20.7 %collective-permute-start.7 = (bf16[512,512]{1,0:T(8,128)(2,1)}, bf16[512,512]{1,0:T(8,128)(2,1)}, u32[]{:S(2)}, u32[]{:S(2)}) collective-permute-start(bf16[512,512]{1,0:T(8,128)(2,1)} %convolution_convert_fusion.1.g_ref), channel_id=1, source_target_pairs={{8,0},{12,4},{16,8},{20,12},{24,16},{28,20},{9,1},{13,5},{17,9},{2... | collective-permute-start | bytes 1572872 | tf_op jit(solution)/shard_map/ppermute | solution.py:23
  74.2 6.9 %copy-start.1 = (bf16[1024,512]{1,0:T(8,128)(2,1)}, bf16[1024,512]{1,0:T(8,128)(2,1)S(1)}, u32[]{:S(2)}) copy-start(bf16[1024,512]{1,0:T(8,128)(2,1)S(1)} %collective-permute-done.rest_0_.rest_1_) | copy-start | bytes 3145732
  74.2 41.9 %collective-permute-start.8 = (bf16[512,512]{1,0:T(8,128)(2,1)}, bf16[512,512]{1,0:T(8,128)(2,1)}, u32[]{:S(2)}, u32[]{:S(2)}) collective-permute-start(bf16[512,512]{1,0:T(8,128)(2,1)} %convolution_convert_fusion.1.g_ref), channel_id=1, source_target_pairs={{16,0},{20,4},{24,8},{28,12},{17,1},{21,5},{25,9},{29,13},{18,2},{... | collective-permute-start | bytes 1572872 | tf_op jit(solution)/shard_map/ppermute | solution.py:23
  81.1 35.0 %copy-start.2 = (bf16[1024,512]{1,0:T(8,128)(2,1)}, bf16[1024,512]{1,0:T(8,128)(2,1)S(1)}, u32[]{:S(2)}) copy-start(bf16[1024,512]{1,0:T(8,128)(2,1)S(1)} %collective-permute-done.1.rest_2_.rest_3_) | copy-start | bytes 3145732
  81.1 35.0 %copy-start.3 = (bf16[1024,512]{1,0:T(8,128)(2,1)}, bf16[1024,512]{1,0:T(8,128)(2,1)S(1)}, u32[]{:S(2)}) copy-start(bf16[1024,512]{1,0:T(8,128)(2,1)S(1)} %collective-permute-done.2.rest_4_.rest_5_) | copy-start | bytes 3145732
  128.6 11.8 %all-to-all-start.1 = ((f32[8,2,4,4,128]{4,3,2,1,0:T(4,128)}), f32[8,2,4,4,128]{4,3,2,1,0:T(4,128)S(1)}, u32[]{:S(2)}, u32[]{:S(2)}) async-start(f32[8,2,4,4,128]{4,3,2,1,0:T(4,128)} %broadcast_in_dim.5), calls=%async_computation.1 | async-start | bytes 262144 | tf_op jit(solution)/shard_map/all_to_all | solution.py:260
  141.0 10.8 %copy-start.4 = (bf16[4,512,512]{2,1,0:T(8,128)(2,1)S(1)}, bf16[4,512,512]{2,1,0:T(8,128)(2,1)}, u32[]{:S(2)}) copy-start(bf16[4,512,512]{2,1,0:T(8,128)(2,1)} %copy.18) | copy-start | bytes 6291460
Sparse Core Ops, SparseCore 0:
  9.6 25.2 all-gather.2
  127.3 19.8 all-gather.4

commit v12 on v6

--- a/solution.py
+++ b/solution.py
@@ -73,9 +73,10 @@
         allowed = candidate_mask(valid_ref, n * n_cand, n_cand, diag)
         scores = jnp.where(allowed, dot_nt(qn, kcat) * scale, neg_large)
         row_max = scores.max(axis=1, keepdims=True)
-        row_total = jnp.sum(jnp.exp(scores - row_max), axis=1, keepdims=True)
+        shifted = jnp.exp(scores - row_max)
+        row_total = jnp.sum(shifted, axis=1, keepdims=True)
         log_total = row_max + jnp.log(row_total)
-        probs = jnp.exp(scores - log_total)
+        probs = shifted * (1.0 / row_total)
         att_b = dot_nn(probs.astype(jnp.bfloat16), vcat).astype(jnp.bfloat16)
         att_ref[rows, :] = att_b
         delta = jnp.sum(gn.astype(jnp.float32) * att_b.astype(jnp.float32), axis=1, keepdims=True)

time: 163 us -> 163 us (level)
  transfers between devices with their start and end apart: 15 -> 15, of which waited for: 8 -> 8; matrix products, arithmetic and copies ran while one was open for 11% -> 12% of each run, Pallas kernels for 7% -> 7%
where the time goes in v12:
time: 163 us; the launch traced here: 162 us
  waiting for transfers between devices  52.3 us (32%)
  starting transfers between devices  46.4 us (28%)
  Pallas kernels  25.6 us (16%)
  local copies, waits for them, and re-layouts  14.9 us (9%)
  between operations  14.3 us (9%)
  matrix products  7.93 us (5%)
    ppermute x12, waiting for transfers between devices, passed_along(): return lax.ppermute(block, axis, route)  51.6 us
    ppermute x12, starting transfers between devices, passed_along(): return lax.ppermute(block, axis, route)  42.6 us
    pallas_call x1, Pallas kernels, query_call(): pl.pallas_call(functools.partial(query_kernel, n_levels), grid_spec=grid_...  14.9 us
    pallas_call x1, Pallas kernels, key_call(): pl.pallas_call(functools.partial(key_kernel, n_levels), grid_spec=grid_sp...  10.6 us
    unnamed x18, local copies, waits for them, and re-layouts  5.24 us
    dot_general x1, matrix products, local(): lax.dot_general(lax.all_gather(d_out, 'head', axis=1, tiled=True), out_we...  4.3 us
    all_to_all x1, starting transfers between devices, local(): weight_cols = lax.all_to_all(out_weight, 'head', 1, 0, tiled=True)  3.74 us
    dot_general x1, matrix products, local(): jnp.dot(lax.all_gather(attended, 'head', axis=1, tiled=True), weight_cols...  3.63 us
  transfers between devices with their start and end apart: 15, of which 8 were waited for; matrix products, arithmetic and copies ran while one was open for 12% of the time, Pallas kernels for 7%

profile of v12, /device:TPU:0, one launch (start us, length us, event | category | flops | bytes accessed | tf_op | source)
XLA Modules:
  0.0 161.6 jit_solution(17970985517513530076)
XLA Ops:
  7.2 0.0 copy-start.2
  7.2 0.0 all-gather.3.cloned.1.call-start
  7.2 0.7 all-gather.3.cloned.1.call-update
  7.9 1.9 %constant_dynamic-update-slice_fusion.1 = bf16[1024,512]{1,0:T(8,128)(2,1)} fusion(bf16[512,512]{1,0:T(8,128)(2,1)} %k_ref.3), kind=kLoop, calls=%fused_computation.15 | loop fusion | bytes 1048576
  9.8 1.9 %constant_dynamic-update-slice_fusion = bf16[1024,512]{1,0:T(8,128)(2,1)} fusion(bf16[1024,512]{1,0:T(8,128)(2,1)} %constant_dynamic-update-slice_fusion.1, bf16[512,512]{1,0:T(8,128)(2,1)} %v_ref.3), kind=kLoop, calls=%fused_computation.14 | loop fusion | bytes 1048576 | tf_op jit(solution)/shard_map/concatenate | solution.py:211
  11.7 4.9 %collective-permute-start = (bf16[1024,512]{1,0:T(8,128)(2,1)}, bf16[1024,512]{1,0:T(8,128)(2,1)S(1)}, u32[]{:S(2)}, u32[]{:S(2)}) collective-permute-start(bf16[1024,512]{1,0:T(8,128)(2,1)} %constant_dynamic-update-slice_fusion), channel_id=1, source_target_pairs={{0,4},{4,8},{8,12},{12,16},{16,20},{20,24},{24,28},{1,5},{5,9},{9,... | collective-permute-start | bytes 3145736 | tf_op jit(solution)/shard_map/ppermute | solution.py:23
  16.6 4.5 %collective-permute-start.1 = (bf16[1024,512]{1,0:T(8,128)(2,1)}, bf16[1024,512]{1,0:T(8,128)(2,1)}, u32[]{:S(2)}, u32[]{:S(2)}) collective-permute-start(bf16[1024,512]{1,0:T(8,128)(2,1)} %constant_dynamic-update-slice_fusion), channel_id=1, source_target_pairs={{0,8},{4,12},{8,16},{12,20},{16,24},{20,28},{1,9},{5,13},{9,17},{1... | collective-permute-start | bytes 3145736 | tf_op jit(solution)/shard_map/ppermute | solution.py:23
  21.1 1.3 collective-permute-start.3
  22.4 1.3 collective-permute-start.4
  23.7 1.3 collective-permute-start.5
  25.0 0.0 copy-done.2
  25.0 2.5 %copy.17 = bf16[512,2048]{0,1:T(8,128)(2,1)} copy(bf16[512,2048]{1,0:T(8,128)(2,1)S(1)} %copy-done.2) | data formatting | bytes 4194304 | tf_op args[3]
  27.5 0.0 copy-start.7
  27.5 0.0 copy-start
  27.5 3.7 %all-to-all-start = ((bf16[512,4,512]{0,2,1:T(8,128)(2,1)}), bf16[512,4,512]{0,2,1:T(8,128)(2,1)S(1)}, u32[]{:S(2)}, u32[]{:S(2)}) async-start(bf16[512,4,512]{0,2,1:T(8,128)(2,1)} %bitcast.32), calls=%async_computation | async-start | bytes 4194304 | tf_op jit(solution)/shard_map/all_to_all | solution.py:223
  31.3 0.0 all-gather.5.cloned.1.call-start
  31.3 0.0 copy-done.7
  31.4 0.6 gather_fusion.5
  32.0 0.6 gather_fusion.4
  32.7 0.6 gather_fusion.3
  33.3 0.0 copy-done
  33.3 0.6 gather_fusion.2
  34.0 0.1 and_bitcast_fusion.6
  34.1 0.1 constant_dynamic-slice_fusion
  34.3 0.1 copy.15
  34.4 0.6 reshape.55.valid_ref
  34.9 1.5 collective-permute-done.3.rest_0_
  36.4 21.5 %collective-permute-start.2 = (bf16[1024,512]{1,0:T(8,128)(2,1)}, bf16[1024,512]{1,0:T(8,128)(2,1)}, u32[]{:S(2)}, u32[]{:S(2)}) collective-permute-start(bf16[1024,512]{1,0:T(8,128)(2,1)} %constant_dynamic-update-slice_fusion), channel_id=1, source_target_pairs={{0,16},{4,20},{8,24},{12,28},{1,17},{5,21},{9,25},{13,29},{2,18},{... | collective-permute-start | bytes 3145736 | tf_op jit(solution)/shard_map/ppermute | solution.py:23
  57.9 0.6 gather_fusion.1
  58.5 4.3 %convolution_convert_fusion.1.g_ref = bf16[512,512]{1,0:T(8,128)(2,1)} fusion(bf16[512,2048]{1,0:T(8,128)(2,1)} %all-gather.3.cloned.1.call-done, bf16[512,2048]{1,0:T(8,128)(2,1)} %param.12), kind=kOutput, calls=%fused_computation.7 | convolution fusion | flops 1074003968 | bytes 4718592 | tf_op jit(solution)/shard_map/dot_general | solution.py:215
  62.8 0.0 collective-permute-done.4.rest_3_
  62.8 1.3 collective-permute-start.6
  64.1 8.8 %collective-permute-done.5.rest_6_ = bf16[512,512]{1,0:T(8,128)(2,1)} collective-permute-done((bf16[512,512]{1,0:T(8,128)(2,1)}, bf16[512,512]{1,0:T(8,128)(2,1)}, u32[]{:S(2)}, u32[]{:S(2)}) %collective-permute-start.5) | collective-permute-done | bytes 524320 | tf_op jit(solution)/shard_map/ppermute | solution.py:23
  72.9 1.3 collective-permute-start.7
  74.2 0.0 collective-permute-done.rest_0_.rest_1_
  74.2 0.0 copy-start.1
  74.2 1.3 collective-permute-start.8
  75.5 0.6 gather_fusion
  76.2 0.1 copy.16
  76.3 0.6 reshape.56.valid_ref
  76.9 0.0 all-to-all-done
  76.9 2.4 %copy.18 = bf16[4,512,512]{2,1,0:T(8,128)(2,1)} copy(bf16[4,512,512]{1,2,0:T(8,128)(2,1)S(1)} %bitcast.31) | data formatting | bytes 4194304 | tf_op jit(solution)/shard_map/all_to_all | solution.py:223
  79.3 0.0 copy-done.1
  79.3 0.0 collective-permute-done.1.rest_2_.rest_3_
  79.3 0.5 collective-permute-done.2.rest_4_.rest_5_
  79.8 0.0 collective-permute-done.6.rest_1_
  79.8 13.8 %collective-permute-done.7.rest_4_ = bf16[512,512]{1,0:T(8,128)(2,1)} collective-permute-done((bf16[512,512]{1,0:T(8,128)(2,1)}, bf16[512,512]{1,0:T(8,128)(2,1)}, u32[]{:S(2)}, u32[]{:S(2)}) %collective-permute-start.7) | collective-permute-done | bytes 524320 | tf_op jit(solution)/shard_map/ppermute | solution.py:23
  93.6 22.5 %collective-permute-done.8.rest_7_ = bf16[512,512]{1,0:T(8,128)(2,1)} collective-permute-done((bf16[512,512]{1,0:T(8,128)(2,1)}, bf16[512,512]{1,0:T(8,128)(2,1)}, u32[]{:S(2)}, u32[]{:S(2)}) %collective-permute-start.8) | collective-permute-done | bytes 524320 | tf_op jit(solution)/shard_map/ppermute | solution.py:23
  116.1 14.9 %query_side.1 = (bf16[512,512]{1,0:T(8,128)(2,1)}, bf16[512,512]{1,0:T(8,128)(2,1)}, f32[2,4,4,128]{3,2,1,0:T(4,128)}) custom-call(s32[28]{0:T(128)} %reshape.55.valid_ref, bf16[512,512]{1,0:T(8,128)(2,1)} %q_ref.3, bf16[512,512]{1,0:T(8,128)(2,1)} %convolution_convert_fusion.1.g_ref, bf16[512,512]{1,0:T(8,128)(2,1)} %k_ref.3, bf16[512,512]{1,0:T(8,128)(2,1)} %v_ref.3, ...), custom_call_target="tpu_custom_call" | custom-call | tf_op jit(solution)/shard_map/query_side/pallas_call | solution.py:145
  131.1 0.0 all-gather.5.cloned.1.call-update
  131.1 0.0 copy-start.3
  131.1 1.4 collective-permute-start.10
  132.5 1.3 collective-permute-start.11
  133.8 1.3 collective-permute-start.9
  135.1 1.9 %collective-permute-done.10.rest_5_ = f32[2,4,4,128]{3,2,1,0:T(4,128)S(1)} collective-permute-done((f32[2,4,4,128]{3,2,1,0:T(4,128)}, f32[2,4,4,128]{3,2,1,0:T(4,128)S(1)}, u32[]{:S(2)}, u32[]{:S(2)}) %collective-permute-start.10) | collective-permute-done | bytes 16416 | tf_op jit(solution)/shard_map/ppermute | solution.py:23
  137.1 2.2 %collective-permute-done.11.rest_8_ = f32[2,4,4,128]{3,2,1,0:T(4,128)S(1)} collective-permute-done((f32[2,4,4,128]{3,2,1,0:T(4,128)}, f32[2,4,4,128]{3,2,1,0:T(4,128)S(1)}, u32[]{:S(2)}, u32[]{:S(2)}) %collective-permute-start.11) | collective-permute-done | bytes 16416 | tf_op jit(solution)/shard_map/ppermute | solution.py:23
  139.3 0.4 collective-permute-done.9.rest_2_
  139.7 0.0 copy-done.4
  139.7 0.2 copy-done.5
  139.9 0.6 copy-done.6
  140.5 10.6 %key_side.1 = (bf16[512,512]{1,0:T(8,128)(2,1)}, bf16[512,512]{1,0:T(8,128)(2,1)}) custom-call(s32[28]{0:T(128)} %reshape.56.valid_ref, bf16[512,512]{1,0:T(8,128)(2,1)} %k_ref.3, bf16[512,512]{1,0:T(8,128)(2,1)} %v_ref.3, bf16[512,512]{1,0:T(8,128)(2,1)} %q_ref.3, bf16[512,512]{1,0:T(8,128)(2,1)} %convolution_convert_fusion.1.g_ref, ...), custom_call_target="tpu_custom_call" | custom-call | tf_op jit(solution)/shard_map/key_side/pallas_call | solution.py:170
  151.1 0.0 all-gather.5.cloned.1.call-done
  151.1 0.0 copy-done.3
  151.1 3.6 %convolution_convert_fusion = bf16[512,512]{1,0:T(8,128)(2,1)} fusion(bf16[512,2048]{1,0:T(8,128)(2,1)} %all-gather.5.cloned.1.call-done, bf16[2048,512]{1,0:T(8,128)(2,1)S(1)} %bitcast.33), kind=kOutput, calls=%fused_computation.6 | convolution fusion | flops 1074003968 | bytes 4718592 | tf_op jit(solution)/shard_map/dot_general | solution.py:231
  (25 shorter events, 0.2 us)
Async XLA Ops:
  7.2 17.8 %copy-start.2 = (bf16[512,2048]{1,0:T(8,128)(2,1)S(1)}, bf16[512,2048]{1,0:T(8,128)(2,1)}, u32[]{:S(2)}) copy-start(bf16[512,2048]{1,0:T(8,128)(2,1)} %param.12) | copy-start | bytes 6291460
  7.2 51.4 %all-gather.3.cloned.1.call-start = ((), (), s32[]{:S(2)}) async-start(), calls=%async_computation.1 | async-start | bytes 2621440 | tf_op jit(solution)/shard_map/all_gather | solution.py:216
  11.7 62.4 %collective-permute-start = (bf16[1024,512]{1,0:T(8,128)(2,1)}, bf16[1024,512]{1,0:T(8,128)(2,1)S(1)}, u32[]{:S(2)}, u32[]{:S(2)}) collective-permute-start(bf16[1024,512]{1,0:T(8,128)(2,1)} %constant_dynamic-update-slice_fusion), channel_id=1, source_target_pairs={{0,4},{4,8},{8,12},{12,16},{16,20},{20,24},{24,28},{1,5},{5,9},{9,... | collective-permute-start | bytes 3145736 | tf_op jit(solution)/shard_map/ppermute | solution.py:23
  16.6 62.7 %collective-permute-start.1 = (bf16[1024,512]{1,0:T(8,128)(2,1)}, bf16[1024,512]{1,0:T(8,128)(2,1)}, u32[]{:S(2)}, u32[]{:S(2)}) collective-permute-start(bf16[1024,512]{1,0:T(8,128)(2,1)} %constant_dynamic-update-slice_fusion), channel_id=1, source_target_pairs={{0,8},{4,12},{8,16},{12,20},{16,24},{20,28},{1,9},{5,13},{9,17},{1... | collective-permute-start | bytes 3145736 | tf_op jit(solution)/shard_map/ppermute | solution.py:23
  21.1 15.3 %collective-permute-start.3 = (bf16[512,512]{1,0:T(8,128)(2,1)}, bf16[512,512]{1,0:T(8,128)(2,1)}, u32[]{:S(2)}, u32[]{:S(2)}) collective-permute-start(bf16[512,512]{1,0:T(8,128)(2,1)} %q_ref.3), channel_id=1, source_target_pairs={{4,0},{8,4},{12,8},{16,12},{20,16},{24,20},{28,24},{5,1},{9,5},{13... | collective-permute-start | bytes 1572872 | tf_op jit(solution)/shard_map/ppermute | solution.py:23
  22.4 40.5 %collective-permute-start.4 = (bf16[512,512]{1,0:T(8,128)(2,1)}, bf16[512,512]{1,0:T(8,128)(2,1)}, u32[]{:S(2)}, u32[]{:S(2)}) collective-permute-start(bf16[512,512]{1,0:T(8,128)(2,1)} %q_ref.3), channel_id=1, source_target_pairs={{8,0},{12,4},{16,8},{20,12},{24,16},{28,20},{9,1},{13,5},{17,9},{2... | collective-permute-start | bytes 1572872 | tf_op jit(solution)/shard_map/ppermute | solution.py:23
  23.7 49.2 %collective-permute-start.5 = (bf16[512,512]{1,0:T(8,128)(2,1)}, bf16[512,512]{1,0:T(8,128)(2,1)}, u32[]{:S(2)}, u32[]{:S(2)}) collective-permute-start(bf16[512,512]{1,0:T(8,128)(2,1)} %q_ref.3), channel_id=1, source_target_pairs={{16,0},{20,4},{24,8},{28,12},{17,1},{21,5},{25,9},{29,13},{18,2},{... | collective-permute-start | bytes 1572872 | tf_op jit(solution)/shard_map/ppermute | solution.py:23
  27.5 3.8 %copy-start.7 = (s32[32,5]{0,1:T(8,128)S(1)}, s32[32,5]{0,1:T(8,128)}, u32[]{:S(2)}) copy-start(s32[32,5]{0,1:T(8,128)} %param.15) | copy-start | bytes 1924
  27.5 5.8 %copy-start = (s32[32]{0:T(128)S(1)}, s32[32]{0:T(128)}, u32[]{:S(2)}) copy-start(s32[32]{0:T(128)} %param.14) | copy-start | bytes 388
  27.5 49.4 %all-to-all-start = ((bf16[512,4,512]{0,2,1:T(8,128)(2,1)}), bf16[512,4,512]{0,2,1:T(8,128)(2,1)S(1)}, u32[]{:S(2)}, u32[]{:S(2)}) async-start(bf16[512,4,512]{0,2,1:T(8,128)(2,1)} %bitcast.32), calls=%async_computation | async-start | bytes 4194304 | tf_op jit(solution)/shard_map/all_to_all | solution.py:223
  31.3 119.8 %all-gather.5.cloned.1.call-start = ((), (), s32[]{:S(2)}) async-start(), calls=%async_computation.2 | async-start | bytes 2621440 | tf_op jit(solution)/shard_map/all_gather | solution.py:232
  36.4 43.4 %collective-permute-start.2 = (bf16[1024,512]{1,0:T(8,128)(2,1)}, bf16[1024,512]{1,0:T(8,128)(2,1)}, u32[]{:S(2)}, u32[]{:S(2)}) collective-permute-start(bf16[1024,512]{1,0:T(8,128)(2,1)} %constant_dynamic-update-slice_fusion), channel_id=1, source_target_pairs={{0,16},{4,20},{8,24},{12,28},{1,17},{5,21},{9,25},{13,29},{2,18},{... | collective-permute-start | bytes 3145736 | tf_op jit(solution)/shard_map/ppermute | solution.py:23
  62.8 17.0 %collective-permute-start.6 = (bf16[512,512]{1,0:T(8,128)(2,1)}, bf16[512,512]{1,0:T(8,128)(2,1)}, u32[]{:S(2)}, u32[]{:S(2)}) collective-permute-start(bf16[512,512]{1,0:T(8,128)(2,1)} %convolution_convert_fusion.1.g_ref), channel_id=1, source_target_pairs={{4,0},{8,4},{12,8},{16,12},{20,16},{24,20},{28,24},{5,1},{9,5},{13... | collective-permute-start | bytes 1572872 | tf_op jit(solution)/shard_map/ppermute | solution.py:23
  72.9 20.7 %collective-permute-start.7 = (bf16[512,512]{1,0:T(8,128)(2,1)}, bf16[512,512]{1,0:T(8,128)(2,1)}, u32[]{:S(2)}, u32[]{:S(2)}) collective-permute-start(bf16[512,512]{1,0:T(8,128)(2,1)} %convolution_convert_fusion.1.g_ref), channel_id=1, source_target_pairs={{8,0},{12,4},{16,8},{20,12},{24,16},{28,20},{9,1},{13,5},{17,9},{2... | collective-permute-start | bytes 1572872 | tf_op jit(solution)/shard_map/ppermute | solution.py:23
  74.2 5.1 %copy-start.1 = (bf16[1024,512]{1,0:T(8,128)(2,1)}, bf16[1024,512]{1,0:T(8,128)(2,1)S(1)}, u32[]{:S(2)}) copy-start(bf16[1024,512]{1,0:T(8,128)(2,1)S(1)} %collective-permute-done.rest_0_.rest_1_) | copy-start | bytes 3145732
  74.2 41.9 %collective-permute-start.8 = (bf16[512,512]{1,0:T(8,128)(2,1)}, bf16[512,512]{1,0:T(8,128)(2,1)}, u32[]{:S(2)}, u32[]{:S(2)}) collective-permute-start(bf16[512,512]{1,0:T(8,128)(2,1)} %convolution_convert_fusion.1.g_ref), channel_id=1, source_target_pairs={{16,0},{20,4},{24,8},{28,12},{17,1},{21,5},{25,9},{29,13},{18,2},{... | collective-permute-start | bytes 1572872 | tf_op jit(solution)/shard_map/ppermute | solution.py:23
  131.1 20.0 %copy-start.3 = (bf16[4,512,512]{2,1,0:T(8,128)(2,1)S(1)}, bf16[4,512,512]{2,1,0:T(8,128)(2,1)}, u32[]{:S(2)}) copy-start(bf16[4,512,512]{2,1,0:T(8,128)(2,1)} %copy.18) | copy-start | bytes 6291460
  131.1 6.0 %collective-permute-start.10 = (f32[2,4,4,128]{3,2,1,0:T(4,128)}, f32[2,4,4,128]{3,2,1,0:T(4,128)S(1)}, u32[]{:S(2)}, u32[]{:S(2)}) collective-permute-start(f32[2,4,4,128]{3,2,1,0:T(4,128)} %get-tuple-element.30.st_ref), channel_id=1, source_target_pairs={{8,0},{12,4},{16,8},{20,12},{24,16},{28,20},{9,1},{13,5},{17,9},{2... | collective-permute-start | bytes 49160 | tf_op jit(solution)/shard_map/ppermute | solution.py:23
  132.5 6.7 %collective-permute-start.11 = (f32[2,4,4,128]{3,2,1,0:T(4,128)}, f32[2,4,4,128]{3,2,1,0:T(4,128)S(1)}, u32[]{:S(2)}, u32[]{:S(2)}) collective-permute-start(f32[2,4,4,128]{3,2,1,0:T(4,128)} %get-tuple-element.30.st_ref), channel_id=1, source_target_pairs={{16,0},{20,4},{24,8},{28,12},{17,1},{21,5},{25,9},{29,13},{18,2},{... | collective-permute-start | bytes 49160 | tf_op jit(solution)/shard_map/ppermute | solution.py:23
  133.8 5.8 %collective-permute-start.9 = (f32[2,4,4,128]{3,2,1,0:T(4,128)}, f32[2,4,4,128]{3,2,1,0:T(4,128)S(1)}, u32[]{:S(2)}, u32[]{:S(2)}) collective-permute-start(f32[2,4,4,128]{3,2,1,0:T(4,128)} %get-tuple-element.30.st_ref), channel_id=1, source_target_pairs={{4,0},{8,4},{12,8},{16,12},{20,16},{24,20},{28,24},{5,1},{9,5},{13... | collective-permute-start | bytes 49160 | tf_op jit(solution)/shard_map/ppermute | solution.py:23
  137.1 2.6 %copy-start.4 = (f32[2,4,4,128]{3,2,1,0:T(4,128)}, f32[2,4,4,128]{3,2,1,0:T(4,128)S(1)}, u32[]{:S(2)}) copy-start(f32[2,4,4,128]{3,2,1,0:T(4,128)S(1)} %collective-permute-done.10.rest_5_) | copy-start | bytes 49156
  139.3 0.6 copy-start.5
  139.9 0.6 copy-start.6
Sparse Core Ops, SparseCore 0:
  9.6 25.2 all-gather.2
  131.2 19.8 all-gather.4

commit v13 on v12

--- a/solution.py
+++ b/solution.py
@@ -121,6 +121,27 @@
         dk_ref[rows, :] = dot_nn(d_score, qcat).astype(jnp.bfloat16)
 
 
+def stack_kernel(a_ref, b_ref, out_ref, sems):
+    rows = a_ref.shape[0]
+    first = pltpu.make_async_copy(a_ref, out_ref.at[pl.ds(0, rows)], sems.at[0])
+    second = pltpu.make_async_copy(b_ref, out_ref.at[pl.ds(rows, rows)], sems.at[1])
+    first.start()
+    second.start()
+    first.wait()
+    second.wait()
+
+
+def stacked_rows(a, b):
+    return pl.pallas_call(
+        stack_kernel,
+        in_specs=[pl.BlockSpec(memory_space=pl.ANY)] * 2,
+        out_specs=pl.BlockSpec(memory_space=pl.ANY),
+        out_shape=jax.ShapeDtypeStruct((2 * a.shape[0], a.shape[1]), a.dtype),
+        scratch_shapes=[pltpu.SemaphoreType.DMA((2,))],
+        name="stack_rows",
+    )(a, b)
+
+
 def head_block(part):
     return pl.BlockSpec((NB * BLK, HD), lambda h, valid: (part, h))
 
@@ -208,7 +229,7 @@
         key_cols.append((qb <= last) & (jnp.take(far_select[:, m], jnp.minimum(qb, last)) == 1))
     valid_k = jnp.stack(key_cols, axis=1).astype(jnp.int32).reshape(-1)
 
-    kv = jnp.concatenate([keys, values], axis=0)
+    kv = stacked_rows(keys, values)
     kv_from = [passed_along(kv, "ctx", 2**m) for m in levels]
     q_from = [passed_along(queries, "ctx", -(2**m)) for m in levels]
 

time: 163 us -> 192 us (1.18)
  Pallas kernels: 25.6 us -> 58.5 us
  local copies, waits for them, and re-layouts: 14.9 us -> 11.1 us
    pallas_call x0 -> x1, Pallas kernels: none -> 32.9 us  [stacked_rows(): pl.pallas_call(stack_kernel, in_specs=[pl.BlockSpec(memory_space=pl.ANY)]...]
    unnamed x18 -> x17, local copies, waits for them, and re-layouts: 5.24 us -> 3.33 us
  transfers between devices with their start and end apart: 15 -> 15, of which waited for: 8 -> 8; matrix products, arithmetic and copies ran while one was open for 12% -> 8% of each run, Pallas kernels for 7% -> 23%
where the time goes in v13:
time: 192 us; the launch traced here: 191 us
  Pallas kernels  58.5 us (30%)
  waiting for transfers between devices  52.3 us (27%)
  starting transfers between devices  46.4 us (24%)
  between operations  14.3 us (7%)
  local copies, waits for them, and re-layouts  11.1 us (6%)
  matrix products  7.94 us (4%)
    ppermute x12, waiting for transfers between devices, passed_along(): return lax.ppermute(block, axis, route)  51.6 us
    ppermute x12, starting transfers between devices, passed_along(): return lax.ppermute(block, axis, route)  42.6 us
    pallas_call x1, Pallas kernels, stacked_rows(): pl.pallas_call(stack_kernel, in_specs=[pl.BlockSpec(memory_space=pl.ANY)]...  32.9 us
    pallas_call x1, Pallas kernels, query_call(): pl.pallas_call(functools.partial(query_kernel, n_levels), grid_spec=grid_...  14.9 us
    pallas_call x1, Pallas kernels, key_call(): pl.pallas_call(functools.partial(key_kernel, n_levels), grid_spec=grid_sp...  10.6 us
    dot_general x1, matrix products, local(): lax.dot_general(lax.all_gather(d_out, 'head', axis=1, tiled=True), out_we...  4.3 us
  transfers between devices with their start and end apart: 15, of which 8 were waited for; matrix products, arithmetic and copies ran while one was open for 8% of the time, Pallas kernels for 23%

profile of v13, /device:TPU:0, one launch (start us, length us, event | category | flops | bytes accessed | tf_op | source)
XLA Modules:
  0.0 190.7 jit_solution(11452869640466509058)
XLA Ops:
  7.2 0.0 copy-start.2
  7.2 0.0 all-gather.3.cloned.1.call-start
  7.2 0.7 all-gather.3.cloned.1.call-update
  7.9 32.9 %stack_rows.1 = bf16[1024,512]{1,0:T(8,128)(2,1)} custom-call(bf16[512,512]{1,0:T(8,128)(2,1)} %k_ref.3, bf16[512,512]{1,0:T(8,128)(2,1)} %v_ref.3), custom_call_target="tpu_custom_call" | custom-call | tf_op jit(solution)/shard_map/stack_rows/pallas_call | solution.py:135
  40.8 4.9 %collective-permute-start = (bf16[1024,512]{1,0:T(8,128)(2,1)}, bf16[1024,512]{1,0:T(8,128)(2,1)S(1)}, u32[]{:S(2)}, u32[]{:S(2)}) collective-permute-start(bf16[1024,512]{1,0:T(8,128)(2,1)} %stack_rows.1), channel_id=1, source_target_pairs={{0,4},{4,8},{8,12},{12,16},{16,20},{20,24},{24,28},{1,5},{5,9},{9,... | collective-permute-start | bytes 3145736 | tf_op jit(solution)/shard_map/ppermute | solution.py:23
  45.7 4.5 %collective-permute-start.1 = (bf16[1024,512]{1,0:T(8,128)(2,1)}, bf16[1024,512]{1,0:T(8,128)(2,1)}, u32[]{:S(2)}, u32[]{:S(2)}) collective-permute-start(bf16[1024,512]{1,0:T(8,128)(2,1)} %stack_rows.1), channel_id=1, source_target_pairs={{0,8},{4,12},{8,16},{12,20},{16,24},{20,28},{1,9},{5,13},{9,17},{1... | collective-permute-start | bytes 3145736 | tf_op jit(solution)/shard_map/ppermute | solution.py:23
  50.2 1.3 collective-permute-start.3
  51.5 1.3 collective-permute-start.4
  52.8 1.3 collective-permute-start.5
  54.1 0.0 copy-done.2
  54.1 2.5 %copy.17 = bf16[512,2048]{0,1:T(8,128)(2,1)} copy(bf16[512,2048]{1,0:T(8,128)(2,1)S(1)} %copy-done.2) | data formatting | bytes 4194304 | tf_op args[3]
  56.6 0.0 copy-start.7
  56.6 0.0 copy-start
  56.6 3.7 %all-to-all-start = ((bf16[512,4,512]{0,2,1:T(8,128)(2,1)}), bf16[512,4,512]{0,2,1:T(8,128)(2,1)S(1)}, u32[]{:S(2)}, u32[]{:S(2)}) async-start(bf16[512,4,512]{0,2,1:T(8,128)(2,1)} %bitcast.32), calls=%async_computation | async-start | bytes 4194304 | tf_op jit(solution)/shard_map/all_to_all | solution.py:244
  60.3 0.0 all-gather.5.cloned.1.call-start
  60.4 0.0 copy-done.7
  60.4 0.6 gather_fusion.5
  61.1 0.6 gather_fusion.4
  61.8 0.6 gather_fusion.3
  62.4 0.0 copy-done
  62.4 0.6 gather_fusion.2
  63.1 0.1 and_bitcast_fusion.6
  63.2 0.1 constant_dynamic-slice_fusion
  63.3 0.1 copy.15
  63.4 0.6 reshape.55.valid_ref
  64.0 1.5 collective-permute-done.3.rest_0_
  65.5 21.5 %collective-permute-start.2 = (bf16[1024,512]{1,0:T(8,128)(2,1)}, bf16[1024,512]{1,0:T(8,128)(2,1)}, u32[]{:S(2)}, u32[]{:S(2)}) collective-permute-start(bf16[1024,512]{1,0:T(8,128)(2,1)} %stack_rows.1), channel_id=1, source_target_pairs={{0,16},{4,20},{8,24},{12,28},{1,17},{5,21},{9,25},{13,29},{2,18},{... | collective-permute-start | bytes 3145736 | tf_op jit(solution)/shard_map/ppermute | solution.py:23
  87.0 0.6 gather_fusion.1
  87.6 0.0 all-gather.3.cloned.1.call-done
  87.6 4.3 %convolution_convert_fusion.1.g_ref = bf16[512,512]{1,0:T(8,128)(2,1)} fusion(bf16[512,2048]{1,0:T(8,128)(2,1)} %all-gather.3.cloned.1.call-done, bf16[512,2048]{1,0:T(8,128)(2,1)} %param.12), kind=kOutput, calls=%fused_computation.7 | convolution fusion | flops 1074003968 | bytes 4718592 | tf_op jit(solution)/shard_map/dot_general | solution.py:236
  91.9 0.0 collective-permute-done.4.rest_3_
  91.9 1.3 collective-permute-start.6
  93.2 8.8 %collective-permute-done.5.rest_6_ = bf16[512,512]{1,0:T(8,128)(2,1)} collective-permute-done((bf16[512,512]{1,0:T(8,128)(2,1)}, bf16[512,512]{1,0:T(8,128)(2,1)}, u32[]{:S(2)}, u32[]{:S(2)}) %collective-permute-start.5) | collective-permute-done | bytes 524320 | tf_op jit(solution)/shard_map/ppermute | solution.py:23
  102.0 1.3 collective-permute-start.7
  103.3 0.0 collective-permute-done.rest_0_.rest_1_
  103.3 0.0 copy-start.1
  103.3 1.3 collective-permute-start.8
  104.6 0.6 gather_fusion
  105.3 0.1 copy.16
  105.4 0.6 reshape.56.valid_ref
  106.0 0.0 all-to-all-done
  106.0 2.4 %copy.18 = bf16[4,512,512]{2,1,0:T(8,128)(2,1)} copy(bf16[4,512,512]{1,2,0:T(8,128)(2,1)S(1)} %bitcast.31) | data formatting | bytes 4194304 | tf_op jit(solution)/shard_map/all_to_all | solution.py:244
  108.4 0.0 copy-done.1
  108.4 0.0 collective-permute-done.1.rest_2_.rest_3_
  108.4 0.5 collective-permute-done.2.rest_4_.rest_5_
  108.9 0.0 collective-permute-done.6.rest_1_
  108.9 13.8 %collective-permute-done.7.rest_4_ = bf16[512,512]{1,0:T(8,128)(2,1)} collective-permute-done((bf16[512,512]{1,0:T(8,128)(2,1)}, bf16[512,512]{1,0:T(8,128)(2,1)}, u32[]{:S(2)}, u32[]{:S(2)}) %collective-permute-start.7) | collective-permute-done | bytes 524320 | tf_op jit(solution)/shard_map/ppermute | solution.py:23
  122.7 22.5 %collective-permute-done.8.rest_7_ = bf16[512,512]{1,0:T(8,128)(2,1)} collective-permute-done((bf16[512,512]{1,0:T(8,128)(2,1)}, bf16[512,512]{1,0:T(8,128)(2,1)}, u32[]{:S(2)}, u32[]{:S(2)}) %collective-permute-start.8) | collective-permute-done | bytes 524320 | tf_op jit(solution)/shard_map/ppermute | solution.py:23
  145.2 14.9 %query_side.1 = (bf16[512,512]{1,0:T(8,128)(2,1)}, bf16[512,512]{1,0:T(8,128)(2,1)}, f32[2,4,4,128]{3,2,1,0:T(4,128)}) custom-call(s32[28]{0:T(128)} %reshape.55.valid_ref, bf16[512,512]{1,0:T(8,128)(2,1)} %q_ref.3, bf16[512,512]{1,0:T(8,128)(2,1)} %convolution_convert_fusion.1.g_ref, bf16[512,512]{1,0:T(8,128)(2,1)} %k_ref.3, bf16[512,512]{1,0:T(8,128)(2,1)} %v_ref.3, ...), custom_call_target="tpu_custom_call" | custom-call | tf_op jit(solution)/shard_map/query_side/pallas_call | solution.py:166
  160.1 0.0 all-gather.5.cloned.1.call-update
  160.2 0.0 copy-start.3
  160.2 1.4 collective-permute-start.10
  161.6 1.3 collective-permute-start.11
  162.9 1.3 collective-permute-start.9
  164.2 1.9 %collective-permute-done.10.rest_5_ = f32[2,4,4,128]{3,2,1,0:T(4,128)S(1)} collective-permute-done((f32[2,4,4,128]{3,2,1,0:T(4,128)}, f32[2,4,4,128]{3,2,1,0:T(4,128)S(1)}, u32[]{:S(2)}, u32[]{:S(2)}) %collective-permute-start.10) | collective-permute-done | bytes 16416 | tf_op jit(solution)/shard_map/ppermute | solution.py:23
  166.2 2.2 %collective-permute-done.11.rest_8_ = f32[2,4,4,128]{3,2,1,0:T(4,128)S(1)} collective-permute-done((f32[2,4,4,128]{3,2,1,0:T(4,128)}, f32[2,4,4,128]{3,2,1,0:T(4,128)S(1)}, u32[]{:S(2)}, u32[]{:S(2)}) %collective-permute-start.11) | collective-permute-done | bytes 16416 | tf_op jit(solution)/shard_map/ppermute | solution.py:23
  168.4 0.4 collective-permute-done.9.rest_2_
  168.8 0.0 copy-done.4
  168.8 0.2 copy-done.5
  169.0 0.6 copy-done.6
  169.6 10.6 %key_side.1 = (bf16[512,512]{1,0:T(8,128)(2,1)}, bf16[512,512]{1,0:T(8,128)(2,1)}) custom-call(s32[28]{0:T(128)} %reshape.56.valid_ref, bf16[512,512]{1,0:T(8,128)(2,1)} %k_ref.3, bf16[512,512]{1,0:T(8,128)(2,1)} %v_ref.3, bf16[512,512]{1,0:T(8,128)(2,1)} %q_ref.3, bf16[512,512]{1,0:T(8,128)(2,1)} %convolution_convert_fusion.1.g_ref, ...), custom_call_target="tpu_custom_call" | custom-call | tf_op jit(solution)/shard_map/key_side/pallas_call | solution.py:191
  180.2 0.0 all-gather.5.cloned.1.call-done
  180.2 0.0 copy-done.3
  180.2 3.6 %convolution_convert_fusion = bf16[512,512]{1,0:T(8,128)(2,1)} fusion(bf16[512,2048]{1,0:T(8,128)(2,1)} %all-gather.5.cloned.1.call-done, bf16[2048,512]{1,0:T(8,128)(2,1)S(1)} %bitcast.33), kind=kOutput, calls=%fused_computation.6 | convolution fusion | flops 1074003968 | bytes 4718592 | tf_op jit(solution)/shard_map/dot_general | solution.py:252
  (24 shorter events, 0.2 us)
Async XLA Ops:
  7.2 46.9 %copy-start.2 = (bf16[512,2048]{1,0:T(8,128)(2,1)S(1)}, bf16[512,2048]{1,0:T(8,128)(2,1)}, u32[]{:S(2)}) copy-start(bf16[512,2048]{1,0:T(8,128)(2,1)} %param.12) | copy-start | bytes 6291460
  7.2 80.4 %all-gather.3.cloned.1.call-start = ((), (), s32[]{:S(2)}) async-start(), calls=%async_computation.1 | async-start | bytes 2621440 | tf_op jit(solution)/shard_map/all_gather | solution.py:237
  40.8 62.5 %collective-permute-start = (bf16[1024,512]{1,0:T(8,128)(2,1)}, bf16[1024,512]{1,0:T(8,128)(2,1)S(1)}, u32[]{:S(2)}, u32[]{:S(2)}) collective-permute-start(bf16[1024,512]{1,0:T(8,128)(2,1)} %stack_rows.1), channel_id=1, source_target_pairs={{0,4},{4,8},{8,12},{12,16},{16,20},{20,24},{24,28},{1,5},{5,9},{9,... | collective-permute-start | bytes 3145736 | tf_op jit(solution)/shard_map/ppermute | solution.py:23
  45.7 62.7 %collective-permute-start.1 = (bf16[1024,512]{1,0:T(8,128)(2,1)}, bf16[1024,512]{1,0:T(8,128)(2,1)}, u32[]{:S(2)}, u32[]{:S(2)}) collective-permute-start(bf16[1024,512]{1,0:T(8,128)(2,1)} %stack_rows.1), channel_id=1, source_target_pairs={{0,8},{4,12},{8,16},{12,20},{16,24},{20,28},{1,9},{5,13},{9,17},{1... | collective-permute-start | bytes 3145736 | tf_op jit(solution)/shard_map/ppermute | solution.py:23
  50.2 15.3 %collective-permute-start.3 = (bf16[512,512]{1,0:T(8,128)(2,1)}, bf16[512,512]{1,0:T(8,128)(2,1)}, u32[]{:S(2)}, u32[]{:S(2)}) collective-permute-start(bf16[512,512]{1,0:T(8,128)(2,1)} %q_ref.3), channel_id=1, source_target_pairs={{4,0},{8,4},{12,8},{16,12},{20,16},{24,20},{28,24},{5,1},{9,5},{13... | collective-permute-start | bytes 1572872 | tf_op jit(solution)/shard_map/ppermute | solution.py:23
  51.5 40.4 %collective-permute-start.4 = (bf16[512,512]{1,0:T(8,128)(2,1)}, bf16[512,512]{1,0:T(8,128)(2,1)}, u32[]{:S(2)}, u32[]{:S(2)}) collective-permute-start(bf16[512,512]{1,0:T(8,128)(2,1)} %q_ref.3), channel_id=1, source_target_pairs={{8,0},{12,4},{16,8},{20,12},{24,16},{28,20},{9,1},{13,5},{17,9},{2... | collective-permute-start | bytes 1572872 | tf_op jit(solution)/shard_map/ppermute | solution.py:23
  52.8 49.2 %collective-permute-start.5 = (bf16[512,512]{1,0:T(8,128)(2,1)}, bf16[512,512]{1,0:T(8,128)(2,1)}, u32[]{:S(2)}, u32[]{:S(2)}) collective-permute-start(bf16[512,512]{1,0:T(8,128)(2,1)} %q_ref.3), channel_id=1, source_target_pairs={{16,0},{20,4},{24,8},{28,12},{17,1},{21,5},{25,9},{29,13},{18,2},{... | collective-permute-start | bytes 1572872 | tf_op jit(solution)/shard_map/ppermute | solution.py:23
  56.6 3.8 %copy-start.7 = (s32[32,5]{0,1:T(8,128)S(1)}, s32[32,5]{0,1:T(8,128)}, u32[]{:S(2)}) copy-start(s32[32,5]{0,1:T(8,128)} %param.15) | copy-start | bytes 1924
  56.6 5.8 %copy-start = (s32[32]{0:T(128)S(1)}, s32[32]{0:T(128)}, u32[]{:S(2)}) copy-start(s32[32]{0:T(128)} %param.14) | copy-start | bytes 388
  56.6 49.4 %all-to-all-start = ((bf16[512,4,512]{0,2,1:T(8,128)(2,1)}), bf16[512,4,512]{0,2,1:T(8,128)(2,1)S(1)}, u32[]{:S(2)}, u32[]{:S(2)}) async-start(bf16[512,4,512]{0,2,1:T(8,128)(2,1)} %bitcast.32), calls=%async_computation | async-start | bytes 4194304 | tf_op jit(solution)/shard_map/all_to_all | solution.py:244
  60.3 119.9 %all-gather.5.cloned.1.call-start = ((), (), s32[]{:S(2)}) async-start(), calls=%async_computation.2 | async-start | bytes 2621440 | tf_op jit(solution)/shard_map/all_gather | solution.py:253
  65.5 43.4 %collective-permute-start.2 = (bf16[1024,512]{1,0:T(8,128)(2,1)}, bf16[1024,512]{1,0:T(8,128)(2,1)}, u32[]{:S(2)}, u32[]{:S(2)}) collective-permute-start(bf16[1024,512]{1,0:T(8,128)(2,1)} %stack_rows.1), channel_id=1, source_target_pairs={{0,16},{4,20},{8,24},{12,28},{1,17},{5,21},{9,25},{13,29},{2,18},{... | collective-permute-start | bytes 3145736 | tf_op jit(solution)/shard_map/ppermute | solution.py:23
  91.9 17.0 %collective-permute-start.6 = (bf16[512,512]{1,0:T(8,128)(2,1)}, bf16[512,512]{1,0:T(8,128)(2,1)}, u32[]{:S(2)}, u32[]{:S(2)}) collective-permute-start(bf16[512,512]{1,0:T(8,128)(2,1)} %convolution_convert_fusion.1.g_ref), channel_id=1, source_target_pairs={{4,0},{8,4},{12,8},{16,12},{20,16},{24,20},{28,24},{5,1},{9,5},{13... | collective-permute-start | bytes 1572872 | tf_op jit(solution)/shard_map/ppermute | solution.py:23
  102.0 20.7 %collective-permute-start.7 = (bf16[512,512]{1,0:T(8,128)(2,1)}, bf16[512,512]{1,0:T(8,128)(2,1)}, u32[]{:S(2)}, u32[]{:S(2)}) collective-permute-start(bf16[512,512]{1,0:T(8,128)(2,1)} %convolution_convert_fusion.1.g_ref), channel_id=1, source_target_pairs={{8,0},{12,4},{16,8},{20,12},{24,16},{28,20},{9,1},{13,5},{17,9},{2... | collective-permute-start | bytes 1572872 | tf_op jit(solution)/shard_map/ppermute | solution.py:23
  103.3 5.1 %copy-start.1 = (bf16[1024,512]{1,0:T(8,128)(2,1)}, bf16[1024,512]{1,0:T(8,128)(2,1)S(1)}, u32[]{:S(2)}) copy-start(bf16[1024,512]{1,0:T(8,128)(2,1)S(1)} %collective-permute-done.rest_0_.rest_1_) | copy-start | bytes 3145732
  103.3 41.9 %collective-permute-start.8 = (bf16[512,512]{1,0:T(8,128)(2,1)}, bf16[512,512]{1,0:T(8,128)(2,1)}, u32[]{:S(2)}, u32[]{:S(2)}) collective-permute-start(bf16[512,512]{1,0:T(8,128)(2,1)} %convolution_convert_fusion.1.g_ref), channel_id=1, source_target_pairs={{16,0},{20,4},{24,8},{28,12},{17,1},{21,5},{25,9},{29,13},{18,2},{... | collective-permute-start | bytes 1572872 | tf_op jit(solution)/shard_map/ppermute | solution.py:23
  160.2 20.0 %copy-start.3 = (bf16[4,512,512]{2,1,0:T(8,128)(2,1)S(1)}, bf16[4,512,512]{2,1,0:T(8,128)(2,1)}, u32[]{:S(2)}) copy-start(bf16[4,512,512]{2,1,0:T(8,128)(2,1)} %copy.18) | copy-start | bytes 6291460
  160.2 6.0 %collective-permute-start.10 = (f32[2,4,4,128]{3,2,1,0:T(4,128)}, f32[2,4,4,128]{3,2,1,0:T(4,128)S(1)}, u32[]{:S(2)}, u32[]{:S(2)}) collective-permute-start(f32[2,4,4,128]{3,2,1,0:T(4,128)} %get-tuple-element.30.st_ref), channel_id=1, source_target_pairs={{8,0},{12,4},{16,8},{20,12},{24,16},{28,20},{9,1},{13,5},{17,9},{2... | collective-permute-start | bytes 49160 | tf_op jit(solution)/shard_map/ppermute | solution.py:23
  161.6 6.7 %collective-permute-start.11 = (f32[2,4,4,128]{3,2,1,0:T(4,128)}, f32[2,4,4,128]{3,2,1,0:T(4,128)S(1)}, u32[]{:S(2)}, u32[]{:S(2)}) collective-permute-start(f32[2,4,4,128]{3,2,1,0:T(4,128)} %get-tuple-element.30.st_ref), channel_id=1, source_target_pairs={{16,0},{20,4},{24,8},{28,12},{17,1},{21,5},{25,9},{29,13},{18,2},{... | collective-permute-start | bytes 49160 | tf_op jit(solution)/shard_map/ppermute | solution.py:23
  162.9 5.8 %collective-permute-start.9 = (f32[2,4,4,128]{3,2,1,0:T(4,128)}, f32[2,4,4,128]{3,2,1,0:T(4,128)S(1)}, u32[]{:S(2)}, u32[]{:S(2)}) collective-permute-start(f32[2,4,4,128]{3,2,1,0:T(4,128)} %get-tuple-element.30.st_ref), channel_id=1, source_target_pairs={{4,0},{8,4},{12,8},{16,12},{20,16},{24,20},{28,24},{5,1},{9,5},{13... | collective-permute-start | bytes 49160 | tf_op jit(solution)/shard_map/ppermute | solution.py:23
  166.2 2.6 %copy-start.4 = (f32[2,4,4,128]{3,2,1,0:T(4,128)}, f32[2,4,4,128]{3,2,1,0:T(4,128)S(1)}, u32[]{:S(2)}) copy-start(f32[2,4,4,128]{3,2,1,0:T(4,128)S(1)} %collective-permute-done.10.rest_5_) | copy-start | bytes 49156
  168.4 0.6 copy-start.5
  169.0 0.6 copy-start.6
Sparse Core Ops, SparseCore 0:
  9.6 25.2 all-gather.2
  160.3 19.8 all-gather.4

commit v14 on v12

--- a/solution.py
+++ b/solution.py
@@ -208,9 +208,10 @@
         key_cols.append((qb <= last) & (jnp.take(far_select[:, m], jnp.minimum(qb, last)) == 1))
     valid_k = jnp.stack(key_cols, axis=1).astype(jnp.int32).reshape(-1)
 
+    q_from = [passed_along(queries, "ctx", -(2**m)) for m in levels]
     kv = jnp.concatenate([keys, values], axis=0)
+    kv, valid_q, valid_k = lax.optimization_barrier((kv, valid_q, valid_k))
     kv_from = [passed_along(kv, "ctx", 2**m) for m in levels]
-    q_from = [passed_along(queries, "ctx", -(2**m)) for m in levels]
 
     grad_att = lax.dot_general(
         lax.all_gather(d_out, "head", axis=1, tiled=True),

time: 163 us -> 172 us (1.055)
  waiting for transfers between devices: 52.3 us -> 78.6 us
  starting transfers between devices: 46.4 us -> 31.5 us
  local copies, waits for them, and re-layouts: 14.9 us -> 12.6 us
    ppermute x12, waiting for transfers between devices: 51.6 us -> 69.4 us  [passed_along(): return lax.ppermute(block, axis, route)]
    ppermute x12, starting transfers between devices: 42.6 us -> 27 us  [passed_along(): return lax.ppermute(block, axis, route)]
    all_gather x1, waiting for transfers between devices: 0.02 us -> 4.63 us  [local(): lax.all_gather(attended, 'head', axis=1, tiled=True)]
    all_gather x1, waiting for transfers between devices: 0.01 us -> 3.9 us  [local(): lax.all_gather(d_out, 'head', axis=1, tiled=True)]
    concatenate x1 -> x0, local copies, waits for them, and re-layouts: 1.91 us -> none  [local(): kv = jnp.concatenate([keys, values], axis=0)]
    unnamed x18 -> x19, local copies, waits for them, and re-layouts: 5.24 us -> 4.76 us
  transfers between devices with their start and end apart: 15 -> 15, of which waited for: 8 -> 9; matrix products, arithmetic and copies ran while one was open for 12% -> 10% of each run, Pallas kernels for 7% -> 6%
where the time goes in v14:
time: 172 us
  waiting for transfers between devices  78.6 us (46%)
  starting transfers between devices  31.5 us (18%)
  Pallas kernels  25.5 us (15%)
  between operations  14.3 us (8%)
  local copies, waits for them, and re-layouts  12.6 us (7%)
  matrix products  7.93 us (5%)
    ppermute x12, waiting for transfers between devices, passed_along(): return lax.ppermute(block, axis, route)  69.4 us
    ppermute x12, starting transfers between devices, passed_along(): return lax.ppermute(block, axis, route)  27 us
    pallas_call x1, Pallas kernels, query_call(): pl.pallas_call(functools.partial(query_kernel, n_levels), grid_spec=grid_...  14.9 us
    pallas_call x1, Pallas kernels, key_call(): pl.pallas_call(functools.partial(key_kernel, n_levels), grid_spec=grid_sp...  10.6 us
    unnamed x19, local copies, waits for them, and re-layouts  4.76 us
    all_gather x1, waiting for transfers between devices, local(): lax.all_gather(attended, 'head', axis=1, tiled=True)  4.63 us
    all_to_all x1, starting transfers between devices, local(): weight_cols = lax.all_to_all(out_weight, 'head', 1, 0, tiled=True)  4.37 us
    dot_general x1, matrix products, local(): lax.dot_general(lax.all_gather(d_out, 'head', axis=1, tiled=True), out_we...  4.3 us
  transfers between devices with their start and end apart: 15, of which 9 were waited for; matrix products, arithmetic and copies ran while one was open for 10% of the time, Pallas kernels for 6%

profile of v14, /device:TPU:0, one launch (start us, length us, event | category | flops | bytes accessed | tf_op | source)
XLA Modules:
  0.0 171.7 jit_solution(2225784060587544105)
XLA Ops:
  7.2 0.0 all-gather.3.cloned.1.call-start
  7.2 0.7 all-gather.3.cloned.1.call-update
  7.9 3.9 %copy.17 = bf16[512,2048]{0,1:T(8,128)(2,1)} copy(bf16[512,2048]{1,0:T(8,128)(2,1)} %param.12) | data formatting | bytes 4194304 | tf_op args[3]
  11.8 0.0 copy-start.8
  11.8 0.0 copy-start
  11.8 4.4 %all-to-all-start = ((bf16[512,4,512]{0,2,1:T(8,128)(2,1)}), bf16[512,4,512]{0,2,1:T(8,128)(2,1)S(1)}, u32[]{:S(2)}, u32[]{:S(2)}) async-start(bf16[512,4,512]{0,2,1:T(8,128)(2,1)} %bitcast.32), calls=%async_computation | async-start | bytes 4194304 | tf_op jit(solution)/shard_map/all_to_all | solution.py:224
  16.2 0.0 all-gather.5.cloned.1.call-start
  16.3 1.4 collective-permute-start.3
  17.7 0.0 copy-done.8
  17.7 0.1 constant_dynamic-slice_fusion
  17.8 0.0 copy-done
  17.8 0.1 and_bitcast_fusion.6
  18.0 0.1 copy.15
  18.1 0.6 reshape.55.valid_ref
  18.7 0.6 gather_fusion.2
  19.3 0.6 gather_fusion.1
  20.0 0.6 gather_fusion
  20.6 0.6 gather_fusion.5
  21.3 0.6 gather_fusion.4
  21.9 0.6 gather_fusion.3
  22.7 0.0 copy-done.1
  22.7 0.0 copy-done.2
  22.7 1.1 pad_maximum_fusion
  23.8 0.1 copy.16
  23.9 0.7 reshape.56.valid_ref
  24.6 4.9 %collective-permute-start = (bf16[1024,512]{1,0:T(8,128)(2,1)}, bf16[1024,512]{1,0:T(8,128)(2,1)S(1)}, u32[]{:S(2)}, u32[]{:S(2)}) collective-permute-start(bf16[1024,512]{1,0:T(8,128)(2,1)} %pad_maximum_fusion), channel_id=1, source_target_pairs={{0,4},{4,8},{8,12},{12,16},{16,20},{20,24},{24,28},{1,5},{5,9},{9,... | collective-permute-start | bytes 3145736 | tf_op jit(solution)/shard_map/ppermute | solution.py:23
  29.5 4.9 %collective-permute-start.1 = (bf16[1024,512]{1,0:T(8,128)(2,1)}, bf16[1024,512]{1,0:T(8,128)(2,1)}, u32[]{:S(2)}, u32[]{:S(2)}) collective-permute-start(bf16[1024,512]{1,0:T(8,128)(2,1)} %pad_maximum_fusion), channel_id=1, source_target_pairs={{0,8},{4,12},{8,16},{12,20},{16,24},{20,28},{1,9},{5,13},{9,17},{1... | collective-permute-start | bytes 3145736 | tf_op jit(solution)/shard_map/ppermute | solution.py:23
  34.5 5.3 %collective-permute-start.2 = (bf16[1024,512]{1,0:T(8,128)(2,1)}, bf16[1024,512]{1,0:T(8,128)(2,1)}, u32[]{:S(2)}, u32[]{:S(2)}) collective-permute-start(bf16[1024,512]{1,0:T(8,128)(2,1)} %pad_maximum_fusion), channel_id=1, source_target_pairs={{0,16},{4,20},{8,24},{12,28},{1,17},{5,21},{9,25},{13,29},{2,18},{... | collective-permute-start | bytes 3145736 | tf_op jit(solution)/shard_map/ppermute | solution.py:23
  39.7 1.3 collective-permute-start.4
  41.0 0.0 collective-permute-done.3.rest_0_
  41.0 1.3 collective-permute-start.5
  42.3 3.9 %all-gather.3.cloned.1.call-done = bf16[512,2048]{1,0:T(8,128)(2,1)} async-done(((bf16[512,512]{1,0:T(8,128)(2,1)}), bf16[512,2048]{1,0:T(8,128)(2,1)}) %all-gather.3.cloned.1.call-update) | async-done | bytes 2097168 | tf_op jit(solution)/shard_map/all_gather | solution.py:217
  46.2 4.3 %convolution_convert_fusion.1.g_ref = bf16[512,512]{1,0:T(8,128)(2,1)} fusion(bf16[512,2048]{1,0:T(8,128)(2,1)} %all-gather.3.cloned.1.call-done, bf16[512,2048]{1,0:T(8,128)(2,1)} %param.12), kind=kOutput, calls=%fused_computation.7 | convolution fusion | flops 1074003968 | bytes 4718592 | tf_op jit(solution)/shard_map/dot_general | solution.py:216
  50.5 4.8 %collective-permute-done.4.rest_3_ = bf16[512,512]{1,0:T(8,128)(2,1)} collective-permute-done((bf16[512,512]{1,0:T(8,128)(2,1)}, bf16[512,512]{1,0:T(8,128)(2,1)}, u32[]{:S(2)}, u32[]{:S(2)}) %collective-permute-start.4) | collective-permute-done | bytes 524320 | tf_op jit(solution)/shard_map/ppermute | solution.py:23
  55.4 1.3 collective-permute-start.6
  56.6 22.2 %collective-permute-done.5.rest_6_ = bf16[512,512]{1,0:T(8,128)(2,1)} collective-permute-done((bf16[512,512]{1,0:T(8,128)(2,1)}, bf16[512,512]{1,0:T(8,128)(2,1)}, u32[]{:S(2)}, u32[]{:S(2)}) %collective-permute-start.5) | collective-permute-done | bytes 524320 | tf_op jit(solution)/shard_map/ppermute | solution.py:23
  78.9 1.3 collective-permute-start.7
  80.2 0.0 collective-permute-done.rest_0_.rest_1_
  80.2 0.0 copy-start.3
  80.2 1.3 collective-permute-start.8
  81.5 0.0 all-to-all-done
  81.5 2.4 %copy.18 = bf16[4,512,512]{2,1,0:T(8,128)(2,1)} copy(bf16[4,512,512]{1,2,0:T(8,128)(2,1)S(1)} %bitcast.31) | data formatting | bytes 4194304 | tf_op jit(solution)/shard_map/all_to_all | solution.py:224
  83.9 0.0 copy-done.3
  83.9 0.0 collective-permute-done.1.rest_2_.rest_3_
  83.9 0.0 collective-permute-done.2.rest_4_.rest_5_
  83.9 0.0 collective-permute-done.6.rest_1_
  83.9 7.9 %collective-permute-done.7.rest_4_ = bf16[512,512]{1,0:T(8,128)(2,1)} collective-permute-done((bf16[512,512]{1,0:T(8,128)(2,1)}, bf16[512,512]{1,0:T(8,128)(2,1)}, u32[]{:S(2)}, u32[]{:S(2)}) %collective-permute-start.7) | collective-permute-done | bytes 524320 | tf_op jit(solution)/shard_map/ppermute | solution.py:23
  91.8 29.9 %collective-permute-done.8.rest_7_ = bf16[512,512]{1,0:T(8,128)(2,1)} collective-permute-done((bf16[512,512]{1,0:T(8,128)(2,1)}, bf16[512,512]{1,0:T(8,128)(2,1)}, u32[]{:S(2)}, u32[]{:S(2)}) %collective-permute-start.8) | collective-permute-done | bytes 524320 | tf_op jit(solution)/shard_map/ppermute | solution.py:23
  121.7 14.9 %query_side.1 = (bf16[512,512]{1,0:T(8,128)(2,1)}, bf16[512,512]{1,0:T(8,128)(2,1)}, f32[2,4,4,128]{3,2,1,0:T(4,128)}) custom-call(s32[28]{0:T(128)} %reshape.55.valid_ref, bf16[512,512]{1,0:T(8,128)(2,1)} %q_ref.3, bf16[512,512]{1,0:T(8,128)(2,1)} %convolution_convert_fusion.1.g_ref, bf16[512,512]{1,0:T(8,128)(2,1)} %k_ref.3, bf16[512,512]{1,0:T(8,128)(2,1)} %v_ref.3, ...), custom_call_target="tpu_custom_call" | custom-call | tf_op jit(solution)/shard_map/query_side/pallas_call | solution.py:145
  136.6 0.0 all-gather.5.cloned.1.call-update
  136.6 0.0 copy-start.4
  136.6 1.4 collective-permute-start.10
  138.1 1.3 collective-permute-start.11
  139.4 1.3 collective-permute-start.9
  140.7 1.9 %collective-permute-done.10.rest_5_ = f32[2,4,4,128]{3,2,1,0:T(4,128)S(1)} collective-permute-done((f32[2,4,4,128]{3,2,1,0:T(4,128)}, f32[2,4,4,128]{3,2,1,0:T(4,128)S(1)}, u32[]{:S(2)}, u32[]{:S(2)}) %collective-permute-start.10) | collective-permute-done | bytes 16416 | tf_op jit(solution)/shard_map/ppermute | solution.py:23
  142.6 2.2 %collective-permute-done.11.rest_8_ = f32[2,4,4,128]{3,2,1,0:T(4,128)S(1)} collective-permute-done((f32[2,4,4,128]{3,2,1,0:T(4,128)}, f32[2,4,4,128]{3,2,1,0:T(4,128)S(1)}, u32[]{:S(2)}, u32[]{:S(2)}) %collective-permute-start.11) | collective-permute-done | bytes 16416 | tf_op jit(solution)/shard_map/ppermute | solution.py:23
  144.8 0.4 collective-permute-done.9.rest_2_
  145.2 0.0 copy-done.5
  145.2 0.2 copy-done.6
  145.4 0.6 copy-done.7
  146.0 10.6 %key_side.1 = (bf16[512,512]{1,0:T(8,128)(2,1)}, bf16[512,512]{1,0:T(8,128)(2,1)}) custom-call(s32[28]{0:T(128)} %reshape.56.valid_ref, bf16[512,512]{1,0:T(8,128)(2,1)} %k_ref.3, bf16[512,512]{1,0:T(8,128)(2,1)} %v_ref.3, bf16[512,512]{1,0:T(8,128)(2,1)} %q_ref.3, bf16[512,512]{1,0:T(8,128)(2,1)} %convolution_convert_fusion.1.g_ref, ...), custom_call_target="tpu_custom_call" | custom-call | tf_op jit(solution)/shard_map/key_side/pallas_call | solution.py:170
  156.6 4.6 %all-gather.5.cloned.1.call-done = bf16[512,2048]{1,0:T(8,128)(2,1)} async-done(((bf16[512,512]{1,0:T(8,128)(2,1)}), bf16[512,2048]{1,0:T(8,128)(2,1)}) %all-gather.5.cloned.1.call-update) | async-done | bytes 2097168 | tf_op jit(solution)/shard_map/all_gather | solution.py:233
  161.3 0.0 copy-done.4
  161.3 3.6 %convolution_convert_fusion = bf16[512,512]{1,0:T(8,128)(2,1)} fusion(bf16[512,2048]{1,0:T(8,128)(2,1)} %all-gather.5.cloned.1.call-done, bf16[2048,512]{1,0:T(8,128)(2,1)S(1)} %bitcast.33), kind=kOutput, calls=%fused_computation.6 | convolution fusion | flops 1074003968 | bytes 4718592 | tf_op jit(solution)/shard_map/dot_general | solution.py:232
  (26 shorter events, 0.2 us)
Async XLA Ops:
  7.2 39.1 %all-gather.3.cloned.1.call-start = ((), (), s32[]{:S(2)}) async-start(), calls=%async_computation.1 | async-start | bytes 2621440 | tf_op jit(solution)/shard_map/all_gather | solution.py:217
  11.8 5.9 %copy-start.8 = (s32[32,5]{0,1:T(8,128)S(1)}, s32[32,5]{0,1:T(8,128)}, u32[]{:S(2)}) copy-start(s32[32,5]{0,1:T(8,128)} %param.15) | copy-start | bytes 1924
  11.8 6.0 %copy-start = (s32[32]{0:T(128)S(1)}, s32[32]{0:T(128)}, u32[]{:S(2)}) copy-start(s32[32]{0:T(128)} %param.14) | copy-start | bytes 388
  11.8 69.6 %all-to-all-start = ((bf16[512,4,512]{0,2,1:T(8,128)(2,1)}), bf16[512,4,512]{0,2,1:T(8,128)(2,1)S(1)}, u32[]{:S(2)}, u32[]{:S(2)}) async-start(bf16[512,4,512]{0,2,1:T(8,128)(2,1)} %bitcast.32), calls=%async_computation | async-start | bytes 4194304 | tf_op jit(solution)/shard_map/all_to_all | solution.py:224
  16.2 6.5 %copy-start.1 = (bf16[512,512]{1,0:T(8,128)(2,1)S(1)}, bf16[512,512]{1,0:T(8,128)(2,1)}, u32[]{:S(2)}) copy-start(bf16[512,512]{1,0:T(8,128)(2,1)} %k_ref.3) | copy-start | bytes 1572868
  16.2 6.5 %copy-start.2 = (bf16[512,512]{1,0:T(8,128)(2,1)S(1)}, bf16[512,512]{1,0:T(8,128)(2,1)}, u32[]{:S(2)}) copy-start(bf16[512,512]{1,0:T(8,128)(2,1)} %v_ref.3) | copy-start | bytes 1572868
  16.2 145.0 %all-gather.5.cloned.1.call-start = ((), (), s32[]{:S(2)}) async-start(), calls=%async_computation.2 | async-start | bytes 2621440 | tf_op jit(solution)/shard_map/all_gather | solution.py:233
  16.3 24.8 %collective-permute-start.3 = (bf16[512,512]{1,0:T(8,128)(2,1)}, bf16[512,512]{1,0:T(8,128)(2,1)}, u32[]{:S(2)}, u32[]{:S(2)}) collective-permute-start(bf16[512,512]{1,0:T(8,128)(2,1)} %q_ref.3), channel_id=1, source_target_pairs={{4,0},{8,4},{12,8},{16,12},{20,16},{24,20},{28,24},{5,1},{9,5},{13... | collective-permute-start | bytes 1572872 | tf_op jit(solution)/shard_map/ppermute | solution.py:23
  24.6 55.6 %collective-permute-start = (bf16[1024,512]{1,0:T(8,128)(2,1)}, bf16[1024,512]{1,0:T(8,128)(2,1)S(1)}, u32[]{:S(2)}, u32[]{:S(2)}) collective-permute-start(bf16[1024,512]{1,0:T(8,128)(2,1)} %pad_maximum_fusion), channel_id=1, source_target_pairs={{0,4},{4,8},{8,12},{12,16},{16,20},{20,24},{24,28},{1,5},{5,9},{9,... | collective-permute-start | bytes 3145736 | tf_op jit(solution)/shard_map/ppermute | solution.py:23
  29.5 54.4 %collective-permute-start.1 = (bf16[1024,512]{1,0:T(8,128)(2,1)}, bf16[1024,512]{1,0:T(8,128)(2,1)}, u32[]{:S(2)}, u32[]{:S(2)}) collective-permute-start(bf16[1024,512]{1,0:T(8,128)(2,1)} %pad_maximum_fusion), channel_id=1, source_target_pairs={{0,8},{4,12},{8,16},{12,20},{16,24},{20,28},{1,9},{5,13},{9,17},{1... | collective-permute-start | bytes 3145736 | tf_op jit(solution)/shard_map/ppermute | solution.py:23
  34.5 49.4 %collective-permute-start.2 = (bf16[1024,512]{1,0:T(8,128)(2,1)}, bf16[1024,512]{1,0:T(8,128)(2,1)}, u32[]{:S(2)}, u32[]{:S(2)}) collective-permute-start(bf16[1024,512]{1,0:T(8,128)(2,1)} %pad_maximum_fusion), channel_id=1, source_target_pairs={{0,16},{4,20},{8,24},{12,28},{1,17},{5,21},{9,25},{13,29},{2,18},{... | collective-permute-start | bytes 3145736 | tf_op jit(solution)/shard_map/ppermute | solution.py:23
  39.7 15.6 %collective-permute-start.4 = (bf16[512,512]{1,0:T(8,128)(2,1)}, bf16[512,512]{1,0:T(8,128)(2,1)}, u32[]{:S(2)}, u32[]{:S(2)}) collective-permute-start(bf16[512,512]{1,0:T(8,128)(2,1)} %q_ref.3), channel_id=1, source_target_pairs={{8,0},{12,4},{16,8},{20,12},{24,16},{28,20},{9,1},{13,5},{17,9},{2... | collective-permute-start | bytes 1572872 | tf_op jit(solution)/shard_map/ppermute | solution.py:23
  41.0 37.8 %collective-permute-start.5 = (bf16[512,512]{1,0:T(8,128)(2,1)}, bf16[512,512]{1,0:T(8,128)(2,1)}, u32[]{:S(2)}, u32[]{:S(2)}) collective-permute-start(bf16[512,512]{1,0:T(8,128)(2,1)} %q_ref.3), channel_id=1, source_target_pairs={{16,0},{20,4},{24,8},{28,12},{17,1},{21,5},{25,9},{29,13},{18,2},{... | collective-permute-start | bytes 1572872 | tf_op jit(solution)/shard_map/ppermute | solution.py:23
  55.4 28.5 %collective-permute-start.6 = (bf16[512,512]{1,0:T(8,128)(2,1)}, bf16[512,512]{1,0:T(8,128)(2,1)}, u32[]{:S(2)}, u32[]{:S(2)}) collective-permute-start(bf16[512,512]{1,0:T(8,128)(2,1)} %convolution_convert_fusion.1.g_ref), channel_id=1, source_target_pairs={{4,0},{8,4},{12,8},{16,12},{20,16},{24,20},{28,24},{5,1},{9,5},{13... | collective-permute-start | bytes 1572872 | tf_op jit(solution)/shard_map/ppermute | solution.py:23
  78.9 12.9 %collective-permute-start.7 = (bf16[512,512]{1,0:T(8,128)(2,1)}, bf16[512,512]{1,0:T(8,128)(2,1)}, u32[]{:S(2)}, u32[]{:S(2)}) collective-permute-start(bf16[512,512]{1,0:T(8,128)(2,1)} %convolution_convert_fusion.1.g_ref), channel_id=1, source_target_pairs={{8,0},{12,4},{16,8},{20,12},{24,16},{28,20},{9,1},{13,5},{17,9},{2... | collective-permute-start | bytes 1572872 | tf_op jit(solution)/shard_map/ppermute | solution.py:23
  80.2 3.7 %copy-start.3 = (bf16[1024,512]{1,0:T(8,128)(2,1)}, bf16[1024,512]{1,0:T(8,128)(2,1)S(1)}, u32[]{:S(2)}) copy-start(bf16[1024,512]{1,0:T(8,128)(2,1)S(1)} %collective-permute-done.rest_0_.rest_1_) | copy-start | bytes 3145732
  80.2 41.5 %collective-permute-start.8 = (bf16[512,512]{1,0:T(8,128)(2,1)}, bf16[512,512]{1,0:T(8,128)(2,1)}, u32[]{:S(2)}, u32[]{:S(2)}) collective-permute-start(bf16[512,512]{1,0:T(8,128)(2,1)} %convolution_convert_fusion.1.g_ref), channel_id=1, source_target_pairs={{16,0},{20,4},{24,8},{28,12},{17,1},{21,5},{25,9},{29,13},{18,2},{... | collective-permute-start | bytes 1572872 | tf_op jit(solution)/shard_map/ppermute | solution.py:23
  136.6 24.6 %copy-start.4 = (bf16[4,512,512]{2,1,0:T(8,128)(2,1)S(1)}, bf16[4,512,512]{2,1,0:T(8,128)(2,1)}, u32[]{:S(2)}) copy-start(bf16[4,512,512]{2,1,0:T(8,128)(2,1)} %copy.18) | copy-start | bytes 6291460
  136.6 6.0 %collective-permute-start.10 = (f32[2,4,4,128]{3,2,1,0:T(4,128)}, f32[2,4,4,128]{3,2,1,0:T(4,128)S(1)}, u32[]{:S(2)}, u32[]{:S(2)}) collective-permute-start(f32[2,4,4,128]{3,2,1,0:T(4,128)} %get-tuple-element.36.st_ref), channel_id=1, source_target_pairs={{8,0},{12,4},{16,8},{20,12},{24,16},{28,20},{9,1},{13,5},{17,9},{2... | collective-permute-start | bytes 49160 | tf_op jit(solution)/shard_map/ppermute | solution.py:23
  138.1 6.7 %collective-permute-start.11 = (f32[2,4,4,128]{3,2,1,0:T(4,128)}, f32[2,4,4,128]{3,2,1,0:T(4,128)S(1)}, u32[]{:S(2)}, u32[]{:S(2)}) collective-permute-start(f32[2,4,4,128]{3,2,1,0:T(4,128)} %get-tuple-element.36.st_ref), channel_id=1, source_target_pairs={{16,0},{20,4},{24,8},{28,12},{17,1},{21,5},{25,9},{29,13},{18,2},{... | collective-permute-start | bytes 49160 | tf_op jit(solution)/shard_map/ppermute | solution.py:23
  139.4 5.8 %collective-permute-start.9 = (f32[2,4,4,128]{3,2,1,0:T(4,128)}, f32[2,4,4,128]{3,2,1,0:T(4,128)S(1)}, u32[]{:S(2)}, u32[]{:S(2)}) collective-permute-start(f32[2,4,4,128]{3,2,1,0:T(4,128)} %get-tuple-element.36.st_ref), channel_id=1, source_target_pairs={{4,0},{8,4},{12,8},{16,12},{20,16},{24,20},{28,24},{5,1},{9,5},{13... | collective-permute-start | bytes 49160 | tf_op jit(solution)/shard_map/ppermute | solution.py:23
  142.6 2.6 %copy-start.5 = (f32[2,4,4,128]{3,2,1,0:T(4,128)}, f32[2,4,4,128]{3,2,1,0:T(4,128)S(1)}, u32[]{:S(2)}) copy-start(f32[2,4,4,128]{3,2,1,0:T(4,128)S(1)} %collective-permute-done.10.rest_5_) | copy-start | bytes 49156
  144.8 0.6 copy-start.6
  145.4 0.6 copy-start.7
Sparse Core Ops, SparseCore 0:
  9.6 36.6 all-gather.2
  136.8 24.4 all-gather.4

commit v15 on v12

--- a/solution.py
+++ b/solution.py
@@ -87,38 +87,51 @@
         st_ref[1, 0, pl.ds(n, 1), :] = col_to_row(delta)
 
 
-def key_kernel(n_levels, valid_ref, k_ref, v_ref, q_ref, g_ref, st_ref, *rest):
-    qf = rest[0 : 3 * n_levels : 3]
-    gf = rest[1 : 3 * n_levels : 3]
-    sf = rest[2 : 3 * n_levels : 3]
-    dk_ref, dv_ref = rest[3 * n_levels :]
+def key_part_kernel(n_levels, remote, valid_ref, k_ref, v_ref, q_ref, g_ref, st_ref, *rest):
     n_cand = 1 + WIN_MAX + n_levels
-    width = n_cand * BLK
     scale = HD ** (-0.5)
-    col = lax.broadcasted_iota(jnp.int32, (BLK, width), 1)
-    row = lax.broadcasted_iota(jnp.int32, (BLK, width), 0)
-    diag = row <= col
+    if remote:
+        qf = rest[0 : 3 * n_levels : 3]
+        gf = rest[1 : 3 * n_levels : 3]
+        sf = rest[2 : 3 * n_levels : 3]
+        dk_in, dv_in, dk_ref, dv_ref = rest[3 * n_levels :]
+    else:
+        dk_ref, dv_ref = rest
     for j in range(NB):
         rows = pl.ds(j * BLK, BLK)
+        if remote:
+            cands = [(qf[0], gf[0], sf[0], j + o - NB, o) for o in range(1, WIN_MAX + 1) if j + o >= NB]
+            cands += [(qf[mi], gf[mi], sf[mi], j, 1 + WIN_MAX + mi) for mi in range(n_levels)]
+        else:
+            cands = [(q_ref, g_ref, st_ref, j, 0)]
+            cands += [(q_ref, g_ref, st_ref, j + o, o) for o in range(1, WIN_MAX + 1) if j + o < NB]
+        width = len(cands) * BLK
+        col = lax.broadcasted_iota(jnp.int32, (BLK, width), 1)
+        row = lax.broadcasted_iota(jnp.int32, (BLK, width), 0)
+        allowed = None
+        for pos, (_, _, _, _, ci) in enumerate(cands):
+            inside = (col >= pos * BLK) & (col < (pos + 1) * BLK)
+            ok = (row <= col) if ci == 0 else (valid_ref[j * n_cand + ci] != 0)
+            term = inside & ok
+            allowed = term if allowed is None else allowed | term
         kj = k_ref[rows, :]
         vj = v_ref[rows, :]
-        cands = [(q_ref, g_ref, st_ref, j)]
-        for o in range(1, WIN_MAX + 1):
-            i = j + o
-            cands.append((q_ref, g_ref, st_ref, i) if i < NB else (qf[0], gf[0], sf[0], i - NB))
-        for mi in range(n_levels):
-            cands.append((qf[mi], gf[mi], sf[mi], j))
-        qcat = jnp.concatenate([qr[pl.ds(i * BLK, BLK), :] for qr, _, _, i in cands], axis=0)
-        gcat = jnp.concatenate([gr[pl.ds(i * BLK, BLK), :] for _, gr, _, i in cands], axis=0)
-        lse = jnp.concatenate([sr[0, 0, pl.ds(i, 1), :] for _, _, sr, i in cands], axis=1)
-        delta = jnp.concatenate([sr[1, 0, pl.ds(i, 1), :] for _, _, sr, i in cands], axis=1)
-        allowed = candidate_mask(valid_ref, j * n_cand, n_cand, diag)
+        qcat = jnp.concatenate([qr[pl.ds(i * BLK, BLK), :] for qr, _, _, i, _ in cands], axis=0)
+        gcat = jnp.concatenate([gr[pl.ds(i * BLK, BLK), :] for _, gr, _, i, _ in cands], axis=0)
+        lse = jnp.concatenate([sr[0, 0, pl.ds(i, 1), :] for _, _, sr, i, _ in cands], axis=1)
+        delta = jnp.concatenate([sr[1, 0, pl.ds(i, 1), :] for _, _, sr, i, _ in cands], axis=1)
         scores = jnp.where(allowed, dot_nt(kj, qcat) * scale, neg_large)
         probs = jnp.exp(scores - lse)
-        dv_ref[rows, :] = dot_nn(probs.astype(jnp.bfloat16), gcat).astype(jnp.bfloat16)
+        dv = dot_nn(probs.astype(jnp.bfloat16), gcat)
         d_prob = dot_nt(vj, gcat)
         d_score = (probs * (d_prob - delta) * scale).astype(jnp.bfloat16)
-        dk_ref[rows, :] = dot_nn(d_score, qcat).astype(jnp.bfloat16)
+        dk = dot_nn(d_score, qcat)
+        if remote:
+            dv_ref[rows, :] = (dv_in[rows, :] + dv).astype(jnp.bfloat16)
+            dk_ref[rows, :] = (dk_in[rows, :] + dk).astype(jnp.bfloat16)
+        else:
+            dv_ref[rows, :] = dv
+            dk_ref[rows, :] = dk
 
 
 def head_block(part):
@@ -158,23 +171,28 @@
     tokens, features = q.shape
     in_specs = [head_block(0)] * 4 + [stats_block(heads)]
     args = [k, v, q, g, stats]
+    own = pl.pallas_call(
+        functools.partial(key_part_kernel, n_levels, False),
+        grid_spec=pltpu.PrefetchScalarGridSpec(
+            num_scalar_prefetch=1, grid=(heads,), in_specs=in_specs,
+            out_specs=[head_block(0), head_block(0)],
+        ),
+        out_shape=[jax.ShapeDtypeStruct((tokens, features), jnp.float32)] * 2,
+        name="key_side_own",
+    )(valid, *args)
     for qa, ga, st in zip(q_from, g_from, st_from):
         in_specs += [head_block(0), head_block(0), stats_block(heads)]
         args += [qa, ga, st]
-    grid_spec = pltpu.PrefetchScalarGridSpec(
-        num_scalar_prefetch=1,
-        grid=(heads,),
-        in_specs=in_specs,
-        out_specs=[head_block(0), head_block(0)],
-    )
+    in_specs += [head_block(0), head_block(0)]
+    args += list(own)
     return pl.pallas_call(
-        functools.partial(key_kernel, n_levels),
-        grid_spec=grid_spec,
-        out_shape=[
-            jax.ShapeDtypeStruct((tokens, features), jnp.bfloat16),
-            jax.ShapeDtypeStruct((tokens, features), jnp.bfloat16),
-        ],
-        name="key_side",
+        functools.partial(key_part_kernel, n_levels, True),
+        grid_spec=pltpu.PrefetchScalarGridSpec(
+            num_scalar_prefetch=1, grid=(heads,), in_specs=in_specs,
+            out_specs=[head_block(0), head_block(0)],
+        ),
+        out_shape=[jax.ShapeDtypeStruct((tokens, features), jnp.bfloat16)] * 2,
+        name="key_side_remote",
     )(valid, *args)
 
 

time: 163 us -> 166 us (1.018)
  Pallas kernels: 25.6 us -> 32.5 us
  waiting for transfers between devices: 52.3 us -> 47 us
    pallas_call x1 -> x2, Pallas kernels: 10.6 us -> 17.5 us  [the longest x1 9.71 us: key_call(): pl.pallas_call(functools.partial(key_part_kernel, n_levels, True), grid_s...]
    ppermute x12, waiting for transfers between devices: 51.6 us -> 46.2 us  [passed_along(): return lax.ppermute(block, axis, route)]
    unnamed x18 -> x22, local copies, waits for them, and re-layouts: 5.24 us -> 6.48 us
  transfers between devices with their start and end apart: 15 -> 15, of which waited for: 8 -> 4; matrix products, arithmetic and copies ran while one was open for 12% -> 12% of each run, Pallas kernels for 7% -> 11%
where the time goes in v15:
time: 166 us; the launch traced here: 164 us
  waiting for transfers between devices  47 us (28%)
  starting transfers between devices  46.2 us (28%)
  Pallas kernels  32.5 us (20%)
  local copies, waits for them, and re-layouts  16.2 us (10%)
  between operations  14.3 us (9%)
  matrix products  7.13 us (4%)
    ppermute x12, waiting for transfers between devices, passed_along(): return lax.ppermute(block, axis, route)  46.2 us
    ppermute x12, starting transfers between devices, passed_along(): return lax.ppermute(block, axis, route)  42.4 us
    pallas_call x1, Pallas kernels, query_call(): pl.pallas_call(functools.partial(query_kernel, n_levels), grid_spec=grid_...  14.9 us
    pallas_call x1, Pallas kernels, key_call(): pl.pallas_call(functools.partial(key_part_kernel, n_levels, True), grid_s...  9.71 us
    pallas_call x1, Pallas kernels, key_call(): pl.pallas_call(functools.partial(key_part_kernel, n_levels, False), grid_...  7.83 us
    unnamed x22, local copies, waits for them, and re-layouts  6.48 us
    all_to_all x1, starting transfers between devices, local(): weight_cols = lax.all_to_all(out_weight, 'head', 1, 0, tiled=True)  3.74 us
    dot_general x1, matrix products, local(): jnp.dot(lax.all_gather(attended, 'head', axis=1, tiled=True), weight_cols...  3.63 us
  transfers between devices with their start and end apart: 15, of which 4 were waited for; matrix products, arithmetic and copies ran while one was open for 12% of the time, Pallas kernels for 11%

profile of v15, /device:TPU:0, one launch (start us, length us, event | category | flops | bytes accessed | tf_op | source)
XLA Modules:
  0.0 163.5 jit_solution(9883053649355185381)
XLA Ops:
  7.2 0.0 copy-start.1
  7.2 0.0 all-gather.3.cloned.1.call-start
  7.2 0.7 all-gather.3.cloned.1.call-update
  7.9 1.9 %constant_dynamic-update-slice_fusion.1 = bf16[1024,512]{1,0:T(8,128)(2,1)} fusion(bf16[512,512]{1,0:T(8,128)(2,1)} %k_ref.5), kind=kLoop, calls=%fused_computation.15 | loop fusion | bytes 1048576
  9.8 1.9 %constant_dynamic-update-slice_fusion = bf16[1024,512]{1,0:T(8,128)(2,1)} fusion(bf16[1024,512]{1,0:T(8,128)(2,1)} %constant_dynamic-update-slice_fusion.1, bf16[512,512]{1,0:T(8,128)(2,1)} %v_ref.5), kind=kLoop, calls=%fused_computation.14 | loop fusion | bytes 1048576 | tf_op jit(solution)/shard_map/concatenate | solution.py:229
  11.7 5.9 %collective-permute-start = (bf16[1024,512]{1,0:T(8,128)(2,1)}, bf16[1024,512]{1,0:T(8,128)(2,1)}, u32[]{:S(2)}, u32[]{:S(2)}) collective-permute-start(bf16[1024,512]{1,0:T(8,128)(2,1)} %constant_dynamic-update-slice_fusion), channel_id=1, source_target_pairs={{0,4},{4,8},{8,12},{12,16},{16,20},{20,24},{24,28},{1,5},{5,9},{9,... | collective-permute-start | bytes 3145736 | tf_op jit(solution)/shard_map/ppermute | solution.py:23
  17.6 3.5 %collective-permute-start.1 = (bf16[1024,512]{1,0:T(8,128)(2,1)}, bf16[1024,512]{1,0:T(8,128)(2,1)}, u32[]{:S(2)}, u32[]{:S(2)}) collective-permute-start(bf16[1024,512]{1,0:T(8,128)(2,1)} %constant_dynamic-update-slice_fusion), channel_id=1, source_target_pairs={{0,8},{4,12},{8,16},{12,20},{16,24},{20,28},{1,9},{5,13},{9,17},{1... | collective-permute-start | bytes 3145736 | tf_op jit(solution)/shard_map/ppermute | solution.py:23
  21.1 0.0 copy-done.1
  21.1 1.3 collective-permute-start.3
  22.4 1.3 collective-permute-start.4
  23.7 1.3 collective-permute-start.5
  25.0 3.9 %copy.17 = bf16[512,2048]{0,1:T(8,128)(2,1)} copy(bf16[512,2048]{1,0:T(8,128)(2,1)} %param.12) | data formatting | bytes 4194304 | tf_op args[3]
  28.9 3.7 %all-to-all-start = ((bf16[512,4,512]{0,2,1:T(8,128)(2,1)}), bf16[512,4,512]{0,2,1:T(8,128)(2,1)S(1)}, u32[]{:S(2)}, u32[]{:S(2)}) async-start(bf16[512,4,512]{0,2,1:T(8,128)(2,1)} %bitcast.32), calls=%async_computation | async-start | bytes 4194304 | tf_op jit(solution)/shard_map/all_to_all | solution.py:241
  32.6 0.0 all-gather.5.cloned.1.call-start
  32.7 0.0 copy-done.9
  32.7 0.6 gather_fusion.5
  33.4 0.6 gather_fusion.4
  34.0 0.6 gather_fusion.3
  34.7 0.0 copy-done
  34.7 0.6 gather_fusion.2
  35.4 0.1 and_bitcast_fusion.6
  35.5 0.1 constant_dynamic-slice_fusion
  35.6 0.1 copy.15
  35.7 0.6 reshape.55.valid_ref
  36.3 0.0 collective-permute-done.3.rest_0_
  36.3 21.4 %collective-permute-start.2 = (bf16[1024,512]{1,0:T(8,128)(2,1)}, bf16[1024,512]{1,0:T(8,128)(2,1)}, u32[]{:S(2)}, u32[]{:S(2)}) collective-permute-start(bf16[1024,512]{1,0:T(8,128)(2,1)} %constant_dynamic-update-slice_fusion), channel_id=1, source_target_pairs={{0,16},{4,20},{8,24},{12,28},{1,17},{5,21},{9,25},{13,29},{2,18},{... | collective-permute-start | bytes 3145736 | tf_op jit(solution)/shard_map/ppermute | solution.py:23
  57.8 0.6 gather_fusion.1
  58.4 0.0 copy-done.4
  58.4 0.0 all-gather.3.cloned.1.call-done
  58.4 3.5 %convolution_convert_fusion.1.g_ref = bf16[512,512]{1,0:T(8,128)(2,1)S(1)} fusion(bf16[512,2048]{1,0:T(8,128)(2,1)} %all-gather.3.cloned.1.call-done, bf16[512,2048]{1,0:T(8,128)(2,1)} %param.12), kind=kOutput, calls=%fused_computation.7 | convolution fusion | flops 1074003968 | bytes 4718592 | tf_op jit(solution)/shard_map/dot_general | solution.py:233
  61.9 0.0 copy-start.2
  61.9 0.0 collective-permute-done.4.rest_3_
  62.0 1.3 collective-permute-start.6
  63.3 9.4 %collective-permute-done.5.rest_6_ = bf16[512,512]{1,0:T(8,128)(2,1)} collective-permute-done((bf16[512,512]{1,0:T(8,128)(2,1)S(1)}, bf16[512,512]{1,0:T(8,128)(2,1)}, u32[]{:S(2)}, u32[]{:S(2)}) %collective-permute-start.5) | collective-permute-done | bytes 524320 | tf_op jit(solution)/shard_map/ppermute | solution.py:23
  72.7 1.3 collective-permute-start.7
  74.0 0.0 collective-permute-done.rest_0_.rest_1_
  74.0 1.3 collective-permute-start.8
  75.3 0.6 gather_fusion
  76.0 0.1 copy.16
  76.1 0.6 reshape.56.valid_ref
  76.8 0.0 all-to-all-done
  76.8 2.4 %copy.18 = bf16[4,512,512]{2,1,0:T(8,128)(2,1)} copy(bf16[4,512,512]{1,2,0:T(8,128)(2,1)S(1)} %bitcast.31) | data formatting | bytes 4194304 | tf_op jit(solution)/shard_map/all_to_all | solution.py:241
  79.1 0.0 collective-permute-done.1.rest_2_.rest_3_
  79.1 0.6 collective-permute-done.2.rest_4_.rest_5_
  79.7 0.0 collective-permute-done.6.rest_1_
  79.7 13.6 %collective-permute-done.7.rest_4_ = bf16[512,512]{1,0:T(8,128)(2,1)S(1)} collective-permute-done((bf16[512,512]{1,0:T(8,128)(2,1)S(1)}, bf16[512,512]{1,0:T(8,128)(2,1)S(1)}, u32[]{:S(2)}, u32[]{:S(2)}) %collective-permute-start.7) | collective-permute-done | bytes 524320 | tf_op jit(solution)/shard_map/ppermute | solution.py:23
  93.3 22.6 %collective-permute-done.8.rest_7_ = bf16[512,512]{1,0:T(8,128)(2,1)} collective-permute-done((bf16[512,512]{1,0:T(8,128)(2,1)S(1)}, bf16[512,512]{1,0:T(8,128)(2,1)}, u32[]{:S(2)}, u32[]{:S(2)}) %collective-permute-start.8) | collective-permute-done | bytes 524320 | tf_op jit(solution)/shard_map/ppermute | solution.py:23
  115.9 14.9 %query_side.1 = (bf16[512,512]{1,0:T(8,128)(2,1)}, bf16[512,512]{1,0:T(8,128)(2,1)}, f32[2,4,4,128]{3,2,1,0:T(4,128)}) custom-call(s32[28]{0:T(128)} %reshape.55.valid_ref, bf16[512,512]{1,0:T(8,128)(2,1)} %q_ref.5, bf16[512,512]{1,0:T(8,128)(2,1)} %copy-done.2, bf16[512,512]{1,0:T(8,128)(2,1)} %k_ref.5, bf16[512,512]{1,0:T(8,128)(2,1)} %v_ref.5, ...), custom_call_target="tpu_custom_call" | custom-call | tf_op jit(solution)/shard_map/query_side/pallas_call | solution.py:158
  130.9 0.0 copy-done.5
  130.9 0.0 all-gather.5.cloned.1.call-update
  130.9 1.3 collective-permute-start.10
  132.2 1.3 collective-permute-start.11
  133.5 1.3 collective-permute-start.9
  134.8 7.8 %key_side_own.1 = (f32[512,512]{1,0:T(8,128)}, f32[512,512]{1,0:T(8,128)}) custom-call(s32[28]{0:T(128)} %reshape.56.valid_ref, bf16[512,512]{1,0:T(8,128)(2,1)} %k_ref.5, bf16[512,512]{1,0:T(8,128)(2,1)} %v_ref.5, bf16[512,512]{1,0:T(8,128)(2,1)} %q_ref.5, bf16[512,512]{1,0:T(8,128)(2,1)} %copy-done.2, f32[2,4,4,128]{3,2,1,0:T(4,128)} %get-tuple-element.32.st_ref), custom_call_target="tpu_custom_call" | custom-call | tf_op jit(solution)/shard_map/key_side_own/pallas_call | solution.py:174
  142.6 0.0 collective-permute-done.10.rest_5_
  142.7 0.0 collective-permute-done.11.rest_8_
  142.7 0.0 collective-permute-done.9.rest_2_
  142.7 0.5 copy-done.6
  143.2 0.0 copy-done.7
  143.3 0.0 copy-done.8
  143.3 9.7 %key_side_remote.1 = (bf16[512,512]{1,0:T(8,128)(2,1)}, bf16[512,512]{1,0:T(8,128)(2,1)}) custom-call(s32[28]{0:T(128)} %reshape.56.valid_ref, bf16[512,512]{1,0:T(8,128)(2,1)} %k_ref.5, bf16[512,512]{1,0:T(8,128)(2,1)} %v_ref.5, bf16[512,512]{1,0:T(8,128)(2,1)} %q_ref.5, bf16[512,512]{1,0:T(8,128)(2,1)} %copy-done.2, ...), custom_call_target="tpu_custom_call" | custom-call | tf_op jit(solution)/shard_map/key_side_remote/pallas_call | solution.py:188
  153.0 0.0 all-gather.5.cloned.1.call-done
  153.0 0.0 copy-done.3
  153.0 3.6 %convolution_convert_fusion = bf16[512,512]{1,0:T(8,128)(2,1)} fusion(bf16[512,2048]{1,0:T(8,128)(2,1)} %all-gather.5.cloned.1.call-done, bf16[2048,512]{1,0:T(8,128)(2,1)S(1)} %bitcast.33), kind=kOutput, calls=%fused_computation.6 | convolution fusion | flops 1074003968 | bytes 4718592 | tf_op jit(solution)/shard_map/dot_general | solution.py:249
  (30 shorter events, 0.2 us)
Async XLA Ops:
  7.2 13.9 %copy-start.1 = (bf16[512,512]{1,0:T(8,128)(2,1)S(1)}, bf16[512,512]{1,0:T(8,128)(2,1)}, u32[]{:S(2)}) copy-start(bf16[512,512]{1,0:T(8,128)(2,1)} %q_ref.5) | copy-start | bytes 1572868
  7.2 51.2 %all-gather.3.cloned.1.call-start = ((), (), s32[]{:S(2)}) async-start(), calls=%async_computation.1 | async-start | bytes 2621440 | tf_op jit(solution)/shard_map/all_gather | solution.py:234
  11.7 62.2 %collective-permute-start = (bf16[1024,512]{1,0:T(8,128)(2,1)}, bf16[1024,512]{1,0:T(8,128)(2,1)}, u32[]{:S(2)}, u32[]{:S(2)}) collective-permute-start(bf16[1024,512]{1,0:T(8,128)(2,1)} %constant_dynamic-update-slice_fusion), channel_id=1, source_target_pairs={{0,4},{4,8},{8,12},{12,16},{16,20},{20,24},{24,28},{1,5},{5,9},{9,... | collective-permute-start | bytes 3145736 | tf_op jit(solution)/shard_map/ppermute | solution.py:23
  17.6 61.5 %collective-permute-start.1 = (bf16[1024,512]{1,0:T(8,128)(2,1)}, bf16[1024,512]{1,0:T(8,128)(2,1)}, u32[]{:S(2)}, u32[]{:S(2)}) collective-permute-start(bf16[1024,512]{1,0:T(8,128)(2,1)} %constant_dynamic-update-slice_fusion), channel_id=1, source_target_pairs={{0,8},{4,12},{8,16},{12,20},{16,24},{20,28},{1,9},{5,13},{9,17},{1... | collective-permute-start | bytes 3145736 | tf_op jit(solution)/shard_map/ppermute | solution.py:23
  21.1 15.3 %collective-permute-start.3 = (bf16[512,512]{1,0:T(8,128)(2,1)S(1)}, bf16[512,512]{1,0:T(8,128)(2,1)S(1)}, u32[]{:S(2)}, u32[]{:S(2)}) collective-permute-start(bf16[512,512]{1,0:T(8,128)(2,1)S(1)} %copy-done.1), channel_id=1, source_target_pairs={{4,0},{8,4},{12,8},{16,12},{20,16},{24,20},{28,24},{5,1},{9,5},{13... | collective-permute-start | bytes 1572872 | tf_op jit(solution)/shard_map/ppermute | solution.py:23
  22.4 39.6 %collective-permute-start.4 = (bf16[512,512]{1,0:T(8,128)(2,1)S(1)}, bf16[512,512]{1,0:T(8,128)(2,1)}, u32[]{:S(2)}, u32[]{:S(2)}) collective-permute-start(bf16[512,512]{1,0:T(8,128)(2,1)S(1)} %copy-done.1), channel_id=1, source_target_pairs={{8,0},{12,4},{16,8},{20,12},{24,16},{28,20},{9,1},{13,5},{17,9},{2... | collective-permute-start | bytes 1572872 | tf_op jit(solution)/shard_map/ppermute | solution.py:23
  23.7 49.0 %collective-permute-start.5 = (bf16[512,512]{1,0:T(8,128)(2,1)S(1)}, bf16[512,512]{1,0:T(8,128)(2,1)}, u32[]{:S(2)}, u32[]{:S(2)}) collective-permute-start(bf16[512,512]{1,0:T(8,128)(2,1)S(1)} %copy-done.1), channel_id=1, source_target_pairs={{16,0},{20,4},{24,8},{28,12},{17,1},{21,5},{25,9},{29,13},{18,2},{... | collective-permute-start | bytes 1572872 | tf_op jit(solution)/shard_map/ppermute | solution.py:23
  28.9 3.8 %copy-start.9 = (s32[32,5]{0,1:T(8,128)S(1)}, s32[32,5]{0,1:T(8,128)}, u32[]{:S(2)}) copy-start(s32[32,5]{0,1:T(8,128)} %param.15) | copy-start | bytes 1924
  28.9 5.8 %copy-start = (s32[32]{0:T(128)S(1)}, s32[32]{0:T(128)}, u32[]{:S(2)}) copy-start(s32[32]{0:T(128)} %param.14) | copy-start | bytes 388
  28.9 47.9 %all-to-all-start = ((bf16[512,4,512]{0,2,1:T(8,128)(2,1)}), bf16[512,4,512]{0,2,1:T(8,128)(2,1)S(1)}, u32[]{:S(2)}, u32[]{:S(2)}) async-start(bf16[512,4,512]{0,2,1:T(8,128)(2,1)} %bitcast.32), calls=%async_computation | async-start | bytes 4194304 | tf_op jit(solution)/shard_map/all_to_all | solution.py:241
  32.6 120.4 %all-gather.5.cloned.1.call-start = ((), (), s32[]{:S(2)}) async-start(), calls=%async_computation.2 | async-start | bytes 2621440 | tf_op jit(solution)/shard_map/all_gather | solution.py:250
  36.3 22.1 %copy-start.4 = (bf16[512,512]{1,0:T(8,128)(2,1)}, bf16[512,512]{1,0:T(8,128)(2,1)S(1)}, u32[]{:S(2)}) copy-start(bf16[512,512]{1,0:T(8,128)(2,1)S(1)} %collective-permute-done.3.rest_0_) | copy-start | bytes 1572868
  36.3 43.4 %collective-permute-start.2 = (bf16[1024,512]{1,0:T(8,128)(2,1)}, bf16[1024,512]{1,0:T(8,128)(2,1)}, u32[]{:S(2)}, u32[]{:S(2)}) collective-permute-start(bf16[1024,512]{1,0:T(8,128)(2,1)} %constant_dynamic-update-slice_fusion), channel_id=1, source_target_pairs={{0,16},{4,20},{8,24},{12,28},{1,17},{5,21},{9,25},{13,29},{2,18},{... | collective-permute-start | bytes 3145736 | tf_op jit(solution)/shard_map/ppermute | solution.py:23
  61.9 17.2 %copy-start.2 = (bf16[512,512]{1,0:T(8,128)(2,1)}, bf16[512,512]{1,0:T(8,128)(2,1)S(1)}, u32[]{:S(2)}) copy-start(bf16[512,512]{1,0:T(8,128)(2,1)S(1)} %convolution_convert_fusion.1.g_ref) | copy-start | bytes 1572868
  62.0 17.8 %collective-permute-start.6 = (bf16[512,512]{1,0:T(8,128)(2,1)S(1)}, bf16[512,512]{1,0:T(8,128)(2,1)}, u32[]{:S(2)}, u32[]{:S(2)}) collective-permute-start(bf16[512,512]{1,0:T(8,128)(2,1)S(1)} %convolution_convert_fusion.1.g_ref), channel_id=1, source_target_pairs={{4,0},{8,4},{12,8},{16,12},{20,16},{24,20},{28,24},{5,1},{9,5},{13... | collective-permute-start | bytes 1572872 | tf_op jit(solution)/shard_map/ppermute | solution.py:23
  72.7 20.6 %collective-permute-start.7 = (bf16[512,512]{1,0:T(8,128)(2,1)S(1)}, bf16[512,512]{1,0:T(8,128)(2,1)S(1)}, u32[]{:S(2)}, u32[]{:S(2)}) collective-permute-start(bf16[512,512]{1,0:T(8,128)(2,1)S(1)} %convolution_convert_fusion.1.g_ref), channel_id=1, source_target_pairs={{8,0},{12,4},{16,8},{20,12},{24,16},{28,20},{9,1},{13,5},{17,9},{2... | collective-permute-start | bytes 1572872 | tf_op jit(solution)/shard_map/ppermute | solution.py:23
  74.0 41.9 %collective-permute-start.8 = (bf16[512,512]{1,0:T(8,128)(2,1)S(1)}, bf16[512,512]{1,0:T(8,128)(2,1)}, u32[]{:S(2)}, u32[]{:S(2)}) collective-permute-start(bf16[512,512]{1,0:T(8,128)(2,1)S(1)} %convolution_convert_fusion.1.g_ref), channel_id=1, source_target_pairs={{16,0},{20,4},{24,8},{28,12},{17,1},{21,5},{25,9},{29,13},{18,2},{... | collective-permute-start | bytes 1572872 | tf_op jit(solution)/shard_map/ppermute | solution.py:23
  93.3 37.6 %copy-start.5 = (bf16[512,512]{1,0:T(8,128)(2,1)}, bf16[512,512]{1,0:T(8,128)(2,1)S(1)}, u32[]{:S(2)}) copy-start(bf16[512,512]{1,0:T(8,128)(2,1)S(1)} %collective-permute-done.7.rest_4_) | copy-start | bytes 1572868
  130.9 11.7 %collective-permute-start.10 = (f32[2,4,4,128]{3,2,1,0:T(4,128)}, f32[2,4,4,128]{3,2,1,0:T(4,128)S(1)}, u32[]{:S(2)}, u32[]{:S(2)}) collective-permute-start(f32[2,4,4,128]{3,2,1,0:T(4,128)} %get-tuple-element.32.st_ref), channel_id=1, source_target_pairs={{8,0},{12,4},{16,8},{20,12},{24,16},{28,20},{9,1},{13,5},{17,9},{2... | collective-permute-start | bytes 49160 | tf_op jit(solution)/shard_map/ppermute | solution.py:23
  132.2 10.5 %collective-permute-start.11 = (f32[2,4,4,128]{3,2,1,0:T(4,128)}, f32[2,4,4,128]{3,2,1,0:T(4,128)S(1)}, u32[]{:S(2)}, u32[]{:S(2)}) collective-permute-start(f32[2,4,4,128]{3,2,1,0:T(4,128)} %get-tuple-element.32.st_ref), channel_id=1, source_target_pairs={{16,0},{20,4},{24,8},{28,12},{17,1},{21,5},{25,9},{29,13},{18,2},{... | collective-permute-start | bytes 49160 | tf_op jit(solution)/shard_map/ppermute | solution.py:23
  133.5 9.2 %collective-permute-start.9 = (f32[2,4,4,128]{3,2,1,0:T(4,128)}, f32[2,4,4,128]{3,2,1,0:T(4,128)S(1)}, u32[]{:S(2)}, u32[]{:S(2)}) collective-permute-start(f32[2,4,4,128]{3,2,1,0:T(4,128)} %get-tuple-element.32.st_ref), channel_id=1, source_target_pairs={{4,0},{8,4},{12,8},{16,12},{20,16},{24,20},{28,24},{5,1},{9,5},{13... | collective-permute-start | bytes 49160 | tf_op jit(solution)/shard_map/ppermute | solution.py:23
  142.6 0.6 copy-start.6
  142.7 0.6 copy-start.7
  142.7 0.6 copy-start.8
  143.3 9.7 %copy-start.3 = (bf16[4,512,512]{2,1,0:T(8,128)(2,1)S(1)}, bf16[4,512,512]{2,1,0:T(8,128)(2,1)}, u32[]{:S(2)}) copy-start(bf16[4,512,512]{2,1,0:T(8,128)(2,1)} %copy.18) | copy-start | bytes 6291460
Sparse Core Ops, SparseCore 0:
  9.6 25.2 all-gather.2
  131.0 19.8 all-gather.4

commit v16 on v12

--- a/solution.py
+++ b/solution.py
@@ -121,6 +121,26 @@
         dk_ref[rows, :] = dot_nn(d_score, qcat).astype(jnp.bfloat16)
 
 
+def project_kernel(a_ref, w_ref, o_ref):
+    o_ref[...] = dot_nn(a_ref[...], w_ref[...]).astype(o_ref.dtype)
+
+
+def projected(a, w):
+    rows = a.shape[0]
+    tile = BLK if rows % BLK == 0 else rows
+    return pl.pallas_call(
+        project_kernel,
+        grid=(rows // tile,),
+        in_specs=[
+            pl.BlockSpec((tile, a.shape[1]), lambda i: (i, 0)),
+            pl.BlockSpec(w.shape, lambda i: (0, 0)),
+        ],
+        out_specs=pl.BlockSpec((tile, w.shape[1]), lambda i: (i, 0)),
+        out_shape=jax.ShapeDtypeStruct((rows, w.shape[1]), jnp.bfloat16),
+        name="output_projection",
+    )(a, w)
+
+
 def head_block(part):
     return pl.BlockSpec((NB * BLK, HD), lambda h, valid: (part, h))
 
@@ -228,11 +248,7 @@
     attended, query_grad, stats = query_call(
         valid_q, queries, g, keys, values, kv_from, heads_local, n_levels
     )
-    output = jnp.dot(
-        lax.all_gather(attended, "head", axis=1, tiled=True),
-        weight_cols,
-        preferred_element_type=jnp.float32,
-    ).astype(jnp.bfloat16)
+    output = projected(lax.all_gather(attended, "head", axis=1, tiled=True), weight_cols)
 
     st_from = [passed_along(stats, "ctx", -(2**m)) for m in levels]
     key_grad, value_grad = key_call(

time: 163 us -> 164 us (level)
  Pallas kernels: 25.6 us -> 30.6 us
  matrix products: 7.93 us -> 4.3 us
  waiting for transfers between devices: 52.3 us -> 55.9 us
  local copies, waits for them, and re-layouts: 14.9 us -> 11.4 us
    pallas_call x0 -> x1, Pallas kernels: none -> 5.06 us  [projected(): pl.pallas_call(project_kernel, grid=(rows // tile,), in_specs=[pl.BlockSp...]
    dot_general x1 -> x0, matrix products: 3.63 us -> none  [local(): jnp.dot(lax.all_gather(attended, 'head', axis=1, tiled=True), weight_cols...]
    ppermute x12, waiting for transfers between devices: 51.6 us -> 55 us  [passed_along(): return lax.ppermute(block, axis, route)]
    unnamed x18 -> x17, local copies, waits for them, and re-layouts: 5.24 us -> 2.69 us
  transfers between devices with their start and end apart: 15 -> 15, of which waited for: 8 -> 9; matrix products, arithmetic and copies ran while one was open for 12% -> 9% of each run, Pallas kernels for 7% -> 7%
where the time goes in v16:
time: 164 us; the launch traced here: 163 us
  waiting for transfers between devices  55.9 us (34%)
  starting transfers between devices  46.3 us (28%)
  Pallas kernels  30.6 us (19%)
  between operations  14.3 us (9%)
  local copies, waits for them, and re-layouts  11.4 us (7%)
  matrix products  4.3 us (3%)
    ppermute x12, waiting for transfers between devices, passed_along(): return lax.ppermute(block, axis, route)  55 us
    ppermute x12, starting transfers between devices, passed_along(): return lax.ppermute(block, axis, route)  42.4 us
    pallas_call x1, Pallas kernels, query_call(): pl.pallas_call(functools.partial(query_kernel, n_levels), grid_spec=grid_...  14.9 us
    pallas_call x1, Pallas kernels, key_call(): pl.pallas_call(functools.partial(key_kernel, n_levels), grid_spec=grid_sp...  10.6 us
    pallas_call x1, Pallas kernels, projected(): pl.pallas_call(project_kernel, grid=(rows // tile,), in_specs=[pl.BlockSp...  5.06 us
    dot_general x1, matrix products, local(): lax.dot_general(lax.all_gather(d_out, 'head', axis=1, tiled=True), out_we...  4.3 us
    all_to_all x1, starting transfers between devices, local(): weight_cols = lax.all_to_all(out_weight, 'head', 1, 0, tiled=True)  3.75 us
  transfers between devices with their start and end apart: 15, of which 9 were waited for; matrix products, arithmetic and copies ran while one was open for 9% of the time, Pallas kernels for 7%

profile of v16, /device:TPU:0, one launch (start us, length us, event | category | flops | bytes accessed | tf_op | source)
XLA Modules:
  0.0 163.0 jit_solution(8530688789345065726)
XLA Ops:
  7.2 0.0 copy-start.3
  7.2 0.0 all-gather.3.cloned.1.call-start
  7.2 0.7 all-gather.3.cloned.1.call-update
  7.9 1.9 %constant_dynamic-update-slice_fusion.1 = bf16[1024,512]{1,0:T(8,128)(2,1)} fusion(bf16[512,512]{1,0:T(8,128)(2,1)} %k_ref.3), kind=kLoop, calls=%fused_computation.15 | loop fusion | bytes 1048576
  9.8 1.9 %constant_dynamic-update-slice_fusion = bf16[1024,512]{1,0:T(8,128)(2,1)} fusion(bf16[1024,512]{1,0:T(8,128)(2,1)} %constant_dynamic-update-slice_fusion.1, bf16[512,512]{1,0:T(8,128)(2,1)} %v_ref.3), kind=kLoop, calls=%fused_computation.14 | loop fusion | bytes 1048576 | tf_op jit(solution)/shard_map/concatenate | solution.py:231
  11.7 4.9 %collective-permute-start = (bf16[1024,512]{1,0:T(8,128)(2,1)}, bf16[1024,512]{1,0:T(8,128)(2,1)S(1)}, u32[]{:S(2)}, u32[]{:S(2)}) collective-permute-start(bf16[1024,512]{1,0:T(8,128)(2,1)} %constant_dynamic-update-slice_fusion), channel_id=1, source_target_pairs={{0,4},{4,8},{8,12},{12,16},{16,20},{20,24},{24,28},{1,5},{5,9},{9,... | collective-permute-start | bytes 3145736 | tf_op jit(solution)/shard_map/ppermute | solution.py:23
  16.6 4.4 %collective-permute-start.1 = (bf16[1024,512]{1,0:T(8,128)(2,1)}, bf16[1024,512]{1,0:T(8,128)(2,1)}, u32[]{:S(2)}, u32[]{:S(2)}) collective-permute-start(bf16[1024,512]{1,0:T(8,128)(2,1)} %constant_dynamic-update-slice_fusion), channel_id=1, source_target_pairs={{0,8},{4,12},{8,16},{12,20},{16,24},{20,28},{1,9},{5,13},{9,17},{1... | collective-permute-start | bytes 3145736 | tf_op jit(solution)/shard_map/ppermute | solution.py:23
  21.0 1.3 collective-permute-start.3
  22.3 1.3 collective-permute-start.4
  23.6 1.3 collective-permute-start.5
  24.9 0.0 copy-done.3
  24.9 1.5 copy.19
  26.4 0.0 copy-start.7
  26.4 0.0 copy-start
  26.4 3.7 %all-to-all-start = ((bf16[512,4,512]{2,0,1:T(8,128)(2,1)}), bf16[512,4,512]{2,0,1:T(8,128)(2,1)S(1)}, u32[]{:S(2)}, u32[]{:S(2)}) async-start(bf16[512,4,512]{2,0,1:T(8,128)(2,1)} %bitcast.34), calls=%async_computation | async-start | bytes 4194304 | tf_op jit(solution)/shard_map/all_to_all | solution.py:243
  30.1 0.0 all-gather.5.cloned.1.call-start
  30.2 0.0 copy-done.7
  30.2 0.6 gather_fusion.5
  30.9 0.6 gather_fusion.4
  31.5 0.6 gather_fusion.3
  32.2 0.0 copy-done
  32.2 0.6 gather_fusion.2
  32.9 0.1 and_bitcast_fusion.6
  33.0 0.1 constant_dynamic-slice_fusion
  33.1 0.1 copy.14
  33.2 0.6 reshape.55.valid_ref
  33.8 2.5 %collective-permute-done.3.rest_0_ = bf16[512,512]{1,0:T(8,128)(2,1)} collective-permute-done((bf16[512,512]{1,0:T(8,128)(2,1)}, bf16[512,512]{1,0:T(8,128)(2,1)}, u32[]{:S(2)}, u32[]{:S(2)}) %collective-permute-start.3) | collective-permute-done | bytes 524320 | tf_op jit(solution)/shard_map/ppermute | solution.py:23
  36.3 21.5 %collective-permute-start.2 = (bf16[1024,512]{1,0:T(8,128)(2,1)}, bf16[1024,512]{1,0:T(8,128)(2,1)}, u32[]{:S(2)}, u32[]{:S(2)}) collective-permute-start(bf16[1024,512]{1,0:T(8,128)(2,1)} %constant_dynamic-update-slice_fusion), channel_id=1, source_target_pairs={{0,16},{4,20},{8,24},{12,28},{1,17},{5,21},{9,25},{13,29},{2,18},{... | collective-permute-start | bytes 3145736 | tf_op jit(solution)/shard_map/ppermute | solution.py:23
  57.8 0.6 gather_fusion.1
  58.5 0.0 all-gather.3.cloned.1.call-done
  58.5 4.3 %convolution_convert_fusion.g_ref = bf16[512,512]{1,0:T(8,128)(2,1)} fusion(bf16[512,2048]{1,0:T(8,128)(2,1)} %all-gather.3.cloned.1.call-done, bf16[512,2048]{1,0:T(8,128)(2,1)} %param.12), kind=kOutput, calls=%fused_computation.7 | convolution fusion | flops 1074003968 | bytes 4718592 | tf_op jit(solution)/shard_map/dot_general | solution.py:235
  62.8 0.0 collective-permute-done.4.rest_3_
  62.8 1.3 collective-permute-start.6
  64.1 8.8 %collective-permute-done.5.rest_6_ = bf16[512,512]{1,0:T(8,128)(2,1)} collective-permute-done((bf16[512,512]{1,0:T(8,128)(2,1)}, bf16[512,512]{1,0:T(8,128)(2,1)}, u32[]{:S(2)}, u32[]{:S(2)}) %collective-permute-start.5) | collective-permute-done | bytes 524320 | tf_op jit(solution)/shard_map/ppermute | solution.py:23
  72.8 1.3 collective-permute-start.7
  74.1 0.0 collective-permute-done.rest_0_.rest_1_
  74.1 0.0 copy-start.2
  74.1 1.3 collective-permute-start.8
  75.4 0.6 gather_fusion
  76.2 0.1 copy.15
  76.3 0.6 reshape.56.valid_ref
  76.8 0.0 collective-permute-done.1.rest_2_.rest_3_
  76.9 2.9 %collective-permute-done.2.rest_4_.rest_5_ = bf16[1024,512]{1,0:T(8,128)(2,1)} collective-permute-done((bf16[1024,512]{1,0:T(8,128)(2,1)}, bf16[1024,512]{1,0:T(8,128)(2,1)}, u32[]{:S(2)}, u32[]{:S(2)}) %collective-permute-start.2) | collective-permute-done | bytes 1048608 | tf_op jit(solution)/shard_map/ppermute | solution.py:23
  79.8 0.0 all-to-all-done
  79.8 0.0 copy-start.1
  79.8 0.0 collective-permute-done.6.rest_1_
  79.8 13.8 %collective-permute-done.7.rest_4_ = bf16[512,512]{1,0:T(8,128)(2,1)} collective-permute-done((bf16[512,512]{1,0:T(8,128)(2,1)}, bf16[512,512]{1,0:T(8,128)(2,1)}, u32[]{:S(2)}, u32[]{:S(2)}) %collective-permute-start.7) | collective-permute-done | bytes 524320 | tf_op jit(solution)/shard_map/ppermute | solution.py:23
  93.5 22.5 %collective-permute-done.8.rest_7_ = bf16[512,512]{1,0:T(8,128)(2,1)} collective-permute-done((bf16[512,512]{1,0:T(8,128)(2,1)}, bf16[512,512]{1,0:T(8,128)(2,1)}, u32[]{:S(2)}, u32[]{:S(2)}) %collective-permute-start.8) | collective-permute-done | bytes 524320 | tf_op jit(solution)/shard_map/ppermute | solution.py:23
  116.1 0.0 copy-done.2
  116.1 14.9 %query_side.1 = (bf16[512,512]{1,0:T(8,128)(2,1)}, bf16[512,512]{1,0:T(8,128)(2,1)}, f32[2,4,4,128]{3,2,1,0:T(4,128)}) custom-call(s32[28]{0:T(128)} %reshape.55.valid_ref, bf16[512,512]{1,0:T(8,128)(2,1)} %q_ref.3, bf16[512,512]{1,0:T(8,128)(2,1)} %convolution_convert_fusion.g_ref, bf16[512,512]{1,0:T(8,128)(2,1)} %k_ref.3, bf16[512,512]{1,0:T(8,128)(2,1)} %v_ref.3, ...), custom_call_target="tpu_custom_call" | custom-call | tf_op jit(solution)/shard_map/query_side/pallas_call | solution.py:165
  131.0 0.0 copy-done.1
  131.0 0.0 all-gather.5.cloned.1.call-update
  131.0 1.3 collective-permute-start.10
  132.3 1.3 collective-permute-start.11
  133.6 1.3 collective-permute-start.9
  134.9 1.9 %collective-permute-done.10.rest_5_ = f32[2,4,4,128]{3,2,1,0:T(4,128)S(1)} collective-permute-done((f32[2,4,4,128]{3,2,1,0:T(4,128)}, f32[2,4,4,128]{3,2,1,0:T(4,128)S(1)}, u32[]{:S(2)}, u32[]{:S(2)}) %collective-permute-start.10) | collective-permute-done | bytes 16416 | tf_op jit(solution)/shard_map/ppermute | solution.py:23
  136.9 2.2 %collective-permute-done.11.rest_8_ = f32[2,4,4,128]{3,2,1,0:T(4,128)S(1)} collective-permute-done((f32[2,4,4,128]{3,2,1,0:T(4,128)}, f32[2,4,4,128]{3,2,1,0:T(4,128)S(1)}, u32[]{:S(2)}, u32[]{:S(2)}) %collective-permute-start.11) | collective-permute-done | bytes 16416 | tf_op jit(solution)/shard_map/ppermute | solution.py:23
  139.1 0.4 collective-permute-done.9.rest_2_
  139.5 0.0 copy-done.4
  139.5 0.2 copy-done.5
  139.7 0.6 copy-done.6
  140.3 10.6 %key_side.1 = (bf16[512,512]{1,0:T(8,128)(2,1)}, bf16[512,512]{1,0:T(8,128)(2,1)}) custom-call(s32[28]{0:T(128)} %reshape.56.valid_ref, bf16[512,512]{1,0:T(8,128)(2,1)} %k_ref.3, bf16[512,512]{1,0:T(8,128)(2,1)} %v_ref.3, bf16[512,512]{1,0:T(8,128)(2,1)} %q_ref.3, bf16[512,512]{1,0:T(8,128)(2,1)} %convolution_convert_fusion.g_ref, ...), custom_call_target="tpu_custom_call" | custom-call | tf_op jit(solution)/shard_map/key_side/pallas_call | solution.py:190
  150.9 0.2 all-gather.5.cloned.1.call-done.a_ref
  151.1 5.1 %output_projection.1 = bf16[512,512]{1,0:T(8,128)(2,1)} custom-call(bf16[512,2048]{1,0:T(8,128)(2,1)} %all-gather.5.cloned.1.call-done.a_ref, bf16[2048,512]{1,0:T(8,128)(2,1)} %bitcast.33), custom_call_target="tpu_custom_call" | custom-call | tf_op jit(solution)/shard_map/output_projection/pallas_call | solution.py:131
  (24 shorter events, 0.2 us)
Async XLA Ops:
  7.2 17.7 %copy-start.3 = (bf16[512,2048]{1,0:T(8,128)(2,1)S(1)}, bf16[512,2048]{1,0:T(8,128)(2,1)}, u32[]{:S(2)}) copy-start(bf16[512,2048]{1,0:T(8,128)(2,1)} %param.12) | copy-start | bytes 6291460
  7.2 51.3 %all-gather.3.cloned.1.call-start = ((), (), s32[]{:S(2)}) async-start(), calls=%async_computation.1 | async-start | bytes 2621440 | tf_op jit(solution)/shard_map/all_gather | solution.py:236
  11.7 62.4 %collective-permute-start = (bf16[1024,512]{1,0:T(8,128)(2,1)}, bf16[1024,512]{1,0:T(8,128)(2,1)S(1)}, u32[]{:S(2)}, u32[]{:S(2)}) collective-permute-start(bf16[1024,512]{1,0:T(8,128)(2,1)} %constant_dynamic-update-slice_fusion), channel_id=1, source_target_pairs={{0,4},{4,8},{8,12},{12,16},{16,20},{20,24},{24,28},{1,5},{5,9},{9,... | collective-permute-start | bytes 3145736 | tf_op jit(solution)/shard_map/ppermute | solution.py:23
  16.6 60.3 %collective-permute-start.1 = (bf16[1024,512]{1,0:T(8,128)(2,1)}, bf16[1024,512]{1,0:T(8,128)(2,1)}, u32[]{:S(2)}, u32[]{:S(2)}) collective-permute-start(bf16[1024,512]{1,0:T(8,128)(2,1)} %constant_dynamic-update-slice_fusion), channel_id=1, source_target_pairs={{0,8},{4,12},{8,16},{12,20},{16,24},{20,28},{1,9},{5,13},{9,17},{1... | collective-permute-start | bytes 3145736 | tf_op jit(solution)/shard_map/ppermute | solution.py:23
  21.0 15.3 %collective-permute-start.3 = (bf16[512,512]{1,0:T(8,128)(2,1)}, bf16[512,512]{1,0:T(8,128)(2,1)}, u32[]{:S(2)}, u32[]{:S(2)}) collective-permute-start(bf16[512,512]{1,0:T(8,128)(2,1)} %q_ref.3), channel_id=1, source_target_pairs={{4,0},{8,4},{12,8},{16,12},{20,16},{24,20},{28,24},{5,1},{9,5},{13... | collective-permute-start | bytes 1572872 | tf_op jit(solution)/shard_map/ppermute | solution.py:23
  22.3 40.5 %collective-permute-start.4 = (bf16[512,512]{1,0:T(8,128)(2,1)}, bf16[512,512]{1,0:T(8,128)(2,1)}, u32[]{:S(2)}, u32[]{:S(2)}) collective-permute-start(bf16[512,512]{1,0:T(8,128)(2,1)} %q_ref.3), channel_id=1, source_target_pairs={{8,0},{12,4},{16,8},{20,12},{24,16},{28,20},{9,1},{13,5},{17,9},{2... | collective-permute-start | bytes 1572872 | tf_op jit(solution)/shard_map/ppermute | solution.py:23
  23.6 49.2 %collective-permute-start.5 = (bf16[512,512]{1,0:T(8,128)(2,1)}, bf16[512,512]{1,0:T(8,128)(2,1)}, u32[]{:S(2)}, u32[]{:S(2)}) collective-permute-start(bf16[512,512]{1,0:T(8,128)(2,1)} %q_ref.3), channel_id=1, source_target_pairs={{16,0},{20,4},{24,8},{28,12},{17,1},{21,5},{25,9},{29,13},{18,2},{... | collective-permute-start | bytes 1572872 | tf_op jit(solution)/shard_map/ppermute | solution.py:23
  26.4 3.8 %copy-start.7 = (s32[32,5]{0,1:T(8,128)S(1)}, s32[32,5]{0,1:T(8,128)}, u32[]{:S(2)}) copy-start(s32[32,5]{0,1:T(8,128)} %param.15) | copy-start | bytes 1924
  26.4 5.8 %copy-start = (s32[32]{0:T(128)S(1)}, s32[32]{0:T(128)}, u32[]{:S(2)}) copy-start(s32[32]{0:T(128)} %param.14) | copy-start | bytes 388
  26.4 53.4 %all-to-all-start = ((bf16[512,4,512]{2,0,1:T(8,128)(2,1)}), bf16[512,4,512]{2,0,1:T(8,128)(2,1)S(1)}, u32[]{:S(2)}, u32[]{:S(2)}) async-start(bf16[512,4,512]{2,0,1:T(8,128)(2,1)} %bitcast.34), calls=%async_computation | async-start | bytes 4194304 | tf_op jit(solution)/shard_map/all_to_all | solution.py:243
  30.1 120.9 %all-gather.5.cloned.1.call-start = ((), (), s32[]{:S(2)}) async-start(), calls=%async_computation.2 | async-start | bytes 2621440 | tf_op jit(solution)/shard_map/all_gather | solution.py:251
  36.3 43.5 %collective-permute-start.2 = (bf16[1024,512]{1,0:T(8,128)(2,1)}, bf16[1024,512]{1,0:T(8,128)(2,1)}, u32[]{:S(2)}, u32[]{:S(2)}) collective-permute-start(bf16[1024,512]{1,0:T(8,128)(2,1)} %constant_dynamic-update-slice_fusion), channel_id=1, source_target_pairs={{0,16},{4,20},{8,24},{12,28},{1,17},{5,21},{9,25},{13,29},{2,18},{... | collective-permute-start | bytes 3145736 | tf_op jit(solution)/shard_map/ppermute | solution.py:23
  62.8 17.0 %collective-permute-start.6 = (bf16[512,512]{1,0:T(8,128)(2,1)}, bf16[512,512]{1,0:T(8,128)(2,1)}, u32[]{:S(2)}, u32[]{:S(2)}) collective-permute-start(bf16[512,512]{1,0:T(8,128)(2,1)} %convolution_convert_fusion.g_ref), channel_id=1, source_target_pairs={{4,0},{8,4},{12,8},{16,12},{20,16},{24,20},{28,24},{5,1},{9,5},{13... | collective-permute-start | bytes 1572872 | tf_op jit(solution)/shard_map/ppermute | solution.py:23
  72.8 20.7 %collective-permute-start.7 = (bf16[512,512]{1,0:T(8,128)(2,1)}, bf16[512,512]{1,0:T(8,128)(2,1)}, u32[]{:S(2)}, u32[]{:S(2)}) collective-permute-start(bf16[512,512]{1,0:T(8,128)(2,1)} %convolution_convert_fusion.g_ref), channel_id=1, source_target_pairs={{8,0},{12,4},{16,8},{20,12},{24,16},{28,20},{9,1},{13,5},{17,9},{2... | collective-permute-start | bytes 1572872 | tf_op jit(solution)/shard_map/ppermute | solution.py:23
  74.1 41.9 %copy-start.2 = (bf16[1024,512]{1,0:T(8,128)(2,1)}, bf16[1024,512]{1,0:T(8,128)(2,1)S(1)}, u32[]{:S(2)}) copy-start(bf16[1024,512]{1,0:T(8,128)(2,1)S(1)} %collective-permute-done.rest_0_.rest_1_) | copy-start | bytes 3145732
  74.1 41.9 %collective-permute-start.8 = (bf16[512,512]{1,0:T(8,128)(2,1)}, bf16[512,512]{1,0:T(8,128)(2,1)}, u32[]{:S(2)}, u32[]{:S(2)}) collective-permute-start(bf16[512,512]{1,0:T(8,128)(2,1)} %convolution_convert_fusion.g_ref), channel_id=1, source_target_pairs={{16,0},{20,4},{24,8},{28,12},{17,1},{21,5},{25,9},{29,13},{18,2},{... | collective-permute-start | bytes 1572872 | tf_op jit(solution)/shard_map/ppermute | solution.py:23
  79.8 51.2 %copy-start.1 = (bf16[512,4,512]{2,0,1:T(8,128)(2,1)}, bf16[512,4,512]{2,0,1:T(8,128)(2,1)S(1)}, u32[]{:S(2)}) copy-start(bf16[512,4,512]{2,0,1:T(8,128)(2,1)S(1)} %all-to-all-done) | copy-start | bytes 6291460
  131.0 5.8 %collective-permute-start.10 = (f32[2,4,4,128]{3,2,1,0:T(4,128)}, f32[2,4,4,128]{3,2,1,0:T(4,128)S(1)}, u32[]{:S(2)}, u32[]{:S(2)}) collective-permute-start(f32[2,4,4,128]{3,2,1,0:T(4,128)} %get-tuple-element.30.st_ref), channel_id=1, source_target_pairs={{8,0},{12,4},{16,8},{20,12},{24,16},{28,20},{9,1},{13,5},{17,9},{2... | collective-permute-start | bytes 49160 | tf_op jit(solution)/shard_map/ppermute | solution.py:23
  132.3 6.7 %collective-permute-start.11 = (f32[2,4,4,128]{3,2,1,0:T(4,128)}, f32[2,4,4,128]{3,2,1,0:T(4,128)S(1)}, u32[]{:S(2)}, u32[]{:S(2)}) collective-permute-start(f32[2,4,4,128]{3,2,1,0:T(4,128)} %get-tuple-element.30.st_ref), channel_id=1, source_target_pairs={{16,0},{20,4},{24,8},{28,12},{17,1},{21,5},{25,9},{29,13},{18,2},{... | collective-permute-start | bytes 49160 | tf_op jit(solution)/shard_map/ppermute | solution.py:23
  133.6 5.8 %collective-permute-start.9 = (f32[2,4,4,128]{3,2,1,0:T(4,128)}, f32[2,4,4,128]{3,2,1,0:T(4,128)S(1)}, u32[]{:S(2)}, u32[]{:S(2)}) collective-permute-start(f32[2,4,4,128]{3,2,1,0:T(4,128)} %get-tuple-element.30.st_ref), channel_id=1, source_target_pairs={{4,0},{8,4},{12,8},{16,12},{20,16},{24,20},{28,24},{5,1},{9,5},{13... | collective-permute-start | bytes 49160 | tf_op jit(solution)/shard_map/ppermute | solution.py:23
  136.9 2.6 %copy-start.4 = (f32[2,4,4,128]{3,2,1,0:T(4,128)}, f32[2,4,4,128]{3,2,1,0:T(4,128)S(1)}, u32[]{:S(2)}) copy-start(f32[2,4,4,128]{3,2,1,0:T(4,128)S(1)} %collective-permute-done.10.rest_5_) | copy-start | bytes 49156
  139.1 0.6 copy-start.5
  139.7 0.6 copy-start.6
Sparse Core Ops, SparseCore 0:
  9.6 25.3 all-gather.2
  131.1 19.8 all-gather.4
